TPU v7x, 32 devices: a whole 2x2x4 slice. The times are simulated.
32 devices in a mesh: grp: 2 (over y), tm: 4 (over z), height: 4 (over x, core).
Axes of the slice: x: 2, y: 2, z: 4, core: 2. Of those that a mesh axis runs over, the one named last changes fastest.
Arguments:
- latents: bfloat16 [8, 8, 160, 384], P(('grp', 'tm'), 'height'), parts along dimension 0, may hold values from -6 to 6
- gain: float32 [384], replicated, may hold values from 0.1 to 1.9
- bias: float32 [384], replicated, may hold values from -3 to 3
- weight: bfloat16 [10368, 384], replicated, may hold values from -0.0625 to 0.0625
- cotangent: bfloat16 [8, 8, 160, 384], P(('grp', 'tm'), 'height'), parts along dimension 0, may hold values from -6 to 6
Outputs:
- output: bfloat16 [8, 8, 160, 384], P(('grp', 'tm'), 'height'), parts along dimension 0
- latent_grad: bfloat16 [8, 8, 160, 384], P(('grp', 'tm'), 'height'), parts along dimension 0
- weight_grad: float32 [20736, 384], P(('grp', 'tm'), 'height'), parts along dimension 0
There are 2 independent parts, one for each index of `grp`. A program takes and returns all parts, laid end to end along the dimension named above; an argument that names none is the same for every part. Nothing has to cross between parts.
All inputs are finite; a program needn't handle non-finite values.
Results may differ from a plain program's by a relative error of at most 0.0029.
Values may be sent and summed in bfloat16 or wider, within the bound.
No kernel may reach another device: no remote copies, remote signals or barrier semaphores. Data moves between devices by JAX's collectives and lax.ppermute only.
A program may use at most 128 MiB of HBM per device.

v0:
```python
import math

import jax
import jax.numpy as jnp
from jax import lax
from jax.sharding import PartitionSpec as P


def shifted_2(value, axis, by):
    devices = lax.axis_size(axis)
    pairs = [(i, i + by) for i in range(devices) if 0 <= i + by < devices]
    return lax.ppermute(value, axis, pairs)


def padded(cells, sides, width):
    for axis, dim in sides:
        count = lax.axis_size(axis)
        ends = count - 1
        head = lax.slice_in_dim(cells, 0, width, axis=dim)
        tail = lax.slice_in_dim(cells, cells.shape[dim] - width, cells.shape[dim], axis=dim)
        cells = jnp.concatenate(
            [
                lax.ppermute(tail, axis, [(i, (i + 1) % count) for i in range(ends)]),
                cells,
                lax.ppermute(head, axis, [((i + 1) % count, i) for i in range(ends)]),
            ],
            axis=dim,
        )
    return cells


def forward_arrange(cube):
    depth, rows_t, cols_t, inputs, outputs = cube.shape
    return cube.transpose(0, 1, 3, 2, 4).reshape(9, inputs, 3 * outputs)


def backward_arrange(cube):
    depth, rows_t, cols_t, inputs, outputs = cube.shape
    return cube.transpose(0, 1, 4, 2, 3).reshape(9, outputs, 3 * inputs)


def forward_sum(window, arranged, row_total, col_total):
    width = window.shape[-1]
    slots = arranged.shape[-1] // 3
    total = None
    for depth_tap in range(3):
        for row_tap in range(3):
            slab = window[depth_tap, row_tap : row_tap + row_total].reshape(
                row_total * (col_total + 2), width
            )
            product = jnp.dot(
                slab, arranged[3 * depth_tap + row_tap], preferred_element_type=jnp.float32
            )
            total = product if total is None else total + product
    total = total.reshape(row_total, col_total + 2, 3, slots)
    return (
        total[:, 0:col_total, 0] + total[:, 1 : col_total + 1, 1] + total[:, 2 : col_total + 2, 2]
    )


def backward_sum(window, arranged, row_total, col_total):
    width = window.shape[-1]
    slots = arranged.shape[-1] // 3
    total = None
    for depth_tap in range(3):
        for row_tap in range(3):
            slab = window[2 - depth_tap, 2 - row_tap : 2 - row_tap + row_total].reshape(
                row_total * (col_total + 2), width
            )
            product = jnp.dot(
                slab, arranged[3 * depth_tap + row_tap], preferred_element_type=jnp.float32
            )
            total = product if total is None else total + product
    total = total.reshape(row_total, col_total + 2, 3, slots)
    return (
        total[:, 2 : col_total + 2, 0] + total[:, 1 : col_total + 1, 1] + total[:, 0:col_total, 2]
    )


def weight_terms(window, cot_block, row_total, col_total):
    width = window.shape[-1]
    slots = cot_block.shape[-1]
    flat_count = row_total * (col_total + 2)
    shifted = [
        jnp.pad(cot_block, ((0, 0), (col_tap, 2 - col_tap), (0, 0))).reshape(flat_count, slots)
        for col_tap in range(3)
    ]
    pieces = []
    for depth_tap in range(3):
        for row_tap in range(3):
            slab = window[depth_tap, row_tap : row_tap + row_total].reshape(flat_count, width)
            for col_tap in range(3):
                pieces.append(
                    lax.dot_general(
                        slab,
                        shifted[col_tap],
                        (((0,), (0,)), ((), ())),
                        preferred_element_type=jnp.float32,
                    )
                )
    return jnp.concatenate(pieces, axis=0)


def column_share(cotangent):
    return lax.all_to_all(cotangent, "height", split_axis=3, concat_axis=1, tiled=True)


def local(latents, gain, bias, weight, cotangent):
    frame_count, row_count, col_count, channels = latents.shape
    latent_wide = latents.astype(jnp.float32)
    root_mean = jnp.sqrt(jnp.mean(latent_wide * latent_wide, axis=-1, keepdims=True) + 1e-06)
    normed = latent_wide / root_mean * gain
    hidden = jax.nn.silu(normed).astype(jnp.bfloat16)
    height_count = lax.axis_size("height")
    share_width = channels // height_count
    first_column = lax.axis_index("height") * share_width
    total_rows = row_count * height_count
    tap_rows = 27 * channels
    inverse_root = 1.0 / math.sqrt(lax.axis_size("tm") * total_rows * col_count)
    weight_cube = weight.reshape(3, 3, 3, channels, channels)
    shared_cot = cotangent
    prior = shifted_2(hidden, "tm", 1)
    second = shifted_2(hidden, "tm", 2)
    stacked = jnp.concatenate([second, prior, hidden], axis=0)
    gathered = lax.all_gather(stacked, "height", axis=1, tiled=True)
    framed = jnp.pad(gathered, ((0, 0), (1, 1), (1, 1), (0, 0)))
    shared_cot = column_share(cotangent)
    share_cube = lax.dynamic_slice_in_dim(weight_cube, first_column, share_width, 4)
    share_arranged = forward_arrange(share_cube)

    def block_step(block_index, carry):
        conv_total, grad_total = carry
        first_row = block_index * row_count
        window = lax.dynamic_slice_in_dim(framed, first_row, row_count + 2, 1)
        conv_block = forward_sum(window, share_arranged, row_count, col_count)
        conv_total = lax.dynamic_update_slice_in_dim(conv_total, conv_block, first_row, 0)
        cot_block = lax.dynamic_slice_in_dim(shared_cot[0], first_row, row_count, 0)
        grad_total = grad_total + weight_terms(window, cot_block, row_count, col_count)
        return (conv_total, grad_total)

    start_carry = (
        jnp.zeros((total_rows, col_count, share_width), jnp.float32),
        jnp.zeros((tap_rows, share_width), jnp.float32),
    )
    conv_share, share_terms = lax.fori_loop(0, height_count, block_step, start_carry)
    weight_grad = lax.psum_scatter(
        share_terms * inverse_root, "tm", scatter_dimension=0, tiled=True
    )
    conv_out = lax.all_to_all(
        conv_share.reshape(1, total_rows, col_count, share_width),
        "height",
        split_axis=1,
        concat_axis=3,
        tiled=True,
    )
    output = (latent_wide + conv_out + bias).astype(jnp.bfloat16)
    cotangent_edged = padded(cotangent, (("height", 1),), 1)
    next_frame = shifted_2(cotangent_edged, "tm", -1)
    second_next = shifted_2(cotangent_edged, "tm", -2)
    future_block = jnp.pad(
        jnp.concatenate([cotangent_edged, next_frame, second_next], axis=0),
        ((0, 0), (0, 0), (1, 1), (0, 0)),
    )
    hidden_grad = backward_sum(
        future_block, backward_arrange(weight_cube), row_count, col_count
    ).reshape(frame_count, row_count, col_count, channels)
    sigmoid_pre = jax.nn.sigmoid(normed)
    normed_grad = hidden_grad * sigmoid_pre * (1.0 + normed * (1.0 - sigmoid_pre))
    scaled_grad = normed_grad * gain
    unit_latent = latent_wide / root_mean
    inner = jnp.mean(scaled_grad * unit_latent, axis=-1, keepdims=True)
    latent_grad = (
        cotangent.astype(jnp.float32) + (scaled_grad - unit_latent * inner) / root_mean
    ).astype(jnp.bfloat16)
    return (output, latent_grad, weight_grad)


def solution(mesh):
    placed = (
        P(("grp", "tm"), "height", None, None),
        P(),
        P(),
        P(),
        P(("grp", "tm"), "height", None, None),
    )
    return jax.shard_map(
        local,
        mesh=mesh,
        in_specs=placed,
        out_specs=(
            P(("grp", "tm"), "height", None, None),
            P(("grp", "tm"), "height", None, None),
            P(("grp", "tm"), "height"),
        ),
        check_vma=False,
    )
```

profile of v0, /device:TPU:0, one launch (start us, length us, event | category | flops | bytes accessed | tf_op | source)
XLA Modules:
  0.0 332.8 jit_solution(15227370439125368091)
XLA Ops:
  8.2 2.4 collective-permute-start.2
  10.6 1.3 collective-permute-start.3
  12.9 3.0 collective-permute-done.3
  15.9 1.3 collective-permute-start.5
  17.2 1.3 collective-permute-start.4
  18.5 1.1 fusion.27
  19.6 22.5 %collective-permute-done.5 = bf16[1,4,160,384]{3,2,1,0:T(8,128)(2,1)S(1)} collective-permute-done((bf16[1,4,160,384]{3,2,1,0:T(8,128)(2,1)S(1)}, bf16[1,4,160,384]{3,2,1,0:T(8,128)(2,1)S(1)}, u32[]{:S(2)}, u32[]{:S(2)}) %collective-permute-start.5) | collective-permute-done | bytes 491552 | tf_op jit(solution)/shard_map/ppermute | solution.py:12
  43.4 1.9 fusion.26
  45.3 1.8 convolution_add_fusion.15
  47.2 2.0 convolution_add_fusion.14
  49.1 1.8 convolution_add_fusion.13
  54.8 1.0 fusion.36
  55.8 2.1 multiply_reduce_fusion
  58.0 13.0 %collective-permute-start.1 = (bf16[1,2,160,384]{3,2,1,0:T(8,128)(2,1)S(1)}, bf16[1,2,160,384]{3,2,1,0:T(8,128)(2,1)S(1)}, u32[]{:S(2)}, u32[]{:S(2)}) collective-permute-start(bf16[1,2,160,384]{3,2,1,0:T(8,128)(2,1)S(1)} %get-tuple-element.240), channel_id=1, source_target_pairs={{0,4},{4,8},{8,12},{1,5},{5,9},{9,13},{2,6},{6,10},{10,14},{3,7},{... | collective-permute-start | bytes 737288 | tf_op jit(solution)/shard_map/ppermute | solution.py:12
  71.0 1.3 collective-permute-start
  72.3 5.0 %collective-permute-done.1 = bf16[1,2,160,384]{3,2,1,0:T(8,128)(2,1)S(1)} collective-permute-done((bf16[1,2,160,384]{3,2,1,0:T(8,128)(2,1)S(1)}, bf16[1,2,160,384]{3,2,1,0:T(8,128)(2,1)S(1)}, u32[]{:S(2)}, u32[]{:S(2)}) %collective-permute-start.1) | collective-permute-done | bytes 245792 | tf_op jit(solution)/shard_map/ppermute | solution.py:12
  77.3 5.3 %collective-permute-done = bf16[1,2,160,384]{3,2,1,0:T(8,128)(2,1)S(1)} collective-permute-done((bf16[1,2,160,384]{3,2,1,0:T(8,128)(2,1)S(1)}, bf16[1,2,160,384]{3,2,1,0:T(8,128)(2,1)S(1)}, u32[]{:S(2)}, u32[]{:S(2)}) %collective-permute-start) | collective-permute-done | bytes 245792 | tf_op jit(solution)/shard_map/ppermute | solution.py:12
  83.6 1.2 copy.31
  84.8 3.5 %all-to-all-start = ((bf16[1,2,160,384]{2,1,0,3:T(2,128)(2,1)}), bf16[1,2,160,384]{2,1,0,3:T(2,128)(2,1)S(1)}, u32[]{:S(2)}, u32[]{:S(2)}) async-start(bf16[1,2,160,384]{2,1,0,3:T(2,128)(2,1)} %copy.31), calls=%async_computation | async-start | bytes 786432 | tf_op jit(solution)/shard_map/all_to_all | solution.py:105
  88.3 3.5 %dynamic-slice_bitcast_fusion.1 = bf16[3,3,384,3,96]{4,2,3,1,0:T(8,128)(2,1)S(1)} fusion(bf16[3,3,3,384,384]{4,3,2,1,0:T(8,128)(2,1)} %bitcast.310, s32[]{:T(128)S(6)} %select_n.24), kind=kLoop, calls=%fused_computation.80 | loop fusion | bytes 3981316 | tf_op jit(solution)/shard_map/transpose | solution.py:34
  91.8 2.6 copy.30
  94.4 4.4 %copy.33 = bf16[9,384,288]{2,1,0:T(8,128)(2,1)} copy(bf16[9,384,288]{1,2,0:T(8,128)(2,1)} %bitcast.318) | data formatting | bytes 3981312
  99.2 16.5 %all-gather.2.cloned.1.call-done = bf16[3,8,160,384]{3,2,1,0:T(8,128)(2,1)} async-done(((bf16[3,2,160,384]{3,2,1,0:T(8,128)(2,1)}), bf16[3,8,160,384]{3,2,1,0:T(8,128)(2,1)}) %all-gather.2.cloned.1.call-update) | async-done | bytes 2949136 | tf_op jit(solution)/shard_map/all_gather | solution.py:125
  115.6 4.9 %pad.41 = bf16[3,10,162,384]{3,2,1,0:T(8,128)(2,1)} pad(bf16[3,8,160,384]{3,2,1,0:T(8,128)(2,1)} %all-gather.2.cloned.1.call-done, bf16[]{:T(256)} %constant.82.clone.1), padding=0_0x1_1x1_1x0_0 | pad | bytes 6681602 | tf_op jit(solution)/shard_map/jit(_pad)/pad | solution.py:126
  121.4 94.6 %while.18 = (s32[]{:T(128)}, f32[8,160,96]{2,1,0:T(8,128)}, f32[10368,96]{0,1:T(8,128)}, bf16[3,10,162,384]{3,2,1,0:T(8,128)(2,1)}, bf16[9,384,288]{2,1,0:T(8,12...) while((s32[]{:T(128)}, f32[8,160,96]{2,1,0:T(8,128)}, ...), condition=%wide.region_2.3_spmd.clone, body=%wide.region_1.2_spmd.clone.sunk | while | flops 1292743680 | bytes 89893304 | solution.py:145
  122.3 2.0 constant_dynamic-slice_fusion.10
  124.8 1.5 fusion.258
  126.3 1.3 convolution_add_fusion.24
  127.7 1.3 convolution_add_fusion.25
  130.9 1.2 convolution_add_fusion.31
  132.1 1.5 reshape.142
  142.1 1.0 select_add_fusion.2
  143.2 1.9 copy-done.1
  146.0 2.0 constant_dynamic-slice_fusion.10
  148.5 1.5 fusion.258
  150.0 1.3 convolution_add_fusion.24
  151.3 1.3 convolution_add_fusion.25
  154.6 1.2 convolution_add_fusion.31
  155.8 1.5 reshape.142
  165.8 1.0 select_add_fusion.2
  166.8 1.9 copy-done.1
  169.6 2.0 constant_dynamic-slice_fusion.10
  172.1 1.5 fusion.258
  173.6 1.3 convolution_add_fusion.24
  175.0 1.3 convolution_add_fusion.25
  178.2 1.2 convolution_add_fusion.31
  179.4 1.5 reshape.142
  189.4 1.0 select_add_fusion.2
  190.5 1.9 copy-done.1
  193.3 2.0 constant_dynamic-slice_fusion.10
  195.8 1.5 fusion.258
  197.3 1.3 convolution_add_fusion.24
  198.6 1.3 convolution_add_fusion.25
  201.9 1.2 convolution_add_fusion.31
  203.1 1.5 reshape.142
  213.1 1.0 select_add_fusion.2
  214.1 1.9 copy-done.1
  216.0 4.4 %broadcast_multiply_fusion = f32[10368,96]{0,1:T(8,128)} fusion(f32[10368,96]{0,1:T(8,128)} %get-tuple-element.159), kind=kLoop, calls=%fused_computation.81 | loop fusion | flops 995328 | bytes 7962624 | tf_op jit(solution)/shard_map/mul | solution.py:147
  220.4 5.9 %copy.39 = f32[10368,96]{1,0:T(8,128)} copy(f32[10368,96]{0,1:T(8,128)} %broadcast_multiply_fusion) | data formatting | bytes 7962624
  226.4 3.6 %all-to-all-start.1 = ((f32[1,8,160,96]{3,2,0,1:T(8,128)}), f32[1,8,160,96]{3,2,0,1:T(8,128)S(1)}, u32[]{:S(2)}, u32[]{:S(2)}) async-start(f32[1,8,160,96]{3,2,0,1:T(8,128)} %bitcast.6), calls=%async_computation.1 | async-start | bytes 1310720 | tf_op jit(solution)/shard_map/all_to_all | solution.py:149
  230.1 10.2 %all-to-all-done.1 = f32[1,8,160,96]{3,2,0,1:T(8,128)S(1)} async-done(((f32[1,8,160,96]{3,2,0,1:T(8,128)}), f32[1,8,160,96]{3,2,0,1:T(8,128)S(1)}, u32[]{:S(2)}, u32[]{:S(2)}) %all-to-all-start.1) | async-done | bytes 491552 | tf_op jit(solution)/shard_map/all_to_all | solution.py:149
  241.1 1.0 add_convert_fusion
  242.1 81.2 %reduce-scatter.4.cloned.1.call-done = f32[2592,96]{1,0:T(8,128)} async-done(((f32[10368,96]{1,0:T(8,128)}), f32[2592,96]{1,0:T(8,128)}) %reduce-scatter.4.cloned.1.call-update) | async-done | bytes 995344
  323.3 2.7 copy.40
  (285 shorter events, 56.1 us)
Async XLA Ops:
  7.2 108.5 %all-gather.2.cloned.1.call-start = ((), (), s32[]{:S(2)}) async-start(), calls=%async_computation.3 | async-start | bytes 3686400 | tf_op jit(solution)/shard_map/all_gather | solution.py:125
  8.2 3.7 %collective-permute-start.2 = (bf16[1,1,160,384]{3,2,1,0:T(8,128)(2,1)S(1)}, bf16[1,1,160,384]{3,2,1,0:T(8,128)(2,1)S(1)}, u32[]{:S(2)}, u32[]{:S(2)}) collective-permute-start(bf16[1,1,160,384]{3,2,1,0:T(8,128)(2,1)S(1)} %get-tuple-element.244), channel_id=1, source_target_pairs={{0,1},{1,2},{2,3},{4,5},{5,6},{6,7},{8,9},{9,10},{10,11},{12,13},{... | collective-permute-start | bytes 368648 | tf_op jit(solution)/shard_map/ppermute | solution.py:23
  10.6 5.3 %collective-permute-start.3 = (bf16[1,1,160,384]{3,2,1,0:T(8,128)(2,1)S(1)}, bf16[1,1,160,384]{3,2,1,0:T(8,128)(2,1)S(1)}, u32[]{:S(2)}, u32[]{:S(2)}) collective-permute-start(bf16[1,1,160,384]{3,2,1,0:T(8,128)(2,1)S(1)} %get-tuple-element.243), channel_id=1, source_target_pairs={{1,0},{2,1},{3,2},{5,4},{6,5},{7,6},{9,8},{10,9},{11,10},{13,12},{... | collective-permute-start | bytes 368648 | tf_op jit(solution)/shard_map/ppermute | solution.py:25
  15.9 26.2 %collective-permute-start.5 = (bf16[1,4,160,384]{3,2,1,0:T(8,128)(2,1)S(1)}, bf16[1,4,160,384]{3,2,1,0:T(8,128)(2,1)S(1)}, u32[]{:S(2)}, u32[]{:S(2)}) collective-permute-start(bf16[1,4,160,384]{3,2,1,0:T(8,128)(2,1)S(1)} %constant_dynamic-update-slice_fusion.1), channel_id=1, source_target_pairs={{8,0},{12,4},{9,1},{13,5},{10,2},{14,6},{11,3},{15,7},{24,16},{28,... | collective-permute-start | bytes 1474568 | tf_op jit(solution)/shard_map/ppermute | solution.py:12
  17.2 24.9 %collective-permute-start.4 = (bf16[1,4,160,384]{3,2,1,0:T(8,128)(2,1)S(1)}, bf16[1,4,160,384]{3,2,1,0:T(8,128)(2,1)S(1)}, u32[]{:S(2)}, u32[]{:S(2)}) collective-permute-start(bf16[1,4,160,384]{3,2,1,0:T(8,128)(2,1)S(1)} %constant_dynamic-update-slice_fusion.1), channel_id=1, source_target_pairs={{4,0},{8,4},{12,8},{5,1},{9,5},{13,9},{6,2},{10,6},{14,10},{7,3},{... | collective-permute-start | bytes 1474568 | tf_op jit(solution)/shard_map/ppermute | solution.py:12
  43.4 7.6 %slice-start = ((s8[7962624]{0:T(1024)(128)(4,1)}), s8[4194304]{0:T(1024)(128)(4,1)S(1)}, s32[]{:S(2)}) async-start(s8[7962624]{0:T(1024)(128)(4,1)} %bitcast.311), calls=%async_computation.5 | async-start | bytes 8388608
  47.1 3.8 %slice-start.1 = ((s8[7962624]{0:T(1024)(128)(4,1)}), s8[3768320]{0:T(1024)(128)(4,1)S(1)}, s32[]{:S(2)}) async-start(s8[7962624]{0:T(1024)(128)(4,1)} %bitcast.311), calls=%async_computation.6 | async-start | bytes 7536640
  54.2 1.7 copy-start.10
  54.8 28.8 %copy-start.3 = (bf16[1,2,160,384]{3,2,1,0:T(8,128)(2,1)S(1)}, bf16[1,2,160,384]{3,2,1,0:T(8,128)(2,1)}, u32[]{:S(2)}) copy-start(bf16[1,2,160,384]{3,2,1,0:T(8,128)(2,1)} %param.11) | copy-start | bytes 737284
  58.0 19.3 %collective-permute-start.1 = (bf16[1,2,160,384]{3,2,1,0:T(8,128)(2,1)S(1)}, bf16[1,2,160,384]{3,2,1,0:T(8,128)(2,1)S(1)}, u32[]{:S(2)}, u32[]{:S(2)}) collective-permute-start(bf16[1,2,160,384]{3,2,1,0:T(8,128)(2,1)S(1)} %get-tuple-element.240), channel_id=1, source_target_pairs={{0,4},{4,8},{8,12},{1,5},{5,9},{9,13},{2,6},{6,10},{10,14},{3,7},{... | collective-permute-start | bytes 737288 | tf_op jit(solution)/shard_map/ppermute | solution.py:12
  71.0 11.6 %collective-permute-start = (bf16[1,2,160,384]{3,2,1,0:T(8,128)(2,1)S(1)}, bf16[1,2,160,384]{3,2,1,0:T(8,128)(2,1)S(1)}, u32[]{:S(2)}, u32[]{:S(2)}) collective-permute-start(bf16[1,2,160,384]{3,2,1,0:T(8,128)(2,1)S(1)} %get-tuple-element.240), channel_id=1, source_target_pairs={{0,8},{4,12},{1,9},{5,13},{2,10},{6,14},{3,11},{7,15},{16,24},{20,... | collective-permute-start | bytes 737288 | tf_op jit(solution)/shard_map/ppermute | solution.py:12
  84.8 14.0 %all-to-all-start = ((bf16[1,2,160,384]{2,1,0,3:T(2,128)(2,1)}), bf16[1,2,160,384]{2,1,0,3:T(2,128)(2,1)S(1)}, u32[]{:S(2)}, u32[]{:S(2)}) async-start(bf16[1,2,160,384]{2,1,0,3:T(2,128)(2,1)} %copy.31), calls=%async_computation | async-start | bytes 786432 | tf_op jit(solution)/shard_map/all_to_all | solution.py:105
  88.2 235.0 %reduce-scatter.4.cloned.1.call-start = ((), (), s32[]{:S(2)}) async-start(), calls=%async_computation.4 | async-start | bytes 6635520
  121.4 0.8 copy-start.7
  124.8 4.2 %copy-start.2 = (bf16[9,384,288]{2,1,0:T(8,128)(2,1)S(1)}, bf16[9,384,288]{2,1,0:T(8,128)(2,1)}, u32[]{:S(2)}) copy-start(bf16[9,384,288]{2,1,0:T(8,128)(2,1)} %get-tuple-element.336) | copy-start | bytes 5971972 | tf_op jit(solution)/shard_map/while
  137.8 4.3 %copy-start = (f32[10368,96]{0,1:T(8,128)S(1)}, f32[10368,96]{0,1:T(8,128)}, u32[]{:S(2)}) copy-start(f32[10368,96]{0,1:T(8,128)} %get-tuple-element.321) | copy-start | bytes 11943940 | tf_op jit(solution)/shard_map/while
  142.1 2.9 copy-start.8
  143.1 1.9 copy-start.1
  145.0 0.8 copy-start.7
  148.5 4.2 %copy-start.2 = (bf16[9,384,288]{2,1,0:T(8,128)(2,1)S(1)}, bf16[9,384,288]{2,1,0:T(8,128)(2,1)}, u32[]{:S(2)}) copy-start(bf16[9,384,288]{2,1,0:T(8,128)(2,1)} %get-tuple-element.336) | copy-start | bytes 5971972 | tf_op jit(solution)/shard_map/while
  161.5 4.3 %copy-start = (f32[10368,96]{0,1:T(8,128)S(1)}, f32[10368,96]{0,1:T(8,128)}, u32[]{:S(2)}) copy-start(f32[10368,96]{0,1:T(8,128)} %get-tuple-element.321) | copy-start | bytes 11943940 | tf_op jit(solution)/shard_map/while
  165.8 2.9 copy-start.8
  166.8 1.9 copy-start.1
  168.7 0.8 copy-start.7
  172.1 4.2 %copy-start.2 = (bf16[9,384,288]{2,1,0:T(8,128)(2,1)S(1)}, bf16[9,384,288]{2,1,0:T(8,128)(2,1)}, u32[]{:S(2)}) copy-start(bf16[9,384,288]{2,1,0:T(8,128)(2,1)} %get-tuple-element.336) | copy-start | bytes 5971972 | tf_op jit(solution)/shard_map/while
  185.1 4.3 %copy-start = (f32[10368,96]{0,1:T(8,128)S(1)}, f32[10368,96]{0,1:T(8,128)}, u32[]{:S(2)}) copy-start(f32[10368,96]{0,1:T(8,128)} %get-tuple-element.321) | copy-start | bytes 11943940 | tf_op jit(solution)/shard_map/while
  189.4 2.9 copy-start.8
  190.5 1.9 copy-start.1
  192.4 0.8 copy-start.7
  195.8 4.2 %copy-start.2 = (bf16[9,384,288]{2,1,0:T(8,128)(2,1)S(1)}, bf16[9,384,288]{2,1,0:T(8,128)(2,1)}, u32[]{:S(2)}) copy-start(bf16[9,384,288]{2,1,0:T(8,128)(2,1)} %get-tuple-element.336) | copy-start | bytes 5971972 | tf_op jit(solution)/shard_map/while
  208.8 4.3 %copy-start = (f32[10368,96]{0,1:T(8,128)S(1)}, f32[10368,96]{0,1:T(8,128)}, u32[]{:S(2)}) copy-start(f32[10368,96]{0,1:T(8,128)} %get-tuple-element.321) | copy-start | bytes 11943940 | tf_op jit(solution)/shard_map/while
  213.1 2.9 copy-start.8
  214.1 1.9 copy-start.1
  226.4 14.6 %copy-start.4 = (bf16[1,2,160,384]{3,2,1,0:T(8,128)(2,1)S(1)}, bf16[1,2,160,384]{3,2,1,0:T(8,128)(2,1)}, u32[]{:S(2)}) copy-start(bf16[1,2,160,384]{3,2,1,0:T(8,128)(2,1)} %param.11) | copy-start | bytes 737284
  226.4 14.7 %copy-start.5 = (bf16[1,2,160,384]{3,2,1,0:T(8,128)(2,1)S(1)}, bf16[1,2,160,384]{3,2,1,0:T(8,128)(2,1)}, u32[]{:S(2)}) copy-start(bf16[1,2,160,384]{3,2,1,0:T(8,128)(2,1)} %param.7) | copy-start | bytes 737284
  226.4 14.7 %copy-start.6 = (f32[1,2,160,384]{3,2,1,0:T(8,128)S(1)}, f32[1,2,160,384]{3,2,1,0:T(8,128)}, u32[]{:S(2)}) copy-start(f32[1,2,160,384]{3,2,1,0:T(8,128)} %get-tuple-element.215) | copy-start | bytes 1474564
  226.4 14.7 %copy-start.9 = (f32[384]{0:T(512)S(1)}, f32[384]{0:T(512)}, u32[]{:S(2)}) copy-start(f32[384]{0:T(512)} %param.9) | copy-start | bytes 4612
  226.4 13.9 %all-to-all-start.1 = ((f32[1,8,160,96]{3,2,0,1:T(8,128)}), f32[1,8,160,96]{3,2,0,1:T(8,128)S(1)}, u32[]{:S(2)}, u32[]{:S(2)}) async-start(f32[1,8,160,96]{3,2,0,1:T(8,128)} %bitcast.6), calls=%async_computation.1 | async-start | bytes 1310720 | tf_op jit(solution)/shard_map/all_to_all | solution.py:149
Sparse Core Ops, SparseCore 0:
  83.7 31.9 all-gather.1
  226.5 96.6 reduce-scatter.3
where the time goes:
time: 334 us; the launch traced here: 333 us
  waiting for transfers between devices  144 us (43%)
  matrix products  67.3 us (20%)
  local copies, waits for them, and re-layouts  61.8 us (19%)
  starting transfers between devices  27.7 us (8%)
  other arithmetic  16 us (5%)
  between operations  14.4 us (4%)
    unnamed x3, waiting for transfers between devices  81.2 us
    ppermute x4, waiting for transfers between devices, shifted_2(): return lax.ppermute(value, axis, pairs)  32.8 us
    dot_general x36, matrix products, forward_sum(): jnp.dot(slab, arranged[3 * depth_tap + row_tap], preferred_element_type=j...  28.8 us
    dot_general x108, matrix products, weight_terms(): lax.dot_general(slab, shifted[col_tap], (((0,), (0,)), ((), ())), preferr...  27.8 us
    ppermute x4, starting transfers between devices, shifted_2(): return lax.ppermute(value, axis, pairs)  16.9 us
    all_gather x1, waiting for transfers between devices, local(): gathered = lax.all_gather(stacked, 'height', axis=1, tiled=True)  16.5 us
    unnamed x22, local copies, waits for them, and re-layouts  15.2 us
    dot_general x9, matrix products, backward_sum(): jnp.dot(slab, arranged[3 * depth_tap + row_tap], preferred_element_type=j...  10.7 us
  transfers between devices with their start and end apart: 10, of which 7 were waited for; matrix products, arithmetic and copies ran while one was open for 5% of the time, Pallas kernels for 0%

commit v1 on v0

--- a/solution.py
+++ b/solution.py
@@ -77,32 +77,46 @@
     )
 
 
-def weight_terms(window, cot_block, row_total, col_total):
-    width = window.shape[-1]
-    slots = cot_block.shape[-1]
-    flat_count = row_total * (col_total + 2)
-    shifted = [
-        jnp.pad(cot_block, ((0, 0), (col_tap, 2 - col_tap), (0, 0))).reshape(flat_count, slots)
-        for col_tap in range(3)
-    ]
-    pieces = []
-    for depth_tap in range(3):
-        for row_tap in range(3):
-            slab = window[depth_tap, row_tap : row_tap + row_total].reshape(flat_count, width)
-            for col_tap in range(3):
-                pieces.append(
-                    lax.dot_general(
-                        slab,
-                        shifted[col_tap],
-                        (((0,), (0,)), ((), ())),
-                        preferred_element_type=jnp.float32,
-                    )
-                )
-    return jnp.concatenate(pieces, axis=0)
+def pair_count(tap_rows, share_rows, pair_rows, parts):
+    most = 1
+    for index in range(parts):
+        first = index * share_rows
+        last = first + share_rows - 1
+        most = max(most, last // pair_rows - first // pair_rows + 1)
+    return most
 
 
-def column_share(cotangent):
-    return lax.all_to_all(cotangent, "height", split_axis=3, concat_axis=1, tiled=True)
+def block_weight_grad(framed, cot_all, frame_index, share_rows, channels):
+    frame_total, row_total, col_total, slots = cot_all.shape
+    pair_rows = 3 * channels
+    tap_rows = 27 * channels
+    flat_count = frame_total * row_total * (col_total + 2)
+    shifted = jnp.concatenate(
+        [
+            jnp.pad(cot_all, ((0, 0), (0, 0), (col_tap, 2 - col_tap), (0, 0)))
+            for col_tap in range(3)
+        ],
+        axis=-1,
+    ).reshape(flat_count, 3 * slots)
+    first_row = frame_index * share_rows
+    first_pair = first_row // pair_rows
+    count = pair_count(tap_rows, share_rows, pair_rows, tap_rows // share_rows)
+    pieces = []
+    for step in range(count):
+        pair = jnp.minimum(first_pair + step, 8)
+        depth_tap = pair // 3
+        row_tap = pair % 3
+        slab = lax.dynamic_slice(
+            framed,
+            (depth_tap, row_tap, 0, 0),
+            (frame_total, row_total, col_total + 2, channels),
+        ).reshape(flat_count, channels)
+        product = lax.dot_general(
+            slab, shifted, (((0,), (0,)), ((), ())), preferred_element_type=jnp.float32
+        )
+        pieces.append(product.reshape(channels, 3, slots).transpose(1, 0, 2).reshape(pair_rows, slots))
+    stacked = jnp.concatenate(pieces, axis=0)
+    return lax.dynamic_slice_in_dim(stacked, first_row - first_pair * pair_rows, share_rows, 0)
 
 
 def local(latents, gain, bias, weight, cotangent):
@@ -112,48 +126,37 @@
     normed = latent_wide / root_mean * gain
     hidden = jax.nn.silu(normed).astype(jnp.bfloat16)
     height_count = lax.axis_size("height")
+    frame_devices = lax.axis_size("tm")
     share_width = channels // height_count
-    first_column = lax.axis_index("height") * share_width
+    frame_index = lax.axis_index("tm")
+    row_index = lax.axis_index("height")
     total_rows = row_count * height_count
+    total_frames = frame_count * frame_devices
     tap_rows = 27 * channels
-    inverse_root = 1.0 / math.sqrt(lax.axis_size("tm") * total_rows * col_count)
+    share_rows = tap_rows // frame_devices
+    inverse_root = 1.0 / math.sqrt(total_frames * total_rows * col_count)
     weight_cube = weight.reshape(3, 3, 3, channels, channels)
-    shared_cot = cotangent
-    prior = shifted_2(hidden, "tm", 1)
-    second = shifted_2(hidden, "tm", 2)
-    stacked = jnp.concatenate([second, prior, hidden], axis=0)
-    gathered = lax.all_gather(stacked, "height", axis=1, tiled=True)
-    framed = jnp.pad(gathered, ((0, 0), (1, 1), (1, 1), (0, 0)))
-    shared_cot = column_share(cotangent)
-    share_cube = lax.dynamic_slice_in_dim(weight_cube, first_column, share_width, 4)
-    share_arranged = forward_arrange(share_cube)
 
-    def block_step(block_index, carry):
-        conv_total, grad_total = carry
-        first_row = block_index * row_count
-        window = lax.dynamic_slice_in_dim(framed, first_row, row_count + 2, 1)
-        conv_block = forward_sum(window, share_arranged, row_count, col_count)
-        conv_total = lax.dynamic_update_slice_in_dim(conv_total, conv_block, first_row, 0)
-        cot_block = lax.dynamic_slice_in_dim(shared_cot[0], first_row, row_count, 0)
-        grad_total = grad_total + weight_terms(window, cot_block, row_count, col_count)
-        return (conv_total, grad_total)
+    hidden_all = lax.all_gather(hidden, ("tm", "height"), axis=0, tiled=True).reshape(
+        total_frames, total_rows, col_count, channels
+    )
+    framed = jnp.pad(hidden_all, ((2, 0), (1, 1), (1, 1), (0, 0)))
 
-    start_carry = (
-        jnp.zeros((total_rows, col_count, share_width), jnp.float32),
-        jnp.zeros((tap_rows, share_width), jnp.float32),
+    shared_cot = lax.all_to_all(cotangent, "height", split_axis=3, concat_axis=1, tiled=True)
+    cot_all = lax.all_gather(shared_cot, "tm", axis=0, tiled=True)
+
+    window = lax.dynamic_slice(
+        framed,
+        (frame_index * frame_count, row_index * row_count, 0, 0),
+        (frame_count + 2, row_count + 2, col_count + 2, channels),
     )
-    conv_share, share_terms = lax.fori_loop(0, height_count, block_step, start_carry)
-    weight_grad = lax.psum_scatter(
-        share_terms * inverse_root, "tm", scatter_dimension=0, tiled=True
-    )
-    conv_out = lax.all_to_all(
-        conv_share.reshape(1, total_rows, col_count, share_width),
-        "height",
-        split_axis=1,
-        concat_axis=3,
-        tiled=True,
+    conv_out = forward_sum(window, forward_arrange(weight_cube), row_count, col_count).reshape(
+        frame_count, row_count, col_count, channels
     )
     output = (latent_wide + conv_out + bias).astype(jnp.bfloat16)
+
+    weight_grad = block_weight_grad(framed, cot_all, frame_index, share_rows, channels) * inverse_root
+
     cotangent_edged = padded(cotangent, (("height", 1),), 1)
     next_frame = shifted_2(cotangent_edged, "tm", -1)
     second_next = shifted_2(cotangent_edged, "tm", -2)

time: 334 us -> 215 us (0.64)
  waiting for transfers between devices: 144 us -> 24.6 us
  blocking collectives: 0 us -> 50 us
  matrix products: 67.3 us -> 33.1 us
  starting transfers between devices: 27.7 us -> 9.74 us
    unnamed x3 -> x1, waiting for transfers between devices: 81.2 us -> 0.02 us
    all_gather x0 -> x1, blocking collectives: none -> 50 us  [local(): cot_all = lax.all_gather(shared_cot, 'tm', axis=0, tiled=True)]
    reshape x12 -> x8, local copies, waits for them, and re-layouts: 0.33 us -> 27.4 us  [the longest x3 15.3 us: block_weight_grad(): slab = lax.dynamic_slice(framed, (depth_tap, row_tap, 0, 0), (frame_total...]
    dot_general x36 -> x9, matrix products: 28.8 us -> 10.7 us  [forward_sum(): jnp.dot(slab, arranged[3 * depth_tap + row_tap], preferred_element_type=j...]
    all_gather x1, waiting for transfers between devices: 16.5 us -> 0.01 us  [local(): lax.all_gather(hidden, ('tm', 'height'), axis=0, tiled=True)]
    dot_general x108 -> x3, matrix products: 27.8 us -> 11.7 us  [block_weight_grad(): lax.dot_general(slab, shifted, (((0,), (0,)), ((), ())), preferred_elemen...]
    ppermute x4 -> x2, starting transfers between devices: 16.9 us -> 2.58 us  [shifted_2(): return lax.ppermute(value, axis, pairs)]
    unnamed x22 -> x23, local copies, waits for them, and re-layouts: 15.2 us -> 3.66 us
  transfers between devices with their start and end apart: 10 -> 6, of which waited for: 7 -> 2; matrix products, arithmetic and copies ran while one was open for 5% -> 17% of each run, Pallas kernels for 0% -> 0%
where the time goes in v1:
time: 215 us; the launch traced here: 212 us
  local copies, waits for them, and re-layouts  60.9 us (28%)
  blocking collectives  50 us (23%)
  matrix products  33.1 us (15%)
  waiting for transfers between devices  24.6 us (11%)
  other arithmetic  18.8 us (9%)
  between operations  14.7 us (7%)
  starting transfers between devices  9.74 us (5%)
    all_gather x1, blocking collectives, local(): cot_all = lax.all_gather(shared_cot, 'tm', axis=0, tiled=True)  50 us
    ppermute x2, waiting for transfers between devices, shifted_2(): return lax.ppermute(value, axis, pairs)  21.5 us
    reshape x3, local copies, waits for them, and re-layouts, block_weight_grad(): slab = lax.dynamic_slice(framed, (depth_tap, row_tap, 0, 0), (frame_total...  15.3 us
    transpose x1, local copies, waits for them, and re-layouts, forward_arrange(): return cube.transpose(0, 1, 3, 2, 4).reshape(9, inputs, 3 * outputs)  15.1 us
    dot_general x3, matrix products, block_weight_grad(): lax.dot_general(slab, shifted, (((0,), (0,)), ((), ())), preferred_elemen...  11.7 us
    reshape x2, local copies, waits for them, and re-layouts, block_weight_grad(): shifted = jnp.concatenate([jnp.pad(cot_all, ((0, 0), (0, 0), (col_tap, 2...  11.3 us
    dot_general x9, matrix products, backward_sum(): jnp.dot(slab, arranged[3 * depth_tap + row_tap], preferred_element_type=j...  10.7 us
    dot_general x9, matrix products, forward_sum(): jnp.dot(slab, arranged[3 * depth_tap + row_tap], preferred_element_type=j...  10.7 us
  transfers between devices with their start and end apart: 6, of which 2 were waited for; matrix products, arithmetic and copies ran while one was open for 17% of the time, Pallas kernels for 0%

profile of v1, /device:TPU:0, one launch (start us, length us, event | category | flops | bytes accessed | tf_op | source)
XLA Modules:
  0.0 211.8 jit_solution(16740439261653948834)
XLA Ops:
  7.2 1.0 fusion.28
  8.2 2.4 %collective-permute-start = (bf16[1,1,160,384]{3,2,1,0:T(8,128)(2,1)S(1)}, bf16[1,1,160,384]{3,2,1,0:T(8,128)(2,1)S(1)}, u32[]{:S(2)}, u32[]{:S(2)}) collective-permute-start(bf16[1,1,160,384]{3,2,1,0:T(8,128)(2,1)S(1)} %get-tuple-element.37), channel_id=1, source_target_pairs={{0,1},{1,2},{2,3},{4,5},{5,6},{6,7},{8,9},{9,10},{10,11},{12,13},{... | collective-permute-start | bytes 368648 | tf_op jit(solution)/shard_map/ppermute | solution.py:23
  10.6 1.3 collective-permute-start.1
  11.9 1.0 constant_dynamic-update-slice_fusion.1
  12.9 3.0 %collective-permute-done.1 = bf16[1,1,160,384]{3,2,1,0:T(8,128)(2,1)S(1)} collective-permute-done((bf16[1,1,160,384]{3,2,1,0:T(8,128)(2,1)S(1)}, bf16[1,1,160,384]{3,2,1,0:T(8,128)(2,1)S(1)}, u32[]{:S(2)}, u32[]{:S(2)}) %collective-permute-start.1) | collective-permute-done | bytes 122912 | tf_op jit(solution)/shard_map/ppermute | solution.py:25
  15.9 1.3 collective-permute-start.3
  17.2 1.3 collective-permute-start.2
  18.5 2.1 multiply_reduce_fusion.1
  20.6 21.5 %collective-permute-done.3 = bf16[1,4,160,384]{3,2,1,0:T(8,128)(2,1)S(1)} collective-permute-done((bf16[1,4,160,384]{3,2,1,0:T(8,128)(2,1)S(1)}, bf16[1,4,160,384]{3,2,1,0:T(8,128)(2,1)S(1)}, u32[]{:S(2)}, u32[]{:S(2)}) %collective-permute-start.3) | collective-permute-done | bytes 491552 | tf_op jit(solution)/shard_map/ppermute | solution.py:12
  42.2 0.4 fusion.11
  42.6 0.2 fusion.27
  42.8 0.1 reshape_squeeze.71
  42.9 0.1 reshape_squeeze.70
  42.9 0.1 reshape_squeeze.69
  43.2 0.1 reshape_squeeze.65
  43.2 0.1 reshape_squeeze.64
  43.3 0.1 reshape_squeeze.63
  43.4 1.9 fusion.15
  45.3 1.8 convolution_add_fusion.7
  47.2 2.0 convolution_add_fusion.6
  49.1 1.8 convolution_add_fusion.5
  51.0 0.6 convolution_add_fusion.4
  51.6 0.6 convolution_add_fusion.3
  52.2 0.6 convolution_add_fusion.2
  52.9 0.6 convolution_add_fusion.1
  53.6 0.6 convolution_add_fusion
  54.2 0.6 reshape.144
  54.8 5.9 %multiply_reduce_fusion = (f32[2,160]{1,0:T(2,128)S(1)}, f32[1,2,160,384]{3,0,2,1:T(1,128)S(1)}, f32[1,2,160,384]{3,0,2,1:T(1,128)S(1)}, f32[1,2,160,384]{3,0,2,1:T(1,128)S(1)}) fusion(f32[384]{0:T(512)S(1)} %copy-done.3, f32[2,162,3,384]{3,2,1,0:T(4,128)S(1)} %reshape.144, f32[2,160]{1,0:T(2,128)S(1)} %add_sqrt_fusion, bf16[1,2,160,384]{3,2,1,0:T(8,128)(2,1)} %param.5), kind=kLoop, calls=%fused_computation.87 | loop fusion | flops 1965760 | bytes 3198976 | tf_op jit(solution)/shard_map/reduce_sum | solution.py:174
  60.8 1.9 fusion.22
  62.7 0.7 copy.35
  63.5 1.2 copy.38
  64.6 3.5 %all-to-all-start = ((bf16[1,2,160,384]{2,1,0,3:T(2,128)(2,1)}), bf16[1,2,160,384]{2,1,0,3:T(2,128)(2,1)S(1)}, u32[]{:S(2)}, u32[]{:S(2)}) async-start(bf16[1,2,160,384]{2,1,0,3:T(2,128)(2,1)} %copy.38), calls=%async_computation | async-start | bytes 786432 | tf_op jit(solution)/shard_map/all_to_all | solution.py:145
  68.2 15.1 %copy.36 = bf16[3,3,384,3,384]{2,4,3,1,0:T(8,128)(2,1)} copy(bf16[3,3,384,3,384]{4,2,3,1,0:T(8,128)(2,1)} %bitcast.124) | data formatting | bytes 15925248 | tf_op jit(solution)/shard_map/transpose | solution.py:34
  83.3 0.8 copy.47
  84.2 50.0 %all_gather.7 = bf16[4,8,160,96]{3,2,1,0:T(8,128)(2,1)S(1)} all-gather(bf16[1,8,160,96]{3,2,1,0:T(8,128)(2,1)S(1)} %bitcast.153), channel_id=1, replica_groups=mesh['grp'=2,'tm'=4,'height'=4] {'tm'}, dimensions={0}, use_global_device_ids=true | all-gather | bytes 1228800 | tf_op jit(solution)/shard_map/all_gather | solution.py:146
  134.2 4.7 %fusion.5 = bf16[4,8,162,288]{3,2,1,0:T(8,128)(2,1)} fusion(bf16[4,8,160,96]{3,2,1,0:T(8,128)(2,1)S(1)} %all_gather.7), kind=kLoop, calls=%fused_computation.23 | loop fusion | flops 20901888 | bytes 3969024 | tf_op jit(solution)/shard_map/concatenate | solution.py:94
  138.9 5.5 %reshape.156 = bf16[5184,288]{1,0:T(8,128)(2,1)} reshape(bf16[4,8,162,288]{3,2,1,0:T(8,128)(2,1)} %fusion.5) | data formatting | bytes 5971968 | tf_op jit(solution)/shard_map/reshape | solution.py:100
  144.5 5.8 %copy.48 = bf16[5184,288]{0,1:T(8,128)(2,1)} copy(bf16[5184,288]{1,0:T(8,128)(2,1)} %reshape.156) | data formatting | bytes 5971968 | tf_op jit(solution)/shard_map/reshape | solution.py:100
  150.2 0.7 copy.46
  151.0 2.0 pad_dynamic-slice_fusion.11
  153.0 0.1 reshape_squeeze.62
  153.0 0.1 reshape_squeeze.54
  153.1 0.1 reshape_squeeze.55
  153.5 1.9 fusion.16
  155.5 1.8 convolution_add_fusion.15
  157.3 2.0 convolution_add_fusion.14
  159.3 1.8 convolution_add_fusion.13
  161.1 0.6 convolution_add_fusion.12
  161.8 0.6 convolution_add_fusion.11
  162.4 0.6 convolution_add_fusion.10
  163.1 0.6 convolution_add_fusion.9
  163.7 0.6 convolution_add_fusion.8
  164.4 0.6 reshape.142
  165.0 2.1 add_convert_fusion
  167.1 0.7 copy.45
  167.8 7.7 %pad_dynamic-slice_fusion.8 = (bf16[4,8,162,384]{3,2,1,0:T(8,128)(2,1)}, bf16[4,8,162,384]{3,2,1,0:T(8,128)(2,1)}, bf16[4,8,162,384]{3,2,1,0:T(8,128)(2,1)}) fusion(s32[]{:T(128)S(6)} %select_n.67, s32[]{:T(128)S(6)} %select_n.69, bf16[4,8,160,384]{3,2,1,0:T(8,128)(2,1)} %bitcast.144, s32[]{:T(128)S(6)} %select_n.59, s32[]{:T(128)S(6)} %select_n.61, ...), kind=kLoop, calls=%fused_computation.8 | loop fusion | bytes 15876120 | tf_op jit(solution)/shard_map/dynamic_slice | solution.py:109
  175.5 5.2 %reshape.154 = bf16[5184,384,1]{1,0,2:T(8,128)(2,1)} reshape(bf16[4,8,162,384]{3,2,1,0:T(8,128)(2,1)} %get-tuple-element.13) | data formatting | bytes 7962624 | tf_op jit(solution)/shard_map/reshape | solution.py:113
  180.7 3.9 %convolution_bitcast_fusion = f32[3,12,8,384]{3,2,1,0:T(8,128)S(1)} fusion(bf16[5184,384,1]{1,0,2:T(8,128)(2,1)} %reshape.154, bf16[3,96,5184]{2,1,0:T(8,128)(2,1)S(1)} %bitcast.145), kind=kOutput, calls=%fused_computation.49 | convolution fusion | flops 1146617856 | bytes 7409664 | tf_op jit(solution)/shard_map/dot_general | solution.py:114
  184.6 5.0 %reshape.152 = bf16[5184,384,1]{1,0,2:T(8,128)(2,1)} reshape(bf16[4,8,162,384]{3,2,1,0:T(8,128)(2,1)} %get-tuple-element.14) | data formatting | bytes 7962624 | tf_op jit(solution)/shard_map/reshape | solution.py:113
  189.7 3.9 %convolution_bitcast_fusion.2 = f32[3,12,8,384]{3,2,1,0:T(8,128)S(1)} fusion(bf16[5184,384,1]{1,0,2:T(8,128)(2,1)} %reshape.152, bf16[3,96,5184]{2,1,0:T(8,128)(2,1)S(1)} %bitcast.146), kind=kOutput, calls=%fused_computation.51 | convolution fusion | flops 1146617856 | bytes 7409664 | tf_op jit(solution)/shard_map/dot_general | solution.py:114
  193.5 0.8 copy.49
  194.3 5.0 %reshape.153 = bf16[5184,384,1]{1,0,2:T(8,128)(2,1)} reshape(bf16[4,8,162,384]{3,2,1,0:T(8,128)(2,1)} %get-tuple-element.15) | data formatting | bytes 7962624 | tf_op jit(solution)/shard_map/reshape | solution.py:113
  199.4 3.9 %convolution_bitcast_fusion.1 = f32[3,12,8,384]{3,2,1,0:T(8,128)S(1)} fusion(bf16[5184,384,1]{1,0,2:T(8,128)(2,1)} %reshape.153, bf16[3,96,5184]{2,1,0:T(8,128)(2,1)S(1)} %bitcast.147), kind=kOutput, calls=%fused_computation.50 | convolution fusion | flops 1146617856 | bytes 7409664 | tf_op jit(solution)/shard_map/dot_general | solution.py:114
  203.3 1.7 fusion.14
  (42 shorter events, 0.8 us)
Async XLA Ops:
  7.2 143.8 %all-gather.2.cloned.1.call-start = ((), (), s32[]{:S(2)}) async-start(), calls=%async_computation.1 | async-start | bytes 4177920 | tf_op jit(solution)/shard_map/all_gather | solution.py:140
  8.2 3.7 %collective-permute-start = (bf16[1,1,160,384]{3,2,1,0:T(8,128)(2,1)S(1)}, bf16[1,1,160,384]{3,2,1,0:T(8,128)(2,1)S(1)}, u32[]{:S(2)}, u32[]{:S(2)}) collective-permute-start(bf16[1,1,160,384]{3,2,1,0:T(8,128)(2,1)S(1)} %get-tuple-element.37), channel_id=1, source_target_pairs={{0,1},{1,2},{2,3},{4,5},{5,6},{6,7},{8,9},{9,10},{10,11},{12,13},{... | collective-permute-start | bytes 368648 | tf_op jit(solution)/shard_map/ppermute | solution.py:23
  10.6 5.3 %collective-permute-start.1 = (bf16[1,1,160,384]{3,2,1,0:T(8,128)(2,1)S(1)}, bf16[1,1,160,384]{3,2,1,0:T(8,128)(2,1)S(1)}, u32[]{:S(2)}, u32[]{:S(2)}) collective-permute-start(bf16[1,1,160,384]{3,2,1,0:T(8,128)(2,1)S(1)} %get-tuple-element.36), channel_id=1, source_target_pairs={{1,0},{2,1},{3,2},{5,4},{6,5},{7,6},{9,8},{10,9},{11,10},{13,12},{... | collective-permute-start | bytes 368648 | tf_op jit(solution)/shard_map/ppermute | solution.py:25
  15.9 26.2 %collective-permute-start.3 = (bf16[1,4,160,384]{3,2,1,0:T(8,128)(2,1)S(1)}, bf16[1,4,160,384]{3,2,1,0:T(8,128)(2,1)S(1)}, u32[]{:S(2)}, u32[]{:S(2)}) collective-permute-start(bf16[1,4,160,384]{3,2,1,0:T(8,128)(2,1)S(1)} %constant_dynamic-update-slice_fusion), channel_id=1, source_target_pairs={{8,0},{12,4},{9,1},{13,5},{10,2},{14,6},{11,3},{15,7},{24,16},{28,... | collective-permute-start | bytes 1474568 | tf_op jit(solution)/shard_map/ppermute | solution.py:12
  17.2 24.9 %collective-permute-start.2 = (bf16[1,4,160,384]{3,2,1,0:T(8,128)(2,1)S(1)}, bf16[1,4,160,384]{3,2,1,0:T(8,128)(2,1)S(1)}, u32[]{:S(2)}, u32[]{:S(2)}) collective-permute-start(bf16[1,4,160,384]{3,2,1,0:T(8,128)(2,1)S(1)} %constant_dynamic-update-slice_fusion), channel_id=1, source_target_pairs={{4,0},{8,4},{12,8},{5,1},{9,5},{13,9},{6,2},{10,6},{14,10},{7,3},{... | collective-permute-start | bytes 1474568 | tf_op jit(solution)/shard_map/ppermute | solution.py:12
  43.4 7.6 %slice-start = ((s8[7962624]{0:T(1024)(128)(4,1)}), s8[4194304]{0:T(1024)(128)(4,1)S(1)}, s32[]{:S(2)}) async-start(s8[7962624]{0:T(1024)(128)(4,1)} %bitcast.125), calls=%async_computation.2 | async-start | bytes 8388608
  47.1 3.8 %slice-start.1 = ((s8[7962624]{0:T(1024)(128)(4,1)}), s8[3768320]{0:T(1024)(128)(4,1)S(1)}, s32[]{:S(2)}) async-start(s8[7962624]{0:T(1024)(128)(4,1)} %bitcast.125), calls=%async_computation.3 | async-start | bytes 7536640
  53.5 1.3 copy-start.3
  54.8 6.0 %copy-start = (bf16[1,2,160,384]{3,2,1,0:T(8,128)(2,1)S(1)}, bf16[1,2,160,384]{3,2,1,0:T(8,128)(2,1)}, u32[]{:S(2)}) copy-start(bf16[1,2,160,384]{3,2,1,0:T(8,128)(2,1)} %param.9) | copy-start | bytes 737284
  64.6 18.7 %all-to-all-start = ((bf16[1,2,160,384]{2,1,0,3:T(2,128)(2,1)}), bf16[1,2,160,384]{2,1,0,3:T(2,128)(2,1)S(1)}, u32[]{:S(2)}, u32[]{:S(2)}) async-start(bf16[1,2,160,384]{2,1,0,3:T(2,128)(2,1)} %copy.38), calls=%async_computation | async-start | bytes 786432 | tf_op jit(solution)/shard_map/all_to_all | solution.py:145
  153.5 7.6 %slice-start.2 = ((s8[7962624]{0:T(1024)(128)(4,1)}), s8[4194304]{0:T(1024)(128)(4,1)S(1)}, s32[]{:S(2)}) async-start(s8[7962624]{0:T(1024)(128)(4,1)} %bitcast.136), calls=%async_computation.4 | async-start | bytes 8388608
  157.3 3.8 %slice-start.3 = ((s8[7962624]{0:T(1024)(128)(4,1)}), s8[3768320]{0:T(1024)(128)(4,1)S(1)}, s32[]{:S(2)}) async-start(s8[7962624]{0:T(1024)(128)(4,1)} %bitcast.136), calls=%async_computation.5 | async-start | bytes 7536640
  163.7 1.3 copy-start.4
  175.5 5.2 %copy-start.1 = (bf16[5184,288]{0,1:T(8,128)(2,1)S(1)}, bf16[5184,288]{0,1:T(8,128)(2,1)}, u32[]{:S(2)}) copy-start(bf16[5184,288]{0,1:T(8,128)(2,1)} %copy.48) | copy-start | bytes 8957956
  199.4 4.0 %copy-start.2 = (f32[3,12,8,384]{3,2,0,1:T(8,128)S(1)}, f32[3,12,8,384]{3,2,0,1:T(8,128)}, u32[]{:S(2)}) copy-start(f32[3,12,8,384]{3,2,0,1:T(8,128)} %copy.49) | copy-start | bytes 1327108
Sparse Core Ops, SparseCore 0:
  63.6 72.2 all-gather.1

commit v2 on v1

--- a/solution.py
+++ b/solution.py
@@ -39,22 +39,25 @@
     return cube.transpose(0, 1, 4, 2, 3).reshape(9, outputs, 3 * inputs)
 
 
-def forward_sum(window, arranged, row_total, col_total):
+def forward_sum(window, cube, row_total, col_total):
     width = window.shape[-1]
-    slots = arranged.shape[-1] // 3
-    total = None
-    for depth_tap in range(3):
-        for row_tap in range(3):
-            slab = window[depth_tap, row_tap : row_tap + row_total].reshape(
-                row_total * (col_total + 2), width
-            )
-            product = jnp.dot(
-                slab, arranged[3 * depth_tap + row_tap], preferred_element_type=jnp.float32
-            )
-            total = product if total is None else total + product
-    total = total.reshape(row_total, col_total + 2, 3, slots)
+    padded_cols = window.shape[2]
+    slots = cube.shape[-1]
+    totals = []
+    for col_tap in range(3):
+        total = None
+        for depth_tap in range(3):
+            for row_tap in range(3):
+                slab = window[depth_tap, row_tap : row_tap + row_total].reshape(
+                    row_total * padded_cols, width
+                )
+                product = jnp.dot(
+                    slab, cube[depth_tap, row_tap, col_tap], preferred_element_type=jnp.float32
+                )
+                total = product if total is None else total + product
+        totals.append(total.reshape(row_total, padded_cols, slots))
     return (
-        total[:, 0:col_total, 0] + total[:, 1 : col_total + 1, 1] + total[:, 2 : col_total + 2, 2]
+        totals[0][:, 0:col_total] + totals[1][:, 1 : col_total + 1] + totals[2][:, 2 : col_total + 2]
     )
 
 
@@ -65,13 +68,13 @@
     for depth_tap in range(3):
         for row_tap in range(3):
             slab = window[2 - depth_tap, 2 - row_tap : 2 - row_tap + row_total].reshape(
-                row_total * (col_total + 2), width
+                row_total * window.shape[2], width
             )
             product = jnp.dot(
                 slab, arranged[3 * depth_tap + row_tap], preferred_element_type=jnp.float32
             )
             total = product if total is None else total + product
-    total = total.reshape(row_total, col_total + 2, 3, slots)
+    total = total.reshape(row_total, window.shape[2], 3, slots)
     return (
         total[:, 2 : col_total + 2, 0] + total[:, 1 : col_total + 1, 1] + total[:, 0:col_total, 2]
     )
@@ -88,12 +91,16 @@
 
 def block_weight_grad(framed, cot_all, frame_index, share_rows, channels):
     frame_total, row_total, col_total, slots = cot_all.shape
+    padded_cols = framed.shape[2]
     pair_rows = 3 * channels
     tap_rows = 27 * channels
-    flat_count = frame_total * row_total * (col_total + 2)
+    flat_count = frame_total * row_total * padded_cols
     shifted = jnp.concatenate(
         [
-            jnp.pad(cot_all, ((0, 0), (0, 0), (col_tap, 2 - col_tap), (0, 0)))
+            jnp.pad(
+                cot_all,
+                ((0, 0), (0, 0), (col_tap, padded_cols - col_total - col_tap), (0, 0)),
+            )
             for col_tap in range(3)
         ],
         axis=-1,
@@ -109,7 +116,7 @@
         slab = lax.dynamic_slice(
             framed,
             (depth_tap, row_tap, 0, 0),
-            (frame_total, row_total, col_total + 2, channels),
+            (frame_total, row_total, padded_cols, channels),
         ).reshape(flat_count, channels)
         product = lax.dot_general(
             slab, shifted, (((0,), (0,)), ((), ())), preferred_element_type=jnp.float32
@@ -127,43 +134,43 @@
     hidden = jax.nn.silu(normed).astype(jnp.bfloat16)
     height_count = lax.axis_size("height")
     frame_devices = lax.axis_size("tm")
-    share_width = channels // height_count
     frame_index = lax.axis_index("tm")
     row_index = lax.axis_index("height")
     total_rows = row_count * height_count
     total_frames = frame_count * frame_devices
     tap_rows = 27 * channels
     share_rows = tap_rows // frame_devices
+    padded_cols = -(-(col_count + 2) // 8) * 8
+    right_pad = padded_cols - col_count - 1
     inverse_root = 1.0 / math.sqrt(total_frames * total_rows * col_count)
     weight_cube = weight.reshape(3, 3, 3, channels, channels)
 
-    hidden_all = lax.all_gather(hidden, ("tm", "height"), axis=0, tiled=True).reshape(
-        total_frames, total_rows, col_count, channels
-    )
-    framed = jnp.pad(hidden_all, ((2, 0), (1, 1), (1, 1), (0, 0)))
-
-    shared_cot = lax.all_to_all(cotangent, "height", split_axis=3, concat_axis=1, tiled=True)
-    cot_all = lax.all_gather(shared_cot, "tm", axis=0, tiled=True)
+    both_frames = lax.all_gather(
+        jnp.concatenate([hidden, cotangent], axis=-1), "tm", axis=0, tiled=True
+    )
+    hidden_all = lax.all_gather(both_frames[..., :channels], "height", axis=1, tiled=True)
+    framed = jnp.pad(hidden_all, ((2, 0), (1, 1), (1, right_pad), (0, 0)))
+
+    cot_frames = both_frames[..., channels:]
+    cot_all = lax.all_to_all(cot_frames, "height", split_axis=3, concat_axis=1, tiled=True)
 
     window = lax.dynamic_slice(
         framed,
         (frame_index * frame_count, row_index * row_count, 0, 0),
-        (frame_count + 2, row_count + 2, col_count + 2, channels),
-    )
-    conv_out = forward_sum(window, forward_arrange(weight_cube), row_count, col_count).reshape(
+        (frame_count + 2, row_count + 2, padded_cols, channels),
+    )
+    conv_out = forward_sum(window, weight_cube, row_count, col_count).reshape(
         frame_count, row_count, col_count, channels
     )
     output = (latent_wide + conv_out + bias).astype(jnp.bfloat16)
 
     weight_grad = block_weight_grad(framed, cot_all, frame_index, share_rows, channels) * inverse_root
 
-    cotangent_edged = padded(cotangent, (("height", 1),), 1)
-    next_frame = shifted_2(cotangent_edged, "tm", -1)
-    second_next = shifted_2(cotangent_edged, "tm", -2)
-    future_block = jnp.pad(
-        jnp.concatenate([cotangent_edged, next_frame, second_next], axis=0),
-        ((0, 0), (0, 0), (1, 1), (0, 0)),
-    )
+    cot_future = lax.dynamic_slice_in_dim(
+        jnp.pad(cot_frames, ((0, 2), (0, 0), (0, 0), (0, 0))), frame_index * frame_count, 3, 0
+    )
+    cotangent_edged = padded(cot_future, (("height", 1),), 1)
+    future_block = jnp.pad(cotangent_edged, ((0, 0), (0, 0), (1, right_pad), (0, 0)))
     hidden_grad = backward_sum(
         future_block, backward_arrange(weight_cube), row_count, col_count
     ).reshape(frame_count, row_count, col_count, channels)

time: 215 us -> 189 us (0.88)
  blocking collectives: 50 us -> 0 us
  waiting for transfers between devices: 24.6 us -> 60.8 us
  local copies, waits for them, and re-layouts: 60.9 us -> 30.4 us
  matrix products: 33.1 us -> 50.9 us
  other arithmetic: 18.8 us -> 22.6 us
    all_gather x1 -> x0, blocking collectives: 50 us -> none  [local(): cot_all = lax.all_gather(shared_cot, 'tm', axis=0, tiled=True)]
    all_gather x1 -> x2, waiting for transfers between devices: 0.01 us -> 46.4 us  [the longest x1 46.4 us: local(): lax.all_gather(jnp.concatenate([hidden, cotangent], axis=-1), 'tm', axis=...]
    dot_general x9 -> x27, matrix products: 10.7 us -> 35.4 us  [forward_sum(): jnp.dot(slab, cube[depth_tap, row_tap, col_tap], preferred_element_type=j...]
    ppermute x2 -> x0, waiting for transfers between devices: 21.5 us -> none  [shifted_2(): return lax.ppermute(value, axis, pairs)]
    reshape x7 -> x2, local copies, waits for them, and re-layouts: 27.8 us -> 8.22 us  [the longest x1 4.7 us: block_weight_grad(): shifted = jnp.concatenate([jnp.pad(cot_all, ((0, 0), (0, 0), (col_tap, pa...]
    transpose x1 -> x0, local copies, waits for them, and re-layouts: 15.1 us -> none  [forward_arrange(): return cube.transpose(0, 1, 3, 2, 4).reshape(9, inputs, 3 * outputs)]
    all_to_all x1, waiting for transfers between devices: 0.01 us -> 14.4 us  [local(): lax.all_to_all(cot_frames, 'height', split_axis=3, concat_axis=1, tiled=T...]
    dot_general x3, matrix products: 11.7 us -> 5.4 us  [block_weight_grad(): lax.dot_general(slab, shifted, (((0,), (0,)), ((), ())), preferred_elemen...]
  transfers between devices with their start and end apart: 6 -> 5, of which waited for: 2 -> 2; matrix products, arithmetic and copies ran while one was open for 17% -> 21% of each run, Pallas kernels for 0% -> 0%
where the time goes in v2:
time: 189 us; the launch traced here: 188 us
  waiting for transfers between devices  60.8 us (32%)
  matrix products  50.9 us (27%)
  local copies, waits for them, and re-layouts  30.4 us (16%)
  other arithmetic  22.6 us (12%)
  between operations  14.7 us (8%)
  starting transfers between devices  8.38 us (4%)
    all_gather x1, waiting for transfers between devices, local(): lax.all_gather(jnp.concatenate([hidden, cotangent], axis=-1), 'tm', axis=...  46.4 us
    dot_general x27, matrix products, forward_sum(): jnp.dot(slab, cube[depth_tap, row_tap, col_tap], preferred_element_type=j...  35.4 us
    all_to_all x1, waiting for transfers between devices, local(): lax.all_to_all(cot_frames, 'height', split_axis=3, concat_axis=1, tiled=T...  14.4 us
    dot_general x9, matrix products, backward_sum(): jnp.dot(slab, arranged[3 * depth_tap + row_tap], preferred_element_type=j...  10.1 us
    dynamic_slice x4, local copies, waits for them, and re-layouts, block_weight_grad(): lax.dynamic_slice(framed, (depth_tap, row_tap, 0, 0), (frame_total, row_t...  7.24 us
    concatenate x1, other arithmetic, block_weight_grad(): jnp.concatenate([jnp.pad(cot_all, ((0, 0), (0, 0), (col_tap, padded_cols...  7.03 us
    dot_general x3, matrix products, block_weight_grad(): lax.dot_general(slab, shifted, (((0,), (0,)), ((), ())), preferred_elemen...  5.4 us
    reduce_sum x1, other arithmetic, local(): inner = jnp.mean(scaled_grad * unit_latent, axis=-1, keepdims=True)  4.96 us
  transfers between devices with their start and end apart: 5, of which 2 were waited for; matrix products, arithmetic and copies ran while one was open for 21% of the time, Pallas kernels for 0%

profile of v2, /device:TPU:0, one launch (start us, length us, event | category | flops | bytes accessed | tf_op | source)
XLA Modules:
  0.0 187.9 jit_solution(11848573941314849512)
XLA Ops:
  7.2 2.1 %multiply_reduce_fusion.1 = f32[2,160]{1,0:T(2,128)S(1)} fusion(bf16[1,2,160,384]{3,2,1,0:T(8,128)(2,1)} %param.5), kind=kLoop, calls=%fused_computation.98 | loop fusion | flops 368320 | bytes 247040 | tf_op jit(solution)/shard_map/reduce_sum | solution.py:132
  9.3 1.3 copy.57
  10.6 2.5 %multiply_convert_fusion = (bf16[1,2,160,384]{3,0,2,1:T(2,128)(2,1)S(1)}, f32[1,2,160,384]{3,0,2,1:T(1,128)S(1)}, f32[1,2,160,384]{3,0,2,1:T(1,128)S(1)}) fusion(f32[384]{0:T(512)} %param.6, f32[2,160]{1,0:T(2,128)S(1)} %add_sqrt_fusion, bf16[1,2,160,384]{3,2,1,0:T(8,128)(2,1)} %param.5), kind=kLoop, calls=%fused_computation.96 | loop fusion | flops 983040 | bytes 1477376 | tf_op jit(solution)/shard_map/convert_element_type | solution.py:134
  13.1 1.0 pad_maximum_fusion
  14.1 0.8 copy.58
  15.1 46.4 %all-gather.3.cloned.1.call-done = bf16[4,2,160,768]{3,2,1,0:T(8,128)(2,1)} async-done(((bf16[1,2,160,768]{3,2,1,0:T(8,128)(2,1)}), bf16[4,2,160,768]{3,2,1,0:T(8,128)(2,1)}) %all-gather.3.cloned.1.call-update) | async-done | bytes 1966096 | tf_op jit(solution)/shard_map/all_gather | solution.py:148
  61.4 1.7 fusion.27
  63.1 1.0 pad_dynamic-slice_fusion.13
  64.1 2.5 %collective-permute-start = (bf16[3,1,160,384]{3,2,1,0:T(8,128)(2,1)}, bf16[3,1,160,384]{3,2,1,0:T(8,128)(2,1)}, u32[]{:S(2)}, u32[]{:S(2)}) collective-permute-start(bf16[3,1,160,384]{3,2,1,0:T(8,128)(2,1)} %get-tuple-element.43), channel_id=1, source_target_pairs={{0,1},{1,2},{2,3},{4,5},{5,6},{6,7},{8,9},{9,10},{10,11},{12,13},{... | collective-permute-start | bytes 1105928 | tf_op jit(solution)/shard_map/ppermute | solution.py:23
  66.6 1.3 collective-permute-start.1
  67.9 1.0 copy.59
  69.1 2.5 %copy.62 = bf16[4,2,160,384]{2,0,1,3:T(4,128)(2,1)} copy(bf16[4,2,160,384]{3,2,1,0:T(8,128)(2,1)S(1)} %get-tuple-element.32) | data formatting | bytes 1966080 | tf_op jit(solution)/shard_map/slice | solution.py:154
  71.7 4.5 %all-to-all-start = ((bf16[4,2,160,384]{2,0,1,3:T(4,128)(2,1)}), bf16[4,2,160,384]{2,0,1,3:T(4,128)(2,1)S(1)}, u32[]{:S(2)}, u32[]{:S(2)}) async-start(bf16[4,2,160,384]{2,0,1,3:T(4,128)(2,1)} %copy.62), calls=%async_computation | async-start | bytes 3145728 | tf_op jit(solution)/shard_map/all_to_all | solution.py:155
  76.4 1.8 fusion.11
  78.4 2.5 %fusion.15 = f32[336,1152]{1,0:T(8,128)S(1)} fusion(bf16[336,384]{1,0:T(8,128)(2,1)S(1)} %bitcast.303, bf16[9,384,1152]{1,2,0:T(8,128)(2,1)} %bitcast.215), kind=kOutput, calls=%fused_computation.84 | convolution fusion | flops 297271296 | bytes 2691072 | tf_op jit(solution)/shard_map/dot_general | solution.py:73
  80.9 1.8 convolution_add_fusion.7
  82.7 0.7 convolution_add_fusion.6
  83.4 0.7 convolution_add_fusion.5
  84.7 0.7 convolution_add_fusion.3
  85.3 0.7 convolution_add_fusion.2
  86.0 0.7 convolution_add_fusion.1
  86.7 1.9 convolution_add_fusion
  88.5 3.5 %reshape.118 = f32[2,168,3,384]{3,2,1,0:T(4,128)} reshape(f32[336,1152]{1,0:T(8,128)} %convolution_add_fusion) | data formatting | bytes 3096576 | tf_op jit(solution)/shard_map/reshape | solution.py:77
  92.1 5.0 %multiply_reduce_fusion = (f32[2,160]{1,0:T(2,128)S(1)}, f32[1,2,160,384]{3,0,2,1:T(1,128)S(1)}) fusion(f32[1,2,160,384]{3,0,2,1:T(1,128)S(1)} %get-tuple-element.19, f32[1,2,160,384]{3,0,2,1:T(1,128)S(1)} %get-tuple-element.18, f32[384]{0:T(512)S(1)} %copy-done.3, f32[2,168,3,384]{3,2,1,0:T(4,128)} %reshape.118), kind=kLoop, calls=%fused_computation.94 | loop fusion | flops 1351360 | bytes 2951936 | tf_op jit(solution)/shard_map/reduce_sum | solution.py:181
  97.1 1.0 fusion.19
  98.0 0.7 copy.72
  98.8 14.4 %all-to-all-done = bf16[4,2,160,384]{2,0,1,3:T(4,128)(2,1)S(1)} async-done(((bf16[4,2,160,384]{2,0,1,3:T(4,128)(2,1)}), bf16[4,2,160,384]{2,0,1,3:T(4,128)(2,1)S(1)}, u32[]{:S(2)}, u32[]{:S(2)}) %all-to-all-start) | async-done | bytes 983072 | tf_op jit(solution)/shard_map/all_to_all | solution.py:155
  113.1 2.5 %copy.64 = bf16[4,4,2,160,96]{4,3,2,1,0:T(8,128)(2,1)} copy(bf16[4,4,2,160,96]{3,0,2,4,1:T(4,128)(2,1)S(1)} %bitcast.254) | data formatting | bytes 1966080 | tf_op jit(solution)/shard_map/all_to_all | solution.py:155
  115.7 7.0 %fusion.5 = bf16[4,8,168,288]{3,2,1,0:T(8,128)(2,1)} fusion(bf16[4,8,160,96]{3,2,1,0:T(8,128)(2,1)} %bitcast.255), kind=kLoop, calls=%fused_computation.23 | loop fusion | flops 21676032 | bytes 4079616 | tf_op jit(solution)/shard_map/concatenate | solution.py:98
  122.7 4.7 %copy.75 = bf16[5376,288]{0,1:T(8,128)(2,1)S(1)} copy(bf16[5376,288]{1,0:T(8,128)(2,1)} %bitcast.253) | data formatting | bytes 6193152 | tf_op jit(solution)/shard_map/reshape | solution.py:107
  127.5 2.1 %pad_dynamic-slice_fusion.11 = (bf16[1,2,168,384]{3,2,0,1:T(8,128)(2,1)S(1)}, bf16[1,2,168,384]{3,2,0,1:T(8,128)(2,1)S(1)}, bf16[1,2,168,384]{3,2,0,1:T(8,128)(2...) fusion(s32[]{:T(128)S(6)} %add.285, ...), kind=kLoop, calls=%fused_computation.11 | loop fusion | bytes 6254616 | tf_op jit(solution)/shard_map/slice | solution.py:51
  129.5 1.3 fusion.21
  130.8 1.3 fusion.22
  132.1 1.3 fusion.23
  133.4 1.3 convolution_add_fusion.15
  134.8 1.3 convolution_add_fusion.23
  136.1 1.3 convolution_add_fusion.14
  137.4 1.3 convolution_add_fusion.22
  138.7 1.3 convolution_add_fusion.13
  140.0 1.3 convolution_add_fusion.21
  141.3 1.3 convolution_add_fusion.12
  142.6 1.3 convolution_add_fusion.20
  144.0 1.3 convolution_add_fusion.11
  145.3 1.3 convolution_add_fusion.19
  146.6 1.3 convolution_add_fusion.10
  147.9 1.3 convolution_add_fusion.18
  149.2 1.3 convolution_add_fusion.9
  150.5 1.3 convolution_add_fusion.17
  151.8 1.3 convolution_add_fusion.8
  153.2 1.3 convolution_add_fusion.16
  154.5 1.3 convolution_add_fusion.31
  155.8 1.3 convolution_add_fusion.30
  157.1 1.3 convolution_add_fusion.29
  158.4 1.3 convolution_add_fusion.28
  159.7 1.3 convolution_add_fusion.27
  161.1 1.5 convolution_add_fusion.26
  162.6 1.3 convolution_add_fusion.25
  163.9 1.3 convolution_add_fusion.24
  165.9 0.7 copy.71
  166.6 5.8 %pad_dynamic-slice_fusion.8 = (bf16[4,8,168,384]{3,2,0,1:T(8,128)(2,1)S(1)}, bf16[4,8,168,384]{3,2,0,1:T(8,128)(2,1)S(1)}, bf16[4,8,168,384]{3,2,0,1:T(8,128)(2,1)S(1)}) fusion(s32[]{:T(128)S(6)} %select_n.68, s32[]{:T(128)S(6)} %select_n.70, bf16[4,8,160,384]{3,2,0,1:T(8,128)(2,1)S(1)} %copy-done, s32[]{:T(128)S(6)} %select_n.60, s32[]{:T(128)S(6)} %select_n.62, ...), kind=kLoop, calls=%fused_computation.8 | loop fusion | bytes 16318488 | tf_op jit(solution)/shard_map/dynamic_slice | solution.py:116
  172.9 1.8 convolution_bitcast_fusion
  175.2 1.8 convolution_bitcast_fusion.2
  177.6 1.8 convolution_bitcast_fusion.1
  179.4 1.7 fusion.14
  (35 shorter events, 3.3 us)
Async XLA Ops:
  7.2 54.2 %all-gather.3.cloned.1.call-start = ((), (), s32[]{:S(2)}) async-start(), calls=%async_computation.1 | async-start | bytes 2457600 | tf_op jit(solution)/shard_map/all_gather | solution.py:148
  15.0 112.5 %all-gather.5.cloned.1.call-start = ((), (), s32[]{:S(2)}) async-start(), calls=%async_computation.2 | async-start | bytes 4915200 | tf_op jit(solution)/shard_map/all_gather | solution.py:151
  64.1 12.2 %collective-permute-start = (bf16[3,1,160,384]{3,2,1,0:T(8,128)(2,1)}, bf16[3,1,160,384]{3,2,1,0:T(8,128)(2,1)}, u32[]{:S(2)}, u32[]{:S(2)}) collective-permute-start(bf16[3,1,160,384]{3,2,1,0:T(8,128)(2,1)} %get-tuple-element.43), channel_id=1, source_target_pairs={{0,1},{1,2},{2,3},{4,5},{5,6},{6,7},{8,9},{9,10},{10,11},{12,13},{... | collective-permute-start | bytes 1105928 | tf_op jit(solution)/shard_map/ppermute | solution.py:23
  66.6 9.7 %collective-permute-start.1 = (bf16[3,1,160,384]{3,2,1,0:T(8,128)(2,1)}, bf16[3,1,160,384]{3,2,1,0:T(8,128)(2,1)}, u32[]{:S(2)}, u32[]{:S(2)}) collective-permute-start(bf16[3,1,160,384]{3,2,1,0:T(8,128)(2,1)} %get-tuple-element.44), channel_id=1, source_target_pairs={{1,0},{2,1},{3,2},{5,4},{6,5},{7,6},{9,8},{10,9},{11,10},{13,12},{... | collective-permute-start | bytes 1105928 | tf_op jit(solution)/shard_map/ppermute | solution.py:25
  71.7 41.5 %all-to-all-start = ((bf16[4,2,160,384]{2,0,1,3:T(4,128)(2,1)}), bf16[4,2,160,384]{2,0,1,3:T(4,128)(2,1)S(1)}, u32[]{:S(2)}, u32[]{:S(2)}) async-start(bf16[4,2,160,384]{2,0,1,3:T(4,128)(2,1)} %copy.62), calls=%async_computation | async-start | bytes 3145728 | tf_op jit(solution)/shard_map/all_to_all | solution.py:155
  76.3 6.3 %slice-start = ((s8[7962624]{0:T(1024)(128)(4,1)}), s8[4194304]{0:T(1024)(128)(4,1)S(1)}, s32[]{:S(2)}) async-start(s8[7962624]{0:T(1024)(128)(4,1)} %bitcast.244), calls=%async_computation.3 | async-start | bytes 8388608
  78.2 4.5 %slice-start.1 = ((s8[7962624]{0:T(1024)(128)(4,1)}), s8[3768320]{0:T(1024)(128)(4,1)S(1)}, s32[]{:S(2)}) async-start(s8[7962624]{0:T(1024)(128)(4,1)} %bitcast.244), calls=%async_computation.4 | async-start | bytes 7536640
  86.7 5.4 %copy-start.3 = (f32[384]{0:T(512)S(1)}, f32[384]{0:T(512)}, u32[]{:S(2)}) copy-start(f32[384]{0:T(512)} %param.6) | copy-start | bytes 4612
  88.5 8.5 %copy-start.2 = (bf16[1,2,160,384]{3,2,1,0:T(8,128)(2,1)S(1)}, bf16[1,2,160,384]{3,2,1,0:T(8,128)(2,1)}, u32[]{:S(2)}) copy-start(bf16[1,2,160,384]{3,2,1,0:T(8,128)(2,1)} %param.9) | copy-start | bytes 737284
  159.7 5.6 %copy-start.1 = (bf16[1,2,160,384]{3,2,1,0:T(8,128)(2,1)S(1)}, bf16[1,2,160,384]{3,2,1,0:T(8,128)(2,1)}, u32[]{:S(2)}) copy-start(bf16[1,2,160,384]{3,2,1,0:T(8,128)(2,1)} %param.5) | copy-start | bytes 737284
  159.7 5.6 %copy-start.4 = (f32[384]{0:T(512)S(1)}, f32[384]{0:T(512)}, u32[]{:S(2)}) copy-start(f32[384]{0:T(512)} %param.7) | copy-start | bytes 4612
  161.1 5.5 %copy-start = (bf16[4,8,160,384]{3,2,0,1:T(8,128)(2,1)S(1)}, bf16[4,8,160,384]{3,2,0,1:T(8,128)(2,1)}, u32[]{:S(2)}) copy-start(bf16[4,8,160,384]{3,2,0,1:T(8,128)(2,1)} %all-gather.5.cloned.1.call-done) | copy-start | bytes 11796484
Sparse Core Ops, SparseCore 0:
  15.1 46.2 all-gather.2
  69.1 49.8 all-gather.4

commit v3 on v2

--- a/solution.py
+++ b/solution.py
@@ -39,26 +39,16 @@
     return cube.transpose(0, 1, 4, 2, 3).reshape(9, outputs, 3 * inputs)
 
 
-def forward_sum(window, cube, row_total, col_total):
-    width = window.shape[-1]
-    padded_cols = window.shape[2]
-    slots = cube.shape[-1]
-    totals = []
-    for col_tap in range(3):
-        total = None
-        for depth_tap in range(3):
-            for row_tap in range(3):
-                slab = window[depth_tap, row_tap : row_tap + row_total].reshape(
-                    row_total * padded_cols, width
+def forward_sum(window, weight, row_total, col_total):
+    pieces = []
+    for depth_tap in range(3):
+        for row_tap in range(3):
+            for col_tap in range(3):
+                pieces.append(
+                    window[depth_tap, row_tap : row_tap + row_total, col_tap : col_tap + col_total]
                 )
-                product = jnp.dot(
-                    slab, cube[depth_tap, row_tap, col_tap], preferred_element_type=jnp.float32
-                )
-                total = product if total is None else total + product
-        totals.append(total.reshape(row_total, padded_cols, slots))
-    return (
-        totals[0][:, 0:col_total] + totals[1][:, 1 : col_total + 1] + totals[2][:, 2 : col_total + 2]
-    )
+    patch = jnp.concatenate(pieces, axis=-1).reshape(row_total * col_total, weight.shape[0])
+    return jnp.dot(patch, weight, preferred_element_type=jnp.float32)
 
 
 def backward_sum(window, arranged, row_total, col_total):
@@ -126,6 +116,43 @@
     return lax.dynamic_slice_in_dim(stacked, first_row - first_pair * pair_rows, share_rows, 0)
 
 
+def gather_rows(own, height_count):
+    frame_total, row_count, col_count, channels = own.shape
+    height_index = lax.axis_index("height")
+    core = height_index % 2
+    chip = height_index // 2
+    chips = height_count // 2
+    first = core == 0
+    sibling = [(i, i ^ 1) for i in range(height_count)]
+    twin = lax.ppermute(own, "height", sibling)
+    chip_rows = jnp.where(
+        first, jnp.concatenate([own, twin], axis=1), jnp.concatenate([twin, own], axis=1)
+    )
+    if chips == 1:
+        return chip_rows
+    half = col_count // 2
+    mine = lax.dynamic_slice_in_dim(chip_rows, core * half, half, axis=2)
+    got = jnp.concatenate(
+        [
+            lax.ppermute(
+                mine, "height", [(i, (i + 2 * step) % height_count) for i in range(height_count)]
+            )
+            for step in range(1, chips)
+        ],
+        axis=1,
+    )
+    other = lax.ppermute(got, "height", sibling)
+    full = jnp.where(
+        first, jnp.concatenate([got, other], axis=2), jnp.concatenate([other, got], axis=2)
+    )
+    relative = jnp.concatenate([chip_rows, full], axis=1)
+    block = 2 * row_count
+    reverse = jnp.concatenate(
+        [relative[:, step * block : (step + 1) * block] for step in reversed(range(chips))], axis=1
+    )
+    return jnp.roll(reverse, (chip + 1) * block, axis=1)
+
+
 def local(latents, gain, bias, weight, cotangent):
     frame_count, row_count, col_count, channels = latents.shape
     latent_wide = latents.astype(jnp.float32)
@@ -148,7 +175,7 @@
     both_frames = lax.all_gather(
         jnp.concatenate([hidden, cotangent], axis=-1), "tm", axis=0, tiled=True
     )
-    hidden_all = lax.all_gather(both_frames[..., :channels], "height", axis=1, tiled=True)
+    hidden_all = gather_rows(both_frames[..., :channels], height_count)
     framed = jnp.pad(hidden_all, ((2, 0), (1, 1), (1, right_pad), (0, 0)))
 
     cot_frames = both_frames[..., channels:]
@@ -159,7 +186,7 @@
         (frame_index * frame_count, row_index * row_count, 0, 0),
         (frame_count + 2, row_count + 2, padded_cols, channels),
     )
-    conv_out = forward_sum(window, weight_cube, row_count, col_count).reshape(
+    conv_out = forward_sum(window, weight, row_count, col_count).reshape(
         frame_count, row_count, col_count, channels
     )
     output = (latent_wide + conv_out + bias).astype(jnp.bfloat16)

time: 189 us -> 166 us (0.88)
  matrix products: 50.9 us -> 19.1 us
  local copies, waits for them, and re-layouts: 30.4 us -> 36.1 us
  starting transfers between devices: 8.38 us -> 11.2 us
    dot_general x27 -> x1, matrix products: 35.4 us -> 4.33 us  [forward_sum(): return jnp.dot(patch, weight, preferred_element_type=jnp.float32)]
    ppermute x0 -> x3, waiting for transfers between devices: none -> 15.5 us  [the longest x1 15.5 us: gather_rows(): lax.ppermute(mine, 'height', [(i, (i + 2 * step) % height_count) for i in...]
    all_to_all x1, waiting for transfers between devices: 14.4 us -> 0.01 us  [local(): lax.all_to_all(cot_frames, 'height', split_axis=3, concat_axis=1, tiled=T...]
    select_n x0 -> x2, other arithmetic: none -> 4.62 us  [the longest x1 2.67 us: gather_rows(): jnp.where(first, jnp.concatenate([got, other], axis=2), jnp.concatenate([...]
    reduce_sum x1, other arithmetic: 4.96 us -> 1.38 us  [local(): inner = jnp.mean(scaled_grad * unit_latent, axis=-1, keepdims=True)]
    all_to_all x1 -> x2, local copies, waits for them, and re-layouts: 2.55 us -> 5.95 us  [local(): lax.all_to_all(cot_frames, 'height', split_axis=3, concat_axis=1, tiled=T...]
    concatenate x0 -> x1, other arithmetic: none -> 3.1 us  [gather_rows(): return jnp.roll(reverse, (chip + 1) * block, axis=1)]
    ppermute x0 -> x3, starting transfers between devices: none -> 2.53 us  [the longest x1 1.98 us: gather_rows(): lax.ppermute(mine, 'height', [(i, (i + 2 * step) % height_count) for i in...]
  transfers between devices with their start and end apart: 5 -> 7, of which waited for: 2 -> 2; matrix products, arithmetic and copies ran while one was open for 21% -> 27% of each run, Pallas kernels for 0% -> 0%
where the time goes in v3:
time: 166 us; the launch traced here: 165 us
  waiting for transfers between devices  61.9 us (37%)
  local copies, waits for them, and re-layouts  36.1 us (22%)
  other arithmetic  22.2 us (13%)
  matrix products  19.1 us (12%)
  between operations  14.4 us (9%)
  starting transfers between devices  11.2 us (7%)
    all_gather x1, waiting for transfers between devices, local(): lax.all_gather(jnp.concatenate([hidden, cotangent], axis=-1), 'tm', axis=...  46.4 us
    ppermute x1, waiting for transfers between devices, gather_rows(): lax.ppermute(mine, 'height', [(i, (i + 2 * step) % height_count) for i in...  15.5 us
    dot_general x9, matrix products, backward_sum(): jnp.dot(slab, arranged[3 * depth_tap + row_tap], preferred_element_type=j...  9.48 us
    all_to_all x2, local copies, waits for them, and re-layouts, local(): lax.all_to_all(cot_frames, 'height', split_axis=3, concat_axis=1, tiled=T...  5.95 us
    dynamic_slice x1, local copies, waits for them, and re-layouts, block_weight_grad(): lax.dynamic_slice(framed, (depth_tap, row_tap, 0, 0), (frame_total, row_t...  5.95 us
    reshape x1, local copies, waits for them, and re-layouts, block_weight_grad(): shifted = jnp.concatenate([jnp.pad(cot_all, ((0, 0), (0, 0), (col_tap, pa...  5.86 us
    dot_general x3, matrix products, block_weight_grad(): lax.dot_general(slab, shifted, (((0,), (0,)), ((), ())), preferred_elemen...  5.28 us
    concatenate x1, other arithmetic, block_weight_grad(): jnp.concatenate([jnp.pad(cot_all, ((0, 0), (0, 0), (col_tap, padded_cols...  4.73 us
  transfers between devices with their start and end apart: 7, of which 2 were waited for; matrix products, arithmetic and copies ran while one was open for 27% of the time, Pallas kernels for 0%

profile of v3, /device:TPU:0, one launch (start us, length us, event | category | flops | bytes accessed | tf_op | source)
XLA Modules:
  0.0 164.9 jit_solution(16844759611404679913)
XLA Ops:
  7.2 1.1 fusion.42
  8.3 1.2 multiply_convert_fusion
  9.5 1.8 %pad_maximum_fusion = bf16[1,2,160,768]{3,2,1,0:T(8,128)(2,1)} fusion(bf16[1,2,160,384]{3,2,1,0:T(8,128)(2,1)} %param.9, bf16[1,2,160,384]{3,2,1,0:T(8,128)(2,1)S(1)} %multiply_convert_fusion), kind=kLoop, calls=%fused_computation.97 | loop fusion | flops 983040 | bytes 983040 | tf_op jit(solution)/shard_map/concatenate | solution.py:176
  11.3 46.4 %all-gather.2.cloned.1.call-done = bf16[4,2,160,768]{3,2,1,0:T(8,128)(2,1)} async-done(((bf16[1,2,160,768]{3,2,1,0:T(8,128)(2,1)}), bf16[4,2,160,768]{3,2,1,0:T(8,128)(2,1)}) %all-gather.2.cloned.1.call-update) | async-done | bytes 1966096 | tf_op jit(solution)/shard_map/all_gather | solution.py:175
  57.7 1.7 %fusion.76 = (bf16[4,2,160,384]{3,2,1,0:T(8,128)(2,1)S(1)}, bf16[4,2,160,384]{3,2,1,0:T(8,128)(2,1)S(1)}) fusion(bf16[4,2,160,768]{3,2,1,0:T(8,128)(2,1)} %all-gather.2.cloned.1.call-done), kind=kLoop, calls=%fused_computation.139 | loop fusion | bytes 3932160 | tf_op jit(solution)/shard_map/slice | solution.py:181
  59.5 1.1 pad_dynamic-slice_fusion.35
  60.6 1.3 collective-permute-start.4
  61.9 3.8 %collective-permute-start.3 = (bf16[3,1,160,384]{3,2,1,0:T(8,128)(2,1)}, bf16[3,1,160,384]{3,2,1,0:T(8,128)(2,1)}, u32[]{:S(2)}, u32[]{:S(2)}) collective-permute-start(bf16[3,1,160,384]{3,2,1,0:T(8,128)(2,1)} %get-tuple-element.22), channel_id=1, source_target_pairs={{0,1},{1,2},{2,3},{4,5},{5,6},{6,7},{8,9},{9,10},{10,11},{12,13},{... | collective-permute-start | bytes 1105928 | tf_op jit(solution)/shard_map/ppermute | solution.py:23
  65.7 3.0 %copy.27 = bf16[4,2,160,384]{2,1,0,3:T(2,128)(2,1)} copy(bf16[4,2,160,384]{3,2,1,0:T(8,128)(2,1)S(1)} %get-tuple-element.11) | data formatting | bytes 1966080 | tf_op jit(solution)/shard_map/slice | solution.py:181
  68.7 0.5 collective-permute-start
  69.2 3.6 %all-to-all-start = ((bf16[4,2,160,384]{2,1,0,3:T(2,128)(2,1)}), bf16[4,2,160,384]{2,1,0,3:T(2,128)(2,1)S(1)}, u32[]{:S(2)}, u32[]{:S(2)}) async-start(bf16[4,2,160,384]{2,1,0,3:T(2,128)(2,1)} %copy.27), calls=%async_computation | async-start | bytes 3145728 | tf_op jit(solution)/shard_map/all_to_all | solution.py:182
  72.8 0.1 pad_dynamic-slice_fusion.36
  73.0 1.7 %fusion.17 = bf16[3,4,168,384]{3,2,1,0:T(8,128)(2,1)S(1)} fusion(bf16[3,1,160,384]{3,2,1,0:T(8,128)(2,1)} %collective-permute-done.4, bf16[3,2,160,384]{3,2,1,0:T(8,128)(2,1)S(1)} %pad_dynamic-slice_fusion.36, bf16[3,1,160,384]{3,2,1,0:T(8,128)(2,1)} %collective-permute-done.3), kind=kLoop, calls=%fused_computation.70 | loop fusion | flops 9289728 | bytes 3022848 | tf_op jit(solution)/shard_map/concatenate | solution.py:21
  74.7 0.2 fusion.77
  74.9 1.9 %fusion.41 = f32[336,1152]{1,0:T(8,128)S(1)} fusion(bf16[336,384]{1,0:T(8,128)(2,1)S(1)} %bitcast.157, bf16[9,384,1152]{1,2,0:T(8,128)(2,1)} %bitcast.124), kind=kOutput, calls=%fused_computation.93 | convolution fusion | flops 297271296 | bytes 2691072 | tf_op jit(solution)/shard_map/dot_general | solution.py:63
  76.9 1.8 %convolution_add_fusion.7 = f32[336,1152]{1,0:T(8,128)S(1)} fusion(f32[336,1152]{1,0:T(8,128)S(1)} %fusion.41, bf16[336,384]{1,0:T(8,128)(2,1)S(1)} %bitcast.156, bf16[9,384,1152]{1,2,0:T(8,128)(2,1)} %bitcast.125), kind=kOutput, calls=%fused_computation.60 | convolution fusion | flops 297658368 | bytes 4239360 | tf_op jit(solution)/shard_map/dot_general | solution.py:63
  78.7 0.7 convolution_add_fusion.6
  79.4 0.7 convolution_add_fusion.5
  80.0 0.7 convolution_add_fusion.4
  80.7 0.6 convolution_add_fusion.3
  81.3 0.7 convolution_add_fusion.2
  82.0 0.7 convolution_add_fusion.1
  82.7 1.9 %maximum_select_fusion = bf16[4,4,160,384]{3,2,1,0:T(8,128)(2,1)S(1)} fusion(bf16[4,2,160,384]{3,2,1,0:T(8,128)(2,1)} %collective-permute-done, bf16[4,2,160,384]{3,2,1,0:T(8,128)(2,1)S(1)} %copy-done.3, pred[]{:T(512)S(6)} %eq.11), kind=kLoop, calls=%fused_computation.61 | loop fusion | flops 2949120 | bytes 3932161 | tf_op jit(solution)/shard_map/jit(_where)/select_n | solution.py:128
  84.6 1.1 constant_dynamic-slice_fusion
  85.7 2.0 %collective-permute-start.1 = (bf16[4,4,80,384]{3,2,1,0:T(8,128)(2,1)}, bf16[4,4,80,384]{3,2,1,0:T(8,128)(2,1)}, u32[]{:S(2)}, u32[]{:S(2)}) collective-permute-start(bf16[4,4,80,384]{3,2,1,0:T(8,128)(2,1)} %constant_dynamic-slice_fusion), channel_id=1, source_target_pairs={{0,2},{1,3},{2,0},{3,1},{4,6},{5,7},{6,4},{7,5},{8,10},{9,11},{10,... | collective-permute-start | bytes 2949128 | tf_op jit(solution)/shard_map/ppermute | solution.py:137
  87.7 1.8 %convolution_add_fusion = f32[336,1152]{1,0:T(8,128)} fusion(f32[336,1152]{1,0:T(8,128)S(1)} %convolution_add_fusion.1, bf16[336,384]{1,0:T(8,128)(2,1)S(1)} %bitcast.149, bf16[9,384,1152]{1,2,0:T(8,128)(2,1)S(1)} %bitcast.134), kind=kOutput, calls=%fused_computation.53 | convolution fusion | flops 297658368 | bytes 4239360 | tf_op jit(solution)/shard_map/dot_general | solution.py:63
  89.5 3.5 %reshape.218 = f32[2,168,3,384]{3,2,1,0:T(4,128)} reshape(f32[336,1152]{1,0:T(8,128)} %convolution_add_fusion) | data formatting | bytes 3096576 | tf_op jit(solution)/shard_map/reshape | solution.py:67
  93.0 4.2 %fusion.75 = (f32[2,160,1,384]{3,2,1,0:T(1,128)S(1)}, f32[2,160,1,384]{3,2,1,0:T(1,128)S(1)}, f32[2,160,1,384]{3,2,1,0:T(1,128)S(1)}) fusion(f32[2,168,3,384]{3,2,1,0:T(4,128)} %reshape.218), kind=kLoop, calls=%fused_computation.138 | loop fusion | bytes 2949120 | tf_op jit(solution)/shard_map/slice | solution.py:69
  97.2 1.4 multiply_reduce_fusion
  98.5 15.5 %collective-permute-done.1 = bf16[4,4,80,384]{3,2,1,0:T(8,128)(2,1)} collective-permute-done((bf16[4,4,80,384]{3,2,1,0:T(8,128)(2,1)}, bf16[4,4,80,384]{3,2,1,0:T(8,128)(2,1)}, u32[]{:S(2)}, u32[]{:S(2)}) %collective-permute-start.1) | collective-permute-done | bytes 983072 | tf_op jit(solution)/shard_map/ppermute | solution.py:137
  114.0 0.9 add_convert_fusion
  114.9 4.4 %copy.34 = bf16[4,2,160,4,96]{4,3,2,1,0:T(4,128)(2,1)} copy(bf16[4,2,160,4,96]{2,1,0,4,3:T(2,128)(2,1)S(1)} %bitcast.137) | data formatting | bytes 1966080 | tf_op jit(solution)/shard_map/all_to_all | solution.py:182
  119.4 1.5 copy.29
  120.9 4.7 %fusion.8 = bf16[4,8,168,288]{3,2,1,0:T(8,128)(2,1)} fusion(bf16[4,8,160,96]{3,2,1,0:T(8,128)(2,1)S(1)} %bitcast.139), kind=kLoop, calls=%fused_computation.48 | loop fusion | flops 21676032 | bytes 4079616 | tf_op jit(solution)/shard_map/concatenate | solution.py:88
  125.6 5.9 %copy.35 = bf16[5376,288]{0,1:T(8,128)(2,1)} copy(bf16[5376,288]{1,0:T(8,128)(2,1)} %bitcast.123) | data formatting | bytes 6193152 | tf_op jit(solution)/shard_map/reshape | solution.py:97
  131.5 2.7 %maximum_select_fusion.1 = bf16[4,4,160,384]{3,2,1,0:T(8,128)(2,1)S(1)} fusion(bf16[4,4,80,384]{3,2,1,0:T(8,128)(2,1)} %collective-permute-done.2, bf16[4,4,80,384]{3,2,1,0:T(8,128)(2,1)} %collective-permute-done.1, pred[]{:T(512)S(6)} %eq.11), kind=kLoop, calls=%fused_computation.62 | loop fusion | flops 8847360 | bytes 3932161 | tf_op jit(solution)/shard_map/jit(_where)/select_n | solution.py:145
  134.2 3.1 %fusion.11 = bf16[4,8,160,384]{3,2,1,0:T(8,128)(2,1)S(1)} fusion(s32[]{:T(128)S(6)} %select_n.97, bf16[4,4,160,384]{3,2,1,0:T(8,128)(2,1)S(1)} %maximum_select_fusion.1, bf16[4,4,160,384]{3,2,1,0:T(8,128)(2,1)S(1)} %maximum_select_fusion), kind=kLoop, calls=%fused_computation.51 | loop fusion | flops 5898240 | bytes 7864324 | tf_op jit(solution)/shard_map/jit(_roll_dynamic)/concatenate | solution.py:153
  137.3 0.1 fusion.47
  137.4 0.1 fusion.57
  137.5 0.1 fusion.58
  137.6 0.1 fusion.48
  137.7 0.1 fusion.59
  137.8 0.1 fusion.60
  137.9 0.1 fusion.49
  138.1 0.1 fusion.62
  138.3 0.1 fusion.50
  138.5 0.1 fusion.64
  138.6 0.1 fusion.51
  138.8 0.1 fusion.66
  138.9 0.1 fusion.52
  139.1 0.1 fusion.68
  139.3 0.1 fusion.53
  139.5 0.1 fusion.70
  139.6 0.1 fusion.54
  139.8 0.1 fusion.72
  139.9 0.1 fusion.55
  140.1 0.1 fusion.56
  140.3 5.9 %pad_dynamic-slice_fusion.26 = (bf16[4,8,168,384]{3,2,1,0:T(8,128)(2,1)S(1)}, bf16[4,8,168,384]{3,2,1,0:T(8,128)(2,1)S(1)}, bf16[4,8,168,384]{3,2,1,0:T(8,128)(2,1)S(1)}) fusion(s32[]{:T(128)S(6)} %select_n.110, s32[]{:T(128)S(6)} %select_n.112, bf16[4,8,160,384]{3,2,1,0:T(8,128)(2,1)S(1)} %fusion.11, s32[]{:T(128)S(6)} %select_n.102, s32[]{:T(128)S(6)} %select_n.104, ...), kind=kLoop, calls=%fused_computation.26 | loop fusion | bytes 16318488 | tf_op jit(solution)/shard_map/dynamic_slice | solution.py:106
  146.2 1.8 %convolution_bitcast_fusion.2 = f32[3,12,8,384]{3,2,1,0:T(8,128)S(1)} fusion(bf16[5376,384,1]{1,0,2:T(8,128)(2,1)S(1)} %bitcast.142, bf16[3,96,5376]{2,1,0:T(8,128)(2,1)S(1)} %bitcast.143), kind=kOutput, calls=%fused_computation.79 | convolution fusion | flops 1189085184 | bytes 7667712 | tf_op jit(solution)/shard_map/dot_general | solution.py:111
  148.1 1.8 %convolution_bitcast_fusion.1 = f32[3,12,8,384]{3,2,1,0:T(8,128)S(1)} fusion(bf16[5376,384,1]{1,0,2:T(8,128)(2,1)S(1)} %bitcast.141, bf16[3,96,5376]{2,1,0:T(8,128)(2,1)S(1)} %bitcast.144), kind=kOutput, calls=%fused_computation.78 | convolution fusion | flops 1189085184 | bytes 7667712 | tf_op jit(solution)/shard_map/dot_general | solution.py:111
  149.9 1.8 %convolution_bitcast_fusion = f32[3,12,8,384]{3,2,1,0:T(8,128)S(1)} fusion(bf16[5376,384,1]{1,0,2:T(8,128)(2,1)S(1)} %bitcast.140, bf16[3,96,5376]{2,1,0:T(8,128)(2,1)S(1)} %bitcast.145), kind=kOutput, calls=%fused_computation.77 | convolution fusion | flops 1189085184 | bytes 7667712 | tf_op jit(solution)/shard_map/dot_general | solution.py:111
  151.7 0.3 slice-done.3
  152.0 4.3 %fusion.33 = bf16[1,2,160,384]{3,2,1,0:T(8,128)(2,1)} fusion(bf16[10368,384]{1,0:T(8,128)(2,1)S(1)} %bitcast.136, bf16[1,2,160,10368]{3,2,1,0:T(8,128)(2,1)S(1)} %fusion.56, bf16[1,2,160,384]{3,2,1,0:T(8,128)(2,1)S(1)} %copy-done.1, f32[384]{0:T(512)S(1)} %copy-done.7), kind=kOutput, calls=%fused_computation.80 | convolution fusion | flops 2548531200 | bytes 15091200 | tf_op jit(solution)/shard_map/dot_general | solution.py:51
  156.4 1.6 fusion.40
  (45 shorter events, 0.9 us)
Async XLA Ops:
  7.2 50.6 %all-gather.2.cloned.1.call-start = ((), (), s32[]{:S(2)}) async-start(), calls=%async_computation.1 | async-start | bytes 2457600 | tf_op jit(solution)/shard_map/all_gather | solution.py:175
  59.4 13.5 %copy-start.2 = (bf16[4,2,160,384]{3,2,1,0:T(8,128)(2,1)}, bf16[4,2,160,384]{3,2,1,0:T(8,128)(2,1)S(1)}, u32[]{:S(2)}) copy-start(bf16[4,2,160,384]{3,2,1,0:T(8,128)(2,1)S(1)} %get-tuple-element.12) | copy-start | bytes 2949124
  60.6 12.3 %collective-permute-start.4 = (bf16[3,1,160,384]{3,2,1,0:T(8,128)(2,1)}, bf16[3,1,160,384]{3,2,1,0:T(8,128)(2,1)}, u32[]{:S(2)}, u32[]{:S(2)}) collective-permute-start(bf16[3,1,160,384]{3,2,1,0:T(8,128)(2,1)} %get-tuple-element.23), channel_id=1, source_target_pairs={{1,0},{2,1},{3,2},{5,4},{6,5},{7,6},{9,8},{10,9},{11,10},{13,12},{... | collective-permute-start | bytes 1105928 | tf_op jit(solution)/shard_map/ppermute | solution.py:25
  61.9 11.1 %collective-permute-start.3 = (bf16[3,1,160,384]{3,2,1,0:T(8,128)(2,1)}, bf16[3,1,160,384]{3,2,1,0:T(8,128)(2,1)}, u32[]{:S(2)}, u32[]{:S(2)}) collective-permute-start(bf16[3,1,160,384]{3,2,1,0:T(8,128)(2,1)} %get-tuple-element.22), channel_id=1, source_target_pairs={{0,1},{1,2},{2,3},{4,5},{5,6},{6,7},{8,9},{9,10},{10,11},{12,13},{... | collective-permute-start | bytes 1105928 | tf_op jit(solution)/shard_map/ppermute | solution.py:23
  68.7 14.0 %collective-permute-start = (bf16[4,2,160,384]{3,2,1,0:T(8,128)(2,1)S(1)}, bf16[4,2,160,384]{3,2,1,0:T(8,128)(2,1)}, u32[]{:S(2)}, u32[]{:S(2)}) collective-permute-start(bf16[4,2,160,384]{3,2,1,0:T(8,128)(2,1)S(1)} %get-tuple-element.12), channel_id=1, source_target_pairs={{0,1},{1,0},{2,3},{3,2},{4,5},{5,4},{6,7},{7,6},{8,9},{9,8},{10,11... | collective-permute-start | bytes 2949128 | tf_op jit(solution)/shard_map/ppermute | solution.py:127
  69.2 45.7 %all-to-all-start = ((bf16[4,2,160,384]{2,1,0,3:T(2,128)(2,1)}), bf16[4,2,160,384]{2,1,0,3:T(2,128)(2,1)S(1)}, u32[]{:S(2)}, u32[]{:S(2)}) async-start(bf16[4,2,160,384]{2,1,0,3:T(2,128)(2,1)} %copy.27), calls=%async_computation | async-start | bytes 3145728 | tf_op jit(solution)/shard_map/all_to_all | solution.py:182
  73.0 5.7 %slice-start = ((s8[7962624]{0:T(1024)(128)(4,1)}), s8[4194304]{0:T(1024)(128)(4,1)S(1)}, s32[]{:S(2)}) async-start(s8[7962624]{0:T(1024)(128)(4,1)} %bitcast.126), calls=%async_computation.2 | async-start | bytes 8388608
  74.7 4.0 %slice-start.1 = ((s8[7962624]{0:T(1024)(128)(4,1)}), s8[3768320]{0:T(1024)(128)(4,1)S(1)}, s32[]{:S(2)}) async-start(s8[7962624]{0:T(1024)(128)(4,1)} %bitcast.126), calls=%async_computation.3 | async-start | bytes 7536640
  81.3 1.3 copy-start.3
  85.7 28.3 %collective-permute-start.1 = (bf16[4,4,80,384]{3,2,1,0:T(8,128)(2,1)}, bf16[4,4,80,384]{3,2,1,0:T(8,128)(2,1)}, u32[]{:S(2)}, u32[]{:S(2)}) collective-permute-start(bf16[4,4,80,384]{3,2,1,0:T(8,128)(2,1)} %constant_dynamic-slice_fusion), channel_id=1, source_target_pairs={{0,2},{1,3},{2,0},{3,1},{4,6},{5,7},{6,4},{7,5},{8,10},{9,11},{10,... | collective-permute-start | bytes 2949128 | tf_op jit(solution)/shard_map/ppermute | solution.py:137
  89.5 7.7 %copy-start.6 = (f32[384]{0:T(512)S(1)}, f32[384]{0:T(512)}, u32[]{:S(2)}) copy-start(f32[384]{0:T(512)} %param.6) | copy-start | bytes 4612
  93.0 21.0 %copy-start = (bf16[1,2,160,384]{3,2,1,0:T(8,128)(2,1)S(1)}, bf16[1,2,160,384]{3,2,1,0:T(8,128)(2,1)}, u32[]{:S(2)}) copy-start(bf16[1,2,160,384]{3,2,1,0:T(8,128)(2,1)} %param.5) | copy-start | bytes 737284
  93.0 21.0 %copy-start.5 = (bf16[1,2,160,384]{3,2,1,0:T(8,128)(2,1)S(1)}, bf16[1,2,160,384]{3,2,1,0:T(8,128)(2,1)}, u32[]{:S(2)}) copy-start(bf16[1,2,160,384]{3,2,1,0:T(8,128)(2,1)} %param.9) | copy-start | bytes 737284
  114.0 17.5 %collective-permute-start.2 = (bf16[4,4,80,384]{3,2,1,0:T(8,128)(2,1)}, bf16[4,4,80,384]{3,2,1,0:T(8,128)(2,1)}, u32[]{:S(2)}, u32[]{:S(2)}) collective-permute-start(bf16[4,4,80,384]{3,2,1,0:T(8,128)(2,1)} %collective-permute-done.1), channel_id=1, source_target_pairs={{0,1},{1,0},{2,3},{3,2},{4,5},{5,4},{6,7},{7,6},{8,9},{9,8},{10,11... | collective-permute-start | bytes 2949128 | tf_op jit(solution)/shard_map/ppermute | solution.py:144
  140.3 6.0 %copy-start.4 = (bf16[5376,288]{0,1:T(8,128)(2,1)S(1)}, bf16[5376,288]{0,1:T(8,128)(2,1)}, u32[]{:S(2)}) copy-start(bf16[5376,288]{0,1:T(8,128)(2,1)} %copy.35) | copy-start | bytes 9289732
  148.1 3.7 %slice-start.2 = ((s8[7962624]{0:T(1024)(128)(4,1)}), s8[4194304]{0:T(1024)(128)(4,1)S(1)}, s32[]{:S(2)}) async-start(s8[7962624]{0:T(1024)(128)(4,1)} %bitcast.135), calls=%async_computation.4 | async-start | bytes 8388608
  149.9 2.2 %slice-start.3 = ((s8[7962624]{0:T(1024)(128)(4,1)}), s8[3768320]{0:T(1024)(128)(4,1)S(1)}, s32[]{:S(2)}) async-start(s8[7962624]{0:T(1024)(128)(4,1)} %bitcast.135), calls=%async_computation.5 | async-start | bytes 7536640
  149.9 2.2 %copy-start.1 = (bf16[1,2,160,384]{3,2,1,0:T(8,128)(2,1)S(1)}, bf16[1,2,160,384]{3,2,1,0:T(8,128)(2,1)}, u32[]{:S(2)}) copy-start(bf16[1,2,160,384]{3,2,1,0:T(8,128)(2,1)} %param.5) | copy-start | bytes 737284
  149.9 2.1 %copy-start.7 = (f32[384]{0:T(512)S(1)}, f32[384]{0:T(512)}, u32[]{:S(2)}) copy-start(f32[384]{0:T(512)} %param.7) | copy-start | bytes 4612
Sparse Core Ops, SparseCore 0:
  11.4 46.2 all-gather.1

commit v4 on v3

--- a/solution.py
+++ b/solution.py
@@ -124,33 +124,27 @@
     chips = height_count // 2
     first = core == 0
     sibling = [(i, i ^ 1) for i in range(height_count)]
-    twin = lax.ppermute(own, "height", sibling)
-    chip_rows = jnp.where(
-        first, jnp.concatenate([own, twin], axis=1), jnp.concatenate([twin, own], axis=1)
-    )
-    if chips == 1:
-        return chip_rows
-    half = col_count // 2
-    mine = lax.dynamic_slice_in_dim(chip_rows, core * half, half, axis=2)
-    got = jnp.concatenate(
-        [
-            lax.ppermute(
-                mine, "height", [(i, (i + 2 * step) % height_count) for i in range(height_count)]
-            )
-            for step in range(1, chips)
-        ],
-        axis=1,
-    )
-    other = lax.ppermute(got, "height", sibling)
-    full = jnp.where(
-        first, jnp.concatenate([got, other], axis=2), jnp.concatenate([other, got], axis=2)
-    )
-    relative = jnp.concatenate([chip_rows, full], axis=1)
+    mine = [own] + [
+        lax.ppermute(
+            own, "height", [(i, (i + 2 * step) % height_count) for i in range(height_count)]
+        )
+        for step in range(1, chips)
+    ]
+    stacked = jnp.concatenate(mine, axis=1)
+    twins = lax.ppermute(stacked, "height", sibling)
     block = 2 * row_count
-    reverse = jnp.concatenate(
-        [relative[:, step * block : (step + 1) * block] for step in reversed(range(chips))], axis=1
-    )
-    return jnp.roll(reverse, (chip + 1) * block, axis=1)
+    relative = []
+    for step in reversed(range(chips)):
+        ours = stacked[:, step * row_count : (step + 1) * row_count]
+        theirs = twins[:, step * row_count : (step + 1) * row_count]
+        relative.append(
+            jnp.where(
+                first,
+                jnp.concatenate([ours, theirs], axis=1),
+                jnp.concatenate([theirs, ours], axis=1),
+            )
+        )
+    return jnp.roll(jnp.concatenate(relative, axis=1), (chip + 1) * block, axis=1)
 
 
 def local(latents, gain, bias, weight, cotangent):

time: 166 us -> 182 us (1.096)
  local copies, waits for them, and re-layouts: 36.1 us -> 55 us
  waiting for transfers between devices: 61.9 us -> 58.6 us
  matrix products: 19.1 us -> 21.4 us
    unnamed x50 -> x44, local copies, waits for them, and re-layouts: 3.19 us -> 21 us
    ppermute x3 -> x2, waiting for transfers between devices: 15.5 us -> 9.57 us  [the longest x1 9.57 us: gather_rows(): lax.ppermute(own, 'height', [(i, (i + 2 * step) % height_count) for i in...]
    concatenate x1 -> x2, other arithmetic: 3.1 us -> 5.81 us  [the longest x1 3.1 us: gather_rows(): jnp.roll(jnp.concatenate(relative, axis=1), (chip + 1) * block, axis=1)]
    all_to_all x1, waiting for transfers between devices: 0.01 us -> 2.63 us  [local(): lax.all_to_all(cot_frames, 'height', split_axis=3, concat_axis=1, tiled=T...]
    select_n x2, other arithmetic: 4.62 us -> 2.31 us  [gather_rows(): jnp.where(first, jnp.concatenate([ours, theirs], axis=1), jnp.concatenate...]
    dot_general x1, matrix products: 4.33 us -> 6.6 us  [forward_sum(): return jnp.dot(patch, weight, preferred_element_type=jnp.float32)]
  transfers between devices with their start and end apart: 7 -> 6, of which waited for: 2 -> 3; matrix products, arithmetic and copies ran while one was open for 27% -> 24% of each run, Pallas kernels for 0% -> 0%
where the time goes in v4:
time: 182 us; the launch traced here: 181 us
  waiting for transfers between devices  58.6 us (32%)
  local copies, waits for them, and re-layouts  55 us (30%)
  other arithmetic  21.6 us (12%)
  matrix products  21.4 us (12%)
  between operations  14.4 us (8%)
  starting transfers between devices  10.3 us (6%)
    all_gather x1, waiting for transfers between devices, local(): lax.all_gather(jnp.concatenate([hidden, cotangent], axis=-1), 'tm', axis=...  46.4 us
    unnamed x44, local copies, waits for them, and re-layouts  21 us
    ppermute x1, waiting for transfers between devices, gather_rows(): lax.ppermute(own, 'height', [(i, (i + 2 * step) % height_count) for i in...  9.57 us
    dot_general x9, matrix products, backward_sum(): jnp.dot(slab, arranged[3 * depth_tap + row_tap], preferred_element_type=j...  9.5 us
    dot_general x1, matrix products, forward_sum(): return jnp.dot(patch, weight, preferred_element_type=jnp.float32)  6.6 us
    all_to_all x2, local copies, waits for them, and re-layouts, local(): lax.all_to_all(cot_frames, 'height', split_axis=3, concat_axis=1, tiled=T...  5.95 us
    reshape x1, local copies, waits for them, and re-layouts, block_weight_grad(): shifted = jnp.concatenate([jnp.pad(cot_all, ((0, 0), (0, 0), (col_tap, pa...  5.83 us
    dynamic_slice x1, local copies, waits for them, and re-layouts, block_weight_grad(): lax.dynamic_slice(framed, (depth_tap, row_tap, 0, 0), (frame_total, row_t...  5.68 us
  transfers between devices with their start and end apart: 6, of which 3 were waited for; matrix products, arithmetic and copies ran while one was open for 24% of the time, Pallas kernels for 0%

profile of v4, /device:TPU:0, one launch (start us, length us, event | category | flops | bytes accessed | tf_op | source)
XLA Modules:
  0.0 181.3 jit_solution(15884534787191387502)
XLA Ops:
  7.2 1.1 fusion.44
  8.3 1.2 multiply_convert_fusion
  9.5 1.8 pad_maximum_fusion.3
  11.3 46.4 %all-gather.2.cloned.1.call-done = bf16[4,2,160,768]{3,2,1,0:T(8,128)(2,1)} async-done(((bf16[1,2,160,768]{3,2,1,0:T(8,128)(2,1)}), bf16[4,2,160,768]{3,2,1,0:T(8,128)(2,1)}) %all-gather.2.cloned.1.call-update) | async-done | bytes 1966096 | tf_op jit(solution)/shard_map/all_gather | solution.py:169
  57.7 1.7 fusion.78
  59.4 1.0 pad_dynamic-slice_fusion.35
  60.4 1.3 collective-permute-start.3
  61.7 3.8 %collective-permute-start.2 = (bf16[3,1,160,384]{3,2,1,0:T(8,128)(2,1)}, bf16[3,1,160,384]{3,2,1,0:T(8,128)(2,1)}, u32[]{:S(2)}, u32[]{:S(2)}) collective-permute-start(bf16[3,1,160,384]{3,2,1,0:T(8,128)(2,1)} %get-tuple-element.24), channel_id=1, source_target_pairs={{0,1},{1,2},{2,3},{4,5},{5,6},{6,7},{8,9},{9,10},{10,11},{12,13},{... | collective-permute-start | bytes 1105928 | tf_op jit(solution)/shard_map/ppermute | solution.py:23
  65.5 3.0 %copy.27 = bf16[4,2,160,384]{2,1,0,3:T(2,128)(2,1)} copy(bf16[4,2,160,384]{3,2,1,0:T(8,128)(2,1)S(1)} %get-tuple-element.11) | data formatting | bytes 1966080 | tf_op jit(solution)/shard_map/slice | solution.py:175
  68.5 1.6 collective-permute-start
  70.2 3.6 %all-to-all-start = ((bf16[4,2,160,384]{2,1,0,3:T(2,128)(2,1)}), bf16[4,2,160,384]{2,1,0,3:T(2,128)(2,1)S(1)}, u32[]{:S(2)}, u32[]{:S(2)}) async-start(bf16[4,2,160,384]{2,1,0,3:T(2,128)(2,1)} %copy.27), calls=%async_computation | async-start | bytes 3145728 | tf_op jit(solution)/shard_map/all_to_all | solution.py:176
  73.9 1.7 fusion.19
  75.8 1.9 %fusion.43 = f32[336,1152]{1,0:T(8,128)S(1)} fusion(bf16[336,384]{1,0:T(8,128)(2,1)S(1)} %bitcast.157, bf16[9,384,1152]{1,2,0:T(8,128)(2,1)} %bitcast.124), kind=kOutput, calls=%fused_computation.96 | convolution fusion | flops 297271296 | bytes 2691072 | tf_op jit(solution)/shard_map/dot_general | solution.py:63
  77.8 1.8 %convolution_add_fusion.7 = f32[336,1152]{1,0:T(8,128)S(1)} fusion(f32[336,1152]{1,0:T(8,128)S(1)} %fusion.43, bf16[336,384]{1,0:T(8,128)(2,1)S(1)} %bitcast.156, bf16[9,384,1152]{1,2,0:T(8,128)(2,1)} %bitcast.125), kind=kOutput, calls=%fused_computation.60 | convolution fusion | flops 297658368 | bytes 4239360 | tf_op jit(solution)/shard_map/dot_general | solution.py:63
  79.7 0.7 convolution_add_fusion.6
  80.3 0.7 convolution_add_fusion.5
  81.0 0.7 convolution_add_fusion.4
  83.6 9.6 %collective-permute-done = bf16[4,2,160,384]{3,2,1,0:T(8,128)(2,1)} collective-permute-done((bf16[4,2,160,384]{3,2,1,0:T(8,128)(2,1)S(1)}, bf16[4,2,160,384]{3,2,1,0:T(8,128)(2,1)}, u32[]{:S(2)}, u32[]{:S(2)}) %collective-permute-start) | collective-permute-done | bytes 983072 | tf_op jit(solution)/shard_map/ppermute | solution.py:128
  93.2 2.7 %pad_maximum_fusion.1 = bf16[4,4,160,384]{3,2,1,0:T(8,128)(2,1)} fusion(bf16[4,2,160,384]{3,2,1,0:T(8,128)(2,1)} %collective-permute-done, bf16[4,2,160,384]{3,2,1,0:T(8,128)(2,1)S(1)} %get-tuple-element.12), kind=kLoop, calls=%fused_computation.62 | loop fusion | flops 983040 | bytes 3932160 | tf_op jit(solution)/shard_map/concatenate | solution.py:133
  95.9 1.8 convolution_add_fusion
  97.7 3.6 %reshape.218 = f32[2,168,3,384]{3,2,1,0:T(4,128)} reshape(f32[336,1152]{1,0:T(8,128)} %convolution_add_fusion) | data formatting | bytes 3096576 | tf_op jit(solution)/shard_map/reshape | solution.py:67
  101.2 4.3 %fusion.77 = (f32[2,160,1,384]{3,2,1,0:T(1,128)S(1)}, f32[2,160,1,384]{3,2,1,0:T(1,128)S(1)}, f32[2,160,1,384]{3,2,1,0:T(1,128)S(1)}) fusion(f32[2,168,3,384]{3,2,1,0:T(4,128)} %reshape.218), kind=kLoop, calls=%fused_computation.140 | loop fusion | bytes 2949120 | tf_op jit(solution)/shard_map/slice | solution.py:69
  106.0 0.9 add_convert_fusion
  106.9 2.6 %all-to-all-done = bf16[4,2,160,384]{2,1,0,3:T(2,128)(2,1)S(1)} async-done(((bf16[4,2,160,384]{2,1,0,3:T(2,128)(2,1)}), bf16[4,2,160,384]{2,1,0,3:T(2,128)(2,1)S(1)}, u32[]{:S(2)}, u32[]{:S(2)}) %all-to-all-start) | async-done | bytes 983072 | tf_op jit(solution)/shard_map/all_to_all | solution.py:176
  109.6 4.4 %copy.34 = bf16[4,2,160,4,96]{4,3,2,1,0:T(4,128)(2,1)} copy(bf16[4,2,160,4,96]{2,1,0,4,3:T(2,128)(2,1)S(1)} %bitcast.137) | data formatting | bytes 1966080 | tf_op jit(solution)/shard_map/all_to_all | solution.py:176
  114.0 1.5 copy.29
  115.5 4.7 %fusion.8 = bf16[4,8,168,288]{3,2,1,0:T(8,128)(2,1)} fusion(bf16[4,8,160,96]{3,2,1,0:T(8,128)(2,1)S(1)} %bitcast.139), kind=kLoop, calls=%fused_computation.48 | loop fusion | flops 21676032 | bytes 4079616 | tf_op jit(solution)/shard_map/concatenate | solution.py:88
  120.3 5.8 %copy.35 = bf16[5376,288]{0,1:T(8,128)(2,1)} copy(bf16[5376,288]{1,0:T(8,128)(2,1)} %bitcast.123) | data formatting | bytes 6193152 | tf_op jit(solution)/shard_map/reshape | solution.py:97
  126.1 1.7 fusion.79
  128.1 2.0 %fusion.14 = bf16[4,4,160,384]{3,2,1,0:T(8,128)(2,1)S(1)} fusion(bf16[4,2,160,384]{3,2,1,0:T(8,128)(2,1)} %collective-permute-done, bf16[4,2,160,384]{3,2,1,0:T(8,128)(2,1)S(1)} %get-tuple-element.14, pred[]{:T(512)S(6)} %eq.11), kind=kLoop, calls=%fused_computation.65 | loop fusion | flops 2949120 | bytes 3932161 | tf_op jit(solution)/shard_map/jit(_where)/select_n | solution.py:141
  130.1 3.1 %fusion.11 = bf16[4,8,160,384]{3,2,1,0:T(8,128)(2,1)S(1)} fusion(s32[]{:T(128)S(6)} %select_n.93, bf16[4,4,160,384]{3,2,1,0:T(8,128)(2,1)S(1)} %fusion.14, bf16[4,4,160,384]{3,2,1,0:T(8,128)(2,1)S(1)} %fusion.13), kind=kLoop, calls=%fused_computation.51 | loop fusion | flops 5898240 | bytes 7864324 | tf_op jit(solution)/shard_map/jit(_roll_dynamic)/concatenate | solution.py:147
  133.2 0.8 fusion.49
  134.0 0.8 fusion.59
  134.8 0.8 fusion.60
  135.6 0.8 fusion.50
  136.4 0.8 fusion.61
  137.2 0.8 fusion.62
  138.0 0.8 fusion.51
  138.8 0.8 fusion.63
  139.6 0.8 fusion.64
  140.4 0.8 fusion.52
  141.2 0.8 fusion.65
  142.0 0.8 fusion.66
  142.8 0.8 fusion.53
  143.6 0.8 fusion.67
  144.4 0.8 fusion.68
  145.2 0.8 fusion.54
  146.0 0.7 fusion.69
  146.7 0.8 fusion.70
  147.5 0.8 fusion.55
  148.3 0.8 fusion.71
  149.1 0.8 fusion.72
  149.9 0.8 fusion.56
  150.7 0.8 fusion.73
  151.5 0.8 fusion.74
  152.3 0.8 fusion.57
  153.1 0.8 fusion.75
  153.9 0.8 fusion.58
  154.7 5.7 %pad_dynamic-slice_fusion.26 = (bf16[4,8,168,384]{3,2,1,0:T(8,128)(2,1)S(1)}, bf16[4,8,168,384]{3,2,1,0:T(8,128)(2,1)S(1)}, bf16[4,8,168,384]{3,2,1,0:T(8,128)(2,1)S(1)}) fusion(s32[]{:T(128)S(6)} %select_n.106, s32[]{:T(128)S(6)} %select_n.108, bf16[4,8,160,384]{3,2,1,0:T(8,128)(2,1)S(1)} %fusion.11, s32[]{:T(128)S(6)} %select_n.98, s32[]{:T(128)S(6)} %select_n.100, ...), kind=kLoop, calls=%fused_computation.26 | loop fusion | bytes 16318488 | tf_op jit(solution)/shard_map/dynamic_slice | solution.py:106
  160.4 1.8 convolution_bitcast_fusion.2
  162.2 1.8 convolution_bitcast_fusion.1
  164.1 1.8 convolution_bitcast_fusion
  166.2 6.6 %fusion.35 = bf16[1,2,160,384]{3,2,1,0:T(8,128)(2,1)} fusion(bf16[10368,384]{1,0:T(8,128)(2,1)S(1)} %bitcast.136, bf16[1,2,160,10368]{3,2,1,0:T(8,128)(2,1)} %fusion.58, bf16[1,2,160,384]{3,2,1,0:T(8,128)(2,1)S(1)} %copy-done, f32[384]{0:T(512)S(1)} %copy-done.4), kind=kOutput, calls=%fused_computation.83 | convolution fusion | flops 2548531200 | bytes 15091200 | tf_op jit(solution)/shard_map/dot_general | solution.py:51
  172.8 1.6 fusion.42
  (38 shorter events, 3.6 us)
Async XLA Ops:
  7.2 50.6 %all-gather.2.cloned.1.call-start = ((), (), s32[]{:S(2)}) async-start(), calls=%async_computation.1 | async-start | bytes 2457600 | tf_op jit(solution)/shard_map/all_gather | solution.py:169
  60.4 13.4 %collective-permute-start.3 = (bf16[3,1,160,384]{3,2,1,0:T(8,128)(2,1)}, bf16[3,1,160,384]{3,2,1,0:T(8,128)(2,1)}, u32[]{:S(2)}, u32[]{:S(2)}) collective-permute-start(bf16[3,1,160,384]{3,2,1,0:T(8,128)(2,1)} %get-tuple-element.25), channel_id=1, source_target_pairs={{1,0},{2,1},{3,2},{5,4},{6,5},{7,6},{9,8},{10,9},{11,10},{13,12},{... | collective-permute-start | bytes 1105928 | tf_op jit(solution)/shard_map/ppermute | solution.py:25
  61.7 12.2 %collective-permute-start.2 = (bf16[3,1,160,384]{3,2,1,0:T(8,128)(2,1)}, bf16[3,1,160,384]{3,2,1,0:T(8,128)(2,1)}, u32[]{:S(2)}, u32[]{:S(2)}) collective-permute-start(bf16[3,1,160,384]{3,2,1,0:T(8,128)(2,1)} %get-tuple-element.24), channel_id=1, source_target_pairs={{0,1},{1,2},{2,3},{4,5},{5,6},{6,7},{8,9},{9,10},{10,11},{12,13},{... | collective-permute-start | bytes 1105928 | tf_op jit(solution)/shard_map/ppermute | solution.py:23
  68.5 24.6 %collective-permute-start = (bf16[4,2,160,384]{3,2,1,0:T(8,128)(2,1)S(1)}, bf16[4,2,160,384]{3,2,1,0:T(8,128)(2,1)}, u32[]{:S(2)}, u32[]{:S(2)}) collective-permute-start(bf16[4,2,160,384]{3,2,1,0:T(8,128)(2,1)S(1)} %get-tuple-element.12), channel_id=1, source_target_pairs={{0,2},{1,3},{2,0},{3,1},{4,6},{5,7},{6,4},{7,5},{8,10},{9,11},{10,... | collective-permute-start | bytes 2949128 | tf_op jit(solution)/shard_map/ppermute | solution.py:128
  70.2 39.4 %all-to-all-start = ((bf16[4,2,160,384]{2,1,0,3:T(2,128)(2,1)}), bf16[4,2,160,384]{2,1,0,3:T(2,128)(2,1)S(1)}, u32[]{:S(2)}, u32[]{:S(2)}) async-start(bf16[4,2,160,384]{2,1,0,3:T(2,128)(2,1)} %copy.27), calls=%async_computation | async-start | bytes 3145728 | tf_op jit(solution)/shard_map/all_to_all | solution.py:176
  73.9 5.7 %slice-start = ((s8[7962624]{0:T(1024)(128)(4,1)}), s8[4194304]{0:T(1024)(128)(4,1)S(1)}, s32[]{:S(2)}) async-start(s8[7962624]{0:T(1024)(128)(4,1)} %bitcast.126), calls=%async_computation.2 | async-start | bytes 8388608
  75.6 4.0 %slice-start.1 = ((s8[7962624]{0:T(1024)(128)(4,1)}), s8[3768320]{0:T(1024)(128)(4,1)S(1)}, s32[]{:S(2)}) async-start(s8[7962624]{0:T(1024)(128)(4,1)} %bitcast.126), calls=%async_computation.3 | async-start | bytes 7536640
  95.9 30.2 %collective-permute-start.1 = (bf16[4,4,160,384]{3,2,1,0:T(8,128)(2,1)}, bf16[4,4,160,384]{3,2,1,0:T(8,128)(2,1)}, u32[]{:S(2)}, u32[]{:S(2)}) collective-permute-start(bf16[4,4,160,384]{3,2,1,0:T(8,128)(2,1)} %pad_maximum_fusion.1), channel_id=1, source_target_pairs={{0,1},{1,0},{2,3},{3,2},{4,5},{5,4},{6,7},{7,6},{8,9},{9,8},{10,11... | collective-permute-start | bytes 5898248 | tf_op jit(solution)/shard_map/ppermute | solution.py:134
  97.7 7.9 %copy-start = (bf16[1,2,160,384]{3,2,1,0:T(8,128)(2,1)S(1)}, bf16[1,2,160,384]{3,2,1,0:T(8,128)(2,1)}, u32[]{:S(2)}) copy-start(bf16[1,2,160,384]{3,2,1,0:T(8,128)(2,1)} %param.5) | copy-start | bytes 737284
  97.7 7.9 %copy-start.3 = (f32[384]{0:T(512)S(1)}, f32[384]{0:T(512)}, u32[]{:S(2)}) copy-start(f32[384]{0:T(512)} %param.6) | copy-start | bytes 4612
  97.7 8.3 %copy-start.2 = (bf16[1,2,160,384]{3,2,1,0:T(8,128)(2,1)S(1)}, bf16[1,2,160,384]{3,2,1,0:T(8,128)(2,1)}, u32[]{:S(2)}) copy-start(bf16[1,2,160,384]{3,2,1,0:T(8,128)(2,1)} %param.9) | copy-start | bytes 737284
  154.7 5.7 %copy-start.1 = (bf16[5376,288]{0,1:T(8,128)(2,1)S(1)}, bf16[5376,288]{0,1:T(8,128)(2,1)}, u32[]{:S(2)}) copy-start(bf16[5376,288]{0,1:T(8,128)(2,1)} %copy.35) | copy-start | bytes 9289732
  162.2 3.7 %slice-start.2 = ((s8[7962624]{0:T(1024)(128)(4,1)}), s8[4194304]{0:T(1024)(128)(4,1)S(1)}, s32[]{:S(2)}) async-start(s8[7962624]{0:T(1024)(128)(4,1)} %bitcast.135), calls=%async_computation.4 | async-start | bytes 8388608
  164.0 2.2 %slice-start.3 = ((s8[7962624]{0:T(1024)(128)(4,1)}), s8[3768320]{0:T(1024)(128)(4,1)S(1)}, s32[]{:S(2)}) async-start(s8[7962624]{0:T(1024)(128)(4,1)} %bitcast.135), calls=%async_computation.5 | async-start | bytes 7536640
  164.0 2.2 %copy-start.4 = (f32[384]{0:T(512)S(1)}, f32[384]{0:T(512)}, u32[]{:S(2)}) copy-start(f32[384]{0:T(512)} %param.7) | copy-start | bytes 4612
Sparse Core Ops, SparseCore 0:
  11.4 46.2 all-gather.1

commit v5 on v3

--- a/solution.py
+++ b/solution.py
@@ -39,35 +39,30 @@
     return cube.transpose(0, 1, 4, 2, 3).reshape(9, outputs, 3 * inputs)
 
 
-def forward_sum(window, weight, row_total, col_total):
-    pieces = []
-    for depth_tap in range(3):
-        for row_tap in range(3):
-            for col_tap in range(3):
-                pieces.append(
-                    window[depth_tap, row_tap : row_tap + row_total, col_tap : col_tap + col_total]
-                )
-    patch = jnp.concatenate(pieces, axis=-1).reshape(row_total * col_total, weight.shape[0])
-    return jnp.dot(patch, weight, preferred_element_type=jnp.float32)
-
-
-def backward_sum(window, arranged, row_total, col_total):
-    width = window.shape[-1]
-    slots = arranged.shape[-1] // 3
-    total = None
-    for depth_tap in range(3):
-        for row_tap in range(3):
-            slab = window[2 - depth_tap, 2 - row_tap : 2 - row_tap + row_total].reshape(
-                row_total * window.shape[2], width
-            )
-            product = jnp.dot(
-                slab, arranged[3 * depth_tap + row_tap], preferred_element_type=jnp.float32
-            )
-            total = product if total is None else total + product
-    total = total.reshape(row_total, window.shape[2], 3, slots)
-    return (
-        total[:, 2 : col_total + 2, 0] + total[:, 1 : col_total + 1, 1] + total[:, 0:col_total, 2]
-    )
+def forward_conv(window, cube, row_total, col_total):
+    window = window[:, :, : col_total + 2]
+    result = lax.conv_general_dilated(
+        window[None],
+        cube,
+        (1, 1, 1),
+        "VALID",
+        dimension_numbers=("NDHWC", "DHWIO", "NDHWC"),
+        preferred_element_type=jnp.float32,
+    )
+    return result[0, 0]
+
+
+def backward_conv(window, cube, row_total, col_total):
+    window = window[:, :, : col_total + 2]
+    result = lax.conv_general_dilated(
+        window[None],
+        jnp.flip(cube, (0, 1, 2)),
+        (1, 1, 1),
+        "VALID",
+        dimension_numbers=("NDHWC", "DHWOI", "NDHWC"),
+        preferred_element_type=jnp.float32,
+    )
+    return result[0, 0]
 
 
 def pair_count(tap_rows, share_rows, pair_rows, parts):
@@ -186,7 +181,7 @@
         (frame_index * frame_count, row_index * row_count, 0, 0),
         (frame_count + 2, row_count + 2, padded_cols, channels),
     )
-    conv_out = forward_sum(window, weight, row_count, col_count).reshape(
+    conv_out = forward_conv(window, weight_cube, row_count, col_count).reshape(
         frame_count, row_count, col_count, channels
     )
     output = (latent_wide + conv_out + bias).astype(jnp.bfloat16)
@@ -198,9 +193,7 @@
     )
     cotangent_edged = padded(cot_future, (("height", 1),), 1)
     future_block = jnp.pad(cotangent_edged, ((0, 0), (0, 0), (1, right_pad), (0, 0)))
-    hidden_grad = backward_sum(
-        future_block, backward_arrange(weight_cube), row_count, col_count
-    ).reshape(frame_count, row_count, col_count, channels)
+    hidden_grad = backward_conv(future_block, weight_cube, row_count, col_count).reshape(frame_count, row_count, col_count, channels)
     sigmoid_pre = jax.nn.sigmoid(normed)
     normed_grad = hidden_grad * sigmoid_pre * (1.0 + normed * (1.0 - sigmoid_pre))
     scaled_grad = normed_grad * gain

time: 166 us -> 163 us (0.982)
  waiting for transfers between devices: 61.9 us -> 74.2 us
  local copies, waits for them, and re-layouts: 36.1 us -> 26.3 us
  matrix products: 19.1 us -> 12.9 us
  other arithmetic: 22.2 us -> 24 us
    dot_general x10 -> x0, matrix products: 13.8 us -> none  [the longest x9 9.48 us: backward_sum(): jnp.dot(slab, arranged[3 * depth_tap + row_tap], preferred_element_type=j...]
    ppermute x1, waiting for transfers between devices: 15.5 us -> 27.8 us  [gather_rows(): lax.ppermute(mine, 'height', [(i, (i + 2 * step) % height_count) for i in...]
    conv_general_dilated x0 -> x2, matrix products: none -> 7.63 us  [the longest x1 3.85 us: forward_conv(): lax.conv_general_dilated(window[None], cube, (1, 1, 1), 'VALID', dimensio...]
    slice x2 -> x0, local copies, waits for them, and re-layouts: 4.38 us -> none  [the longest x1 4.18 us: backward_sum(): total[:, 2:col_total + 2, 0] + total[:, 1:col_total + 1, 1]]
    reshape x1 -> x0, local copies, waits for them, and re-layouts: 3.51 us -> none  [backward_sum(): total = total.reshape(row_total, window.shape[2], 3, slots)]
    all_to_all x2 -> x1, local copies, waits for them, and re-layouts: 5.95 us -> 2.56 us  [local(): lax.all_to_all(cot_frames, 'height', split_axis=3, concat_axis=1, tiled=T...]
    concatenate x1, other arithmetic: 4.73 us -> 6.85 us  [block_weight_grad(): jnp.concatenate([jnp.pad(cot_all, ((0, 0), (0, 0), (col_tap, padded_cols...]
    concatenate x1 -> x0, other arithmetic: 1.7 us -> none  [padded(): jnp.concatenate([lax.ppermute(tail, axis, [(i, (i + 1) % count) for i in...]
  transfers between devices with their start and end apart: 7 -> 7, of which waited for: 2 -> 2; matrix products, arithmetic and copies ran while one was open for 27% -> 18% of each run, Pallas kernels for 0% -> 0%
where the time goes in v5:
time: 163 us
  waiting for transfers between devices  74.2 us (46%)
  local copies, waits for them, and re-layouts  26.3 us (16%)
  other arithmetic  24 us (15%)
  between operations  14.7 us (9%)
  matrix products  12.9 us (8%)
  starting transfers between devices  10.8 us (7%)
    all_gather x1, waiting for transfers between devices, local(): lax.all_gather(jnp.concatenate([hidden, cotangent], axis=-1), 'tm', axis=...  46.4 us
    ppermute x1, waiting for transfers between devices, gather_rows(): lax.ppermute(mine, 'height', [(i, (i + 2 * step) % height_count) for i in...  27.8 us
    concatenate x1, other arithmetic, block_weight_grad(): jnp.concatenate([jnp.pad(cot_all, ((0, 0), (0, 0), (col_tap, padded_cols...  6.85 us
    dynamic_slice x1, local copies, waits for them, and re-layouts, block_weight_grad(): lax.dynamic_slice(framed, (depth_tap, row_tap, 0, 0), (frame_total, row_t...  5.95 us
    reshape x1, local copies, waits for them, and re-layouts, block_weight_grad(): shifted = jnp.concatenate([jnp.pad(cot_all, ((0, 0), (0, 0), (col_tap, pa...  5.83 us
    dot_general x3, matrix products, block_weight_grad(): lax.dot_general(slab, shifted, (((0,), (0,)), ((), ())), preferred_elemen...  5.29 us
    slice x2, local copies, waits for them, and re-layouts, local(): cot_frames = both_frames[..., channels:]  4.22 us
    all_to_all x1, starting transfers between devices, local(): lax.all_to_all(cot_frames, 'height', split_axis=3, concat_axis=1, tiled=T...  3.99 us
  transfers between devices with their start and end apart: 7, of which 2 were waited for; matrix products, arithmetic and copies ran while one was open for 18% of the time, Pallas kernels for 0%

profile of v5, /device:TPU:0, one launch (start us, length us, event | category | flops | bytes accessed | tf_op | source)
XLA Modules:
  0.0 162.9 jit_solution(1942063175031027070)
XLA Ops:
  7.2 0.0 all-gather.2.cloned.1.call-start
  7.2 1.1 fusion.43
  8.3 1.2 multiply_convert_fusion
  9.5 1.8 %pad_maximum_fusion = bf16[1,2,160,768]{3,2,1,0:T(8,128)(2,1)} fusion(bf16[1,2,160,384]{3,2,1,0:T(8,128)(2,1)} %param.9, bf16[1,2,160,384]{3,2,1,0:T(8,128)(2,1)S(1)} %multiply_convert_fusion), kind=kLoop, calls=%fused_computation.71 | loop fusion | flops 983040 | bytes 983040 | tf_op jit(solution)/shard_map/concatenate | solution.py:171
  11.3 0.0 all-gather.2.cloned.1.call-update
  11.3 46.4 %all-gather.2.cloned.1.call-done = bf16[4,2,160,768]{3,2,1,0:T(8,128)(2,1)} async-done(((bf16[1,2,160,768]{3,2,1,0:T(8,128)(2,1)}), bf16[4,2,160,768]{3,2,1,0:T(8,128)(2,1)}) %all-gather.2.cloned.1.call-update) | async-done | bytes 1966096 | tf_op jit(solution)/shard_map/all_gather | solution.py:170
  57.7 1.7 %fusion.55 = (bf16[4,2,160,384]{3,2,1,0:T(8,128)(2,1)S(1)}, bf16[4,2,160,384]{3,2,1,0:T(8,128)(2,1)S(1)}) fusion(bf16[4,2,160,768]{3,2,1,0:T(8,128)(2,1)} %all-gather.2.cloned.1.call-done), kind=kLoop, calls=%fused_computation.90 | loop fusion | bytes 3932160 | tf_op jit(solution)/shard_map/slice | solution.py:176
  59.4 0.0 copy-start.4
  59.4 0.1 collective-permute-start
  59.5 1.1 pad_dynamic-slice_fusion.9
  60.6 3.0 %collective-permute-start.3 = (bf16[3,1,160,384]{3,2,1,0:T(8,128)(2,1)}, bf16[3,1,160,384]{3,2,1,0:T(8,128)(2,1)}, u32[]{:S(2)}, u32[]{:S(2)}) collective-permute-start(bf16[3,1,160,384]{3,2,1,0:T(8,128)(2,1)} %get-tuple-element.20), channel_id=1, source_target_pairs={{0,1},{1,2},{2,3},{4,5},{5,6},{6,7},{8,9},{9,10},{10,11},{12,13},{... | collective-permute-start | bytes 1105928 | tf_op jit(solution)/shard_map/ppermute | solution.py:23
  63.6 1.3 collective-permute-start.4
  65.1 2.5 %copy.98 = bf16[4,2,160,384]{2,0,1,3:T(4,128)(2,1)} copy(bf16[4,2,160,384]{3,2,1,0:T(8,128)(2,1)S(1)} %get-tuple-element.18) | data formatting | bytes 1966080 | tf_op jit(solution)/shard_map/slice | solution.py:176
  67.7 4.0 %all-to-all-start = ((bf16[4,2,160,384]{2,0,1,3:T(4,128)(2,1)}), bf16[4,2,160,384]{2,0,1,3:T(4,128)(2,1)S(1)}, u32[]{:S(2)}, u32[]{:S(2)}) async-start(bf16[4,2,160,384]{2,0,1,3:T(4,128)(2,1)} %copy.98), calls=%async_computation | async-start | bytes 3145728 | tf_op jit(solution)/shard_map/all_to_all | solution.py:177
  71.6 0.1 pad_dynamic-slice_fusion.10
  71.8 0.0 collective-permute-done.3
  71.8 1.6 fusion.30
  73.3 0.0 slice-start
  73.4 0.6 copy.111
  73.9 0.0 copy-start.5
  74.0 0.6 pad.32.clone
  74.5 0.0 slice-start.1
  74.6 0.2 copy.95
  74.8 0.0 copy-start.10
  74.8 0.0 collective-permute-done
  74.8 0.6 copy-done.5
  75.4 2.5 %maximum_select_fusion = bf16[4,4,160,384]{3,2,1,0:T(8,128)(2,1)S(1)} fusion(bf16[4,2,160,384]{3,2,1,0:T(8,128)(2,1)} %collective-permute-done, bf16[4,2,160,384]{3,2,1,0:T(8,128)(2,1)S(1)} %copy-done.5, pred[]{:T(512)S(6)} %eq.11), kind=kLoop, calls=%fused_computation.28 | loop fusion | flops 2949120 | bytes 3932161 | tf_op jit(solution)/shard_map/jit(_where)/select_n | solution.py:123
  77.9 0.1 constant_dynamic-slice_fusion
  78.0 2.4 %collective-permute-start.1 = (bf16[4,4,80,384]{3,2,1,0:T(8,128)(2,1)S(1)}, bf16[4,4,80,384]{3,2,1,0:T(8,128)(2,1)}, u32[]{:S(2)}, u32[]{:S(2)}) collective-permute-start(bf16[4,4,80,384]{3,2,1,0:T(8,128)(2,1)S(1)} %constant_dynamic-slice_fusion), channel_id=1, source_target_pairs={{0,2},{1,3},{2,0},{3,1},{4,6},{5,7},{6,4},{7,5},{8,10},{9,11},{10,... | collective-permute-start | bytes 2949128 | tf_op jit(solution)/shard_map/ppermute | solution.py:132
  80.4 0.0 copy-start.2
  80.4 0.0 copy-start.8
  80.4 3.8 %fusion.32 = f32[1,2,8,21,384]{4,2,3,1,0:T(8,128)S(1)} fusion(bf16[3,3,3,384,384]{4,3,2,1,0:T(8,128)(2,1)S(1)} %bitcast.91, bf16[3,4,1,7,2,384]{5,3,4,1,0,2:T(8,128)(2,1)S(1)} %slice.32, bf16[3,4,1,8,21,384]{5,3,4,1,0,2:T(8,128)(2,1)S(1)} %copy.95, pred[8,21]{0,1:T(8,128)(4,1)S(1)} %copy-done.10), kind=kOutput, calls=%fused_computation.58 | convolution fusion | flops 2680657920 | bytes 10156200 | tf_op jit(solution)/shard_map/conv_general_dilated | solution.py:57
  84.2 0.3 copy.96
  84.5 0.2 slice.33
  84.7 0.0 copy-start
  84.7 0.4 multiply_reduce_fusion
  85.1 27.8 %collective-permute-done.1 = bf16[4,4,80,384]{3,2,1,0:T(8,128)(2,1)} collective-permute-done((bf16[4,4,80,384]{3,2,1,0:T(8,128)(2,1)S(1)}, bf16[4,4,80,384]{3,2,1,0:T(8,128)(2,1)}, u32[]{:S(2)}, u32[]{:S(2)}) %collective-permute-start.1) | collective-permute-done | bytes 983072 | tf_op jit(solution)/shard_map/ppermute | solution.py:132
  112.9 0.0 collective-permute-start.2
  112.9 2.6 %copy.100 = bf16[4,4,2,160,96]{4,3,2,1,0:T(8,128)(2,1)} copy(bf16[4,4,2,160,96]{3,0,2,4,1:T(4,128)(2,1)S(1)} %bitcast.74) | data formatting | bytes 1966080 | tf_op jit(solution)/shard_map/all_to_all | solution.py:177
  115.5 6.9 %fusion.5 = bf16[4,8,168,288]{3,2,1,0:T(8,128)(2,1)} fusion(bf16[4,8,160,96]{3,2,1,0:T(8,128)(2,1)} %bitcast.77), kind=kLoop, calls=%fused_computation.17 | loop fusion | flops 21676032 | bytes 4079616 | tf_op jit(solution)/shard_map/concatenate | solution.py:83
  122.3 5.8 %copy.107 = bf16[5376,288]{0,1:T(8,128)(2,1)} copy(bf16[5376,288]{1,0:T(8,128)(2,1)} %bitcast.73) | data formatting | bytes 6193152 | tf_op jit(solution)/shard_map/reshape | solution.py:92
  128.2 2.7 %maximum_select_fusion.1 = bf16[4,4,160,384]{3,2,1,0:T(8,128)(2,1)S(1)} fusion(bf16[4,4,80,384]{3,2,1,0:T(8,128)(2,1)} %collective-permute-done.2, bf16[4,4,80,384]{3,2,1,0:T(8,128)(2,1)} %collective-permute-done.1, pred[]{:T(512)S(6)} %eq.11), kind=kLoop, calls=%fused_computation.29 | loop fusion | flops 8847360 | bytes 3932161 | tf_op jit(solution)/shard_map/jit(_where)/select_n | solution.py:140
  130.8 3.1 %fusion.8 = bf16[4,8,160,384]{3,2,1,0:T(8,128)(2,1)S(1)} fusion(s32[]{:T(128)S(6)} %select_n.97, bf16[4,4,160,384]{3,2,1,0:T(8,128)(2,1)S(1)} %maximum_select_fusion.1, bf16[4,4,160,384]{3,2,1,0:T(8,128)(2,1)S(1)} %maximum_select_fusion), kind=kLoop, calls=%fused_computation.20 | loop fusion | flops 5898240 | bytes 7864324 | tf_op jit(solution)/shard_map/jit(_roll_dynamic)/concatenate | solution.py:148
  134.0 0.0 slice-start.2
  134.0 0.5 fusion.28
  134.5 0.0 slice-start.3
  134.5 0.6 copy.110
  135.1 0.6 pad.30.clone
  135.6 0.2 copy.90
  135.9 0.2 slice-done.2
  136.1 1.3 slice-done.3
  137.4 3.9 %fusion.35 = f32[1,2,8,21,384]{4,2,3,1,0:T(8,128)S(1)} fusion(bf16[3,3,3,384,384]{4,3,2,1,0:T(8,128)(2,1)S(1)} %bitcast.94, bf16[3,4,1,7,2,384]{5,3,4,1,0,2:T(8,128)(2,1)S(1)} %slice.29, bf16[3,4,1,8,21,384]{5,3,4,1,0,2:T(8,128)(2,1)S(1)} %copy.90, pred[8,21]{0,1:T(8,128)(4,1)S(1)} %copy-done.10), kind=kOutput, calls=%fused_computation.59 | convolution fusion | flops 2680657920 | bytes 10156200 | tf_op jit(solution)/shard_map/conv_general_dilated | solution.py:44
  141.3 0.3 copy.91
  141.6 0.2 slice.30
  141.8 5.9 %pad_dynamic-slice_fusion = (bf16[4,8,168,384]{3,2,1,0:T(8,128)(2,1)S(1)}, bf16[4,8,168,384]{3,2,1,0:T(8,128)(2,1)S(1)}, bf16[4,8,168,384]{3,2,1,0:T(8,128)(2,1)S(1)}) fusion(s32[]{:T(128)S(6)} %select_n.110, s32[]{:T(128)S(6)} %select_n.112, bf16[4,8,160,384]{3,2,1,0:T(8,128)(2,1)S(1)} %fusion.8, s32[]{:T(128)S(6)} %select_n.102, s32[]{:T(128)S(6)} %select_n.104, ...), kind=kLoop, calls=%fused_computation.2 | loop fusion | bytes 16318488 | tf_op jit(solution)/shard_map/dynamic_slice | solution.py:101
  147.7 1.8 %convolution_bitcast_fusion = f32[3,12,8,384]{3,2,1,0:T(8,128)S(1)} fusion(bf16[5376,384,1]{1,0,2:T(8,128)(2,1)S(1)} %bitcast.80, bf16[3,96,5376]{2,1,0:T(8,128)(2,1)S(1)} %bitcast.81), kind=kOutput, calls=%fused_computation.55 | convolution fusion | flops 1189085184 | bytes 7667712 | tf_op jit(solution)/shard_map/dot_general | solution.py:106
  149.5 1.8 %convolution_bitcast_fusion.2 = f32[3,12,8,384]{3,2,1,0:T(8,128)S(1)} fusion(bf16[5376,384,1]{1,0,2:T(8,128)(2,1)S(1)} %bitcast.79, bf16[3,96,5376]{2,1,0:T(8,128)(2,1)S(1)} %bitcast.82), kind=kOutput, calls=%fused_computation.57 | convolution fusion | flops 1189085184 | bytes 7667712 | tf_op jit(solution)/shard_map/dot_general | solution.py:106
  151.3 0.0 copy-start.1
  151.3 0.0 copy-start.3
  151.3 0.0 copy-start.7
  151.3 0.0 copy-start.9
  151.3 1.8 %convolution_bitcast_fusion.1 = f32[3,12,8,384]{3,2,1,0:T(8,128)S(1)} fusion(bf16[5376,384,1]{1,0,2:T(8,128)(2,1)S(1)} %bitcast.78, bf16[3,96,5376]{2,1,0:T(8,128)(2,1)S(1)} %bitcast.83), kind=kOutput, calls=%fused_computation.56 | convolution fusion | flops 1189085184 | bytes 7667712 | tf_op jit(solution)/shard_map/dot_general | solution.py:106
  153.2 1.2 add_convert_fusion
  154.4 1.6 %fusion.40 = f32[2592,96]{0,1:T(8,128)} fusion(s32[]{:T(128)S(6)} %select_n.113, f32[1152,96]{0,1:T(8,128)S(1)} %bitcast.88, f32[1152,96]{0,1:T(8,128)S(1)} %bitcast.87, f32[1152,96]{0,1:T(8,128)S(1)} %bitcast.86), kind=kLoop, calls=%fused_computation.62 | loop fusion | flops 746496 | bytes 2322436 | tf_op jit(solution)/shard_map/mul | solution.py:189
  (25 shorter events, 0.2 us)
Async XLA Ops:
  7.2 50.6 %all-gather.2.cloned.1.call-start = ((), (), s32[]{:S(2)}) async-start(), calls=%async_computation.1 | async-start | bytes 2457600 | tf_op jit(solution)/shard_map/all_gather | solution.py:170
  59.4 8.2 %copy-start.4 = (bf16[4,2,160,384]{3,2,1,0:T(8,128)(2,1)}, bf16[4,2,160,384]{3,2,1,0:T(8,128)(2,1)S(1)}, u32[]{:S(2)}) copy-start(bf16[4,2,160,384]{3,2,1,0:T(8,128)(2,1)S(1)} %get-tuple-element.19) | copy-start | bytes 2949124
  59.4 15.4 %collective-permute-start = (bf16[4,2,160,384]{3,2,1,0:T(8,128)(2,1)S(1)}, bf16[4,2,160,384]{3,2,1,0:T(8,128)(2,1)}, u32[]{:S(2)}, u32[]{:S(2)}) collective-permute-start(bf16[4,2,160,384]{3,2,1,0:T(8,128)(2,1)S(1)} %get-tuple-element.19), channel_id=1, source_target_pairs={{0,1},{1,0},{2,3},{3,2},{4,5},{5,4},{6,7},{7,6},{8,9},{9,8},{10,11... | collective-permute-start | bytes 2949128 | tf_op jit(solution)/shard_map/ppermute | solution.py:122
  60.6 11.1 %collective-permute-start.3 = (bf16[3,1,160,384]{3,2,1,0:T(8,128)(2,1)}, bf16[3,1,160,384]{3,2,1,0:T(8,128)(2,1)}, u32[]{:S(2)}, u32[]{:S(2)}) collective-permute-start(bf16[3,1,160,384]{3,2,1,0:T(8,128)(2,1)} %get-tuple-element.20), channel_id=1, source_target_pairs={{0,1},{1,2},{2,3},{4,5},{5,6},{6,7},{8,9},{9,10},{10,11},{12,13},{... | collective-permute-start | bytes 1105928 | tf_op jit(solution)/shard_map/ppermute | solution.py:23
  63.6 8.1 %collective-permute-start.4 = (bf16[3,1,160,384]{3,2,1,0:T(8,128)(2,1)}, bf16[3,1,160,384]{3,2,1,0:T(8,128)(2,1)}, u32[]{:S(2)}, u32[]{:S(2)}) collective-permute-start(bf16[3,1,160,384]{3,2,1,0:T(8,128)(2,1)} %get-tuple-element.21), channel_id=1, source_target_pairs={{1,0},{2,1},{3,2},{5,4},{6,5},{7,6},{9,8},{10,9},{11,10},{13,12},{... | collective-permute-start | bytes 1105928 | tf_op jit(solution)/shard_map/ppermute | solution.py:25
  67.7 45.3 %all-to-all-start = ((bf16[4,2,160,384]{2,0,1,3:T(4,128)(2,1)}), bf16[4,2,160,384]{2,0,1,3:T(4,128)(2,1)S(1)}, u32[]{:S(2)}, u32[]{:S(2)}) async-start(bf16[4,2,160,384]{2,0,1,3:T(4,128)(2,1)} %copy.98), calls=%async_computation | async-start | bytes 3145728 | tf_op jit(solution)/shard_map/all_to_all | solution.py:177
  73.3 7.1 %slice-start = ((s8[7962624]{0:T(1024)(128)(4,1)}), s8[4194304]{0:T(1024)(128)(4,1)S(1)}, s32[]{:S(2)}) async-start(s8[7962624]{0:T(1024)(128)(4,1)} %bitcast.89), calls=%async_computation.2 | async-start | bytes 8388608
  73.9 1.5 copy-start.5
  74.5 5.9 %slice-start.1 = ((s8[7962624]{0:T(1024)(128)(4,1)}), s8[3768320]{0:T(1024)(128)(4,1)S(1)}, s32[]{:S(2)}) async-start(s8[7962624]{0:T(1024)(128)(4,1)} %bitcast.89), calls=%async_computation.3 | async-start | bytes 7536640
  74.8 5.6 %copy-start.10 = (pred[8,21]{0,1:T(8,128)(4,1)S(1)}, pred[8,21]{0,1:T(8,128)(4,1)}, u32[]{:S(2)}) copy-start(pred[8,21]{0,1:T(8,128)(4,1)} %constant.134) | copy-start | bytes 508
  78.0 34.9 %collective-permute-start.1 = (bf16[4,4,80,384]{3,2,1,0:T(8,128)(2,1)S(1)}, bf16[4,4,80,384]{3,2,1,0:T(8,128)(2,1)}, u32[]{:S(2)}, u32[]{:S(2)}) collective-permute-start(bf16[4,4,80,384]{3,2,1,0:T(8,128)(2,1)S(1)} %constant_dynamic-slice_fusion), channel_id=1, source_target_pairs={{0,2},{1,3},{2,0},{3,1},{4,6},{5,7},{6,4},{7,5},{8,10},{9,11},{10,... | collective-permute-start | bytes 2949128 | tf_op jit(solution)/shard_map/ppermute | solution.py:132
  80.4 4.3 %copy-start.2 = (bf16[1,2,160,384]{3,2,1,0:T(8,128)(2,1)S(1)}, bf16[1,2,160,384]{3,2,1,0:T(8,128)(2,1)}, u32[]{:S(2)}) copy-start(bf16[1,2,160,384]{3,2,1,0:T(8,128)(2,1)} %param.5) | copy-start | bytes 737284
  80.4 4.3 %copy-start.8 = (f32[384]{0:T(512)S(1)}, f32[384]{0:T(512)}, u32[]{:S(2)}) copy-start(f32[384]{0:T(512)} %param.6) | copy-start | bytes 4612
  84.7 28.2 %copy-start = (f32[1,2,1,160,384]{4,1,3,2,0:T(2,128)}, f32[1,2,1,160,384]{4,1,3,2,0:T(2,128)S(1)}, u32[]{:S(2)}) copy-start(f32[1,2,1,160,384]{4,1,3,2,0:T(2,128)S(1)} %slice.33) | copy-start | bytes 1474564
  112.9 15.3 %collective-permute-start.2 = (bf16[4,4,80,384]{3,2,1,0:T(8,128)(2,1)}, bf16[4,4,80,384]{3,2,1,0:T(8,128)(2,1)}, u32[]{:S(2)}, u32[]{:S(2)}) collective-permute-start(bf16[4,4,80,384]{3,2,1,0:T(8,128)(2,1)} %collective-permute-done.1), channel_id=1, source_target_pairs={{0,1},{1,0},{2,3},{3,2},{4,5},{5,4},{6,7},{7,6},{8,9},{9,8},{10,11... | collective-permute-start | bytes 2949128 | tf_op jit(solution)/shard_map/ppermute | solution.py:139
  134.0 2.2 %slice-start.2 = ((s8[7962624]{0:T(1024)(128)(4,1)}), s8[4194304]{0:T(1024)(128)(4,1)S(1)}, s32[]{:S(2)}) async-start(s8[7962624]{0:T(1024)(128)(4,1)} %bitcast.92), calls=%async_computation.4 | async-start | bytes 8388608
  134.5 3.0 %slice-start.3 = ((s8[7962624]{0:T(1024)(128)(4,1)}), s8[3768320]{0:T(1024)(128)(4,1)S(1)}, s32[]{:S(2)}) async-start(s8[7962624]{0:T(1024)(128)(4,1)} %bitcast.92), calls=%async_computation.5 | async-start | bytes 7536640
  141.7 6.0 %copy-start.6 = (bf16[5376,288]{0,1:T(8,128)(2,1)S(1)}, bf16[5376,288]{0,1:T(8,128)(2,1)}, u32[]{:S(2)}) copy-start(bf16[5376,288]{0,1:T(8,128)(2,1)} %copy.107) | copy-start | bytes 9289732
  151.3 1.9 %copy-start.1 = (f32[1,2,1,160,384]{4,1,3,2,0:T(2,128)S(1)}, f32[1,2,1,160,384]{4,1,3,2,0:T(2,128)}, u32[]{:S(2)}) copy-start(f32[1,2,1,160,384]{4,1,3,2,0:T(2,128)} %copy-done) | copy-start | bytes 1474564
  151.3 1.9 %copy-start.3 = (bf16[1,2,160,384]{3,2,1,0:T(8,128)(2,1)S(1)}, bf16[1,2,160,384]{3,2,1,0:T(8,128)(2,1)}, u32[]{:S(2)}) copy-start(bf16[1,2,160,384]{3,2,1,0:T(8,128)(2,1)} %param.5) | copy-start | bytes 737284
  151.3 1.9 %copy-start.7 = (bf16[1,2,160,384]{3,2,1,0:T(8,128)(2,1)S(1)}, bf16[1,2,160,384]{3,2,1,0:T(8,128)(2,1)}, u32[]{:S(2)}) copy-start(bf16[1,2,160,384]{3,2,1,0:T(8,128)(2,1)} %param.9) | copy-start | bytes 737284
  151.3 1.9 %copy-start.9 = (f32[384]{0:T(512)S(1)}, f32[384]{0:T(512)}, u32[]{:S(2)}) copy-start(f32[384]{0:T(512)} %param.7) | copy-start | bytes 4612
Sparse Core Ops, SparseCore 0:
  11.4 46.2 all-gather.1

commit v6 on v5

--- a/solution.py
+++ b/solution.py
@@ -119,33 +119,27 @@
     chips = height_count // 2
     first = core == 0
     sibling = [(i, i ^ 1) for i in range(height_count)]
-    twin = lax.ppermute(own, "height", sibling)
-    chip_rows = jnp.where(
-        first, jnp.concatenate([own, twin], axis=1), jnp.concatenate([twin, own], axis=1)
-    )
-    if chips == 1:
-        return chip_rows
-    half = col_count // 2
-    mine = lax.dynamic_slice_in_dim(chip_rows, core * half, half, axis=2)
-    got = jnp.concatenate(
-        [
-            lax.ppermute(
-                mine, "height", [(i, (i + 2 * step) % height_count) for i in range(height_count)]
+    mine = [own] + [
+        lax.ppermute(
+            own, "height", [(i, (i + 2 * step) % height_count) for i in range(height_count)]
+        )
+        for step in range(1, chips)
+    ]
+    stacked = jnp.concatenate(mine, axis=1)
+    twins = lax.ppermute(stacked, "height", sibling)
+    block = 2 * row_count
+    relative = []
+    for step in reversed(range(chips)):
+        ours = stacked[:, step * row_count : (step + 1) * row_count]
+        theirs = twins[:, step * row_count : (step + 1) * row_count]
+        relative.append(
+            jnp.where(
+                first,
+                jnp.concatenate([ours, theirs], axis=1),
+                jnp.concatenate([theirs, ours], axis=1),
             )
-            for step in range(1, chips)
-        ],
-        axis=1,
-    )
-    other = lax.ppermute(got, "height", sibling)
-    full = jnp.where(
-        first, jnp.concatenate([got, other], axis=2), jnp.concatenate([other, got], axis=2)
-    )
-    relative = jnp.concatenate([chip_rows, full], axis=1)
-    block = 2 * row_count
-    reverse = jnp.concatenate(
-        [relative[:, step * block : (step + 1) * block] for step in reversed(range(chips))], axis=1
-    )
-    return jnp.roll(reverse, (chip + 1) * block, axis=1)
+        )
+    return jnp.roll(jnp.concatenate(relative, axis=1), (chip + 1) * block, axis=1)
 
 
 def local(latents, gain, bias, weight, cotangent):

time: 163 us -> 156 us (0.957)
  waiting for transfers between devices: 74.2 us -> 56.2 us
  starting transfers between devices: 10.8 us -> 20.1 us
    ppermute x3 -> x2, waiting for transfers between devices: 27.8 us -> 8.85 us  [the longest x1 8.84 us: gather_rows(): lax.ppermute(own, 'height', [(i, (i + 2 * step) % height_count) for i in...]
    ppermute x3 -> x2, starting transfers between devices: 2.44 us -> 12.6 us  [the longest x1 11.1 us: gather_rows(): twins = lax.ppermute(stacked, 'height', sibling)]
    select_n x2, other arithmetic: 5.14 us -> 2.19 us  [gather_rows(): jnp.where(first, jnp.concatenate([ours, theirs], axis=1), jnp.concatenate...]
    concatenate x1 -> x2, other arithmetic: 3.1 us -> 5.89 us  [the longest x1 3.1 us: gather_rows(): jnp.roll(jnp.concatenate(relative, axis=1), (chip + 1) * block, axis=1)]
    slice x0 -> x1, local copies, waits for them, and re-layouts: none -> 1.7 us  [gather_rows(): theirs = twins[:, step * row_count:(step + 1) * row_count]]
    unnamed x32 -> x28, local copies, waits for them, and re-layouts: 3.38 us -> 2.76 us
  transfers between devices with their start and end apart: 7 -> 6, of which waited for: 2 -> 3; matrix products, arithmetic and copies ran while one was open for 18% -> 19% of each run, Pallas kernels for 0% -> 0%
where the time goes in v6:
time: 156 us; the launch traced here: 155 us
  waiting for transfers between devices  56.2 us (36%)
  local copies, waits for them, and re-layouts  27.2 us (17%)
  other arithmetic  23.9 us (15%)
  starting transfers between devices  20.1 us (13%)
  between operations  14.6 us (9%)
  matrix products  12.9 us (8%)
    all_gather x1, waiting for transfers between devices, local(): lax.all_gather(jnp.concatenate([hidden, cotangent], axis=-1), 'tm', axis=...  46.4 us
    ppermute x1, starting transfers between devices, gather_rows(): twins = lax.ppermute(stacked, 'height', sibling)  11.1 us
    ppermute x1, waiting for transfers between devices, gather_rows(): lax.ppermute(own, 'height', [(i, (i + 2 * step) % height_count) for i in...  8.84 us
    concatenate x1, other arithmetic, block_weight_grad(): jnp.concatenate([jnp.pad(cot_all, ((0, 0), (0, 0), (col_tap, padded_cols...  6.82 us
    dynamic_slice x1, local copies, waits for them, and re-layouts, block_weight_grad(): lax.dynamic_slice(framed, (depth_tap, row_tap, 0, 0), (frame_total, row_t...  5.95 us
    reshape x1, local copies, waits for them, and re-layouts, block_weight_grad(): shifted = jnp.concatenate([jnp.pad(cot_all, ((0, 0), (0, 0), (col_tap, pa...  5.82 us
    dot_general x3, matrix products, block_weight_grad(): lax.dot_general(slab, shifted, (((0,), (0,)), ((), ())), preferred_elemen...  5.29 us
    slice x2, local copies, waits for them, and re-layouts, local(): cot_frames = both_frames[..., channels:]  4.21 us
  transfers between devices with their start and end apart: 6, of which 3 were waited for; matrix products, arithmetic and copies ran while one was open for 19% of the time, Pallas kernels for 0%

profile of v6, /device:TPU:0, one launch (start us, length us, event | category | flops | bytes accessed | tf_op | source)
XLA Modules:
  0.0 154.9 jit_solution(18178282372170327557)
XLA Ops:
  7.2 0.0 all-gather.2.cloned.1.call-start
  7.2 1.1 fusion.45
  8.3 1.2 multiply_convert_fusion
  9.5 1.8 %pad_maximum_fusion.3 = bf16[1,2,160,768]{3,2,1,0:T(8,128)(2,1)} fusion(bf16[1,2,160,384]{3,2,1,0:T(8,128)(2,1)} %param.9, bf16[1,2,160,384]{3,2,1,0:T(8,128)(2,1)S(1)} %multiply_convert_fusion), kind=kLoop, calls=%fused_computation.74 | loop fusion | flops 983040 | bytes 983040 | tf_op jit(solution)/shard_map/concatenate | solution.py:165
  11.3 0.0 all-gather.2.cloned.1.call-update
  11.3 46.4 %all-gather.2.cloned.1.call-done = bf16[4,2,160,768]{3,2,1,0:T(8,128)(2,1)} async-done(((bf16[1,2,160,768]{3,2,1,0:T(8,128)(2,1)}), bf16[4,2,160,768]{3,2,1,0:T(8,128)(2,1)}) %all-gather.2.cloned.1.call-update) | async-done | bytes 1966096 | tf_op jit(solution)/shard_map/all_gather | solution.py:164
  57.7 1.7 %fusion.57 = (bf16[4,2,160,384]{3,2,1,0:T(8,128)(2,1)S(1)}, bf16[4,2,160,384]{3,2,1,0:T(8,128)(2,1)S(1)}) fusion(bf16[4,2,160,768]{3,2,1,0:T(8,128)(2,1)} %all-gather.2.cloned.1.call-done), kind=kLoop, calls=%fused_computation.92 | loop fusion | bytes 3932160 | tf_op jit(solution)/shard_map/slice | solution.py:170
  59.4 1.5 collective-permute-start
  61.0 1.0 pad_dynamic-slice_fusion.9
  62.0 2.2 %collective-permute-start.2 = (bf16[3,1,160,384]{3,2,1,0:T(8,128)(2,1)}, bf16[3,1,160,384]{3,2,1,0:T(8,128)(2,1)}, u32[]{:S(2)}, u32[]{:S(2)}) collective-permute-start(bf16[3,1,160,384]{3,2,1,0:T(8,128)(2,1)} %get-tuple-element.22), channel_id=1, source_target_pairs={{0,1},{1,2},{2,3},{4,5},{5,6},{6,7},{8,9},{9,10},{10,11},{12,13},{... | collective-permute-start | bytes 1105928 | tf_op jit(solution)/shard_map/ppermute | solution.py:23
  64.2 1.3 collective-permute-start.3
  65.7 2.5 %copy.98 = bf16[4,2,160,384]{2,0,1,3:T(4,128)(2,1)} copy(bf16[4,2,160,384]{3,2,1,0:T(8,128)(2,1)S(1)} %get-tuple-element.18) | data formatting | bytes 1966080 | tf_op jit(solution)/shard_map/slice | solution.py:170
  68.2 3.9 %all-to-all-start = ((bf16[4,2,160,384]{2,0,1,3:T(4,128)(2,1)}), bf16[4,2,160,384]{2,0,1,3:T(4,128)(2,1)S(1)}, u32[]{:S(2)}, u32[]{:S(2)}) async-start(bf16[4,2,160,384]{2,0,1,3:T(4,128)(2,1)} %copy.98), calls=%async_computation | async-start | bytes 3145728 | tf_op jit(solution)/shard_map/all_to_all | solution.py:171
  72.1 0.1 pad_dynamic-slice_fusion.10
  72.2 0.0 collective-permute-done.2
  72.2 0.0 collective-permute-done.3
  72.2 0.0 slice-start
  72.2 1.7 %fusion.32 = bf16[3,4,1,162,384]{4,3,1,0,2:T(8,128)(2,1)S(1)} fusion(bf16[3,1,160,384]{3,2,1,0:T(8,128)(2,1)} %collective-permute-done.3, bf16[3,2,160,384]{3,2,1,0:T(8,128)(2,1)S(1)} %pad_dynamic-slice_fusion.10, bf16[3,1,160,384]{3,2,1,0:T(8,128)(2,1)} %collective-permute-done.2), kind=kLoop, calls=%fused_computation.51 | loop fusion | flops 9704448 | bytes 2967552 | tf_op jit(solution)/shard_map/broadcast_in_dim | solution.py:58
  74.0 0.6 copy.111
  74.5 0.0 slice-start.1
  74.5 0.6 pad.32.clone
  75.1 0.0 copy-start.8
  75.1 0.2 copy.95
  75.4 8.8 %collective-permute-done = bf16[4,2,160,384]{3,2,1,0:T(8,128)(2,1)} collective-permute-done((bf16[4,2,160,384]{3,2,1,0:T(8,128)(2,1)S(1)}, bf16[4,2,160,384]{3,2,1,0:T(8,128)(2,1)}, u32[]{:S(2)}, u32[]{:S(2)}) %collective-permute-start) | collective-permute-done | bytes 983072 | tf_op jit(solution)/shard_map/ppermute | solution.py:123
  84.2 2.8 %pad_maximum_fusion.1 = bf16[4,4,160,384]{3,2,1,0:T(8,128)(2,1)} fusion(bf16[4,2,160,384]{3,2,1,0:T(8,128)(2,1)} %collective-permute-done, bf16[4,2,160,384]{3,2,1,0:T(8,128)(2,1)S(1)} %get-tuple-element.19), kind=kLoop, calls=%fused_computation.29 | loop fusion | flops 983040 | bytes 3932160 | tf_op jit(solution)/shard_map/concatenate | solution.py:128
  87.0 11.1 %collective-permute-start.1 = (bf16[4,4,160,384]{3,2,1,0:T(8,128)(2,1)}, bf16[4,4,160,384]{3,2,1,0:T(8,128)(2,1)}, u32[]{:S(2)}, u32[]{:S(2)}) collective-permute-start(bf16[4,4,160,384]{3,2,1,0:T(8,128)(2,1)} %pad_maximum_fusion.1), channel_id=1, source_target_pairs={{0,1},{1,0},{2,3},{3,2},{4,5},{5,4},{6,7},{7,6},{8,9},{9,8},{10,11... | collective-permute-start | bytes 5898248 | tf_op jit(solution)/shard_map/ppermute | solution.py:129
  98.1 0.0 slice-done
  98.2 0.0 copy-start.2
  98.2 0.0 copy-start.6
  98.2 3.8 %fusion.34 = f32[1,2,8,21,384]{4,2,3,1,0:T(8,128)S(1)} fusion(bf16[3,3,3,384,384]{4,3,2,1,0:T(8,128)(2,1)S(1)} %bitcast.91, bf16[3,4,1,7,2,384]{5,3,4,1,0,2:T(8,128)(2,1)S(1)} %slice.42, bf16[3,4,1,8,21,384]{5,3,4,1,0,2:T(8,128)(2,1)S(1)} %copy.95, pred[8,21]{0,1:T(8,128)(4,1)S(1)} %copy-done.8), kind=kOutput, calls=%fused_computation.61 | convolution fusion | flops 2680657920 | bytes 10156200 | tf_op jit(solution)/shard_map/conv_general_dilated | solution.py:57
  102.0 0.3 copy.96
  102.2 0.2 slice.43
  102.4 0.0 copy-start
  102.4 0.4 multiply_reduce_fusion
  102.9 0.9 all-to-all-done
  103.8 2.5 %copy.100 = bf16[4,4,2,160,96]{4,3,2,1,0:T(8,128)(2,1)} copy(bf16[4,4,2,160,96]{3,0,2,4,1:T(4,128)(2,1)S(1)} %bitcast.74) | data formatting | bytes 1966080 | tf_op jit(solution)/shard_map/all_to_all | solution.py:171
  106.3 6.8 %fusion.5 = bf16[4,8,168,288]{3,2,1,0:T(8,128)(2,1)} fusion(bf16[4,8,160,96]{3,2,1,0:T(8,128)(2,1)} %bitcast.77), kind=kLoop, calls=%fused_computation.17 | loop fusion | flops 21676032 | bytes 4079616 | tf_op jit(solution)/shard_map/concatenate | solution.py:83
  113.2 5.8 %copy.107 = bf16[5376,288]{0,1:T(8,128)(2,1)} copy(bf16[5376,288]{1,0:T(8,128)(2,1)} %bitcast.73) | data formatting | bytes 6193152 | tf_op jit(solution)/shard_map/reshape | solution.py:92
  119.0 0.0 collective-permute-done.1
  119.0 1.7 %fusion.58 = (bf16[4,2,160,384]{3,2,1,0:T(8,128)(2,1)S(1)}, bf16[4,2,160,384]{3,2,1,0:T(8,128)(2,1)S(1)}) fusion(bf16[4,4,160,384]{3,2,1,0:T(8,128)(2,1)} %collective-permute-done.1), kind=kLoop, calls=%fused_computation.93 | loop fusion | bytes 3932160 | tf_op jit(solution)/shard_map/slice | solution.py:134
  120.7 0.3 fusion.14
  121.0 1.8 %fusion.15 = bf16[4,4,160,384]{3,2,1,0:T(8,128)(2,1)S(1)} fusion(bf16[4,2,160,384]{3,2,1,0:T(8,128)(2,1)} %collective-permute-done, bf16[4,2,160,384]{3,2,1,0:T(8,128)(2,1)S(1)} %get-tuple-element.21, pred[]{:T(512)S(6)} %eq.11), kind=kLoop, calls=%fused_computation.32 | loop fusion | flops 2949120 | bytes 3932161 | tf_op jit(solution)/shard_map/jit(_where)/select_n | solution.py:136
  122.9 3.1 %fusion.8 = bf16[4,8,160,384]{3,2,1,0:T(8,128)(2,1)S(1)} fusion(s32[]{:T(128)S(6)} %select_n.93, bf16[4,4,160,384]{3,2,1,0:T(8,128)(2,1)S(1)} %fusion.15, bf16[4,4,160,384]{3,2,1,0:T(8,128)(2,1)S(1)} %fusion.14), kind=kLoop, calls=%fused_computation.20 | loop fusion | flops 5898240 | bytes 7864324 | tf_op jit(solution)/shard_map/jit(_roll_dynamic)/concatenate | solution.py:142
  126.0 0.0 slice-start.2
  126.0 0.5 fusion.30
  126.5 0.0 slice-start.3
  126.5 0.6 copy.110
  127.1 0.6 pad.30.clone
  127.7 0.2 copy.90
  127.9 0.2 slice-done.2
  128.2 1.3 slice-done.3
  129.5 3.9 %fusion.37 = f32[1,2,8,21,384]{4,2,3,1,0:T(8,128)S(1)} fusion(bf16[3,3,3,384,384]{4,3,2,1,0:T(8,128)(2,1)S(1)} %bitcast.94, bf16[3,4,1,7,2,384]{5,3,4,1,0,2:T(8,128)(2,1)S(1)} %slice.39, bf16[3,4,1,8,21,384]{5,3,4,1,0,2:T(8,128)(2,1)S(1)} %copy.90, pred[8,21]{0,1:T(8,128)(4,1)S(1)} %copy-done.8), kind=kOutput, calls=%fused_computation.62 | convolution fusion | flops 2680657920 | bytes 10156200 | tf_op jit(solution)/shard_map/conv_general_dilated | solution.py:44
  133.3 0.3 copy.91
  133.6 0.2 slice.40
  133.8 5.9 %pad_dynamic-slice_fusion = (bf16[4,8,168,384]{3,2,1,0:T(8,128)(2,1)S(1)}, bf16[4,8,168,384]{3,2,1,0:T(8,128)(2,1)S(1)}, bf16[4,8,168,384]{3,2,1,0:T(8,128)(2,1)S(1)}) fusion(s32[]{:T(128)S(6)} %select_n.106, s32[]{:T(128)S(6)} %select_n.108, bf16[4,8,160,384]{3,2,1,0:T(8,128)(2,1)S(1)} %fusion.8, s32[]{:T(128)S(6)} %select_n.98, s32[]{:T(128)S(6)} %select_n.100, ...), kind=kLoop, calls=%fused_computation.2 | loop fusion | bytes 16318488 | tf_op jit(solution)/shard_map/dynamic_slice | solution.py:101
  139.8 1.8 %convolution_bitcast_fusion = f32[3,12,8,384]{3,2,1,0:T(8,128)S(1)} fusion(bf16[5376,384,1]{1,0,2:T(8,128)(2,1)S(1)} %bitcast.80, bf16[3,96,5376]{2,1,0:T(8,128)(2,1)S(1)} %bitcast.81), kind=kOutput, calls=%fused_computation.58 | convolution fusion | flops 1189085184 | bytes 7667712 | tf_op jit(solution)/shard_map/dot_general | solution.py:106
  141.6 1.8 %convolution_bitcast_fusion.2 = f32[3,12,8,384]{3,2,1,0:T(8,128)S(1)} fusion(bf16[5376,384,1]{1,0,2:T(8,128)(2,1)S(1)} %bitcast.79, bf16[3,96,5376]{2,1,0:T(8,128)(2,1)S(1)} %bitcast.82), kind=kOutput, calls=%fused_computation.60 | convolution fusion | flops 1189085184 | bytes 7667712 | tf_op jit(solution)/shard_map/dot_general | solution.py:106
  143.3 0.0 copy-start.1
  143.3 0.0 copy-start.3
  143.4 0.0 copy-start.5
  143.4 0.0 copy-start.7
  143.4 1.8 %convolution_bitcast_fusion.1 = f32[3,12,8,384]{3,2,1,0:T(8,128)S(1)} fusion(bf16[5376,384,1]{1,0,2:T(8,128)(2,1)S(1)} %bitcast.78, bf16[3,96,5376]{2,1,0:T(8,128)(2,1)S(1)} %bitcast.83), kind=kOutput, calls=%fused_computation.59 | convolution fusion | flops 1189085184 | bytes 7667712 | tf_op jit(solution)/shard_map/dot_general | solution.py:106
  145.3 1.2 add_convert_fusion
  146.5 1.6 %fusion.42 = f32[2592,96]{0,1:T(8,128)} fusion(s32[]{:T(128)S(6)} %select_n.109, f32[1152,96]{0,1:T(8,128)S(1)} %bitcast.88, f32[1152,96]{0,1:T(8,128)S(1)} %bitcast.87, f32[1152,96]{0,1:T(8,128)S(1)} %bitcast.86), kind=kLoop, calls=%fused_computation.65 | loop fusion | flops 746496 | bytes 2322436 | tf_op jit(solution)/shard_map/mul | solution.py:183
  (20 shorter events, 0.2 us)
Async XLA Ops:
  7.2 50.6 %all-gather.2.cloned.1.call-start = ((), (), s32[]{:S(2)}) async-start(), calls=%async_computation.1 | async-start | bytes 2457600 | tf_op jit(solution)/shard_map/all_gather | solution.py:164
  59.4 24.8 %collective-permute-start = (bf16[4,2,160,384]{3,2,1,0:T(8,128)(2,1)S(1)}, bf16[4,2,160,384]{3,2,1,0:T(8,128)(2,1)}, u32[]{:S(2)}, u32[]{:S(2)}) collective-permute-start(bf16[4,2,160,384]{3,2,1,0:T(8,128)(2,1)S(1)} %get-tuple-element.19), channel_id=1, source_target_pairs={{0,2},{1,3},{2,0},{3,1},{4,6},{5,7},{6,4},{7,5},{8,10},{9,11},{10,... | collective-permute-start | bytes 2949128 | tf_op jit(solution)/shard_map/ppermute | solution.py:123
  62.0 10.2 %collective-permute-start.2 = (bf16[3,1,160,384]{3,2,1,0:T(8,128)(2,1)}, bf16[3,1,160,384]{3,2,1,0:T(8,128)(2,1)}, u32[]{:S(2)}, u32[]{:S(2)}) collective-permute-start(bf16[3,1,160,384]{3,2,1,0:T(8,128)(2,1)} %get-tuple-element.22), channel_id=1, source_target_pairs={{0,1},{1,2},{2,3},{4,5},{5,6},{6,7},{8,9},{9,10},{10,11},{12,13},{... | collective-permute-start | bytes 1105928 | tf_op jit(solution)/shard_map/ppermute | solution.py:23
  64.2 8.0 %collective-permute-start.3 = (bf16[3,1,160,384]{3,2,1,0:T(8,128)(2,1)}, bf16[3,1,160,384]{3,2,1,0:T(8,128)(2,1)}, u32[]{:S(2)}, u32[]{:S(2)}) collective-permute-start(bf16[3,1,160,384]{3,2,1,0:T(8,128)(2,1)} %get-tuple-element.23), channel_id=1, source_target_pairs={{1,0},{2,1},{3,2},{5,4},{6,5},{7,6},{9,8},{10,9},{11,10},{13,12},{... | collective-permute-start | bytes 1105928 | tf_op jit(solution)/shard_map/ppermute | solution.py:25
  68.2 35.6 %all-to-all-start = ((bf16[4,2,160,384]{2,0,1,3:T(4,128)(2,1)}), bf16[4,2,160,384]{2,0,1,3:T(4,128)(2,1)S(1)}, u32[]{:S(2)}, u32[]{:S(2)}) async-start(bf16[4,2,160,384]{2,0,1,3:T(4,128)(2,1)} %copy.98), calls=%async_computation | async-start | bytes 3145728 | tf_op jit(solution)/shard_map/all_to_all | solution.py:171
  72.2 25.9 %slice-start = ((s8[7962624]{0:T(1024)(128)(4,1)}), s8[4194304]{0:T(1024)(128)(4,1)S(1)}, s32[]{:S(2)}) async-start(s8[7962624]{0:T(1024)(128)(4,1)} %bitcast.89), calls=%async_computation.2 | async-start | bytes 8388608
  74.5 23.6 %slice-start.1 = ((s8[7962624]{0:T(1024)(128)(4,1)}), s8[3768320]{0:T(1024)(128)(4,1)S(1)}, s32[]{:S(2)}) async-start(s8[7962624]{0:T(1024)(128)(4,1)} %bitcast.89), calls=%async_computation.3 | async-start | bytes 7536640
  75.1 23.0 %copy-start.8 = (pred[8,21]{0,1:T(8,128)(4,1)S(1)}, pred[8,21]{0,1:T(8,128)(4,1)}, u32[]{:S(2)}) copy-start(pred[8,21]{0,1:T(8,128)(4,1)} %constant.130) | copy-start | bytes 508
  87.0 31.9 %collective-permute-start.1 = (bf16[4,4,160,384]{3,2,1,0:T(8,128)(2,1)}, bf16[4,4,160,384]{3,2,1,0:T(8,128)(2,1)}, u32[]{:S(2)}, u32[]{:S(2)}) collective-permute-start(bf16[4,4,160,384]{3,2,1,0:T(8,128)(2,1)} %pad_maximum_fusion.1), channel_id=1, source_target_pairs={{0,1},{1,0},{2,3},{3,2},{4,5},{5,4},{6,7},{7,6},{8,9},{9,8},{10,11... | collective-permute-start | bytes 5898248 | tf_op jit(solution)/shard_map/ppermute | solution.py:129
  98.2 4.3 %copy-start.2 = (bf16[1,2,160,384]{3,2,1,0:T(8,128)(2,1)S(1)}, bf16[1,2,160,384]{3,2,1,0:T(8,128)(2,1)}, u32[]{:S(2)}) copy-start(bf16[1,2,160,384]{3,2,1,0:T(8,128)(2,1)} %param.5) | copy-start | bytes 737284
  98.2 4.3 %copy-start.6 = (f32[384]{0:T(512)S(1)}, f32[384]{0:T(512)}, u32[]{:S(2)}) copy-start(f32[384]{0:T(512)} %param.6) | copy-start | bytes 4612
  102.4 10.7 %copy-start = (f32[1,2,1,160,384]{4,1,3,2,0:T(2,128)}, f32[1,2,1,160,384]{4,1,3,2,0:T(2,128)S(1)}, u32[]{:S(2)}) copy-start(f32[1,2,1,160,384]{4,1,3,2,0:T(2,128)S(1)} %slice.43) | copy-start | bytes 1474564
  126.0 2.2 %slice-start.2 = ((s8[7962624]{0:T(1024)(128)(4,1)}), s8[4194304]{0:T(1024)(128)(4,1)S(1)}, s32[]{:S(2)}) async-start(s8[7962624]{0:T(1024)(128)(4,1)} %bitcast.92), calls=%async_computation.4 | async-start | bytes 8388608
  126.5 3.0 %slice-start.3 = ((s8[7962624]{0:T(1024)(128)(4,1)}), s8[3768320]{0:T(1024)(128)(4,1)S(1)}, s32[]{:S(2)}) async-start(s8[7962624]{0:T(1024)(128)(4,1)} %bitcast.92), calls=%async_computation.5 | async-start | bytes 7536640
  133.8 6.0 %copy-start.4 = (bf16[5376,288]{0,1:T(8,128)(2,1)S(1)}, bf16[5376,288]{0,1:T(8,128)(2,1)}, u32[]{:S(2)}) copy-start(bf16[5376,288]{0,1:T(8,128)(2,1)} %copy.107) | copy-start | bytes 9289732
  143.3 1.9 %copy-start.1 = (f32[1,2,1,160,384]{4,1,3,2,0:T(2,128)S(1)}, f32[1,2,1,160,384]{4,1,3,2,0:T(2,128)}, u32[]{:S(2)}) copy-start(f32[1,2,1,160,384]{4,1,3,2,0:T(2,128)} %copy-done) | copy-start | bytes 1474564
  143.3 1.9 %copy-start.3 = (bf16[1,2,160,384]{3,2,1,0:T(8,128)(2,1)S(1)}, bf16[1,2,160,384]{3,2,1,0:T(8,128)(2,1)}, u32[]{:S(2)}) copy-start(bf16[1,2,160,384]{3,2,1,0:T(8,128)(2,1)} %param.5) | copy-start | bytes 737284
  143.4 1.9 %copy-start.5 = (bf16[1,2,160,384]{3,2,1,0:T(8,128)(2,1)S(1)}, bf16[1,2,160,384]{3,2,1,0:T(8,128)(2,1)}, u32[]{:S(2)}) copy-start(bf16[1,2,160,384]{3,2,1,0:T(8,128)(2,1)} %param.9) | copy-start | bytes 737284
  143.4 1.9 %copy-start.7 = (f32[384]{0:T(512)S(1)}, f32[384]{0:T(512)}, u32[]{:S(2)}) copy-start(f32[384]{0:T(512)} %param.7) | copy-start | bytes 4612
Sparse Core Ops, SparseCore 0:
  11.4 46.2 all-gather.1

commit v7 on v6

--- a/solution.py
+++ b/solution.py
@@ -74,41 +74,34 @@
     return most
 
 
+def depth_span(share_rows, tap_rows, channels):
+    plane_rows = 9 * channels
+    most = 1
+    for index in range(tap_rows // share_rows):
+        first = index * share_rows
+        last = first + share_rows - 1
+        most = max(most, last // plane_rows - first // plane_rows + 1)
+    return most
+
+
 def block_weight_grad(framed, cot_all, frame_index, share_rows, channels):
     frame_total, row_total, col_total, slots = cot_all.shape
-    padded_cols = framed.shape[2]
-    pair_rows = 3 * channels
+    plane_rows = 9 * channels
     tap_rows = 27 * channels
-    flat_count = frame_total * row_total * padded_cols
-    shifted = jnp.concatenate(
-        [
-            jnp.pad(
-                cot_all,
-                ((0, 0), (0, 0), (col_tap, padded_cols - col_total - col_tap), (0, 0)),
-            )
-            for col_tap in range(3)
-        ],
-        axis=-1,
-    ).reshape(flat_count, 3 * slots)
+    span = depth_span(share_rows, tap_rows, channels)
     first_row = frame_index * share_rows
-    first_pair = first_row // pair_rows
-    count = pair_count(tap_rows, share_rows, pair_rows, tap_rows // share_rows)
-    pieces = []
-    for step in range(count):
-        pair = jnp.minimum(first_pair + step, 8)
-        depth_tap = pair // 3
-        row_tap = pair % 3
-        slab = lax.dynamic_slice(
-            framed,
-            (depth_tap, row_tap, 0, 0),
-            (frame_total, row_total, padded_cols, channels),
-        ).reshape(flat_count, channels)
-        product = lax.dot_general(
-            slab, shifted, (((0,), (0,)), ((), ())), preferred_element_type=jnp.float32
-        )
-        pieces.append(product.reshape(channels, 3, slots).transpose(1, 0, 2).reshape(pair_rows, slots))
-    stacked = jnp.concatenate(pieces, axis=0)
-    return lax.dynamic_slice_in_dim(stacked, first_row - first_pair * pair_rows, share_rows, 0)
+    first_depth = jnp.minimum(first_row // plane_rows, 3 - span)
+    frames = lax.dynamic_slice_in_dim(framed, first_depth, frame_total + span - 1, 0)
+    frames = frames[:, :, : col_total + 2]
+    terms = lax.conv_general_dilated(
+        frames[..., None],
+        cot_all[:, :, :, None, :],
+        (1, 1, 1),
+        "VALID",
+        dimension_numbers=("DHWNC", "DHWIO", "DHWNC"),
+        preferred_element_type=jnp.float32,
+    ).reshape(span * plane_rows, slots)
+    return lax.dynamic_slice_in_dim(terms, first_row - first_depth * plane_rows, share_rows, 0)
 
 
 def gather_rows(own, height_count):
@@ -139,7 +132,14 @@
                 jnp.concatenate([theirs, ours], axis=1),
             )
         )
-    return jnp.roll(jnp.concatenate(relative, axis=1), (chip + 1) * block, axis=1)
+    relative = jnp.concatenate(relative, axis=1)
+    return jnp.concatenate(
+        [
+            lax.dynamic_slice_in_dim(relative, ((place - chip - 1) % chips) * block, block, 1)
+            for place in range(chips)
+        ],
+        axis=1,
+    )
 
 
 def local(latents, gain, bias, weight, cotangent):
@@ -156,7 +156,7 @@
     total_frames = frame_count * frame_devices
     tap_rows = 27 * channels
     share_rows = tap_rows // frame_devices
-    padded_cols = -(-(col_count + 2) // 8) * 8
+    padded_cols = col_count + 2
     right_pad = padded_cols - col_count - 1
     inverse_root = 1.0 / math.sqrt(total_frames * total_rows * col_count)
     weight_cube = weight.reshape(3, 3, 3, channels, channels)

time: 156 us -> 225 us (1.44)
  matrix products: 12.9 us -> 85.4 us
  waiting for transfers between devices: 56.2 us -> 71.6 us
  starting transfers between devices: 20.1 us -> 10.5 us
  local copies, waits for them, and re-layouts: 27.2 us -> 21.8 us
  other arithmetic: 23.9 us -> 20.9 us
    conv_general_dilated x0 -> x1, matrix products: none -> 74.5 us  [block_weight_grad(): lax.conv_general_dilated(frames[..., None], cot_all[:, :, :, None, :], (1...]
    ppermute x1, starting transfers between devices: 11.1 us -> 0.01 us  [gather_rows(): twins = lax.ppermute(stacked, 'height', sibling)]
    all_to_all x1, waiting for transfers between devices: 0.94 us -> 9.06 us  [local(): lax.all_to_all(cot_frames, 'height', split_axis=3, concat_axis=1, tiled=T...]
    ppermute x1, waiting for transfers between devices: 8.84 us -> 16.1 us  [gather_rows(): lax.ppermute(own, 'height', [(i, (i + 2 * step) % height_count) for i in...]
    dynamic_slice x1 -> x0, local copies, waits for them, and re-layouts: 5.95 us -> none  [block_weight_grad(): lax.dynamic_slice(framed, (depth_tap, row_tap, 0, 0), (frame_total, row_t...]
    dot_general x3 -> x0, matrix products: 5.29 us -> none  [block_weight_grad(): lax.dot_general(slab, shifted, (((0,), (0,)), ((), ())), preferred_elemen...]
    conv_general_dilated x1, matrix products: 3.78 us -> 7.08 us  [backward_conv(): lax.conv_general_dilated(window[None], jnp.flip(cube, (0, 1, 2)), (1, 1,...]
    reshape x4 -> x1, local copies, waits for them, and re-layouts: 5.91 us -> 2.8 us  [block_weight_grad(): terms = lax.conv_general_dilated(frames[..., None], cot_all[:, :, :, None...]
  transfers between devices with their start and end apart: 6 -> 6, of which waited for: 3 -> 3; matrix products, arithmetic and copies ran while one was open for 19% -> 8% of each run, Pallas kernels for 0% -> 0%
where the time goes in v7:
time: 225 us; the launch traced here: 224 us
  matrix products  85.4 us (38%)
  waiting for transfers between devices  71.6 us (32%)
  local copies, waits for them, and re-layouts  21.8 us (10%)
  other arithmetic  20.9 us (9%)
  between operations  14.3 us (6%)
  starting transfers between devices  10.5 us (5%)
    conv_general_dilated x1, matrix products, block_weight_grad(): lax.conv_general_dilated(frames[..., None], cot_all[:, :, :, None, :], (1...  74.5 us
    all_gather x1, waiting for transfers between devices, local(): lax.all_gather(jnp.concatenate([hidden, cotangent], axis=-1), 'tm', axis=...  46.4 us
    ppermute x1, waiting for transfers between devices, gather_rows(): lax.ppermute(own, 'height', [(i, (i + 2 * step) % height_count) for i in...  16.1 us
    all_to_all x1, waiting for transfers between devices, local(): lax.all_to_all(cot_frames, 'height', split_axis=3, concat_axis=1, tiled=T...  9.06 us
    conv_general_dilated x1, matrix products, backward_conv(): lax.conv_general_dilated(window[None], jnp.flip(cube, (0, 1, 2)), (1, 1,...  7.08 us
    concatenate x1, other arithmetic, gather_rows(): jnp.concatenate([lax.dynamic_slice_in_dim(relative, (place - chip - 1) %...  5.81 us
  transfers between devices with their start and end apart: 6, of which 3 were waited for; matrix products, arithmetic and copies ran while one was open for 8% of the time, Pallas kernels for 0%

profile of v7, /device:TPU:0, one launch (start us, length us, event | category | flops | bytes accessed | tf_op | source)
XLA Modules:
  0.0 224.5 jit_solution(6320341675211582955)
XLA Ops:
  7.2 0.0 all-gather.2.cloned.1.call-start
  7.2 1.1 fusion.49
  8.3 1.2 multiply_convert_fusion
  9.5 1.8 pad_maximum_fusion.3
  11.3 0.0 all-gather.2.cloned.1.call-update
  11.3 46.4 %all-gather.2.cloned.1.call-done = bf16[4,2,160,768]{3,2,1,0:T(8,128)(2,1)} async-done(((bf16[1,2,160,768]{3,2,1,0:T(8,128)(2,1)}), bf16[4,2,160,768]{3,2,1,0:T(8,128)(2,1)}) %all-gather.2.cloned.1.call-update) | async-done | bytes 1966096 | tf_op jit(solution)/shard_map/all_gather | solution.py:164
  57.7 1.7 fusion.61
  59.4 1.5 collective-permute-start
  61.0 1.0 pad_dynamic-slice_fusion.5
  62.0 1.3 collective-permute-start.3
  63.3 3.8 %collective-permute-start.2 = (bf16[3,1,160,384]{3,2,1,0:T(8,128)(2,1)}, bf16[3,1,160,384]{3,2,1,0:T(8,128)(2,1)}, u32[]{:S(2)}, u32[]{:S(2)}) collective-permute-start(bf16[3,1,160,384]{3,2,1,0:T(8,128)(2,1)} %get-tuple-element.21), channel_id=1, source_target_pairs={{0,1},{1,2},{2,3},{4,5},{5,6},{6,7},{8,9},{9,10},{10,11},{12,13},{... | collective-permute-start | bytes 1105928 | tf_op jit(solution)/shard_map/ppermute | solution.py:23
  67.1 16.1 %collective-permute-done = bf16[4,2,160,384]{3,2,1,0:T(8,128)(2,1)S(1)} collective-permute-done((bf16[4,2,160,384]{3,2,1,0:T(8,128)(2,1)S(1)}, bf16[4,2,160,384]{3,2,1,0:T(8,128)(2,1)S(1)}, u32[]{:S(2)}, u32[]{:S(2)}) %collective-permute-start) | collective-permute-done | bytes 983072 | tf_op jit(solution)/shard_map/ppermute | solution.py:116
  83.1 1.6 pad_maximum_fusion.1
  84.7 0.0 collective-permute-start.1
  84.8 2.5 %copy.92 = bf16[4,2,160,384]{2,0,1,3:T(4,128)(2,1)} copy(bf16[4,2,160,384]{3,2,1,0:T(8,128)(2,1)S(1)} %get-tuple-element.17) | data formatting | bytes 1966080 | tf_op jit(solution)/shard_map/slice | solution.py:170
  87.3 0.0 copy-done.2
  87.3 3.9 %all-to-all-start = ((bf16[4,2,160,384]{2,0,1,3:T(4,128)(2,1)}), bf16[4,2,160,384]{2,0,1,3:T(4,128)(2,1)S(1)}, u32[]{:S(2)}, u32[]{:S(2)}) async-start(bf16[4,2,160,384]{2,0,1,3:T(4,128)(2,1)} %copy.92), calls=%async_computation | async-start | bytes 3145728 | tf_op jit(solution)/shard_map/all_to_all | solution.py:171
  91.2 0.1 pad_dynamic-slice_fusion.6
  91.3 0.0 collective-permute-done.3
  91.3 0.0 collective-permute-done.2
  91.3 1.6 fusion.40
  92.9 0.6 copy.103
  93.4 0.0 copy-start.7
  93.4 0.6 pad.17.clone
  94.0 0.2 copy.89
  94.3 0.0 copy-done.7
  94.3 0.0 copy-start.1
  94.3 0.0 copy-start.5
  94.3 7.1 %fusion.41 = f32[1,2,8,21,384]{4,2,3,1,0:T(8,128)S(1)} fusion(bf16[3,3,3,384,384]{4,3,2,1,0:T(8,128)(2,1)} %bitcast.52, bf16[3,4,1,7,2,384]{5,3,4,1,0,2:T(8,128)(2,1)S(1)} %slice.34, bf16[3,4,1,8,21,384]{5,3,4,1,0,2:T(8,128)(2,1)S(1)} %copy.89, pred[8,21]{0,1:T(8,128)(4,1)S(1)} %copy-done.7), kind=kOutput, calls=%fused_computation.59 | convolution fusion | flops 2680657920 | bytes 10156200 | tf_op jit(solution)/shard_map/conv_general_dilated | solution.py:57
  101.4 0.3 copy.90
  101.7 0.2 slice.35
  101.9 0.0 copy-done.1
  101.9 0.0 copy-done.5
  101.9 0.4 multiply_reduce_fusion
  102.3 0.4 copy-done
  102.7 9.1 %all-to-all-done = bf16[4,2,160,384]{2,0,1,3:T(4,128)(2,1)S(1)} async-done(((bf16[4,2,160,384]{2,0,1,3:T(4,128)(2,1)}), bf16[4,2,160,384]{2,0,1,3:T(4,128)(2,1)S(1)}, u32[]{:S(2)}, u32[]{:S(2)}) %all-to-all-start) | async-done | bytes 983072 | tf_op jit(solution)/shard_map/all_to_all | solution.py:171
  111.7 2.5 %copy.94 = bf16[4,4,2,160,96]{4,3,2,1,0:T(8,128)(2,1)} copy(bf16[4,4,2,160,96]{3,0,2,4,1:T(4,128)(2,1)S(1)} %bitcast.46) | data formatting | bytes 1966080 | tf_op jit(solution)/shard_map/all_to_all | solution.py:171
  114.3 0.0 collective-permute-done.1
  114.3 1.7 fusion.62
  116.0 0.0 copy-start.3
  116.0 0.3 fusion.17
  116.3 0.8 copy-done.3
  117.2 0.3 fusion.18
  117.5 1.6 fusion.20
  119.2 0.0 slice-start
  119.2 5.8 %fusion.10 = bf16[6,10,162,384]{3,2,1,0:T(8,128)(2,1)S(1)} fusion(bf16[4,4,160,384]{3,2,1,0:T(8,128)(2,1)S(1)} %get-tuple-element.16, bf16[4,4,160,384]{3,2,1,0:T(8,128)(2,1)S(1)} %get-tuple-element.15), kind=kLoop, calls=%fused_computation.15 | loop fusion | flops 70917120 | bytes 11397120 | tf_op jit(solution)/shard_map/concatenate | solution.py:136
  125.0 0.0 slice-start.1
  125.0 0.2 dynamic-slice_bitcast_fusion.1
  125.2 0.6 copy.102
  125.8 0.6 pad.15.clone
  126.3 0.2 copy.84
  126.6 0.4 slice-done.1
  127.1 3.8 %fusion.44 = f32[1,2,8,21,384]{4,2,3,1,0:T(8,128)S(1)} fusion(bf16[3,3,3,384,384]{4,3,2,1,0:T(8,128)(2,1)S(1)} %bitcast.55, bf16[3,4,1,7,2,384]{5,3,4,1,0,2:T(8,128)(2,1)S(1)} %slice.31, bf16[3,4,1,8,21,384]{5,3,4,1,0,2:T(8,128)(2,1)S(1)} %copy.84, pred[8,21]{0,1:T(8,128)(4,1)S(1)} %copy-done.7), kind=kOutput, calls=%fused_computation.60 | convolution fusion | flops 2680657920 | bytes 10156200 | tf_op jit(solution)/shard_map/conv_general_dilated | solution.py:44
  130.9 0.3 copy.85
  131.2 1.0 slice.32
  132.1 0.6 dynamic-slice_bitcast_fusion
  132.8 0.7 copy-done.4
  133.5 74.5 %fusion.6 = f32[2,3,3,384,96]{3,4,2,1,0:T(8,128)S(1)} fusion(bf16[5,10,162,384,1]{3,2,1,0,4:T(8,128)(2,1)S(1)} %dynamic-slice_bitcast_fusion, bf16[4,8,160,1,96]{4,2,1,0,3:T(8,128)(2,1)S(1)} %bitcast.51), kind=kOutput, calls=%fused_computation.11 | convolution fusion | flops 6794772480 | bytes 9858048 | tf_op jit(solution)/shard_map/conv_general_dilated | solution.py:96
  207.9 1.8 copy.97
  209.7 0.0 copy-start.6
  209.8 2.8 %reshape.42 = f32[6912,96]{0,1:T(8,128)} reshape(f32[2,3,3,384,96]{3,2,1,0,4:T(4,128)S(1)} %copy.97) | data formatting | bytes 5308416 | tf_op jit(solution)/shard_map/reshape | solution.py:103
  212.6 2.5 %dynamic-slice_multiply_fusion = f32[2592,96]{0,1:T(8,128)} fusion(f32[6912,96]{0,1:T(8,128)} %reshape.42, s32[]{:T(128)S(6)} %select_n.66), kind=kLoop, calls=%fused_computation.61 | loop fusion | flops 248832 | bytes 1990660 | tf_op jit(solution)/shard_map/mul | solution.py:183
  215.1 0.0 copy-done.6
  215.1 2.6 %add_convert_fusion = (bf16[1,2,160,384]{3,2,1,0:T(8,128)(2,1)}, bf16[1,2,160,384]{3,2,1,0:T(8,128)(2,1)}) fusion(bf16[1,2,160,384]{3,2,1,0:T(8,128)(2,1)} %param.9, f32[2,160]{1,0:T(2,128)S(1)} %broadcast_multiply_fusion, f32[2,160]{1,0:T(2,128)S(1)} %add_sqrt_fusion, f32[384]{0:T(512)S(1)} %copy-done.5, f32[1,2,1,160,384]{4,1,3,2,0:T(2,128)} %copy-done, ...), kind=kLoop, calls=%fused_computation.76 | loop fusion | flops 2580480 | bytes 1971712 | tf_op jit(solution)/shard_map/convert_element_type | solution.py:198
  (9 shorter events, 0.1 us)
Async XLA Ops:
  7.2 50.6 %all-gather.2.cloned.1.call-start = ((), (), s32[]{:S(2)}) async-start(), calls=%async_computation.1 | async-start | bytes 2457600 | tf_op jit(solution)/shard_map/all_gather | solution.py:164
  59.4 23.7 %collective-permute-start = (bf16[4,2,160,384]{3,2,1,0:T(8,128)(2,1)S(1)}, bf16[4,2,160,384]{3,2,1,0:T(8,128)(2,1)S(1)}, u32[]{:S(2)}, u32[]{:S(2)}) collective-permute-start(bf16[4,2,160,384]{3,2,1,0:T(8,128)(2,1)S(1)} %get-tuple-element.18), channel_id=1, source_target_pairs={{0,2},{1,3},{2,0},{3,1},{4,6},{5,7},{6,4},{7,5},{8,10},{9,11},{10,... | collective-permute-start | bytes 2949128 | tf_op jit(solution)/shard_map/ppermute | solution.py:116
  62.0 29.3 %collective-permute-start.3 = (bf16[3,1,160,384]{3,2,1,0:T(8,128)(2,1)}, bf16[3,1,160,384]{3,2,1,0:T(8,128)(2,1)}, u32[]{:S(2)}, u32[]{:S(2)}) collective-permute-start(bf16[3,1,160,384]{3,2,1,0:T(8,128)(2,1)} %get-tuple-element.22), channel_id=1, source_target_pairs={{1,0},{2,1},{3,2},{5,4},{6,5},{7,6},{9,8},{10,9},{11,10},{13,12},{... | collective-permute-start | bytes 1105928 | tf_op jit(solution)/shard_map/ppermute | solution.py:25
  63.3 28.0 %collective-permute-start.2 = (bf16[3,1,160,384]{3,2,1,0:T(8,128)(2,1)}, bf16[3,1,160,384]{3,2,1,0:T(8,128)(2,1)}, u32[]{:S(2)}, u32[]{:S(2)}) collective-permute-start(bf16[3,1,160,384]{3,2,1,0:T(8,128)(2,1)} %get-tuple-element.21), channel_id=1, source_target_pairs={{0,1},{1,2},{2,3},{4,5},{5,6},{6,7},{8,9},{9,10},{10,11},{12,13},{... | collective-permute-start | bytes 1105928 | tf_op jit(solution)/shard_map/ppermute | solution.py:23
  83.1 4.2 %copy-start.2 = (bf16[4,2,160,384]{3,2,1,0:T(8,128)(2,1)}, bf16[4,2,160,384]{3,2,1,0:T(8,128)(2,1)S(1)}, u32[]{:S(2)}) copy-start(bf16[4,2,160,384]{3,2,1,0:T(8,128)(2,1)S(1)} %collective-permute-done) | copy-start | bytes 2949124
  84.7 29.5 %collective-permute-start.1 = (bf16[4,4,160,384]{3,2,1,0:T(8,128)(2,1)}, bf16[4,4,160,384]{3,2,1,0:T(8,128)(2,1)}, u32[]{:S(2)}, u32[]{:S(2)}) collective-permute-start(bf16[4,4,160,384]{3,2,1,0:T(8,128)(2,1)} %pad_maximum_fusion.1), channel_id=1, source_target_pairs={{0,1},{1,0},{2,3},{3,2},{4,5},{5,4},{6,7},{7,6},{8,9},{9,8},{10,11... | collective-permute-start | bytes 5898248 | tf_op jit(solution)/shard_map/ppermute | solution.py:122
  87.3 24.4 %all-to-all-start = ((bf16[4,2,160,384]{2,0,1,3:T(4,128)(2,1)}), bf16[4,2,160,384]{2,0,1,3:T(4,128)(2,1)S(1)}, u32[]{:S(2)}, u32[]{:S(2)}) async-start(bf16[4,2,160,384]{2,0,1,3:T(4,128)(2,1)} %copy.92), calls=%async_computation | async-start | bytes 3145728 | tf_op jit(solution)/shard_map/all_to_all | solution.py:171
  93.4 0.9 copy-start.7
  94.3 7.6 %copy-start.1 = (bf16[1,2,160,384]{3,2,1,0:T(8,128)(2,1)S(1)}, bf16[1,2,160,384]{3,2,1,0:T(8,128)(2,1)}, u32[]{:S(2)}) copy-start(bf16[1,2,160,384]{3,2,1,0:T(8,128)(2,1)} %param.5) | copy-start | bytes 737284
  94.3 7.6 %copy-start.5 = (f32[384]{0:T(512)S(1)}, f32[384]{0:T(512)}, u32[]{:S(2)}) copy-start(f32[384]{0:T(512)} %param.6) | copy-start | bytes 4612
  101.9 0.8 copy-start
  116.0 1.2 copy-start.3
  119.2 7.5 %slice-start = ((s8[7962624]{0:T(1024)(128)(4,1)}), s8[4194304]{0:T(1024)(128)(4,1)S(1)}, s32[]{:S(2)}) async-start(s8[7962624]{0:T(1024)(128)(4,1)} %bitcast.53), calls=%async_computation.2 | async-start | bytes 8388608
  125.0 2.1 slice-start.1
  132.1 1.3 copy-start.4
  209.7 5.3 %copy-start.6 = (f32[384]{0:T(512)S(1)}, f32[384]{0:T(512)}, u32[]{:S(2)}) copy-start(f32[384]{0:T(512)} %param.7) | copy-start | bytes 4612
Sparse Core Ops, SparseCore 0:
  11.4 46.2 all-gather.1

commit v8 on v6

--- a/solution.py
+++ b/solution.py
@@ -80,7 +80,7 @@
     pair_rows = 3 * channels
     tap_rows = 27 * channels
     flat_count = frame_total * row_total * padded_cols
-    shifted = jnp.concatenate(
+    shifted = jnp.stack(
         [
             jnp.pad(
                 cot_all,
@@ -88,8 +88,8 @@
             )
             for col_tap in range(3)
         ],
-        axis=-1,
-    ).reshape(flat_count, 3 * slots)
+        axis=3,
+    )
     first_row = frame_index * share_rows
     first_pair = first_row // pair_rows
     count = pair_count(tap_rows, share_rows, pair_rows, tap_rows // share_rows)
@@ -102,11 +102,11 @@
             framed,
             (depth_tap, row_tap, 0, 0),
             (frame_total, row_total, padded_cols, channels),
-        ).reshape(flat_count, channels)
+        )
         product = lax.dot_general(
-            slab, shifted, (((0,), (0,)), ((), ())), preferred_element_type=jnp.float32
-        )
-        pieces.append(product.reshape(channels, 3, slots).transpose(1, 0, 2).reshape(pair_rows, slots))
+            shifted, slab, (((0, 1, 2), (0, 1, 2)), ((), ())), preferred_element_type=jnp.float32
+        )
+        pieces.append(product.transpose(0, 2, 1).reshape(pair_rows, slots))
     stacked = jnp.concatenate(pieces, axis=0)
     return lax.dynamic_slice_in_dim(stacked, first_row - first_pair * pair_rows, share_rows, 0)
 
@@ -139,7 +139,14 @@
                 jnp.concatenate([theirs, ours], axis=1),
             )
         )
-    return jnp.roll(jnp.concatenate(relative, axis=1), (chip + 1) * block, axis=1)
+    relative = jnp.concatenate(relative, axis=1)
+    return jnp.concatenate(
+        [
+            lax.dynamic_slice_in_dim(relative, ((place - chip - 1) % chips) * block, block, 1)
+            for place in range(chips)
+        ],
+        axis=1,
+    )
 
 
 def local(latents, gain, bias, weight, cotangent):

time: 156 us -> 145 us (0.929)
  starting transfers between devices: 20.1 us -> 10.2 us
  waiting for transfers between devices: 56.2 us -> 64.8 us
  local copies, waits for them, and re-layouts: 27.2 us -> 20.4 us
  other arithmetic: 23.9 us -> 21.4 us
    ppermute x1, starting transfers between devices: 11.1 us -> 0.01 us  [gather_rows(): twins = lax.ppermute(stacked, 'height', sibling)]
    all_to_all x1, waiting for transfers between devices: 0.94 us -> 7.74 us  [local(): lax.all_to_all(cot_frames, 'height', split_axis=3, concat_axis=1, tiled=T...]
    dynamic_slice x1 -> x0, local copies, waits for them, and re-layouts: 5.95 us -> none  [block_weight_grad(): lax.dynamic_slice(framed, (depth_tap, row_tap, 0, 0), (frame_total, row_t...]
    reshape x4 -> x3, local copies, waits for them, and re-layouts: 5.91 us -> 0.09 us  [block_weight_grad(): pieces.append(product.transpose(0, 2, 1).reshape(pair_rows, slots))]
    another operation x0 -> x1, local copies, waits for them, and re-layouts: none -> 3.53 us  [block_weight_grad(): jnp.stack([jnp.pad(cot_all, ((0, 0), (0, 0), (col_tap, padded_cols - col_...]
    concatenate x2, other arithmetic: 9.92 us -> 7.43 us  [the longest x1 5.8 us: gather_rows(): jnp.concatenate([lax.dynamic_slice_in_dim(relative, (place - chip - 1) %...]
    ppermute x1, waiting for transfers between devices: 8.84 us -> 10.6 us  [gather_rows(): lax.ppermute(own, 'height', [(i, (i + 2 * step) % height_count) for i in...]
    ppermute x1, starting transfers between devices: 2.2 us -> 3.78 us  [padded(): lax.ppermute(tail, axis, [(i, (i + 1) % count) for i in range(ends)])]
  transfers between devices with their start and end apart: 6 -> 6, of which waited for: 3 -> 3; matrix products, arithmetic and copies ran while one was open for 19% -> 15% of each run, Pallas kernels for 0% -> 0%
where the time goes in v8:
time: 145 us; the launch traced here: 144 us
  waiting for transfers between devices  64.8 us (45%)
  other arithmetic  21.4 us (15%)
  local copies, waits for them, and re-layouts  20.4 us (14%)
  between operations  14.4 us (10%)
  matrix products  13.1 us (9%)
  starting transfers between devices  10.2 us (7%)
    all_gather x1, waiting for transfers between devices, local(): lax.all_gather(jnp.concatenate([hidden, cotangent], axis=-1), 'tm', axis=...  46.4 us
    ppermute x1, waiting for transfers between devices, gather_rows(): lax.ppermute(own, 'height', [(i, (i + 2 * step) % height_count) for i in...  10.6 us
    all_to_all x1, waiting for transfers between devices, local(): lax.all_to_all(cot_frames, 'height', split_axis=3, concat_axis=1, tiled=T...  7.74 us
    concatenate x1, other arithmetic, gather_rows(): jnp.concatenate([lax.dynamic_slice_in_dim(relative, (place - chip - 1) %...  5.8 us
    dot_general x3, matrix products, block_weight_grad(): lax.dot_general(shifted, slab, (((0, 1, 2), (0, 1, 2)), ((), ())), prefer...  5.49 us
    slice x2, local copies, waits for them, and re-layouts, local(): cot_frames = both_frames[..., channels:]  4.71 us
    conv_general_dilated x1, matrix products, forward_conv(): lax.conv_general_dilated(window[None], cube, (1, 1, 1), 'VALID', dimensio...  3.84 us
    all_to_all x1, local copies, waits for them, and re-layouts, local(): lax.all_to_all(cot_frames, 'height', split_axis=3, concat_axis=1, tiled=T...  3.79 us
  transfers between devices with their start and end apart: 6, of which 3 were waited for; matrix products, arithmetic and copies ran while one was open for 15% of the time, Pallas kernels for 0%

profile of v8, /device:TPU:0, one launch (start us, length us, event | category | flops | bytes accessed | tf_op | source)
XLA Modules:
  0.0 144.3 jit_solution(12800398374471290939)
XLA Ops:
  7.2 0.0 all-gather.2.cloned.1.call-start
  7.2 1.1 fusion.66
  8.3 1.2 multiply_convert_fusion
  9.5 1.8 %pad_maximum_fusion.4 = bf16[1,2,160,768]{3,2,1,0:T(8,128)(2,1)} fusion(bf16[1,2,160,384]{3,2,1,0:T(8,128)(2,1)} %param.9, bf16[1,2,160,384]{3,2,1,0:T(8,128)(2,1)S(1)} %multiply_convert_fusion), kind=kLoop, calls=%fused_computation.88 | loop fusion | flops 983040 | bytes 983040 | tf_op jit(solution)/shard_map/concatenate | solution.py:172
  11.3 0.0 all-gather.2.cloned.1.call-update
  11.3 46.4 %all-gather.2.cloned.1.call-done = bf16[4,2,160,768]{3,2,1,0:T(8,128)(2,1)} async-done(((bf16[1,2,160,768]{3,2,1,0:T(8,128)(2,1)}), bf16[4,2,160,768]{3,2,1,0:T(8,128)(2,1)}) %all-gather.2.cloned.1.call-update) | async-done | bytes 1966096 | tf_op jit(solution)/shard_map/all_gather | solution.py:171
  57.7 1.7 %fusion.81 = (bf16[4,2,160,384]{3,2,1,0:T(8,128)(2,1)S(1)}, bf16[4,2,160,384]{3,2,1,0:T(8,128)(2,1)S(1)}) fusion(bf16[4,2,160,768]{3,2,1,0:T(8,128)(2,1)} %all-gather.2.cloned.1.call-done), kind=kLoop, calls=%fused_computation.109 | loop fusion | bytes 3932160 | tf_op jit(solution)/shard_map/slice | solution.py:177
  59.4 1.5 %collective-permute-start = (bf16[4,2,160,384]{3,2,1,0:T(8,128)(2,1)S(1)}, bf16[4,2,160,384]{3,2,1,0:T(8,128)(2,1)}, u32[]{:S(2)}, u32[]{:S(2)}) collective-permute-start(bf16[4,2,160,384]{3,2,1,0:T(8,128)(2,1)S(1)} %get-tuple-element.9), channel_id=1, source_target_pairs={{0,2},{1,3},{2,0},{3,1},{4,6},{5,7},{6,4},{7,5},{8,10},{9,11},{10,... | collective-permute-start | bytes 2949128 | tf_op jit(solution)/shard_map/ppermute | solution.py:123
  61.0 1.0 pad_dynamic-slice_fusion.5
  62.0 1.3 collective-permute-start.3
  63.2 3.8 %collective-permute-start.2 = (bf16[3,1,160,384]{3,2,1,0:T(8,128)(2,1)}, bf16[3,1,160,384]{3,2,1,0:T(8,128)(2,1)}, u32[]{:S(2)}, u32[]{:S(2)}) collective-permute-start(bf16[3,1,160,384]{3,2,1,0:T(8,128)(2,1)} %get-tuple-element.15), channel_id=1, source_target_pairs={{0,1},{1,2},{2,3},{4,5},{5,6},{6,7},{8,9},{9,10},{10,11},{12,13},{... | collective-permute-start | bytes 1105928 | tf_op jit(solution)/shard_map/ppermute | solution.py:23
  67.0 3.0 %copy.54 = bf16[4,2,160,384]{2,1,0,3:T(2,128)(2,1)} copy(bf16[4,2,160,384]{3,2,1,0:T(8,128)(2,1)S(1)} %get-tuple-element.8) | data formatting | bytes 1966080 | tf_op jit(solution)/shard_map/slice | solution.py:177
  70.0 3.6 %all-to-all-start = ((bf16[4,2,160,384]{2,1,0,3:T(2,128)(2,1)}), bf16[4,2,160,384]{2,1,0,3:T(2,128)(2,1)S(1)}, u32[]{:S(2)}, u32[]{:S(2)}) async-start(bf16[4,2,160,384]{2,1,0,3:T(2,128)(2,1)} %copy.54), calls=%async_computation | async-start | bytes 3145728 | tf_op jit(solution)/shard_map/all_to_all | solution.py:178
  73.6 10.6 %collective-permute-done = bf16[4,2,160,384]{3,2,1,0:T(8,128)(2,1)} collective-permute-done((bf16[4,2,160,384]{3,2,1,0:T(8,128)(2,1)S(1)}, bf16[4,2,160,384]{3,2,1,0:T(8,128)(2,1)}, u32[]{:S(2)}, u32[]{:S(2)}) %collective-permute-start) | collective-permute-done | bytes 983072 | tf_op jit(solution)/shard_map/ppermute | solution.py:123
  84.3 2.9 %pad_maximum_fusion.2 = bf16[4,4,160,384]{3,2,1,0:T(8,128)(2,1)} fusion(bf16[4,2,160,384]{3,2,1,0:T(8,128)(2,1)} %collective-permute-done, bf16[4,2,160,384]{3,2,1,0:T(8,128)(2,1)S(1)} %get-tuple-element.9), kind=kLoop, calls=%fused_computation.38 | loop fusion | flops 983040 | bytes 3932160 | tf_op jit(solution)/shard_map/concatenate | solution.py:128
  87.1 0.0 collective-permute-start.1
  87.1 0.1 pad_dynamic-slice_fusion.6
  87.3 0.0 collective-permute-done.3
  87.3 0.0 collective-permute-done.2
  87.3 1.6 %fusion.44 = bf16[3,4,1,162,384]{4,3,1,0,2:T(8,128)(2,1)S(1)} fusion(bf16[3,1,160,384]{3,2,1,0:T(8,128)(2,1)} %collective-permute-done.3, bf16[3,2,160,384]{3,2,1,0:T(8,128)(2,1)S(1)} %pad_dynamic-slice_fusion.6, bf16[3,1,160,384]{3,2,1,0:T(8,128)(2,1)} %collective-permute-done.2), kind=kLoop, calls=%fused_computation.61 | loop fusion | flops 9704448 | bytes 2967552 | tf_op jit(solution)/shard_map/broadcast_in_dim | solution.py:58
  88.8 0.0 slice-start.1
  88.8 0.6 copy.70
  89.4 0.6 pad.32.clone
  90.0 0.0 copy-start.7
  90.0 0.2 copy.51
  90.3 0.0 slice-done
  90.3 0.6 slice-done.1
  90.9 3.8 %fusion.55 = f32[1,2,8,21,384]{4,2,3,1,0:T(8,128)S(1)} fusion(bf16[3,3,3,384,384]{4,3,2,1,0:T(8,128)(2,1)S(1)} %bitcast.107, bf16[3,4,1,7,2,384]{5,3,4,1,0,2:T(8,128)(2,1)S(1)} %slice.42, bf16[3,4,1,8,21,384]{5,3,4,1,0,2:T(8,128)(2,1)S(1)} %copy.51, pred[8,21]{0,1:T(8,128)(4,1)S(1)} %copy-done.7), kind=kOutput, calls=%fused_computation.75 | convolution fusion | flops 2680657920 | bytes 10156200 | tf_op jit(solution)/shard_map/conv_general_dilated | solution.py:57
  94.7 0.0 copy-start.2
  94.7 0.0 copy-start.5
  94.7 0.3 copy.52
  95.0 0.2 slice.43
  95.2 0.5 copy-done.2
  95.6 0.0 copy-done.5
  95.6 0.4 multiply_reduce_fusion
  96.1 7.7 %all-to-all-done = bf16[4,2,160,384]{2,1,0,3:T(2,128)(2,1)S(1)} async-done(((bf16[4,2,160,384]{2,1,0,3:T(2,128)(2,1)}), bf16[4,2,160,384]{2,1,0,3:T(2,128)(2,1)S(1)}, u32[]{:S(2)}, u32[]{:S(2)}) %all-to-all-start) | async-done | bytes 983072 | tf_op jit(solution)/shard_map/all_to_all | solution.py:178
  103.8 3.8 %copy.55 = bf16[4,2,160,4,96]{4,2,1,3,0:T(8,128)(2,1)} copy(bf16[4,2,160,4,96]{2,1,0,4,3:T(2,128)(2,1)S(1)} %bitcast.96) | data formatting | bytes 1966080 | tf_op jit(solution)/shard_map/all_to_all | solution.py:178
  107.6 3.5 %pad_bitcast_fusion.2 = (bf16[4,8,168,1,96]{4,2,1,3,0:T(8,128)(2,1)S(1)}, bf16[4,8,168,1,96]{4,2,1,3,0:T(8,128)(2,1)S(1)}, bf16[4,8,168,1,96]{4,2,1,3,0:T(8,128)(2,1)S(1)}) fusion(bf16[4,8,160,96]{3,2,1,0:T(8,128)(2,1)} %bitcast.99), kind=kLoop, calls=%fused_computation.68 | loop fusion | bytes 4079616 | tf_op jit(solution)/shard_map/stack | solution.py:83
  111.1 0.0 collective-permute-done.1
  111.2 1.7 %fusion.82 = (bf16[4,2,160,384]{3,2,1,0:T(8,128)(2,1)S(1)}, bf16[4,2,160,384]{3,2,1,0:T(8,128)(2,1)S(1)}) fusion(bf16[4,4,160,384]{3,2,1,0:T(8,128)(2,1)} %collective-permute-done.1), kind=kLoop, calls=%fused_computation.110 | loop fusion | bytes 3932160 | tf_op jit(solution)/shard_map/slice | solution.py:134
  112.9 0.3 fusion.25
  113.2 1.8 %fusion.26 = bf16[4,4,160,384]{3,2,1,0:T(8,128)(2,1)S(1)} fusion(bf16[4,2,160,384]{3,2,1,0:T(8,128)(2,1)} %collective-permute-done, bf16[4,2,160,384]{3,2,1,0:T(8,128)(2,1)S(1)} %get-tuple-element.11, pred[]{:T(512)S(6)} %eq.10), kind=kLoop, calls=%fused_computation.41 | loop fusion | flops 2949120 | bytes 3932161 | tf_op jit(solution)/shard_map/jit(_where)/select_n | solution.py:136
  115.1 1.6 %fusion.28 = (bf16[4,4,160,384]{3,2,1,0:T(8,128)(2,1)S(1)}, bf16[4,4,160,384]{3,2,1,0:T(8,128)(2,1)S(1)}) fusion(s32[]{:T(128)S(6)} %select_n.95, bf16[4,4,160,384]{3,2,1,0:T(8,128)(2,1)S(1)} %fusion.26, bf16[4,4,160,384]{3,2,1,0:T(8,128)(2,1)S(1)} %fusion.25, s32[]{:T(128)S(6)} %select_n.97), kind=kLoop, calls=%fused_computation.43 | loop fusion | flops 1966080 | bytes 7864328 | tf_op jit(solution)/shard_map/concatenate | solution.py:142
  116.7 0.0 slice-start.2
  116.7 5.8 %fusion.8 = bf16[6,10,168,384]{3,2,1,0:T(8,128)(2,1)S(1)} fusion(bf16[4,4,160,384]{3,2,1,0:T(8,128)(2,1)S(1)} %get-tuple-element.7, bf16[4,4,160,384]{3,2,1,0:T(8,128)(2,1)S(1)} %get-tuple-element.6), kind=kLoop, calls=%fused_computation.13 | loop fusion | flops 73543680 | bytes 11673600 | tf_op jit(solution)/shard_map/concatenate | solution.py:143
  122.5 0.0 slice-start.3
  122.5 0.2 dynamic-slice_bitcast_fusion
  122.7 0.6 copy.69
  123.3 0.6 pad.30.clone
  123.9 0.2 copy.46
  124.1 0.0 slice-done.2
  124.1 0.4 slice-done.3
  124.6 3.8 %fusion.58 = f32[1,2,8,21,384]{4,2,3,1,0:T(8,128)S(1)} fusion(bf16[3,3,3,384,384]{4,3,2,1,0:T(8,128)(2,1)S(1)} %bitcast.110, bf16[3,4,1,7,2,384]{5,3,4,1,0,2:T(8,128)(2,1)S(1)} %slice.39, bf16[3,4,1,8,21,384]{5,3,4,1,0,2:T(8,128)(2,1)S(1)} %copy.46, pred[8,21]{0,1:T(8,128)(4,1)S(1)} %copy-done.7), kind=kOutput, calls=%fused_computation.76 | convolution fusion | flops 2680657920 | bytes 10156200 | tf_op jit(solution)/shard_map/conv_general_dilated | solution.py:44
  128.4 0.3 copy.47
  128.7 0.2 slice.40
  128.9 1.8 %fusion.46 = f32[3,12,8,384]{3,2,1,0:T(8,128)S(1)} fusion(bf16[6,10,168,384]{3,2,1,0:T(8,128)(2,1)S(1)} %fusion.8, s32[]{:T(128)S(6)} %select_n.102, s32[]{:T(128)S(6)} %select_n.104, bf16[4,8,168,1,96]{4,2,1,3,0:T(8,128)(2,1)S(1)} %get-tuple-element.13, bf16[4,8,168,1,96]{4,2,1,3,0:T(8,128)(2,1)S(1)} %get-tuple-element.14, ...), kind=kOutput, calls=%fused_computation.72 | convolution fusion | flops 1192181760 | bytes 8699912 | tf_op jit(solution)/shard_map/dot_general | solution.py:106
  130.8 1.8 %fusion.49 = f32[3,12,8,384]{3,2,1,0:T(8,128)S(1)} fusion(bf16[6,10,168,384]{3,2,1,0:T(8,128)(2,1)S(1)} %fusion.8, s32[]{:T(128)S(6)} %select_n.106, s32[]{:T(128)S(6)} %select_n.108, bf16[4,8,168,1,96]{4,2,1,3,0:T(8,128)(2,1)S(1)} %get-tuple-element.13, bf16[4,8,168,1,96]{4,2,1,3,0:T(8,128)(2,1)S(1)} %get-tuple-element.14, ...), kind=kOutput, calls=%fused_computation.73 | convolution fusion | flops 1192181760 | bytes 8699912 | tf_op jit(solution)/shard_map/dot_general | solution.py:106
  132.7 0.0 copy-start.1
  132.7 0.0 copy-start.3
  132.7 0.0 copy-start.4
  132.7 0.0 copy-start.6
  132.7 1.8 %fusion.52 = f32[3,12,8,384]{3,2,1,0:T(8,128)S(1)} fusion(bf16[6,10,168,384]{3,2,1,0:T(8,128)(2,1)S(1)} %fusion.8, s32[]{:T(128)S(6)} %select_n.110, s32[]{:T(128)S(6)} %select_n.112, bf16[4,8,168,1,96]{4,2,1,3,0:T(8,128)(2,1)S(1)} %get-tuple-element.13, bf16[4,8,168,1,96]{4,2,1,3,0:T(8,128)(2,1)S(1)} %get-tuple-element.14, ...), kind=kOutput, calls=%fused_computation.74 | convolution fusion | flops 1192181760 | bytes 8699912 | tf_op jit(solution)/shard_map/dot_general | solution.py:106
  134.6 1.2 add_convert_fusion
  135.8 1.6 %fusion.63 = f32[2592,96]{0,1:T(8,128)} fusion(s32[]{:T(128)S(6)} %select_n.113, f32[1152,96]{0,1:T(8,128)S(1)} %bitcast.102, f32[1152,96]{0,1:T(8,128)S(1)} %bitcast.103, f32[1152,96]{0,1:T(8,128)S(1)} %bitcast.104), kind=kLoop, calls=%fused_computation.79 | loop fusion | flops 746496 | bytes 2322436 | tf_op jit(solution)/shard_map/mul | solution.py:190
  (17 shorter events, 0.2 us)
Async XLA Ops:
  7.2 50.6 %all-gather.2.cloned.1.call-start = ((), (), s32[]{:S(2)}) async-start(), calls=%async_computation.1 | async-start | bytes 2457600 | tf_op jit(solution)/shard_map/all_gather | solution.py:171
  59.4 24.8 %collective-permute-start = (bf16[4,2,160,384]{3,2,1,0:T(8,128)(2,1)S(1)}, bf16[4,2,160,384]{3,2,1,0:T(8,128)(2,1)}, u32[]{:S(2)}, u32[]{:S(2)}) collective-permute-start(bf16[4,2,160,384]{3,2,1,0:T(8,128)(2,1)S(1)} %get-tuple-element.9), channel_id=1, source_target_pairs={{0,2},{1,3},{2,0},{3,1},{4,6},{5,7},{6,4},{7,5},{8,10},{9,11},{10,... | collective-permute-start | bytes 2949128 | tf_op jit(solution)/shard_map/ppermute | solution.py:123
  62.0 25.3 %collective-permute-start.3 = (bf16[3,1,160,384]{3,2,1,0:T(8,128)(2,1)}, bf16[3,1,160,384]{3,2,1,0:T(8,128)(2,1)}, u32[]{:S(2)}, u32[]{:S(2)}) collective-permute-start(bf16[3,1,160,384]{3,2,1,0:T(8,128)(2,1)} %get-tuple-element.16), channel_id=1, source_target_pairs={{1,0},{2,1},{3,2},{5,4},{6,5},{7,6},{9,8},{10,9},{11,10},{13,12},{... | collective-permute-start | bytes 1105928 | tf_op jit(solution)/shard_map/ppermute | solution.py:25
  63.2 24.0 %collective-permute-start.2 = (bf16[3,1,160,384]{3,2,1,0:T(8,128)(2,1)}, bf16[3,1,160,384]{3,2,1,0:T(8,128)(2,1)}, u32[]{:S(2)}, u32[]{:S(2)}) collective-permute-start(bf16[3,1,160,384]{3,2,1,0:T(8,128)(2,1)} %get-tuple-element.15), channel_id=1, source_target_pairs={{0,1},{1,2},{2,3},{4,5},{5,6},{6,7},{8,9},{9,10},{10,11},{12,13},{... | collective-permute-start | bytes 1105928 | tf_op jit(solution)/shard_map/ppermute | solution.py:23
  70.0 33.8 %all-to-all-start = ((bf16[4,2,160,384]{2,1,0,3:T(2,128)(2,1)}), bf16[4,2,160,384]{2,1,0,3:T(2,128)(2,1)S(1)}, u32[]{:S(2)}, u32[]{:S(2)}) async-start(bf16[4,2,160,384]{2,1,0,3:T(2,128)(2,1)} %copy.54), calls=%async_computation | async-start | bytes 3145728 | tf_op jit(solution)/shard_map/all_to_all | solution.py:178
  84.2 6.0 %slice-start = ((s8[7962624]{0:T(1024)(128)(4,1)}), s8[4194304]{0:T(1024)(128)(4,1)S(1)}, s32[]{:S(2)}) async-start(s8[7962624]{0:T(1024)(128)(4,1)} %bitcast.105), calls=%async_computation.2 | async-start | bytes 8388608
  87.1 24.0 %collective-permute-start.1 = (bf16[4,4,160,384]{3,2,1,0:T(8,128)(2,1)}, bf16[4,4,160,384]{3,2,1,0:T(8,128)(2,1)}, u32[]{:S(2)}, u32[]{:S(2)}) collective-permute-start(bf16[4,4,160,384]{3,2,1,0:T(8,128)(2,1)} %pad_maximum_fusion.2), channel_id=1, source_target_pairs={{0,1},{1,0},{2,3},{3,2},{4,5},{5,4},{6,7},{7,6},{8,9},{9,8},{10,11... | collective-permute-start | bytes 5898248 | tf_op jit(solution)/shard_map/ppermute | solution.py:129
  88.8 2.1 %slice-start.1 = ((s8[7962624]{0:T(1024)(128)(4,1)}), s8[3768320]{0:T(1024)(128)(4,1)S(1)}, s32[]{:S(2)}) async-start(s8[7962624]{0:T(1024)(128)(4,1)} %bitcast.105), calls=%async_computation.3 | async-start | bytes 7536640
  90.0 0.9 copy-start.7
  94.7 0.9 copy-start.2
  94.7 0.9 copy-start.5
  95.6 15.5 %copy-start = (f32[1,2,1,160,384]{4,1,3,2,0:T(2,128)}, f32[1,2,1,160,384]{4,1,3,2,0:T(2,128)S(1)}, u32[]{:S(2)}) copy-start(f32[1,2,1,160,384]{4,1,3,2,0:T(2,128)S(1)} %slice.43) | copy-start | bytes 1474564
  116.7 7.4 %slice-start.2 = ((s8[7962624]{0:T(1024)(128)(4,1)}), s8[4194304]{0:T(1024)(128)(4,1)S(1)}, s32[]{:S(2)}) async-start(s8[7962624]{0:T(1024)(128)(4,1)} %bitcast.108), calls=%async_computation.4 | async-start | bytes 8388608
  122.5 2.1 %slice-start.3 = ((s8[7962624]{0:T(1024)(128)(4,1)}), s8[3768320]{0:T(1024)(128)(4,1)S(1)}, s32[]{:S(2)}) async-start(s8[7962624]{0:T(1024)(128)(4,1)} %bitcast.108), calls=%async_computation.5 | async-start | bytes 7536640
  132.7 1.9 %copy-start.1 = (f32[1,2,1,160,384]{4,1,3,2,0:T(2,128)S(1)}, f32[1,2,1,160,384]{4,1,3,2,0:T(2,128)}, u32[]{:S(2)}) copy-start(f32[1,2,1,160,384]{4,1,3,2,0:T(2,128)} %copy-done) | copy-start | bytes 1474564
  132.7 1.9 %copy-start.3 = (bf16[1,2,160,384]{3,2,1,0:T(8,128)(2,1)S(1)}, bf16[1,2,160,384]{3,2,1,0:T(8,128)(2,1)}, u32[]{:S(2)}) copy-start(bf16[1,2,160,384]{3,2,1,0:T(8,128)(2,1)} %param.5) | copy-start | bytes 737284
  132.7 1.9 %copy-start.4 = (bf16[1,2,160,384]{3,2,1,0:T(8,128)(2,1)S(1)}, bf16[1,2,160,384]{3,2,1,0:T(8,128)(2,1)}, u32[]{:S(2)}) copy-start(bf16[1,2,160,384]{3,2,1,0:T(8,128)(2,1)} %param.9) | copy-start | bytes 737284
  132.7 1.9 %copy-start.6 = (f32[384]{0:T(512)S(1)}, f32[384]{0:T(512)}, u32[]{:S(2)}) copy-start(f32[384]{0:T(512)} %param.7) | copy-start | bytes 4612
Sparse Core Ops, SparseCore 0:
  11.4 46.2 all-gather.1

commit v9 on v8

--- a/solution.py
+++ b/solution.py
@@ -147,6 +147,22 @@
         ],
         axis=1,
     )
+
+
+def gather_frames(block):
+    count = lax.axis_size("tm")
+    position = lax.axis_index("tm")
+    up = [(i, i + 1) for i in range(count - 1)]
+    down = [(i + 1, i) for i in range(count - 1)]
+    earlier, later = [], []
+    rising, falling = block, block
+    for step in range(1, count):
+        rising = lax.ppermute(rising, "tm", up)
+        falling = lax.ppermute(falling, "tm", down)
+        earlier.append(rising)
+        later.append(falling)
+    relative = jnp.concatenate(earlier[::-1] + [block] + later, axis=0)
+    return lax.dynamic_slice_in_dim(relative, count - 1 - position, count * block.shape[0], 0)
 
 
 def local(latents, gain, bias, weight, cotangent):
@@ -168,9 +184,7 @@
     inverse_root = 1.0 / math.sqrt(total_frames * total_rows * col_count)
     weight_cube = weight.reshape(3, 3, 3, channels, channels)
 
-    both_frames = lax.all_gather(
-        jnp.concatenate([hidden, cotangent], axis=-1), "tm", axis=0, tiled=True
-    )
+    both_frames = gather_frames(jnp.concatenate([hidden, cotangent], axis=-1))
     hidden_all = gather_rows(both_frames[..., :channels], height_count)
     framed = jnp.pad(hidden_all, ((2, 0), (1, 1), (1, right_pad), (0, 0)))
 

time: 145 us -> 126 us (0.87)
  waiting for transfers between devices: 64.8 us -> 44.2 us
  starting transfers between devices: 10.2 us -> 28 us
  between operations: 14.4 us -> 1.19 us
  local copies, waits for them, and re-layouts: 20.4 us -> 18.6 us
    all_gather x1 -> x0, waiting for transfers between devices: 46.4 us -> none  [local(): lax.all_gather(jnp.concatenate([hidden, cotangent], axis=-1), 'tm', axis=...]
    ppermute x0 -> x6, waiting for transfers between devices: none -> 28.6 us  [the longest x3 24.7 us: gather_frames(): rising = lax.ppermute(rising, 'tm', up)]
    ppermute x0 -> x6, starting transfers between devices: none -> 17.6 us  [the longest x3 13.8 us: gather_frames(): rising = lax.ppermute(rising, 'tm', up)]
    all_to_all x1, waiting for transfers between devices: 7.74 us -> 6.27 us  [local(): lax.all_to_all(cot_frames, 'height', split_axis=3, concat_axis=1, tiled=T...]
  transfers between devices with their start and end apart: 6 -> 11, of which waited for: 3 -> 6; matrix products, arithmetic and copies ran while one was open for 15% -> 18% of each run, Pallas kernels for 0% -> 0%
where the time goes in v9:
time: 126 us
  waiting for transfers between devices  44.2 us (35%)
  starting transfers between devices  28 us (22%)
  other arithmetic  20.7 us (16%)
  local copies, waits for them, and re-layouts  18.6 us (15%)
  matrix products  13.1 us (10%)
    ppermute x3, waiting for transfers between devices, gather_frames(): rising = lax.ppermute(rising, 'tm', up)  24.7 us
    ppermute x3, starting transfers between devices, gather_frames(): rising = lax.ppermute(rising, 'tm', up)  13.8 us
    ppermute x1, waiting for transfers between devices, gather_rows(): lax.ppermute(own, 'height', [(i, (i + 2 * step) % height_count) for i in...  9.36 us
    all_to_all x1, waiting for transfers between devices, local(): lax.all_to_all(cot_frames, 'height', split_axis=3, concat_axis=1, tiled=T...  6.27 us
    concatenate x1, other arithmetic, gather_rows(): jnp.concatenate([lax.dynamic_slice_in_dim(relative, (place - chip - 1) %...  5.84 us
    dot_general x3, matrix products, block_weight_grad(): lax.dot_general(shifted, slab, (((0, 1, 2), (0, 1, 2)), ((), ())), prefer...  5.5 us
    ppermute x3, waiting for transfers between devices, gather_frames(): falling = lax.ppermute(falling, 'tm', down)  3.9 us
    ppermute x3, starting transfers between devices, gather_frames(): falling = lax.ppermute(falling, 'tm', down)  3.88 us
  transfers between devices with their start and end apart: 11, of which 6 were waited for; matrix products, arithmetic and copies ran while one was open for 18% of the time, Pallas kernels for 0%

profile of v9, /device:TPU:0, one launch (start us, length us, event | category | flops | bytes accessed | tf_op | source)
XLA Modules:
  0.0 125.9 jit_solution(12577006524046259524)
XLA Ops:
  0.6 0.0 copy-start.4
  0.6 1.1 fusion.66
  1.8 1.2 multiply_convert_fusion
  3.0 1.0 pad_maximum_fusion.4
  4.0 5.0 %collective-permute-start = (bf16[1,2,160,768]{3,2,1,0:T(8,128)(2,1)S(1)}, bf16[1,2,160,768]{3,2,1,0:T(8,128)(2,1)S(1)}, u32[]{:S(2)}, u32[]{:S(2)}) collective-permute-start(bf16[1,2,160,768]{3,2,1,0:T(8,128)(2,1)S(1)} %pad_maximum_fusion.4), channel_id=1, source_target_pairs={{0,4},{4,8},{8,12},{1,5},{5,9},{9,13},{2,6},{6,10},{10,14},{3,7},{... | collective-permute-start | bytes 1474568 | tf_op jit(solution)/shard_map/ppermute | solution.py:160
  9.0 1.3 %collective-permute-start.3 = (bf16[1,2,160,768]{3,2,1,0:T(8,128)(2,1)S(1)}, bf16[1,2,160,768]{3,2,1,0:T(8,128)(2,1)S(1)}, u32[]{:S(2)}, u32[]{:S(2)}) collective-permute-start(bf16[1,2,160,768]{3,2,1,0:T(8,128)(2,1)S(1)} %pad_maximum_fusion.4), channel_id=1, source_target_pairs={{4,0},{8,4},{12,8},{5,1},{9,5},{13,9},{6,2},{10,6},{14,10},{7,3},{... | collective-permute-start | bytes 1474568 | tf_op jit(solution)/shard_map/ppermute | solution.py:161
  10.3 9.1 %collective-permute-done = bf16[1,2,160,768]{3,2,1,0:T(8,128)(2,1)S(1)} collective-permute-done((bf16[1,2,160,768]{3,2,1,0:T(8,128)(2,1)S(1)}, bf16[1,2,160,768]{3,2,1,0:T(8,128)(2,1)S(1)}, u32[]{:S(2)}, u32[]{:S(2)}) %collective-permute-start) | collective-permute-done | bytes 491552 | tf_op jit(solution)/shard_map/ppermute | solution.py:160
  19.4 4.4 %collective-permute-start.1 = (bf16[1,2,160,768]{3,2,1,0:T(8,128)(2,1)S(1)}, bf16[1,2,160,768]{3,2,1,0:T(8,128)(2,1)S(1)}, u32[]{:S(2)}, u32[]{:S(2)}) collective-permute-start(bf16[1,2,160,768]{3,2,1,0:T(8,128)(2,1)S(1)} %collective-permute-done), channel_id=1, source_target_pairs={{0,4},{4,8},{8,12},{1,5},{5,9},{9,13},{2,6},{6,10},{10,14},{3,7},{... | collective-permute-start | bytes 1474568 | tf_op jit(solution)/shard_map/ppermute | solution.py:160
  23.8 1.3 %collective-permute-start.4 = (bf16[1,2,160,768]{3,2,1,0:T(8,128)(2,1)S(1)}, bf16[1,2,160,768]{3,2,1,0:T(8,128)(2,1)S(1)}, u32[]{:S(2)}, u32[]{:S(2)}) collective-permute-start(bf16[1,2,160,768]{3,2,1,0:T(8,128)(2,1)S(1)} %collective-permute-done.3), channel_id=1, source_target_pairs={{4,0},{8,4},{12,8},{5,1},{9,5},{13,9},{6,2},{10,6},{14,10},{7,3},{... | collective-permute-start | bytes 1474568 | tf_op jit(solution)/shard_map/ppermute | solution.py:161
  25.1 8.2 %collective-permute-done.1 = bf16[1,2,160,768]{3,2,1,0:T(8,128)(2,1)S(1)} collective-permute-done((bf16[1,2,160,768]{3,2,1,0:T(8,128)(2,1)S(1)}, bf16[1,2,160,768]{3,2,1,0:T(8,128)(2,1)S(1)}, u32[]{:S(2)}, u32[]{:S(2)}) %collective-permute-start.1) | collective-permute-done | bytes 491552 | tf_op jit(solution)/shard_map/ppermute | solution.py:160
  33.4 4.4 %collective-permute-start.2 = (bf16[1,2,160,768]{3,2,1,0:T(8,128)(2,1)S(1)}, bf16[1,2,160,768]{3,2,1,0:T(8,128)(2,1)S(1)}, u32[]{:S(2)}, u32[]{:S(2)}) collective-permute-start(bf16[1,2,160,768]{3,2,1,0:T(8,128)(2,1)S(1)} %collective-permute-done.1), channel_id=1, source_target_pairs={{0,4},{4,8},{8,12},{1,5},{5,9},{9,13},{2,6},{6,10},{10,14},{3,7},{... | collective-permute-start | bytes 1474568 | tf_op jit(solution)/shard_map/ppermute | solution.py:160
  37.8 1.3 %collective-permute-start.5 = (bf16[1,2,160,768]{3,2,1,0:T(8,128)(2,1)S(1)}, bf16[1,2,160,768]{3,2,1,0:T(8,128)(2,1)S(1)}, u32[]{:S(2)}, u32[]{:S(2)}) collective-permute-start(bf16[1,2,160,768]{3,2,1,0:T(8,128)(2,1)S(1)} %collective-permute-done.4), channel_id=1, source_target_pairs={{4,0},{8,4},{12,8},{5,1},{9,5},{13,9},{6,2},{10,6},{14,10},{7,3},{... | collective-permute-start | bytes 1474568 | tf_op jit(solution)/shard_map/ppermute | solution.py:161
  39.1 7.3 %collective-permute-done.2 = bf16[1,2,160,768]{3,2,1,0:T(8,128)(2,1)S(1)} collective-permute-done((bf16[1,2,160,768]{3,2,1,0:T(8,128)(2,1)S(1)}, bf16[1,2,160,768]{3,2,1,0:T(8,128)(2,1)S(1)}, u32[]{:S(2)}, u32[]{:S(2)}) %collective-permute-start.2) | collective-permute-done | bytes 491552 | tf_op jit(solution)/shard_map/ppermute | solution.py:160
  46.7 3.9 %collective-permute-done.5 = bf16[1,2,160,768]{3,2,1,0:T(8,128)(2,1)S(1)} collective-permute-done((bf16[1,2,160,768]{3,2,1,0:T(8,128)(2,1)S(1)}, bf16[1,2,160,768]{3,2,1,0:T(8,128)(2,1)S(1)}, u32[]{:S(2)}, u32[]{:S(2)}) %collective-permute-start.5) | collective-permute-done | bytes 491552 | tf_op jit(solution)/shard_map/ppermute | solution.py:161
  50.6 0.3 constant_dynamic-slice_fusion.1
  50.9 1.6 %collective-permute-start.6 = (bf16[4,2,160,384]{3,2,1,0:T(8,128)(2,1)S(1)}, bf16[4,2,160,384]{3,2,1,0:T(8,128)(2,1)}, u32[]{:S(2)}, u32[]{:S(2)}) collective-permute-start(bf16[4,2,160,384]{3,2,1,0:T(8,128)(2,1)S(1)} %get-tuple-element.6), channel_id=1, source_target_pairs={{0,2},{1,3},{2,0},{3,1},{4,6},{5,7},{6,4},{7,5},{8,10},{9,11},{10,... | collective-permute-start | bytes 2949128 | tf_op jit(solution)/shard_map/ppermute | solution.py:123
  52.4 1.0 pad_dynamic-slice_fusion.5
  53.4 1.3 %collective-permute-start.9 = (bf16[3,1,160,384]{3,2,1,0:T(8,128)(2,1)}, bf16[3,1,160,384]{3,2,1,0:T(8,128)(2,1)}, u32[]{:S(2)}, u32[]{:S(2)}) collective-permute-start(bf16[3,1,160,384]{3,2,1,0:T(8,128)(2,1)} %get-tuple-element.13), channel_id=1, source_target_pairs={{1,0},{2,1},{3,2},{5,4},{6,5},{7,6},{9,8},{10,9},{11,10},{13,12},{... | collective-permute-start | bytes 1105928 | tf_op jit(solution)/shard_map/ppermute | solution.py:25
  54.7 3.8 %collective-permute-start.8 = (bf16[3,1,160,384]{3,2,1,0:T(8,128)(2,1)}, bf16[3,1,160,384]{3,2,1,0:T(8,128)(2,1)}, u32[]{:S(2)}, u32[]{:S(2)}) collective-permute-start(bf16[3,1,160,384]{3,2,1,0:T(8,128)(2,1)} %get-tuple-element.12), channel_id=1, source_target_pairs={{0,1},{1,2},{2,3},{4,5},{5,6},{6,7},{8,9},{9,10},{10,11},{12,13},{... | collective-permute-start | bytes 1105928 | tf_op jit(solution)/shard_map/ppermute | solution.py:23
  58.5 3.0 %copy.33 = bf16[4,2,160,384]{2,1,0,3:T(2,128)(2,1)} copy(bf16[4,2,160,384]{3,2,1,0:T(8,128)(2,1)S(1)} %get-tuple-element.5) | data formatting | bytes 1966080 | tf_op jit(solution)/shard_map/slice | solution.py:191
  61.5 3.7 %all-to-all-start = ((bf16[4,2,160,384]{2,1,0,3:T(2,128)(2,1)}), bf16[4,2,160,384]{2,1,0,3:T(2,128)(2,1)S(1)}, u32[]{:S(2)}, u32[]{:S(2)}) async-start(bf16[4,2,160,384]{2,1,0,3:T(2,128)(2,1)} %copy.33), calls=%async_computation | async-start | bytes 3145728 | tf_op jit(solution)/shard_map/all_to_all | solution.py:192
  65.3 9.4 %collective-permute-done.6 = bf16[4,2,160,384]{3,2,1,0:T(8,128)(2,1)} collective-permute-done((bf16[4,2,160,384]{3,2,1,0:T(8,128)(2,1)S(1)}, bf16[4,2,160,384]{3,2,1,0:T(8,128)(2,1)}, u32[]{:S(2)}, u32[]{:S(2)}) %collective-permute-start.6) | collective-permute-done | bytes 983072 | tf_op jit(solution)/shard_map/ppermute | solution.py:123
  74.7 2.9 %pad_maximum_fusion.2 = bf16[4,4,160,384]{3,2,1,0:T(8,128)(2,1)} fusion(bf16[4,2,160,384]{3,2,1,0:T(8,128)(2,1)} %collective-permute-done.6, bf16[4,2,160,384]{3,2,1,0:T(8,128)(2,1)S(1)} %get-tuple-element.6), kind=kLoop, calls=%fused_computation.38 | loop fusion | flops 983040 | bytes 3932160 | tf_op jit(solution)/shard_map/concatenate | solution.py:128
  77.5 0.1 pad_dynamic-slice_fusion.6
  77.6 0.0 collective-permute-done.9
  77.7 1.6 %fusion.44 = bf16[3,4,1,162,384]{4,3,1,0,2:T(8,128)(2,1)S(1)} fusion(bf16[3,1,160,384]{3,2,1,0:T(8,128)(2,1)} %collective-permute-done.9, bf16[3,2,160,384]{3,2,1,0:T(8,128)(2,1)S(1)} %pad_dynamic-slice_fusion.6, bf16[3,1,160,384]{3,2,1,0:T(8,128)(2,1)} %collective-permute-done.8), kind=kLoop, calls=%fused_computation.61 | loop fusion | flops 9704448 | bytes 2967552 | tf_op jit(solution)/shard_map/broadcast_in_dim | solution.py:58
  79.2 0.0 slice-start.1
  79.2 0.6 copy.49
  79.8 0.0 copy-start.8
  79.8 0.6 pad.32.clone
  80.4 0.2 copy.30
  80.7 0.6 slice-done.1
  81.3 3.8 %fusion.55 = f32[1,2,8,21,384]{4,2,3,1,0:T(8,128)S(1)} fusion(bf16[3,3,3,384,384]{4,3,2,1,0:T(8,128)(2,1)S(1)} %bitcast.107, bf16[3,4,1,7,2,384]{5,3,4,1,0,2:T(8,128)(2,1)S(1)} %slice.40, bf16[3,4,1,8,21,384]{5,3,4,1,0,2:T(8,128)(2,1)S(1)} %copy.30, pred[8,21]{0,1:T(8,128)(4,1)S(1)} %copy-done.8), kind=kOutput, calls=%fused_computation.75 | convolution fusion | flops 2680657920 | bytes 10156200 | tf_op jit(solution)/shard_map/conv_general_dilated | solution.py:57
  85.1 0.3 copy.31
  85.3 0.2 slice.41
  85.5 0.0 copy-start
  85.6 0.4 multiply_reduce_fusion
  86.0 6.3 %all-to-all-done = bf16[4,2,160,384]{2,1,0,3:T(2,128)(2,1)S(1)} async-done(((bf16[4,2,160,384]{2,1,0,3:T(2,128)(2,1)}), bf16[4,2,160,384]{2,1,0,3:T(2,128)(2,1)S(1)}, u32[]{:S(2)}, u32[]{:S(2)}) %all-to-all-start) | async-done | bytes 983072 | tf_op jit(solution)/shard_map/all_to_all | solution.py:192
  92.2 3.8 %copy.34 = bf16[4,2,160,4,96]{4,2,1,3,0:T(8,128)(2,1)} copy(bf16[4,2,160,4,96]{2,1,0,4,3:T(2,128)(2,1)S(1)} %bitcast.96) | data formatting | bytes 1966080 | tf_op jit(solution)/shard_map/all_to_all | solution.py:192
  96.0 3.5 %pad_bitcast_fusion.2 = (bf16[4,8,168,1,96]{4,2,1,3,0:T(8,128)(2,1)S(1)}, bf16[4,8,168,1,96]{4,2,1,3,0:T(8,128)(2,1)S(1)}, bf16[4,8,168,1,96]{4,2,1,3,0:T(8,128)(2,1)S(1)}) fusion(bf16[4,8,160,96]{3,2,1,0:T(8,128)(2,1)} %bitcast.99), kind=kLoop, calls=%fused_computation.68 | loop fusion | bytes 4079616 | tf_op jit(solution)/shard_map/stack | solution.py:83
  99.6 1.7 %fusion.81 = (bf16[4,2,160,384]{3,2,1,0:T(8,128)(2,1)S(1)}, bf16[4,2,160,384]{3,2,1,0:T(8,128)(2,1)S(1)}) fusion(bf16[4,4,160,384]{3,2,1,0:T(8,128)(2,1)} %collective-permute-done.7), kind=kLoop, calls=%fused_computation.118 | loop fusion | bytes 3932160 | tf_op jit(solution)/shard_map/slice | solution.py:134
  101.3 0.3 fusion.25
  101.6 1.8 %fusion.26 = bf16[4,4,160,384]{3,2,1,0:T(8,128)(2,1)S(1)} fusion(bf16[4,2,160,384]{3,2,1,0:T(8,128)(2,1)} %collective-permute-done.6, bf16[4,2,160,384]{3,2,1,0:T(8,128)(2,1)S(1)} %get-tuple-element.8, pred[]{:T(512)S(6)} %eq.10), kind=kLoop, calls=%fused_computation.41 | loop fusion | flops 2949120 | bytes 3932161 | tf_op jit(solution)/shard_map/jit(_where)/select_n | solution.py:136
  103.5 1.6 %fusion.28 = (bf16[4,4,160,384]{3,2,1,0:T(8,128)(2,1)S(1)}, bf16[4,4,160,384]{3,2,1,0:T(8,128)(2,1)S(1)}) fusion(s32[]{:T(128)S(6)} %select_n.99, bf16[4,4,160,384]{3,2,1,0:T(8,128)(2,1)S(1)} %fusion.26, bf16[4,4,160,384]{3,2,1,0:T(8,128)(2,1)S(1)} %fusion.25, s32[]{:T(128)S(6)} %select_n.101), kind=kLoop, calls=%fused_computation.43 | loop fusion | flops 1966080 | bytes 7864328 | tf_op jit(solution)/shard_map/concatenate | solution.py:142
  105.1 0.0 slice-start.2
  105.1 5.8 %fusion.8 = bf16[6,10,168,384]{3,2,1,0:T(8,128)(2,1)S(1)} fusion(bf16[4,4,160,384]{3,2,1,0:T(8,128)(2,1)S(1)} %get-tuple-element.4, bf16[4,4,160,384]{3,2,1,0:T(8,128)(2,1)S(1)} %get-tuple-element.3), kind=kLoop, calls=%fused_computation.13 | loop fusion | flops 73543680 | bytes 11673600 | tf_op jit(solution)/shard_map/concatenate | solution.py:143
  111.0 0.0 slice-start.3
  111.0 0.2 dynamic-slice_bitcast_fusion
  111.2 0.6 copy.48
  111.7 0.6 pad.30.clone
  112.3 0.2 copy.25
  112.6 0.4 slice-done.3
  113.0 3.8 %fusion.58 = f32[1,2,8,21,384]{4,2,3,1,0:T(8,128)S(1)} fusion(bf16[3,3,3,384,384]{4,3,2,1,0:T(8,128)(2,1)S(1)} %bitcast.110, bf16[3,4,1,7,2,384]{5,3,4,1,0,2:T(8,128)(2,1)S(1)} %slice.38, bf16[3,4,1,8,21,384]{5,3,4,1,0,2:T(8,128)(2,1)S(1)} %copy.25, pred[8,21]{0,1:T(8,128)(4,1)S(1)} %copy-done.8), kind=kOutput, calls=%fused_computation.76 | convolution fusion | flops 2680657920 | bytes 10156200 | tf_op jit(solution)/shard_map/conv_general_dilated | solution.py:44
  116.9 0.3 copy.26
  117.2 0.2 slice.39
  117.3 1.8 %fusion.46 = f32[3,12,8,384]{3,2,1,0:T(8,128)S(1)} fusion(bf16[6,10,168,384]{3,2,1,0:T(8,128)(2,1)S(1)} %fusion.8, s32[]{:T(128)S(6)} %select_n.106, s32[]{:T(128)S(6)} %select_n.108, bf16[4,8,168,1,96]{4,2,1,3,0:T(8,128)(2,1)S(1)} %get-tuple-element.10, bf16[4,8,168,1,96]{4,2,1,3,0:T(8,128)(2,1)S(1)} %get-tuple-element.11, ...), kind=kOutput, calls=%fused_computation.72 | convolution fusion | flops 1192181760 | bytes 8699912 | tf_op jit(solution)/shard_map/dot_general | solution.py:106
  119.2 1.8 %fusion.49 = f32[3,12,8,384]{3,2,1,0:T(8,128)S(1)} fusion(bf16[6,10,168,384]{3,2,1,0:T(8,128)(2,1)S(1)} %fusion.8, s32[]{:T(128)S(6)} %select_n.110, s32[]{:T(128)S(6)} %select_n.112, bf16[4,8,168,1,96]{4,2,1,3,0:T(8,128)(2,1)S(1)} %get-tuple-element.10, bf16[4,8,168,1,96]{4,2,1,3,0:T(8,128)(2,1)S(1)} %get-tuple-element.11, ...), kind=kOutput, calls=%fused_computation.73 | convolution fusion | flops 1192181760 | bytes 8699912 | tf_op jit(solution)/shard_map/dot_general | solution.py:106
  121.1 0.0 copy-start.1
  121.1 0.0 copy-start.3
  121.1 0.0 copy-start.5
  121.1 0.0 copy-start.7
  121.2 1.8 %fusion.52 = f32[3,12,8,384]{3,2,1,0:T(8,128)S(1)} fusion(bf16[6,10,168,384]{3,2,1,0:T(8,128)(2,1)S(1)} %fusion.8, s32[]{:T(128)S(6)} %select_n.114, s32[]{:T(128)S(6)} %select_n.116, bf16[4,8,168,1,96]{4,2,1,3,0:T(8,128)(2,1)S(1)} %get-tuple-element.10, bf16[4,8,168,1,96]{4,2,1,3,0:T(8,128)(2,1)S(1)} %get-tuple-element.11, ...), kind=kOutput, calls=%fused_computation.74 | convolution fusion | flops 1192181760 | bytes 8699912 | tf_op jit(solution)/shard_map/dot_general | solution.py:106
  123.1 1.2 add_convert_fusion
  124.2 1.6 %fusion.63 = f32[2592,96]{0,1:T(8,128)} fusion(s32[]{:T(128)S(6)} %select_n.117, f32[1152,96]{0,1:T(8,128)S(1)} %bitcast.102, f32[1152,96]{0,1:T(8,128)S(1)} %bitcast.103, f32[1152,96]{0,1:T(8,128)S(1)} %bitcast.104), kind=kLoop, calls=%fused_computation.79 | loop fusion | flops 746496 | bytes 2322436 | tf_op jit(solution)/shard_map/mul | solution.py:204
  (35 shorter events, 0.5 us)
Async XLA Ops:
  0.6 45.9 %copy-start.4 = (bf16[1,2,160,384]{3,2,1,0:T(8,128)(2,1)S(1)}, bf16[1,2,160,384]{3,2,1,0:T(8,128)(2,1)}, u32[]{:S(2)}) copy-start(bf16[1,2,160,384]{3,2,1,0:T(8,128)(2,1)} %param.9) | copy-start | bytes 737284
  4.0 15.4 %collective-permute-start = (bf16[1,2,160,768]{3,2,1,0:T(8,128)(2,1)S(1)}, bf16[1,2,160,768]{3,2,1,0:T(8,128)(2,1)S(1)}, u32[]{:S(2)}, u32[]{:S(2)}) collective-permute-start(bf16[1,2,160,768]{3,2,1,0:T(8,128)(2,1)S(1)} %pad_maximum_fusion.4), channel_id=1, source_target_pairs={{0,4},{4,8},{8,12},{1,5},{5,9},{9,13},{2,6},{6,10},{10,14},{3,7},{... | collective-permute-start | bytes 1474568 | tf_op jit(solution)/shard_map/ppermute | solution.py:160
  9.0 14.8 %collective-permute-start.3 = (bf16[1,2,160,768]{3,2,1,0:T(8,128)(2,1)S(1)}, bf16[1,2,160,768]{3,2,1,0:T(8,128)(2,1)S(1)}, u32[]{:S(2)}, u32[]{:S(2)}) collective-permute-start(bf16[1,2,160,768]{3,2,1,0:T(8,128)(2,1)S(1)} %pad_maximum_fusion.4), channel_id=1, source_target_pairs={{4,0},{8,4},{12,8},{5,1},{9,5},{13,9},{6,2},{10,6},{14,10},{7,3},{... | collective-permute-start | bytes 1474568 | tf_op jit(solution)/shard_map/ppermute | solution.py:161
  19.4 14.0 %collective-permute-start.1 = (bf16[1,2,160,768]{3,2,1,0:T(8,128)(2,1)S(1)}, bf16[1,2,160,768]{3,2,1,0:T(8,128)(2,1)S(1)}, u32[]{:S(2)}, u32[]{:S(2)}) collective-permute-start(bf16[1,2,160,768]{3,2,1,0:T(8,128)(2,1)S(1)} %collective-permute-done), channel_id=1, source_target_pairs={{0,4},{4,8},{8,12},{1,5},{5,9},{9,13},{2,6},{6,10},{10,14},{3,7},{... | collective-permute-start | bytes 1474568 | tf_op jit(solution)/shard_map/ppermute | solution.py:160
  23.8 14.0 %collective-permute-start.4 = (bf16[1,2,160,768]{3,2,1,0:T(8,128)(2,1)S(1)}, bf16[1,2,160,768]{3,2,1,0:T(8,128)(2,1)S(1)}, u32[]{:S(2)}, u32[]{:S(2)}) collective-permute-start(bf16[1,2,160,768]{3,2,1,0:T(8,128)(2,1)S(1)} %collective-permute-done.3), channel_id=1, source_target_pairs={{4,0},{8,4},{12,8},{5,1},{9,5},{13,9},{6,2},{10,6},{14,10},{7,3},{... | collective-permute-start | bytes 1474568 | tf_op jit(solution)/shard_map/ppermute | solution.py:161
  33.4 13.1 %collective-permute-start.2 = (bf16[1,2,160,768]{3,2,1,0:T(8,128)(2,1)S(1)}, bf16[1,2,160,768]{3,2,1,0:T(8,128)(2,1)S(1)}, u32[]{:S(2)}, u32[]{:S(2)}) collective-permute-start(bf16[1,2,160,768]{3,2,1,0:T(8,128)(2,1)S(1)} %collective-permute-done.1), channel_id=1, source_target_pairs={{0,4},{4,8},{8,12},{1,5},{5,9},{9,13},{2,6},{6,10},{10,14},{3,7},{... | collective-permute-start | bytes 1474568 | tf_op jit(solution)/shard_map/ppermute | solution.py:160
  37.8 12.8 %collective-permute-start.5 = (bf16[1,2,160,768]{3,2,1,0:T(8,128)(2,1)S(1)}, bf16[1,2,160,768]{3,2,1,0:T(8,128)(2,1)S(1)}, u32[]{:S(2)}, u32[]{:S(2)}) collective-permute-start(bf16[1,2,160,768]{3,2,1,0:T(8,128)(2,1)S(1)} %collective-permute-done.4), channel_id=1, source_target_pairs={{4,0},{8,4},{12,8},{5,1},{9,5},{13,9},{6,2},{10,6},{14,10},{7,3},{... | collective-permute-start | bytes 1474568 | tf_op jit(solution)/shard_map/ppermute | solution.py:161
  50.9 23.8 %collective-permute-start.6 = (bf16[4,2,160,384]{3,2,1,0:T(8,128)(2,1)S(1)}, bf16[4,2,160,384]{3,2,1,0:T(8,128)(2,1)}, u32[]{:S(2)}, u32[]{:S(2)}) collective-permute-start(bf16[4,2,160,384]{3,2,1,0:T(8,128)(2,1)S(1)} %get-tuple-element.6), channel_id=1, source_target_pairs={{0,2},{1,3},{2,0},{3,1},{4,6},{5,7},{6,4},{7,5},{8,10},{9,11},{10,... | collective-permute-start | bytes 2949128 | tf_op jit(solution)/shard_map/ppermute | solution.py:123
  53.4 24.2 %collective-permute-start.9 = (bf16[3,1,160,384]{3,2,1,0:T(8,128)(2,1)}, bf16[3,1,160,384]{3,2,1,0:T(8,128)(2,1)}, u32[]{:S(2)}, u32[]{:S(2)}) collective-permute-start(bf16[3,1,160,384]{3,2,1,0:T(8,128)(2,1)} %get-tuple-element.13), channel_id=1, source_target_pairs={{1,0},{2,1},{3,2},{5,4},{6,5},{7,6},{9,8},{10,9},{11,10},{13,12},{... | collective-permute-start | bytes 1105928 | tf_op jit(solution)/shard_map/ppermute | solution.py:25
  54.7 22.9 %collective-permute-start.8 = (bf16[3,1,160,384]{3,2,1,0:T(8,128)(2,1)}, bf16[3,1,160,384]{3,2,1,0:T(8,128)(2,1)}, u32[]{:S(2)}, u32[]{:S(2)}) collective-permute-start(bf16[3,1,160,384]{3,2,1,0:T(8,128)(2,1)} %get-tuple-element.12), channel_id=1, source_target_pairs={{0,1},{1,2},{2,3},{4,5},{5,6},{6,7},{8,9},{9,10},{10,11},{12,13},{... | collective-permute-start | bytes 1105928 | tf_op jit(solution)/shard_map/ppermute | solution.py:23
  61.5 30.7 %all-to-all-start = ((bf16[4,2,160,384]{2,1,0,3:T(2,128)(2,1)}), bf16[4,2,160,384]{2,1,0,3:T(2,128)(2,1)S(1)}, u32[]{:S(2)}, u32[]{:S(2)}) async-start(bf16[4,2,160,384]{2,1,0,3:T(2,128)(2,1)} %copy.33), calls=%async_computation | async-start | bytes 3145728 | tf_op jit(solution)/shard_map/all_to_all | solution.py:192
  74.6 6.0 %slice-start = ((s8[7962624]{0:T(1024)(128)(4,1)}), s8[4194304]{0:T(1024)(128)(4,1)S(1)}, s32[]{:S(2)}) async-start(s8[7962624]{0:T(1024)(128)(4,1)} %bitcast.105), calls=%async_computation.1 | async-start | bytes 8388608
  77.5 22.0 %collective-permute-start.7 = (bf16[4,4,160,384]{3,2,1,0:T(8,128)(2,1)}, bf16[4,4,160,384]{3,2,1,0:T(8,128)(2,1)}, u32[]{:S(2)}, u32[]{:S(2)}) collective-permute-start(bf16[4,4,160,384]{3,2,1,0:T(8,128)(2,1)} %pad_maximum_fusion.2), channel_id=1, source_target_pairs={{0,1},{1,0},{2,3},{3,2},{4,5},{5,4},{6,7},{7,6},{8,9},{9,8},{10,11... | collective-permute-start | bytes 5898248 | tf_op jit(solution)/shard_map/ppermute | solution.py:129
  79.2 2.1 %slice-start.1 = ((s8[7962624]{0:T(1024)(128)(4,1)}), s8[3768320]{0:T(1024)(128)(4,1)S(1)}, s32[]{:S(2)}) async-start(s8[7962624]{0:T(1024)(128)(4,1)} %bitcast.105), calls=%async_computation.2 | async-start | bytes 7536640
  79.8 1.5 %copy-start.8 = (pred[8,21]{0,1:T(8,128)(4,1)S(1)}, pred[8,21]{0,1:T(8,128)(4,1)}, u32[]{:S(2)}) copy-start(pred[8,21]{0,1:T(8,128)(4,1)} %constant.123) | copy-start | bytes 508
  81.3 4.2 %copy-start.2 = (bf16[1,2,160,384]{3,2,1,0:T(8,128)(2,1)S(1)}, bf16[1,2,160,384]{3,2,1,0:T(8,128)(2,1)}, u32[]{:S(2)}) copy-start(bf16[1,2,160,384]{3,2,1,0:T(8,128)(2,1)} %param.5) | copy-start | bytes 737284
  81.3 4.2 %copy-start.6 = (f32[384]{0:T(512)S(1)}, f32[384]{0:T(512)}, u32[]{:S(2)}) copy-start(f32[384]{0:T(512)} %param.6) | copy-start | bytes 4612
  85.5 14.0 %copy-start = (f32[1,2,1,160,384]{4,1,3,2,0:T(2,128)}, f32[1,2,1,160,384]{4,1,3,2,0:T(2,128)S(1)}, u32[]{:S(2)}) copy-start(f32[1,2,1,160,384]{4,1,3,2,0:T(2,128)S(1)} %slice.41) | copy-start | bytes 1474564
  105.1 7.5 %slice-start.2 = ((s8[7962624]{0:T(1024)(128)(4,1)}), s8[4194304]{0:T(1024)(128)(4,1)S(1)}, s32[]{:S(2)}) async-start(s8[7962624]{0:T(1024)(128)(4,1)} %bitcast.108), calls=%async_computation.3 | async-start | bytes 8388608
  111.0 2.1 %slice-start.3 = ((s8[7962624]{0:T(1024)(128)(4,1)}), s8[3768320]{0:T(1024)(128)(4,1)S(1)}, s32[]{:S(2)}) async-start(s8[7962624]{0:T(1024)(128)(4,1)} %bitcast.108), calls=%async_computation.4 | async-start | bytes 7536640
  121.1 1.9 %copy-start.1 = (f32[1,2,1,160,384]{4,1,3,2,0:T(2,128)S(1)}, f32[1,2,1,160,384]{4,1,3,2,0:T(2,128)}, u32[]{:S(2)}) copy-start(f32[1,2,1,160,384]{4,1,3,2,0:T(2,128)} %copy-done) | copy-start | bytes 1474564
  121.1 1.9 %copy-start.3 = (bf16[1,2,160,384]{3,2,1,0:T(8,128)(2,1)S(1)}, bf16[1,2,160,384]{3,2,1,0:T(8,128)(2,1)}, u32[]{:S(2)}) copy-start(bf16[1,2,160,384]{3,2,1,0:T(8,128)(2,1)} %param.5) | copy-start | bytes 737284
  121.1 1.9 %copy-start.5 = (bf16[1,2,160,384]{3,2,1,0:T(8,128)(2,1)S(1)}, bf16[1,2,160,384]{3,2,1,0:T(8,128)(2,1)}, u32[]{:S(2)}) copy-start(bf16[1,2,160,384]{3,2,1,0:T(8,128)(2,1)} %param.9) | copy-start | bytes 737284
  121.1 1.9 %copy-start.7 = (f32[384]{0:T(512)S(1)}, f32[384]{0:T(512)}, u32[]{:S(2)}) copy-start(f32[384]{0:T(512)} %param.7) | copy-start | bytes 4612

commit v10 on v9

--- a/solution.py
+++ b/solution.py
@@ -151,18 +151,44 @@
 
 def gather_frames(block):
     count = lax.axis_size("tm")
-    position = lax.axis_index("tm")
     up = [(i, i + 1) for i in range(count - 1)]
     down = [(i + 1, i) for i in range(count - 1)]
-    earlier, later = [], []
+    groups = [block]
     rising, falling = block, block
     for step in range(1, count):
         rising = lax.ppermute(rising, "tm", up)
         falling = lax.ppermute(falling, "tm", down)
-        earlier.append(rising)
-        later.append(falling)
-    relative = jnp.concatenate(earlier[::-1] + [block] + later, axis=0)
-    return lax.dynamic_slice_in_dim(relative, count - 1 - position, count * block.shape[0], 0)
+        groups.append(jnp.concatenate([rising, falling], axis=0))
+    return groups
+
+
+def in_order(groups):
+    count = len(groups)
+    position = lax.axis_index("tm")
+    size = groups[0].shape[0]
+    relative = jnp.concatenate(
+        [groups[step][:size] for step in reversed(range(1, count))]
+        + [groups[0]]
+        + [groups[step][size:] for step in range(1, count)],
+        axis=0,
+    )
+    return lax.dynamic_slice_in_dim(relative, (count - 1 - position) * size, count * size, 0)
+
+
+def place_frames(groups, offsets, frame_total, padded_cols):
+    position = lax.axis_index("tm")
+    _, row_total, _, channels = groups[0].shape
+    framed = jnp.zeros(
+        (frame_total + 2, row_total + 2, padded_cols, channels), groups[0].dtype
+    )
+    writes = [
+        (abs(offset), group[index : index + 1], offset)
+        for group, shifts in zip(groups, offsets)
+        for index, offset in enumerate(shifts)
+    ]
+    for _, piece, offset in sorted(writes, key=lambda item: -item[0]):
+        framed = lax.dynamic_update_slice(framed, piece, (2 + position + offset, 1, 1, 0))
+    return framed
 
 
 def local(latents, gain, bias, weight, cotangent):
@@ -184,9 +210,18 @@
     inverse_root = 1.0 / math.sqrt(total_frames * total_rows * col_count)
     weight_cube = weight.reshape(3, 3, 3, channels, channels)
 
-    both_frames = gather_frames(jnp.concatenate([hidden, cotangent], axis=-1))
-    hidden_all = gather_rows(both_frames[..., :channels], height_count)
-    framed = jnp.pad(hidden_all, ((2, 0), (1, 1), (1, right_pad), (0, 0)))
+    groups = gather_frames(jnp.concatenate([hidden, cotangent], axis=-1))
+    both_frames = in_order(groups)
+    if len(groups) <= 4:
+        framed = place_frames(
+            [gather_rows(group[..., :channels], height_count) for group in groups],
+            [[0]] + [[-step, step] for step in range(1, len(groups))],
+            total_frames,
+            padded_cols,
+        )
+    else:
+        hidden_all = gather_rows(both_frames[..., :channels], height_count)
+        framed = jnp.pad(hidden_all, ((2, 0), (1, 1), (1, right_pad), (0, 0)))
 
     cot_frames = both_frames[..., channels:]
     cot_all = lax.all_to_all(cot_frames, "height", split_axis=3, concat_axis=1, tiled=True)

time: 126 us -> 188 us (1.49); the launches traced: 126 us -> 185 us
  local copies, waits for them, and re-layouts: 18.6 us -> 66.7 us
  other arithmetic: 20.7 us -> 29.1 us
  matrix products: 13.1 us -> 19.8 us
  waiting for transfers between devices: 44.2 us -> 38.5 us
  starting transfers between devices: 28 us -> 30.1 us
    dynamic_update_slice x0 -> x7, local copies, waits for them, and re-layouts: none -> 42.9 us  [place_frames(): lax.dynamic_update_slice(framed, piece, (2 + position + offset, 1, 1, 0))]
    ppermute x3, waiting for transfers between devices: 3.9 us -> 15.6 us  [gather_frames(): falling = lax.ppermute(falling, 'tm', down)]
    ppermute x1 -> x4, waiting for transfers between devices: 9.36 us -> 0.16 us  [gather_rows(): lax.ppermute(own, 'height', [(i, (i + 2 * step) % height_count) for i in...]
    ppermute x3, waiting for transfers between devices: 24.7 us -> 17.1 us  [gather_frames(): rising = lax.ppermute(rising, 'tm', up)]
    select_n x2 -> x8, other arithmetic: 2.19 us -> 6.74 us  [gather_rows(): jnp.where(first, jnp.concatenate([ours, theirs], axis=1), jnp.concatenate...]
    ppermute x1 -> x4, starting transfers between devices: 1.56 us -> 5.71 us  [gather_rows(): lax.ppermute(own, 'height', [(i, (i + 2 * step) % height_count) for i in...]
    broadcast_in_dim x0 -> x1, local copies, waits for them, and re-layouts: none -> 3.69 us  [place_frames(): jnp.zeros((frame_total + 2, row_total + 2, padded_cols, channels), groups...]
    concatenate x1 -> x4, other arithmetic: 2.86 us -> 6.32 us  [gather_rows(): stacked = jnp.concatenate(mine, axis=1)]
  transfers between devices with their start and end apart: 11 -> 17, of which waited for: 6 -> 7; matrix products, arithmetic and copies ran while one was open for 18% -> 21% of each run, Pallas kernels for 0% -> 0%
where the time goes in v10:
time: 188 us; the launch traced here: 185 us
  local copies, waits for them, and re-layouts  66.7 us (35%)
  waiting for transfers between devices  38.5 us (20%)
  starting transfers between devices  30.1 us (16%)
  other arithmetic  29.1 us (15%)
  matrix products  19.8 us (11%)
    dynamic_update_slice x7, local copies, waits for them, and re-layouts, place_frames(): lax.dynamic_update_slice(framed, piece, (2 + position + offset, 1, 1, 0))  42.9 us
    ppermute x3, waiting for transfers between devices, gather_frames(): rising = lax.ppermute(rising, 'tm', up)  17.1 us
    ppermute x3, waiting for transfers between devices, gather_frames(): falling = lax.ppermute(falling, 'tm', down)  15.6 us
    ppermute x3, starting transfers between devices, gather_frames(): rising = lax.ppermute(rising, 'tm', up)  11.4 us
    conv_general_dilated x1, matrix products, forward_conv(): lax.conv_general_dilated(window[None], cube, (1, 1, 1), 'VALID', dimensio...  7.23 us
    conv_general_dilated x1, matrix products, backward_conv(): lax.conv_general_dilated(window[None], jnp.flip(cube, (0, 1, 2)), (1, 1,...  7.08 us
    select_n x8, other arithmetic, gather_rows(): jnp.where(first, jnp.concatenate([ours, theirs], axis=1), jnp.concatenate...  6.74 us
    concatenate x4, other arithmetic, gather_rows(): stacked = jnp.concatenate(mine, axis=1)  6.32 us
  transfers between devices with their start and end apart: 17, of which 7 were waited for; matrix products, arithmetic and copies ran while one was open for 21% of the time, Pallas kernels for 0%

profile of v10, /device:TPU:0, one launch (start us, length us, event | category | flops | bytes accessed | tf_op | source)
XLA Modules:
  0.0 185.5 jit_solution(4150714548460968267)
XLA Ops:
  0.6 1.1 fusion.68
  1.7 1.2 multiply_convert_fusion
  3.0 3.0 %collective-permute-start.12 = (bf16[1,2,160,384]{3,2,1,0:T(8,128)(2,1)S(1)}, bf16[1,2,160,384]{3,2,1,0:T(8,128)(2,1)S(1)}, u32[]{:S(2)}, u32[]{:S(2)}) collective-permute-start(bf16[1,2,160,384]{3,2,1,0:T(8,128)(2,1)S(1)} %multiply_convert_fusion), channel_id=1, source_target_pairs={{0,2},{1,3},{2,0},{3,1},{4,6},{5,7},{6,4},{7,5},{8,10},{9,11},{10,... | collective-permute-start | bytes 737288 | tf_op jit(solution)/shard_map/ppermute | solution.py:123
  6.0 1.0 pad_maximum_fusion.20
  6.9 3.5 %collective-permute-start = (bf16[1,2,160,768]{3,2,1,0:T(8,128)(2,1)S(1)}, bf16[1,2,160,768]{3,2,1,0:T(8,128)(2,1)S(1)}, u32[]{:S(2)}, u32[]{:S(2)}) collective-permute-start(bf16[1,2,160,768]{3,2,1,0:T(8,128)(2,1)S(1)} %pad_maximum_fusion.20), channel_id=1, source_target_pairs={{0,4},{4,8},{8,12},{1,5},{5,9},{9,13},{2,6},{6,10},{10,14},{3,7},{... | collective-permute-start | bytes 1474568 | tf_op jit(solution)/shard_map/ppermute | solution.py:159
  10.5 1.3 collective-permute-start.3
  11.9 0.8 pad_maximum_fusion.15
  12.8 7.9 %collective-permute-done = bf16[1,2,160,768]{3,2,1,0:T(8,128)(2,1)S(1)} collective-permute-done((bf16[1,2,160,768]{3,2,1,0:T(8,128)(2,1)S(1)}, bf16[1,2,160,768]{3,2,1,0:T(8,128)(2,1)S(1)}, u32[]{:S(2)}, u32[]{:S(2)}) %collective-permute-start) | collective-permute-done | bytes 491552 | tf_op jit(solution)/shard_map/ppermute | solution.py:159
  20.6 4.1 %collective-permute-done.3 = bf16[1,2,160,768]{3,2,1,0:T(8,128)(2,1)S(1)} collective-permute-done((bf16[1,2,160,768]{3,2,1,0:T(8,128)(2,1)S(1)}, bf16[1,2,160,768]{3,2,1,0:T(8,128)(2,1)S(1)}, u32[]{:S(2)}, u32[]{:S(2)}) %collective-permute-start.3) | collective-permute-done | bytes 491552 | tf_op jit(solution)/shard_map/ppermute | solution.py:160
  24.8 0.6 collective-permute-start.10
  25.4 3.5 %collective-permute-start.1 = (bf16[1,2,160,768]{3,2,1,0:T(8,128)(2,1)S(1)}, bf16[1,2,160,768]{3,2,1,0:T(8,128)(2,1)S(1)}, u32[]{:S(2)}, u32[]{:S(2)}) collective-permute-start(bf16[1,2,160,768]{3,2,1,0:T(8,128)(2,1)S(1)} %collective-permute-done), channel_id=1, source_target_pairs={{0,4},{4,8},{8,12},{1,5},{5,9},{9,13},{2,6},{6,10},{10,14},{3,7},{... | collective-permute-start | bytes 1474568 | tf_op jit(solution)/shard_map/ppermute | solution.py:159
  28.9 1.3 collective-permute-start.4
  30.5 7.1 %collective-permute-done.1 = bf16[1,2,160,768]{3,2,1,0:T(8,128)(2,1)S(1)} collective-permute-done((bf16[1,2,160,768]{3,2,1,0:T(8,128)(2,1)S(1)}, bf16[1,2,160,768]{3,2,1,0:T(8,128)(2,1)S(1)}, u32[]{:S(2)}, u32[]{:S(2)}) %collective-permute-start.1) | collective-permute-done | bytes 491552 | tf_op jit(solution)/shard_map/ppermute | solution.py:159
  37.6 4.4 %collective-permute-start.2 = (bf16[1,2,160,768]{3,2,1,0:T(8,128)(2,1)S(1)}, bf16[1,2,160,768]{3,2,1,0:T(8,128)(2,1)S(1)}, u32[]{:S(2)}, u32[]{:S(2)}) collective-permute-start(bf16[1,2,160,768]{3,2,1,0:T(8,128)(2,1)S(1)} %collective-permute-done.1), channel_id=1, source_target_pairs={{0,4},{4,8},{8,12},{1,5},{5,9},{9,13},{2,6},{6,10},{10,14},{3,7},{... | collective-permute-start | bytes 1474568 | tf_op jit(solution)/shard_map/ppermute | solution.py:159
  42.4 1.1 pad_maximum_fusion.13
  43.5 1.1 pad_maximum_fusion.8
  44.7 1.6 collective-permute-start.8
  46.2 1.3 collective-permute-start.5
  47.5 2.2 %collective-permute-done.2 = bf16[1,2,160,768]{3,2,1,0:T(8,128)(2,1)S(1)} collective-permute-done((bf16[1,2,160,768]{3,2,1,0:T(8,128)(2,1)S(1)}, bf16[1,2,160,768]{3,2,1,0:T(8,128)(2,1)S(1)}, u32[]{:S(2)}, u32[]{:S(2)}) %collective-permute-start.2) | collective-permute-done | bytes 491552 | tf_op jit(solution)/shard_map/ppermute | solution.py:159
  50.0 11.5 %collective-permute-done.5 = bf16[1,2,160,768]{3,2,1,0:T(8,128)(2,1)S(1)} collective-permute-done((bf16[1,2,160,768]{3,2,1,0:T(8,128)(2,1)S(1)}, bf16[1,2,160,768]{3,2,1,0:T(8,128)(2,1)S(1)}, u32[]{:S(2)}, u32[]{:S(2)}) %collective-permute-start.5) | collective-permute-done | bytes 491552 | tf_op jit(solution)/shard_map/ppermute | solution.py:160
  61.5 0.8 copy-done.11
  62.4 3.0 %copy.33 = bf16[4,2,160,384]{2,1,0,3:T(2,128)(2,1)} copy(bf16[4,2,160,384]{3,2,1,0:T(8,128)(2,1)S(1)} %constant_dynamic-slice_fusion) | data formatting | bytes 1966080 | tf_op jit(solution)/shard_map/slice | solution.py:226
  65.5 1.0 pad_dynamic-slice_fusion.13
  66.5 1.3 collective-permute-start.15
  67.7 3.8 %collective-permute-start.14 = (bf16[3,1,160,384]{3,2,1,0:T(8,128)(2,1)}, bf16[3,1,160,384]{3,2,1,0:T(8,128)(2,1)}, u32[]{:S(2)}, u32[]{:S(2)}) collective-permute-start(bf16[3,1,160,384]{3,2,1,0:T(8,128)(2,1)} %get-tuple-element.18), channel_id=1, source_target_pairs={{0,1},{1,2},{2,3},{4,5},{5,6},{6,7},{8,9},{9,10},{10,11},{12,13},{... | collective-permute-start | bytes 1105928 | tf_op jit(solution)/shard_map/ppermute | solution.py:23
  71.5 0.8 pad_maximum_fusion.19
  72.9 2.1 %pad_maximum_fusion.5 = bf16[2,4,160,384]{3,2,1,0:T(8,128)(2,1)} fusion(bf16[2,2,160,384]{3,2,1,0:T(8,128)(2,1)} %collective-permute-done.8, bf16[2,2,160,384]{3,2,1,0:T(8,128)(2,1)S(1)} %pad_maximum_fusion.18), kind=kLoop, calls=%fused_computation.72 | loop fusion | flops 491520 | bytes 1966080 | tf_op jit(solution)/shard_map/concatenate | solution.py:128
  75.1 3.6 %all-to-all-start = ((bf16[4,2,160,384]{2,1,0,3:T(2,128)(2,1)}), bf16[4,2,160,384]{2,1,0,3:T(2,128)(2,1)S(1)}, u32[]{:S(2)}, u32[]{:S(2)}) async-start(bf16[4,2,160,384]{2,1,0,3:T(2,128)(2,1)} %copy.33), calls=%async_computation | async-start | bytes 3145728 | tf_op jit(solution)/shard_map/all_to_all | solution.py:227
  78.8 1.6 fusion.29
  81.0 0.6 pad.27.clone
  81.8 7.1 %fusion.40 = f32[1,2,8,21,384]{4,2,3,1,0:T(8,128)S(1)} fusion(bf16[3,3,3,384,384]{4,3,2,1,0:T(8,128)(2,1)} %bitcast.107, bf16[3,4,1,7,2,384]{5,3,4,1,0,2:T(8,128)(2,1)S(1)} %slice.108, bf16[3,4,1,8,21,384]{5,3,4,1,0,2:T(8,128)(2,1)S(1)} %copy.30, pred[8,21]{0,1:T(8,128)(4,1)S(1)} %copy-done.20), kind=kOutput, calls=%fused_computation.66 | convolution fusion | flops 2680657920 | bytes 10156200 | tf_op jit(solution)/shard_map/conv_general_dilated | solution.py:57
  89.4 0.8 copy-done
  90.6 2.3 %pad_maximum_fusion.2 = bf16[2,4,160,384]{3,2,1,0:T(8,128)(2,1)} fusion(bf16[2,2,160,384]{3,2,1,0:T(8,128)(2,1)} %collective-permute-done.6, bf16[2,2,160,384]{3,2,1,0:T(8,128)(2,1)} %pad_maximum_fusion.19), kind=kLoop, calls=%fused_computation.69 | loop fusion | flops 491520 | bytes 1966080 | tf_op jit(solution)/shard_map/concatenate | solution.py:128
  93.4 1.3 fusion.85
  94.7 1.1 fusion.49
  95.8 1.1 fusion.50
  96.9 5.6 %all-to-all-done = bf16[4,2,160,384]{2,1,0,3:T(2,128)(2,1)S(1)} async-done(((bf16[4,2,160,384]{2,1,0,3:T(2,128)(2,1)}), bf16[4,2,160,384]{2,1,0,3:T(2,128)(2,1)S(1)}, u32[]{:S(2)}, u32[]{:S(2)}) %all-to-all-start) | async-done | bytes 983072 | tf_op jit(solution)/shard_map/all_to_all | solution.py:227
  102.5 2.1 %copy.34 = bf16[4,2,160,4,96]{4,2,1,3,0:T(8,128)(2,1)S(1)} copy(bf16[4,2,160,4,96]{2,1,0,4,3:T(2,128)(2,1)S(1)} %bitcast.98) | data formatting | bytes 1966080 | tf_op jit(solution)/shard_map/all_to_all | solution.py:227
  104.7 2.5 %pad_bitcast_fusion.2 = (bf16[4,8,168,1,96]{4,2,1,3,0:T(8,128)(2,1)}, bf16[4,8,168,1,96]{4,2,1,3,0:T(8,128)(2,1)}, bf16[4,8,168,1,96]{4,2,1,3,0:T(8,128)(2,1)}) fusion(bf16[4,8,160,96]{3,2,1,0:T(8,128)(2,1)S(1)} %bitcast.101), kind=kLoop, calls=%fused_computation.59 | loop fusion | bytes 4079616 | tf_op jit(solution)/shard_map/stack | solution.py:83
  107.1 1.4 fusion.86
  108.8 1.4 fusion.52
  110.2 1.7 fusion.58
  112.1 1.2 pad_maximum_fusion.10
  113.3 1.3 fusion.87
  114.5 1.4 fusion.53
  115.9 1.4 fusion.54
  117.3 0.8 fusion.62
  118.1 1.5 pad_maximum_fusion.12
  119.6 3.7 %broadcast_in_dim.6 = bf16[6,10,168,384]{3,2,1,0:T(8,128)(2,1)} broadcast(bf16[]{:T(256)} %constant.121.clone.1), dimensions={} | broadcast | bytes 7741442 | tf_op jit(solution)/shard_map/broadcast_in_dim | solution.py:181
  123.3 6.4 %dynamic_update_slice.21 = bf16[6,10,168,384]{3,2,1,0:T(8,128)(2,1)} dynamic-update-slice(bf16[6,10,168,384]{3,2,1,0:T(8,128)(2,1)} %broadcast_in_dim.6, bf16[1,8,160,384]{3,2,1,0:T(8,128)(2,1)} %get-tuple-element.12, s32[]{:T(128)S(6)} %select_n.191, s32[]{:T(128)} %constant.124.clone.1, s32[]{:T(128)} %constant.124.clone.1, s32[]{:T(128)} %constant.123.clone.1) | dynamic-update-slice | bytes 1966084 | tf_op jit(solution)/shard_map/dynamic_update_slice | solution.py:190
  129.6 6.4 %dynamic_update_slice.22 = bf16[6,10,168,384]{3,2,1,0:T(8,128)(2,1)} dynamic-update-slice(bf16[6,10,168,384]{3,2,1,0:T(8,128)(2,1)} %dynamic_update_slice.21, bf16[1,8,160,384]{3,2,1,0:T(8,128)(2,1)} %get-tuple-element.11, s32[]{:T(128)S(6)} %select_n.192, s32[]{:T(128)} %constant.124.clone.1, s32[]{:T(128)} %constant.124.clone.1, s32[]{:T(128)} %constant.123.clone.1) | dynamic-update-slice | bytes 1966084 | tf_op jit(solution)/shard_map/dynamic_update_slice | solution.py:190
  136.0 5.9 %dynamic_update_slice.23 = bf16[6,10,168,384]{3,2,1,0:T(8,128)(2,1)} dynamic-update-slice(bf16[6,10,168,384]{3,2,1,0:T(8,128)(2,1)} %dynamic_update_slice.22, bf16[1,8,160,384]{3,2,1,0:T(8,128)(2,1)S(1)} %get-tuple-element.8, s32[]{:T(128)S(6)} %select_n.195, s32[]{:T(128)} %constant.124.clone.1, s32[]{:T(128)} %constant.124.clone.1, s32[]{:T(128)} %constant.123.clone.1) | dynamic-update-slice | bytes 1966084 | tf_op jit(solution)/shard_map/dynamic_update_slice | solution.py:190
  141.9 6.0 %dynamic_update_slice.24 = bf16[6,10,168,384]{3,2,1,0:T(8,128)(2,1)} dynamic-update-slice(bf16[6,10,168,384]{3,2,1,0:T(8,128)(2,1)} %dynamic_update_slice.23, bf16[1,8,160,384]{3,2,1,0:T(8,128)(2,1)S(1)} %get-tuple-element.7, s32[]{:T(128)S(6)} %select_n.196, s32[]{:T(128)} %constant.124.clone.1, s32[]{:T(128)} %constant.124.clone.1, s32[]{:T(128)} %constant.123.clone.1) | dynamic-update-slice | bytes 1966084 | tf_op jit(solution)/shard_map/dynamic_update_slice | solution.py:190
  147.9 6.3 %dynamic_update_slice.25 = bf16[6,10,168,384]{3,2,1,0:T(8,128)(2,1)} dynamic-update-slice(bf16[6,10,168,384]{3,2,1,0:T(8,128)(2,1)} %dynamic_update_slice.24, bf16[1,8,160,384]{3,2,1,0:T(8,128)(2,1)} %get-tuple-element.4, s32[]{:T(128)S(6)} %select_n.199, s32[]{:T(128)} %constant.124.clone.1, s32[]{:T(128)} %constant.124.clone.1, s32[]{:T(128)} %constant.123.clone.1) | dynamic-update-slice | bytes 1966084 | tf_op jit(solution)/shard_map/dynamic_update_slice | solution.py:190
  154.3 6.0 %dynamic_update_slice.26 = bf16[6,10,168,384]{3,2,1,0:T(8,128)(2,1)} dynamic-update-slice(bf16[6,10,168,384]{3,2,1,0:T(8,128)(2,1)} %dynamic_update_slice.25, bf16[1,8,160,384]{3,2,1,0:T(8,128)(2,1)S(1)} %get-tuple-element.3, s32[]{:T(128)S(6)} %select_n.200, s32[]{:T(128)} %constant.124.clone.1, s32[]{:T(128)} %constant.124.clone.1, s32[]{:T(128)} %constant.123.clone.1) | dynamic-update-slice | bytes 1966084 | tf_op jit(solution)/shard_map/dynamic_update_slice | solution.py:190
  160.3 5.9 %dynamic_update_slice.27 = bf16[6,10,168,384]{3,2,1,0:T(8,128)(2,1)} dynamic-update-slice(bf16[6,10,168,384]{3,2,1,0:T(8,128)(2,1)} %dynamic_update_slice.26, bf16[1,8,160,384]{3,2,1,0:T(8,128)(2,1)S(1)} %copy-done.4, s32[]{:T(128)S(6)} %select_n.204, s32[]{:T(128)} %constant.124.clone.1, s32[]{:T(128)} %constant.124.clone.1, s32[]{:T(128)} %constant.123.clone.1) | dynamic-update-slice | bytes 1966084 | tf_op jit(solution)/shard_map/dynamic_update_slice | solution.py:190
  166.2 1.6 dynamic-slice_bitcast_fusion
  168.3 0.6 pad.25.clone
  169.2 7.2 %fusion.43 = f32[1,2,8,21,384]{4,2,3,1,0:T(8,128)S(1)} fusion(bf16[3,3,3,384,384]{4,3,2,1,0:T(8,128)(2,1)} %bitcast.108, bf16[3,4,1,7,2,384]{5,3,4,1,0,2:T(8,128)(2,1)S(1)} %slice.106, bf16[3,4,1,8,21,384]{5,3,4,1,0,2:T(8,128)(2,1)S(1)} %copy.25, pred[8,21]{0,1:T(8,128)(4,1)S(1)} %copy-done.20), kind=kOutput, calls=%fused_computation.67 | convolution fusion | flops 2680657920 | bytes 10156200 | tf_op jit(solution)/shard_map/conv_general_dilated | solution.py:44
  177.0 1.8 fusion.31
  178.8 1.8 fusion.34
  180.7 1.8 fusion.37
  182.6 1.2 add_convert_fusion
  183.8 1.6 fusion.48
  (94 shorter events, 6.0 us)
Async XLA Ops:
  3.0 9.0 %collective-permute-start.12 = (bf16[1,2,160,384]{3,2,1,0:T(8,128)(2,1)S(1)}, bf16[1,2,160,384]{3,2,1,0:T(8,128)(2,1)S(1)}, u32[]{:S(2)}, u32[]{:S(2)}) collective-permute-start(bf16[1,2,160,384]{3,2,1,0:T(8,128)(2,1)S(1)} %multiply_convert_fusion), channel_id=1, source_target_pairs={{0,2},{1,3},{2,0},{3,1},{4,6},{5,7},{6,4},{7,5},{8,10},{9,11},{10,... | collective-permute-start | bytes 737288 | tf_op jit(solution)/shard_map/ppermute | solution.py:123
  6.9 13.7 %collective-permute-start = (bf16[1,2,160,768]{3,2,1,0:T(8,128)(2,1)S(1)}, bf16[1,2,160,768]{3,2,1,0:T(8,128)(2,1)S(1)}, u32[]{:S(2)}, u32[]{:S(2)}) collective-permute-start(bf16[1,2,160,768]{3,2,1,0:T(8,128)(2,1)S(1)} %pad_maximum_fusion.20), channel_id=1, source_target_pairs={{0,4},{4,8},{8,12},{1,5},{5,9},{9,13},{2,6},{6,10},{10,14},{3,7},{... | collective-permute-start | bytes 1474568 | tf_op jit(solution)/shard_map/ppermute | solution.py:159
  10.5 14.3 %collective-permute-start.3 = (bf16[1,2,160,768]{3,2,1,0:T(8,128)(2,1)S(1)}, bf16[1,2,160,768]{3,2,1,0:T(8,128)(2,1)S(1)}, u32[]{:S(2)}, u32[]{:S(2)}) collective-permute-start(bf16[1,2,160,768]{3,2,1,0:T(8,128)(2,1)S(1)} %pad_maximum_fusion.20), channel_id=1, source_target_pairs={{4,0},{8,4},{12,8},{5,1},{9,5},{13,9},{6,2},{10,6},{14,10},{7,3},{... | collective-permute-start | bytes 1474568 | tf_op jit(solution)/shard_map/ppermute | solution.py:160
  12.8 17.4 %collective-permute-start.13 = (bf16[1,4,160,384]{3,2,1,0:T(8,128)(2,1)}, bf16[1,4,160,384]{3,2,1,0:T(8,128)(2,1)S(1)}, u32[]{:S(2)}, u32[]{:S(2)}) collective-permute-start(bf16[1,4,160,384]{3,2,1,0:T(8,128)(2,1)} %pad_maximum_fusion.15), channel_id=1, source_target_pairs={{0,1},{1,0},{2,3},{3,2},{4,5},{5,4},{6,7},{7,6},{8,9},{9,8},{10,11... | collective-permute-start | bytes 1474568 | tf_op jit(solution)/shard_map/ppermute | solution.py:129
  24.8 18.7 %collective-permute-start.10 = (bf16[2,2,160,384]{3,2,1,0:T(8,128)(2,1)S(1)}, bf16[2,2,160,384]{3,2,1,0:T(8,128)(2,1)S(1)}, u32[]{:S(2)}, u32[]{:S(2)}) collective-permute-start(bf16[2,2,160,384]{3,2,1,0:T(8,128)(2,1)S(1)} %pad_maximum_fusion.17), channel_id=1, source_target_pairs={{0,2},{1,3},{2,0},{3,1},{4,6},{5,7},{6,4},{7,5},{8,10},{9,11},{10,... | collective-permute-start | bytes 1474568 | tf_op jit(solution)/shard_map/ppermute | solution.py:123
  25.4 12.1 %collective-permute-start.1 = (bf16[1,2,160,768]{3,2,1,0:T(8,128)(2,1)S(1)}, bf16[1,2,160,768]{3,2,1,0:T(8,128)(2,1)S(1)}, u32[]{:S(2)}, u32[]{:S(2)}) collective-permute-start(bf16[1,2,160,768]{3,2,1,0:T(8,128)(2,1)S(1)} %collective-permute-done), channel_id=1, source_target_pairs={{0,4},{4,8},{8,12},{1,5},{5,9},{9,13},{2,6},{6,10},{10,14},{3,7},{... | collective-permute-start | bytes 1474568 | tf_op jit(solution)/shard_map/ppermute | solution.py:159
  28.9 15.7 %collective-permute-start.4 = (bf16[1,2,160,768]{3,2,1,0:T(8,128)(2,1)S(1)}, bf16[1,2,160,768]{3,2,1,0:T(8,128)(2,1)S(1)}, u32[]{:S(2)}, u32[]{:S(2)}) collective-permute-start(bf16[1,2,160,768]{3,2,1,0:T(8,128)(2,1)S(1)} %collective-permute-done.3), channel_id=1, source_target_pairs={{4,0},{8,4},{12,8},{5,1},{9,5},{13,9},{6,2},{10,6},{14,10},{7,3},{... | collective-permute-start | bytes 1474568 | tf_op jit(solution)/shard_map/ppermute | solution.py:160
  37.6 12.2 %collective-permute-start.2 = (bf16[1,2,160,768]{3,2,1,0:T(8,128)(2,1)S(1)}, bf16[1,2,160,768]{3,2,1,0:T(8,128)(2,1)S(1)}, u32[]{:S(2)}, u32[]{:S(2)}) collective-permute-start(bf16[1,2,160,768]{3,2,1,0:T(8,128)(2,1)S(1)} %collective-permute-done.1), channel_id=1, source_target_pairs={{0,4},{4,8},{8,12},{1,5},{5,9},{9,13},{2,6},{6,10},{10,14},{3,7},{... | collective-permute-start | bytes 1474568 | tf_op jit(solution)/shard_map/ppermute | solution.py:159
  43.5 6.3 %copy-start.8 = (bf16[1,2,160,384]{3,2,1,0:T(8,128)(2,1)S(1)}, bf16[1,2,160,384]{3,2,1,0:T(8,128)(2,1)}, u32[]{:S(2)}) copy-start(bf16[1,2,160,384]{3,2,1,0:T(8,128)(2,1)} %param.9) | copy-start | bytes 737284
  43.5 6.3 %copy-start.13 = (bf16[2,2,160,384]{3,2,1,0:T(8,128)(2,1)}, bf16[2,2,160,384]{3,2,1,0:T(8,128)(2,1)S(1)}, u32[]{:S(2)}) copy-start(bf16[2,2,160,384]{3,2,1,0:T(8,128)(2,1)S(1)} %collective-permute-done.10) | copy-start | bytes 1474564
  44.6 48.8 %collective-permute-start.11 = (bf16[2,4,160,384]{3,2,1,0:T(8,128)(2,1)}, bf16[2,4,160,384]{3,2,1,0:T(8,128)(2,1)}, u32[]{:S(2)}, u32[]{:S(2)}) collective-permute-start(bf16[2,4,160,384]{3,2,1,0:T(8,128)(2,1)} %pad_maximum_fusion.8), channel_id=1, source_target_pairs={{0,1},{1,0},{2,3},{3,2},{4,5},{5,4},{6,7},{7,6},{8,9},{9,8},{10,11... | collective-permute-start | bytes 2949128 | tf_op jit(solution)/shard_map/ppermute | solution.py:129
  44.7 28.3 %copy-start.2 = (bf16[2,2,160,384]{3,2,1,0:T(8,128)(2,1)}, bf16[2,2,160,384]{3,2,1,0:T(8,128)(2,1)S(1)}, u32[]{:S(2)}) copy-start(bf16[2,2,160,384]{3,2,1,0:T(8,128)(2,1)S(1)} %pad_maximum_fusion.18) | copy-start | bytes 1474564
  44.7 28.3 %collective-permute-start.8 = (bf16[2,2,160,384]{3,2,1,0:T(8,128)(2,1)S(1)}, bf16[2,2,160,384]{3,2,1,0:T(8,128)(2,1)}, u32[]{:S(2)}, u32[]{:S(2)}) collective-permute-start(bf16[2,2,160,384]{3,2,1,0:T(8,128)(2,1)S(1)} %pad_maximum_fusion.18), channel_id=1, source_target_pairs={{0,2},{1,3},{2,0},{3,1},{4,6},{5,7},{6,4},{7,5},{8,10},{9,11},{10,... | collective-permute-start | bytes 1474568 | tf_op jit(solution)/shard_map/ppermute | solution.py:123
  46.2 15.2 %collective-permute-start.5 = (bf16[1,2,160,768]{3,2,1,0:T(8,128)(2,1)S(1)}, bf16[1,2,160,768]{3,2,1,0:T(8,128)(2,1)S(1)}, u32[]{:S(2)}, u32[]{:S(2)}) collective-permute-start(bf16[1,2,160,768]{3,2,1,0:T(8,128)(2,1)S(1)} %collective-permute-done.4), channel_id=1, source_target_pairs={{4,0},{8,4},{12,8},{5,1},{9,5},{13,9},{6,2},{10,6},{14,10},{7,3},{... | collective-permute-start | bytes 1474568 | tf_op jit(solution)/shard_map/ppermute | solution.py:160
  49.7 11.8 %copy-start.9 = (bf16[1,2,160,768]{3,2,1,0:T(8,128)(2,1)}, bf16[1,2,160,768]{3,2,1,0:T(8,128)(2,1)S(1)}, u32[]{:S(2)}) copy-start(bf16[1,2,160,768]{3,2,1,0:T(8,128)(2,1)S(1)} %collective-permute-done.2) | copy-start | bytes 1474564
  61.5 0.8 copy-start.11
  62.3 9.2 %copy-start.10 = (bf16[1,2,160,768]{3,2,1,0:T(8,128)(2,1)S(1)}, bf16[1,2,160,768]{3,2,1,0:T(8,128)(2,1)}, u32[]{:S(2)}) copy-start(bf16[1,2,160,768]{3,2,1,0:T(8,128)(2,1)} %copy-done.9) | copy-start | bytes 1474564
  62.3 9.2 %copy-start.12 = (bf16[1,2,160,768]{3,2,1,0:T(8,128)(2,1)S(1)}, bf16[1,2,160,768]{3,2,1,0:T(8,128)(2,1)}, u32[]{:S(2)}) copy-start(bf16[1,2,160,768]{3,2,1,0:T(8,128)(2,1)} %copy-done.11) | copy-start | bytes 1474564
  66.5 12.3 %collective-permute-start.15 = (bf16[3,1,160,384]{3,2,1,0:T(8,128)(2,1)}, bf16[3,1,160,384]{3,2,1,0:T(8,128)(2,1)}, u32[]{:S(2)}, u32[]{:S(2)}) collective-permute-start(bf16[3,1,160,384]{3,2,1,0:T(8,128)(2,1)} %get-tuple-element.19), channel_id=1, source_target_pairs={{1,0},{2,1},{3,2},{5,4},{6,5},{7,6},{9,8},{10,9},{11,10},{13,12},{... | collective-permute-start | bytes 1105928 | tf_op jit(solution)/shard_map/ppermute | solution.py:25
  67.7 11.0 %collective-permute-start.14 = (bf16[3,1,160,384]{3,2,1,0:T(8,128)(2,1)}, bf16[3,1,160,384]{3,2,1,0:T(8,128)(2,1)}, u32[]{:S(2)}, u32[]{:S(2)}) collective-permute-start(bf16[3,1,160,384]{3,2,1,0:T(8,128)(2,1)} %get-tuple-element.18), channel_id=1, source_target_pairs={{0,1},{1,2},{2,3},{4,5},{5,6},{6,7},{8,9},{9,10},{10,11},{12,13},{... | collective-permute-start | bytes 1105928 | tf_op jit(solution)/shard_map/ppermute | solution.py:23
  72.4 18.2 %collective-permute-start.6 = (bf16[2,2,160,384]{3,2,1,0:T(8,128)(2,1)}, bf16[2,2,160,384]{3,2,1,0:T(8,128)(2,1)}, u32[]{:S(2)}, u32[]{:S(2)}) collective-permute-start(bf16[2,2,160,384]{3,2,1,0:T(8,128)(2,1)} %pad_maximum_fusion.19), channel_id=1, source_target_pairs={{0,2},{1,3},{2,0},{3,1},{4,6},{5,7},{6,4},{7,5},{8,10},{9,11},{10,... | collective-permute-start | bytes 1474568 | tf_op jit(solution)/shard_map/ppermute | solution.py:123
  75.1 32.1 %collective-permute-start.9 = (bf16[2,4,160,384]{3,2,1,0:T(8,128)(2,1)}, bf16[2,4,160,384]{3,2,1,0:T(8,128)(2,1)}, u32[]{:S(2)}, u32[]{:S(2)}) collective-permute-start(bf16[2,4,160,384]{3,2,1,0:T(8,128)(2,1)} %pad_maximum_fusion.5), channel_id=1, source_target_pairs={{0,1},{1,0},{2,3},{3,2},{4,5},{5,4},{6,7},{7,6},{8,9},{9,8},{10,11... | collective-permute-start | bytes 2949128 | tf_op jit(solution)/shard_map/ppermute | solution.py:129
  75.1 27.4 %all-to-all-start = ((bf16[4,2,160,384]{2,1,0,3:T(2,128)(2,1)}), bf16[4,2,160,384]{2,1,0,3:T(2,128)(2,1)S(1)}, u32[]{:S(2)}, u32[]{:S(2)}) async-start(bf16[4,2,160,384]{2,1,0,3:T(2,128)(2,1)} %copy.33), calls=%async_computation | async-start | bytes 3145728 | tf_op jit(solution)/shard_map/all_to_all | solution.py:227
  80.9 0.9 copy-start.20
  81.8 8.4 %copy-start.7 = (bf16[1,2,160,384]{3,2,1,0:T(8,128)(2,1)S(1)}, bf16[1,2,160,384]{3,2,1,0:T(8,128)(2,1)}, u32[]{:S(2)}) copy-start(bf16[1,2,160,384]{3,2,1,0:T(8,128)(2,1)} %param.5) | copy-start | bytes 737284
  81.8 8.4 %copy-start.18 = (f32[384]{0:T(512)S(1)}, f32[384]{0:T(512)}, u32[]{:S(2)}) copy-start(f32[384]{0:T(512)} %param.6) | copy-start | bytes 4612
  89.4 0.8 copy-start
  90.6 5.2 %copy-start.14 = (bf16[2,2,160,384]{3,2,1,0:T(8,128)(2,1)S(1)}, bf16[2,2,160,384]{3,2,1,0:T(8,128)(2,1)}, u32[]{:S(2)}) copy-start(bf16[2,2,160,384]{3,2,1,0:T(8,128)(2,1)} %copy-done.13) | copy-start | bytes 1474564
  92.9 20.3 %collective-permute-start.7 = (bf16[2,4,160,384]{3,2,1,0:T(8,128)(2,1)}, bf16[2,4,160,384]{3,2,1,0:T(8,128)(2,1)}, u32[]{:S(2)}, u32[]{:S(2)}) collective-permute-start(bf16[2,4,160,384]{3,2,1,0:T(8,128)(2,1)} %pad_maximum_fusion.2), channel_id=1, source_target_pairs={{0,1},{1,0},{2,3},{3,2},{4,5},{5,4},{6,7},{7,6},{8,9},{9,8},{10,11... | collective-permute-start | bytes 2949128 | tf_op jit(solution)/shard_map/ppermute | solution.py:129
  104.6 3.9 %copy-start.3 = (bf16[2,2,160,384]{3,2,1,0:T(8,128)(2,1)S(1)}, bf16[2,2,160,384]{3,2,1,0:T(8,128)(2,1)}, u32[]{:S(2)}) copy-start(bf16[2,2,160,384]{3,2,1,0:T(8,128)(2,1)} %copy-done.2) | copy-start | bytes 1474564
  107.1 3.0 %copy-start.5 = (bf16[2,4,160,384]{3,2,1,0:T(8,128)(2,1)S(1)}, bf16[2,4,160,384]{3,2,1,0:T(8,128)(2,1)}, u32[]{:S(2)}) copy-start(bf16[2,4,160,384]{3,2,1,0:T(8,128)(2,1)} %fusion.49) | copy-start | bytes 2949124
  107.1 3.0 %copy-start.6 = (bf16[2,4,160,384]{3,2,1,0:T(8,128)(2,1)S(1)}, bf16[2,4,160,384]{3,2,1,0:T(8,128)(2,1)}, u32[]{:S(2)}) copy-start(bf16[2,4,160,384]{3,2,1,0:T(8,128)(2,1)} %fusion.50) | copy-start | bytes 2949124
  141.9 18.3 %copy-start.4 = (bf16[1,8,160,384]{3,2,1,0:T(8,128)(2,1)S(1)}, bf16[1,8,160,384]{3,2,1,0:T(8,128)(2,1)}, u32[]{:S(2)}) copy-start(bf16[1,8,160,384]{3,2,1,0:T(8,128)(2,1)} %pad_maximum_fusion.13) | copy-start | bytes 2949124
  168.9 8.0 %slice-start = ((s8[7741440]{0:T(1024)(128)(4,1)}), s8[4194304]{0:T(1024)(128)(4,1)S(1)}, s32[]{:S(2)}) async-start(s8[7741440]{0:T(1024)(128)(4,1)} %bitcast.96), calls=%async_computation.1 | async-start | bytes 8388608
  169.2 7.7 %slice-start.1 = ((s8[7741440]{0:T(1024)(128)(4,1)}), s8[3547136]{0:T(1024)(128)(4,1)S(1)}, s32[]{:S(2)}) async-start(s8[7741440]{0:T(1024)(128)(4,1)} %bitcast.96), calls=%async_computation.2 | async-start | bytes 7094272
  169.2 7.7 %copy-start.15 = (bf16[4,8,168,1,96]{4,2,1,3,0:T(8,128)(2,1)S(1)}, bf16[4,8,168,1,96]{4,2,1,3,0:T(8,128)(2,1)}, u32[]{:S(2)}) copy-start(bf16[4,8,168,1,96]{4,2,1,3,0:T(8,128)(2,1)} %get-tuple-element.15) | copy-start | bytes 3096580
  169.2 7.7 %copy-start.16 = (bf16[4,8,168,1,96]{4,2,1,3,0:T(8,128)(2,1)S(1)}, bf16[4,8,168,1,96]{4,2,1,3,0:T(8,128)(2,1)}, u32[]{:S(2)}) copy-start(bf16[4,8,168,1,96]{4,2,1,3,0:T(8,128)(2,1)} %get-tuple-element.16) | copy-start | bytes 3096580
  169.2 7.7 %copy-start.17 = (bf16[4,8,168,1,96]{4,2,1,3,0:T(8,128)(2,1)S(1)}, bf16[4,8,168,1,96]{4,2,1,3,0:T(8,128)(2,1)}, u32[]{:S(2)}) copy-start(bf16[4,8,168,1,96]{4,2,1,3,0:T(8,128)(2,1)} %get-tuple-element.17) | copy-start | bytes 3096580
  180.7 1.9 %copy-start.1 = (f32[1,2,1,160,384]{4,1,3,2,0:T(2,128)S(1)}, f32[1,2,1,160,384]{4,1,3,2,0:T(2,128)}, u32[]{:S(2)}) copy-start(f32[1,2,1,160,384]{4,1,3,2,0:T(2,128)} %copy-done) | copy-start | bytes 1474564
  180.7 1.9 %copy-start.19 = (f32[384]{0:T(512)S(1)}, f32[384]{0:T(512)}, u32[]{:S(2)}) copy-start(f32[384]{0:T(512)} %param.7) | copy-start | bytes 4612

commit v11 on v9

--- a/solution.py
+++ b/solution.py
@@ -152,15 +152,14 @@
 def gather_frames(block):
     count = lax.axis_size("tm")
     position = lax.axis_index("tm")
-    up = [(i, i + 1) for i in range(count - 1)]
-    down = [(i + 1, i) for i in range(count - 1)]
-    earlier, later = [], []
-    rising, falling = block, block
-    for step in range(1, count):
-        rising = lax.ppermute(rising, "tm", up)
-        falling = lax.ppermute(falling, "tm", down)
-        earlier.append(rising)
-        later.append(falling)
+    earlier = [
+        lax.ppermute(block, "tm", [(i, i + step) for i in range(count - step)])
+        for step in range(1, count)
+    ]
+    later = [
+        lax.ppermute(block, "tm", [(i + step, i) for i in range(count - step)])
+        for step in range(1, count)
+    ]
     relative = jnp.concatenate(earlier[::-1] + [block] + later, axis=0)
     return lax.dynamic_slice_in_dim(relative, count - 1 - position, count * block.shape[0], 0)
 

time: 126 us -> 138 us (1.095)
  waiting for transfers between devices: 44.2 us -> 58.9 us
  starting transfers between devices: 28 us -> 25 us
    ppermute x6, waiting for transfers between devices: 28.6 us -> 41.5 us  [the longest x3 23.8 us: gather_frames(): lax.ppermute(block, 'tm', [(i, i + step) for i in range(count - step)])]
    ppermute x6, starting transfers between devices: 17.6 us -> 14.6 us  [the longest x3 10.8 us: gather_frames(): lax.ppermute(block, 'tm', [(i, i + step) for i in range(count - step)])]
  transfers between devices with their start and end apart: 11 -> 11, of which waited for: 6 -> 6; matrix products, arithmetic and copies ran while one was open for 18% -> 16% of each run, Pallas kernels for 0% -> 0%
where the time goes in v11:
time: 138 us
  waiting for transfers between devices  58.9 us (43%)
  starting transfers between devices  25 us (18%)
  other arithmetic  20.7 us (15%)
  local copies, waits for them, and re-layouts  18.6 us (13%)
  matrix products  13.1 us (9%)
    ppermute x3, waiting for transfers between devices, gather_frames(): lax.ppermute(block, 'tm', [(i, i + step) for i in range(count - step)])  23.8 us
    ppermute x3, waiting for transfers between devices, gather_frames(): lax.ppermute(block, 'tm', [(i + step, i) for i in range(count - step)])  17.7 us
    ppermute x3, starting transfers between devices, gather_frames(): lax.ppermute(block, 'tm', [(i, i + step) for i in range(count - step)])  10.8 us
    ppermute x1, waiting for transfers between devices, gather_rows(): lax.ppermute(own, 'height', [(i, (i + 2 * step) % height_count) for i in...  10.5 us
    all_to_all x1, waiting for transfers between devices, local(): lax.all_to_all(cot_frames, 'height', split_axis=3, concat_axis=1, tiled=T...  6.99 us
    concatenate x1, other arithmetic, gather_rows(): jnp.concatenate([lax.dynamic_slice_in_dim(relative, (place - chip - 1) %...  5.84 us
    dot_general x3, matrix products, block_weight_grad(): lax.dot_general(shifted, slab, (((0, 1, 2), (0, 1, 2)), ((), ())), prefer...  5.48 us
    ppermute x3, starting transfers between devices, gather_frames(): lax.ppermute(block, 'tm', [(i + step, i) for i in range(count - step)])  3.86 us
  transfers between devices with their start and end apart: 11, of which 6 were waited for; matrix products, arithmetic and copies ran while one was open for 16% of the time, Pallas kernels for 0%

profile of v11, /device:TPU:0, one launch (start us, length us, event | category | flops | bytes accessed | tf_op | source)
XLA Modules:
  0.0 137.6 jit_solution(15945182838785871542)
XLA Ops:
  0.6 0.0 copy-start.4
  0.6 1.1 fusion.66
  1.8 1.2 multiply_convert_fusion
  3.0 1.0 pad_maximum_fusion.4
  4.0 7.0 %collective-permute-start = (bf16[1,2,160,768]{3,2,1,0:T(8,128)(2,1)S(1)}, bf16[1,2,160,768]{3,2,1,0:T(8,128)(2,1)S(1)}, u32[]{:S(2)}, u32[]{:S(2)}) collective-permute-start(bf16[1,2,160,768]{3,2,1,0:T(8,128)(2,1)S(1)} %pad_maximum_fusion.4), channel_id=1, source_target_pairs={{0,12},{1,13},{2,14},{3,15},{16,28},{17,29},{18,30},{19,31}} | collective-permute-start | bytes 1474568 | tf_op jit(solution)/shard_map/ppermute | solution.py:156
  11.0 1.3 collective-permute-start.1
  12.3 2.5 %collective-permute-start.2 = (bf16[1,2,160,768]{3,2,1,0:T(8,128)(2,1)S(1)}, bf16[1,2,160,768]{3,2,1,0:T(8,128)(2,1)S(1)}, u32[]{:S(2)}, u32[]{:S(2)}) collective-permute-start(bf16[1,2,160,768]{3,2,1,0:T(8,128)(2,1)S(1)} %pad_maximum_fusion.4), channel_id=1, source_target_pairs={{0,4},{4,8},{8,12},{1,5},{5,9},{9,13},{2,6},{6,10},{10,14},{3,7},{... | collective-permute-start | bytes 1474568 | tf_op jit(solution)/shard_map/ppermute | solution.py:156
  14.8 1.3 collective-permute-start.3
  16.1 1.3 collective-permute-start.4
  17.4 5.3 %collective-permute-done = bf16[1,2,160,768]{3,2,1,0:T(8,128)(2,1)S(1)} collective-permute-done((bf16[1,2,160,768]{3,2,1,0:T(8,128)(2,1)S(1)}, bf16[1,2,160,768]{3,2,1,0:T(8,128)(2,1)S(1)}, u32[]{:S(2)}, u32[]{:S(2)}) %collective-permute-start) | collective-permute-done | bytes 491552 | tf_op jit(solution)/shard_map/ppermute | solution.py:156
  22.7 1.3 collective-permute-start.5
  24.0 9.2 %collective-permute-done.1 = bf16[1,2,160,768]{3,2,1,0:T(8,128)(2,1)S(1)} collective-permute-done((bf16[1,2,160,768]{3,2,1,0:T(8,128)(2,1)S(1)}, bf16[1,2,160,768]{3,2,1,0:T(8,128)(2,1)S(1)}, u32[]{:S(2)}, u32[]{:S(2)}) %collective-permute-start.1) | collective-permute-done | bytes 491552 | tf_op jit(solution)/shard_map/ppermute | solution.py:156
  33.2 9.3 %collective-permute-done.2 = bf16[1,2,160,768]{3,2,1,0:T(8,128)(2,1)S(1)} collective-permute-done((bf16[1,2,160,768]{3,2,1,0:T(8,128)(2,1)S(1)}, bf16[1,2,160,768]{3,2,1,0:T(8,128)(2,1)S(1)}, u32[]{:S(2)}, u32[]{:S(2)}) %collective-permute-start.2) | collective-permute-done | bytes 491552 | tf_op jit(solution)/shard_map/ppermute | solution.py:156
  42.7 0.0 collective-permute-done.3
  42.7 17.7 %collective-permute-done.4 = bf16[1,2,160,768]{3,2,1,0:T(8,128)(2,1)S(1)} collective-permute-done((bf16[1,2,160,768]{3,2,1,0:T(8,128)(2,1)S(1)}, bf16[1,2,160,768]{3,2,1,0:T(8,128)(2,1)S(1)}, u32[]{:S(2)}, u32[]{:S(2)}) %collective-permute-start.4) | collective-permute-done | bytes 491552 | tf_op jit(solution)/shard_map/ppermute | solution.py:160
  60.5 0.3 constant_dynamic-slice_fusion.1
  60.7 1.6 %collective-permute-start.6 = (bf16[4,2,160,384]{3,2,1,0:T(8,128)(2,1)S(1)}, bf16[4,2,160,384]{3,2,1,0:T(8,128)(2,1)}, u32[]{:S(2)}, u32[]{:S(2)}) collective-permute-start(bf16[4,2,160,384]{3,2,1,0:T(8,128)(2,1)S(1)} %get-tuple-element.6), channel_id=1, source_target_pairs={{0,2},{1,3},{2,0},{3,1},{4,6},{5,7},{6,4},{7,5},{8,10},{9,11},{10,... | collective-permute-start | bytes 2949128 | tf_op jit(solution)/shard_map/ppermute | solution.py:123
  62.3 1.0 pad_dynamic-slice_fusion.5
  63.3 1.3 collective-permute-start.9
  64.6 3.8 %collective-permute-start.8 = (bf16[3,1,160,384]{3,2,1,0:T(8,128)(2,1)}, bf16[3,1,160,384]{3,2,1,0:T(8,128)(2,1)}, u32[]{:S(2)}, u32[]{:S(2)}) collective-permute-start(bf16[3,1,160,384]{3,2,1,0:T(8,128)(2,1)} %get-tuple-element.12), channel_id=1, source_target_pairs={{0,1},{1,2},{2,3},{4,5},{5,6},{6,7},{8,9},{9,10},{10,11},{12,13},{... | collective-permute-start | bytes 1105928 | tf_op jit(solution)/shard_map/ppermute | solution.py:23
  68.4 3.0 %copy.33 = bf16[4,2,160,384]{2,1,0,3:T(2,128)(2,1)} copy(bf16[4,2,160,384]{3,2,1,0:T(8,128)(2,1)S(1)} %get-tuple-element.5) | data formatting | bytes 1966080 | tf_op jit(solution)/shard_map/slice | solution.py:190
  71.4 3.7 %all-to-all-start = ((bf16[4,2,160,384]{2,1,0,3:T(2,128)(2,1)}), bf16[4,2,160,384]{2,1,0,3:T(2,128)(2,1)S(1)}, u32[]{:S(2)}, u32[]{:S(2)}) async-start(bf16[4,2,160,384]{2,1,0,3:T(2,128)(2,1)} %copy.33), calls=%async_computation | async-start | bytes 3145728 | tf_op jit(solution)/shard_map/all_to_all | solution.py:191
  75.2 10.5 %collective-permute-done.6 = bf16[4,2,160,384]{3,2,1,0:T(8,128)(2,1)} collective-permute-done((bf16[4,2,160,384]{3,2,1,0:T(8,128)(2,1)S(1)}, bf16[4,2,160,384]{3,2,1,0:T(8,128)(2,1)}, u32[]{:S(2)}, u32[]{:S(2)}) %collective-permute-start.6) | collective-permute-done | bytes 983072 | tf_op jit(solution)/shard_map/ppermute | solution.py:123
  85.6 2.9 %pad_maximum_fusion.2 = bf16[4,4,160,384]{3,2,1,0:T(8,128)(2,1)} fusion(bf16[4,2,160,384]{3,2,1,0:T(8,128)(2,1)} %collective-permute-done.6, bf16[4,2,160,384]{3,2,1,0:T(8,128)(2,1)S(1)} %get-tuple-element.6), kind=kLoop, calls=%fused_computation.38 | loop fusion | flops 983040 | bytes 3932160 | tf_op jit(solution)/shard_map/concatenate | solution.py:128
  88.5 0.1 pad_dynamic-slice_fusion.6
  88.6 1.6 %fusion.44 = bf16[3,4,1,162,384]{4,3,1,0,2:T(8,128)(2,1)S(1)} fusion(bf16[3,1,160,384]{3,2,1,0:T(8,128)(2,1)} %collective-permute-done.9, bf16[3,2,160,384]{3,2,1,0:T(8,128)(2,1)S(1)} %pad_dynamic-slice_fusion.6, bf16[3,1,160,384]{3,2,1,0:T(8,128)(2,1)} %collective-permute-done.8), kind=kLoop, calls=%fused_computation.61 | loop fusion | flops 9704448 | bytes 2967552 | tf_op jit(solution)/shard_map/broadcast_in_dim | solution.py:58
  90.2 0.0 slice-start.1
  90.2 0.6 copy.49
  90.8 0.0 copy-start.8
  90.8 0.6 pad.32.clone
  91.4 0.2 copy.30
  91.6 0.6 slice-done.1
  92.3 3.8 %fusion.55 = f32[1,2,8,21,384]{4,2,3,1,0:T(8,128)S(1)} fusion(bf16[3,3,3,384,384]{4,3,2,1,0:T(8,128)(2,1)S(1)} %bitcast.107, bf16[3,4,1,7,2,384]{5,3,4,1,0,2:T(8,128)(2,1)S(1)} %slice.40, bf16[3,4,1,8,21,384]{5,3,4,1,0,2:T(8,128)(2,1)S(1)} %copy.30, pred[8,21]{0,1:T(8,128)(4,1)S(1)} %copy-done.8), kind=kOutput, calls=%fused_computation.75 | convolution fusion | flops 2680657920 | bytes 10156200 | tf_op jit(solution)/shard_map/conv_general_dilated | solution.py:57
  96.0 0.3 copy.31
  96.3 0.2 slice.41
  96.5 0.0 copy-start
  96.5 0.4 multiply_reduce_fusion
  96.9 7.0 %all-to-all-done = bf16[4,2,160,384]{2,1,0,3:T(2,128)(2,1)S(1)} async-done(((bf16[4,2,160,384]{2,1,0,3:T(2,128)(2,1)}), bf16[4,2,160,384]{2,1,0,3:T(2,128)(2,1)S(1)}, u32[]{:S(2)}, u32[]{:S(2)}) %all-to-all-start) | async-done | bytes 983072 | tf_op jit(solution)/shard_map/all_to_all | solution.py:191
  103.9 3.8 %copy.34 = bf16[4,2,160,4,96]{4,2,1,3,0:T(8,128)(2,1)} copy(bf16[4,2,160,4,96]{2,1,0,4,3:T(2,128)(2,1)S(1)} %bitcast.96) | data formatting | bytes 1966080 | tf_op jit(solution)/shard_map/all_to_all | solution.py:191
  107.7 3.5 %pad_bitcast_fusion.2 = (bf16[4,8,168,1,96]{4,2,1,3,0:T(8,128)(2,1)S(1)}, bf16[4,8,168,1,96]{4,2,1,3,0:T(8,128)(2,1)S(1)}, bf16[4,8,168,1,96]{4,2,1,3,0:T(8,128)(2,1)S(1)}) fusion(bf16[4,8,160,96]{3,2,1,0:T(8,128)(2,1)} %bitcast.99), kind=kLoop, calls=%fused_computation.68 | loop fusion | bytes 4079616 | tf_op jit(solution)/shard_map/stack | solution.py:83
  111.2 1.7 %fusion.81 = (bf16[4,2,160,384]{3,2,1,0:T(8,128)(2,1)S(1)}, bf16[4,2,160,384]{3,2,1,0:T(8,128)(2,1)S(1)}) fusion(bf16[4,4,160,384]{3,2,1,0:T(8,128)(2,1)} %collective-permute-done.7), kind=kLoop, calls=%fused_computation.118 | loop fusion | bytes 3932160 | tf_op jit(solution)/shard_map/slice | solution.py:134
  112.9 0.3 fusion.25
  113.3 1.8 %fusion.26 = bf16[4,4,160,384]{3,2,1,0:T(8,128)(2,1)S(1)} fusion(bf16[4,2,160,384]{3,2,1,0:T(8,128)(2,1)} %collective-permute-done.6, bf16[4,2,160,384]{3,2,1,0:T(8,128)(2,1)S(1)} %get-tuple-element.8, pred[]{:T(512)S(6)} %eq.10), kind=kLoop, calls=%fused_computation.41 | loop fusion | flops 2949120 | bytes 3932161 | tf_op jit(solution)/shard_map/jit(_where)/select_n | solution.py:136
  115.1 1.6 %fusion.28 = (bf16[4,4,160,384]{3,2,1,0:T(8,128)(2,1)S(1)}, bf16[4,4,160,384]{3,2,1,0:T(8,128)(2,1)S(1)}) fusion(s32[]{:T(128)S(6)} %select_n.99, bf16[4,4,160,384]{3,2,1,0:T(8,128)(2,1)S(1)} %fusion.26, bf16[4,4,160,384]{3,2,1,0:T(8,128)(2,1)S(1)} %fusion.25, s32[]{:T(128)S(6)} %select_n.101), kind=kLoop, calls=%fused_computation.43 | loop fusion | flops 1966080 | bytes 7864328 | tf_op jit(solution)/shard_map/concatenate | solution.py:142
  116.8 0.0 slice-start.2
  116.8 5.8 %fusion.8 = bf16[6,10,168,384]{3,2,1,0:T(8,128)(2,1)S(1)} fusion(bf16[4,4,160,384]{3,2,1,0:T(8,128)(2,1)S(1)} %get-tuple-element.4, bf16[4,4,160,384]{3,2,1,0:T(8,128)(2,1)S(1)} %get-tuple-element.3), kind=kLoop, calls=%fused_computation.13 | loop fusion | flops 73543680 | bytes 11673600 | tf_op jit(solution)/shard_map/concatenate | solution.py:143
  122.6 0.0 slice-start.3
  122.6 0.2 dynamic-slice_bitcast_fusion
  122.8 0.6 copy.48
  123.4 0.6 pad.30.clone
  124.0 0.2 copy.25
  124.3 0.4 slice-done.3
  124.7 3.9 %fusion.58 = f32[1,2,8,21,384]{4,2,3,1,0:T(8,128)S(1)} fusion(bf16[3,3,3,384,384]{4,3,2,1,0:T(8,128)(2,1)S(1)} %bitcast.110, bf16[3,4,1,7,2,384]{5,3,4,1,0,2:T(8,128)(2,1)S(1)} %slice.38, bf16[3,4,1,8,21,384]{5,3,4,1,0,2:T(8,128)(2,1)S(1)} %copy.25, pred[8,21]{0,1:T(8,128)(4,1)S(1)} %copy-done.8), kind=kOutput, calls=%fused_computation.76 | convolution fusion | flops 2680657920 | bytes 10156200 | tf_op jit(solution)/shard_map/conv_general_dilated | solution.py:44
  128.6 0.3 copy.26
  128.8 0.2 slice.39
  129.0 1.8 %fusion.46 = f32[3,12,8,384]{3,2,1,0:T(8,128)S(1)} fusion(bf16[6,10,168,384]{3,2,1,0:T(8,128)(2,1)S(1)} %fusion.8, s32[]{:T(128)S(6)} %select_n.106, s32[]{:T(128)S(6)} %select_n.108, bf16[4,8,168,1,96]{4,2,1,3,0:T(8,128)(2,1)S(1)} %get-tuple-element.10, bf16[4,8,168,1,96]{4,2,1,3,0:T(8,128)(2,1)S(1)} %get-tuple-element.11, ...), kind=kOutput, calls=%fused_computation.72 | convolution fusion | flops 1192181760 | bytes 8699912 | tf_op jit(solution)/shard_map/dot_general | solution.py:106
  130.9 1.8 %fusion.49 = f32[3,12,8,384]{3,2,1,0:T(8,128)S(1)} fusion(bf16[6,10,168,384]{3,2,1,0:T(8,128)(2,1)S(1)} %fusion.8, s32[]{:T(128)S(6)} %select_n.110, s32[]{:T(128)S(6)} %select_n.112, bf16[4,8,168,1,96]{4,2,1,3,0:T(8,128)(2,1)S(1)} %get-tuple-element.10, bf16[4,8,168,1,96]{4,2,1,3,0:T(8,128)(2,1)S(1)} %get-tuple-element.11, ...), kind=kOutput, calls=%fused_computation.73 | convolution fusion | flops 1192181760 | bytes 8699912 | tf_op jit(solution)/shard_map/dot_general | solution.py:106
  132.8 0.0 copy-start.1
  132.8 0.0 copy-start.3
  132.8 0.0 copy-start.5
  132.8 0.0 copy-start.7
  132.8 1.8 %fusion.52 = f32[3,12,8,384]{3,2,1,0:T(8,128)S(1)} fusion(bf16[6,10,168,384]{3,2,1,0:T(8,128)(2,1)S(1)} %fusion.8, s32[]{:T(128)S(6)} %select_n.114, s32[]{:T(128)S(6)} %select_n.116, bf16[4,8,168,1,96]{4,2,1,3,0:T(8,128)(2,1)S(1)} %get-tuple-element.10, bf16[4,8,168,1,96]{4,2,1,3,0:T(8,128)(2,1)S(1)} %get-tuple-element.11, ...), kind=kOutput, calls=%fused_computation.74 | convolution fusion | flops 1192181760 | bytes 8699912 | tf_op jit(solution)/shard_map/dot_general | solution.py:106
  134.7 1.2 add_convert_fusion
  135.9 1.6 %fusion.63 = f32[2592,96]{0,1:T(8,128)} fusion(s32[]{:T(128)S(6)} %select_n.117, f32[1152,96]{0,1:T(8,128)S(1)} %bitcast.102, f32[1152,96]{0,1:T(8,128)S(1)} %bitcast.103, f32[1152,96]{0,1:T(8,128)S(1)} %bitcast.104), kind=kLoop, calls=%fused_computation.79 | loop fusion | flops 746496 | bytes 2322436 | tf_op jit(solution)/shard_map/mul | solution.py:203
  (35 shorter events, 0.5 us)
Async XLA Ops:
  0.6 42.0 %copy-start.4 = (bf16[1,2,160,384]{3,2,1,0:T(8,128)(2,1)S(1)}, bf16[1,2,160,384]{3,2,1,0:T(8,128)(2,1)}, u32[]{:S(2)}) copy-start(bf16[1,2,160,384]{3,2,1,0:T(8,128)(2,1)} %param.9) | copy-start | bytes 737284
  4.0 18.7 %collective-permute-start = (bf16[1,2,160,768]{3,2,1,0:T(8,128)(2,1)S(1)}, bf16[1,2,160,768]{3,2,1,0:T(8,128)(2,1)S(1)}, u32[]{:S(2)}, u32[]{:S(2)}) collective-permute-start(bf16[1,2,160,768]{3,2,1,0:T(8,128)(2,1)S(1)} %pad_maximum_fusion.4), channel_id=1, source_target_pairs={{0,12},{1,13},{2,14},{3,15},{16,28},{17,29},{18,30},{19,31}} | collective-permute-start | bytes 1474568 | tf_op jit(solution)/shard_map/ppermute | solution.py:156
  11.0 22.2 %collective-permute-start.1 = (bf16[1,2,160,768]{3,2,1,0:T(8,128)(2,1)S(1)}, bf16[1,2,160,768]{3,2,1,0:T(8,128)(2,1)S(1)}, u32[]{:S(2)}, u32[]{:S(2)}) collective-permute-start(bf16[1,2,160,768]{3,2,1,0:T(8,128)(2,1)S(1)} %pad_maximum_fusion.4), channel_id=1, source_target_pairs={{0,8},{4,12},{1,9},{5,13},{2,10},{6,14},{3,11},{7,15},{16,24},{20,... | collective-permute-start | bytes 1474568 | tf_op jit(solution)/shard_map/ppermute | solution.py:156
  12.3 30.3 %collective-permute-start.2 = (bf16[1,2,160,768]{3,2,1,0:T(8,128)(2,1)S(1)}, bf16[1,2,160,768]{3,2,1,0:T(8,128)(2,1)S(1)}, u32[]{:S(2)}, u32[]{:S(2)}) collective-permute-start(bf16[1,2,160,768]{3,2,1,0:T(8,128)(2,1)S(1)} %pad_maximum_fusion.4), channel_id=1, source_target_pairs={{0,4},{4,8},{8,12},{1,5},{5,9},{9,13},{2,6},{6,10},{10,14},{3,7},{... | collective-permute-start | bytes 1474568 | tf_op jit(solution)/shard_map/ppermute | solution.py:156
  14.8 27.9 %collective-permute-start.3 = (bf16[1,2,160,768]{3,2,1,0:T(8,128)(2,1)S(1)}, bf16[1,2,160,768]{3,2,1,0:T(8,128)(2,1)S(1)}, u32[]{:S(2)}, u32[]{:S(2)}) collective-permute-start(bf16[1,2,160,768]{3,2,1,0:T(8,128)(2,1)S(1)} %pad_maximum_fusion.4), channel_id=1, source_target_pairs={{4,0},{8,4},{12,8},{5,1},{9,5},{13,9},{6,2},{10,6},{14,10},{7,3},{... | collective-permute-start | bytes 1474568 | tf_op jit(solution)/shard_map/ppermute | solution.py:160
  16.1 44.3 %collective-permute-start.4 = (bf16[1,2,160,768]{3,2,1,0:T(8,128)(2,1)S(1)}, bf16[1,2,160,768]{3,2,1,0:T(8,128)(2,1)S(1)}, u32[]{:S(2)}, u32[]{:S(2)}) collective-permute-start(bf16[1,2,160,768]{3,2,1,0:T(8,128)(2,1)S(1)} %pad_maximum_fusion.4), channel_id=1, source_target_pairs={{8,0},{12,4},{9,1},{13,5},{10,2},{14,6},{11,3},{15,7},{24,16},{28,... | collective-permute-start | bytes 1474568 | tf_op jit(solution)/shard_map/ppermute | solution.py:160
  22.7 37.8 %collective-permute-start.5 = (bf16[1,2,160,768]{3,2,1,0:T(8,128)(2,1)S(1)}, bf16[1,2,160,768]{3,2,1,0:T(8,128)(2,1)S(1)}, u32[]{:S(2)}, u32[]{:S(2)}) collective-permute-start(bf16[1,2,160,768]{3,2,1,0:T(8,128)(2,1)S(1)} %pad_maximum_fusion.4), channel_id=1, source_target_pairs={{12,0},{13,1},{14,2},{15,3},{28,16},{29,17},{30,18},{31,19}} | collective-permute-start | bytes 1474568 | tf_op jit(solution)/shard_map/ppermute | solution.py:160
  60.7 24.9 %collective-permute-start.6 = (bf16[4,2,160,384]{3,2,1,0:T(8,128)(2,1)S(1)}, bf16[4,2,160,384]{3,2,1,0:T(8,128)(2,1)}, u32[]{:S(2)}, u32[]{:S(2)}) collective-permute-start(bf16[4,2,160,384]{3,2,1,0:T(8,128)(2,1)S(1)} %get-tuple-element.6), channel_id=1, source_target_pairs={{0,2},{1,3},{2,0},{3,1},{4,6},{5,7},{6,4},{7,5},{8,10},{9,11},{10,... | collective-permute-start | bytes 2949128 | tf_op jit(solution)/shard_map/ppermute | solution.py:123
  63.3 25.3 %collective-permute-start.9 = (bf16[3,1,160,384]{3,2,1,0:T(8,128)(2,1)}, bf16[3,1,160,384]{3,2,1,0:T(8,128)(2,1)}, u32[]{:S(2)}, u32[]{:S(2)}) collective-permute-start(bf16[3,1,160,384]{3,2,1,0:T(8,128)(2,1)} %get-tuple-element.13), channel_id=1, source_target_pairs={{1,0},{2,1},{3,2},{5,4},{6,5},{7,6},{9,8},{10,9},{11,10},{13,12},{... | collective-permute-start | bytes 1105928 | tf_op jit(solution)/shard_map/ppermute | solution.py:25
  64.6 24.0 %collective-permute-start.8 = (bf16[3,1,160,384]{3,2,1,0:T(8,128)(2,1)}, bf16[3,1,160,384]{3,2,1,0:T(8,128)(2,1)}, u32[]{:S(2)}, u32[]{:S(2)}) collective-permute-start(bf16[3,1,160,384]{3,2,1,0:T(8,128)(2,1)} %get-tuple-element.12), channel_id=1, source_target_pairs={{0,1},{1,2},{2,3},{4,5},{5,6},{6,7},{8,9},{9,10},{10,11},{12,13},{... | collective-permute-start | bytes 1105928 | tf_op jit(solution)/shard_map/ppermute | solution.py:23
  71.4 32.5 %all-to-all-start = ((bf16[4,2,160,384]{2,1,0,3:T(2,128)(2,1)}), bf16[4,2,160,384]{2,1,0,3:T(2,128)(2,1)S(1)}, u32[]{:S(2)}, u32[]{:S(2)}) async-start(bf16[4,2,160,384]{2,1,0,3:T(2,128)(2,1)} %copy.33), calls=%async_computation | async-start | bytes 3145728 | tf_op jit(solution)/shard_map/all_to_all | solution.py:191
  85.6 6.0 %slice-start = ((s8[7962624]{0:T(1024)(128)(4,1)}), s8[4194304]{0:T(1024)(128)(4,1)S(1)}, s32[]{:S(2)}) async-start(s8[7962624]{0:T(1024)(128)(4,1)} %bitcast.105), calls=%async_computation.1 | async-start | bytes 8388608
  88.5 22.7 %collective-permute-start.7 = (bf16[4,4,160,384]{3,2,1,0:T(8,128)(2,1)}, bf16[4,4,160,384]{3,2,1,0:T(8,128)(2,1)}, u32[]{:S(2)}, u32[]{:S(2)}) collective-permute-start(bf16[4,4,160,384]{3,2,1,0:T(8,128)(2,1)} %pad_maximum_fusion.2), channel_id=1, source_target_pairs={{0,1},{1,0},{2,3},{3,2},{4,5},{5,4},{6,7},{7,6},{8,9},{9,8},{10,11... | collective-permute-start | bytes 5898248 | tf_op jit(solution)/shard_map/ppermute | solution.py:129
  90.2 2.1 %slice-start.1 = ((s8[7962624]{0:T(1024)(128)(4,1)}), s8[3768320]{0:T(1024)(128)(4,1)S(1)}, s32[]{:S(2)}) async-start(s8[7962624]{0:T(1024)(128)(4,1)} %bitcast.105), calls=%async_computation.2 | async-start | bytes 7536640
  90.8 1.5 %copy-start.8 = (pred[8,21]{0,1:T(8,128)(4,1)S(1)}, pred[8,21]{0,1:T(8,128)(4,1)}, u32[]{:S(2)}) copy-start(pred[8,21]{0,1:T(8,128)(4,1)} %constant.123) | copy-start | bytes 508
  92.3 4.2 %copy-start.2 = (bf16[1,2,160,384]{3,2,1,0:T(8,128)(2,1)S(1)}, bf16[1,2,160,384]{3,2,1,0:T(8,128)(2,1)}, u32[]{:S(2)}) copy-start(bf16[1,2,160,384]{3,2,1,0:T(8,128)(2,1)} %param.5) | copy-start | bytes 737284
  92.3 4.2 %copy-start.6 = (f32[384]{0:T(512)S(1)}, f32[384]{0:T(512)}, u32[]{:S(2)}) copy-start(f32[384]{0:T(512)} %param.6) | copy-start | bytes 4612
  96.5 14.7 %copy-start = (f32[1,2,1,160,384]{4,1,3,2,0:T(2,128)}, f32[1,2,1,160,384]{4,1,3,2,0:T(2,128)S(1)}, u32[]{:S(2)}) copy-start(f32[1,2,1,160,384]{4,1,3,2,0:T(2,128)S(1)} %slice.41) | copy-start | bytes 1474564
  116.8 7.5 %slice-start.2 = ((s8[7962624]{0:T(1024)(128)(4,1)}), s8[4194304]{0:T(1024)(128)(4,1)S(1)}, s32[]{:S(2)}) async-start(s8[7962624]{0:T(1024)(128)(4,1)} %bitcast.108), calls=%async_computation.3 | async-start | bytes 8388608
  122.6 2.1 %slice-start.3 = ((s8[7962624]{0:T(1024)(128)(4,1)}), s8[3768320]{0:T(1024)(128)(4,1)S(1)}, s32[]{:S(2)}) async-start(s8[7962624]{0:T(1024)(128)(4,1)} %bitcast.108), calls=%async_computation.4 | async-start | bytes 7536640
  132.8 1.9 %copy-start.1 = (f32[1,2,1,160,384]{4,1,3,2,0:T(2,128)S(1)}, f32[1,2,1,160,384]{4,1,3,2,0:T(2,128)}, u32[]{:S(2)}) copy-start(f32[1,2,1,160,384]{4,1,3,2,0:T(2,128)} %copy-done) | copy-start | bytes 1474564
  132.8 1.9 %copy-start.3 = (bf16[1,2,160,384]{3,2,1,0:T(8,128)(2,1)S(1)}, bf16[1,2,160,384]{3,2,1,0:T(8,128)(2,1)}, u32[]{:S(2)}) copy-start(bf16[1,2,160,384]{3,2,1,0:T(8,128)(2,1)} %param.5) | copy-start | bytes 737284
  132.8 1.9 %copy-start.5 = (bf16[1,2,160,384]{3,2,1,0:T(8,128)(2,1)S(1)}, bf16[1,2,160,384]{3,2,1,0:T(8,128)(2,1)}, u32[]{:S(2)}) copy-start(bf16[1,2,160,384]{3,2,1,0:T(8,128)(2,1)} %param.9) | copy-start | bytes 737284
  132.8 1.9 %copy-start.7 = (f32[384]{0:T(512)S(1)}, f32[384]{0:T(512)}, u32[]{:S(2)}) copy-start(f32[384]{0:T(512)} %param.7) | copy-start | bytes 4612

commit v12 on v10

--- a/solution.py
+++ b/solution.py
@@ -173,22 +173,6 @@
         axis=0,
     )
     return lax.dynamic_slice_in_dim(relative, (count - 1 - position) * size, count * size, 0)
-
-
-def place_frames(groups, offsets, frame_total, padded_cols):
-    position = lax.axis_index("tm")
-    _, row_total, _, channels = groups[0].shape
-    framed = jnp.zeros(
-        (frame_total + 2, row_total + 2, padded_cols, channels), groups[0].dtype
-    )
-    writes = [
-        (abs(offset), group[index : index + 1], offset)
-        for group, shifts in zip(groups, offsets)
-        for index, offset in enumerate(shifts)
-    ]
-    for _, piece, offset in sorted(writes, key=lambda item: -item[0]):
-        framed = lax.dynamic_update_slice(framed, piece, (2 + position + offset, 1, 1, 0))
-    return framed
 
 
 def local(latents, gain, bias, weight, cotangent):
@@ -213,15 +197,10 @@
     groups = gather_frames(jnp.concatenate([hidden, cotangent], axis=-1))
     both_frames = in_order(groups)
     if len(groups) <= 4:
-        framed = place_frames(
-            [gather_rows(group[..., :channels], height_count) for group in groups],
-            [[0]] + [[-step, step] for step in range(1, len(groups))],
-            total_frames,
-            padded_cols,
-        )
+        hidden_all = in_order([gather_rows(group[..., :channels], height_count) for group in groups])
     else:
         hidden_all = gather_rows(both_frames[..., :channels], height_count)
-        framed = jnp.pad(hidden_all, ((2, 0), (1, 1), (1, right_pad), (0, 0)))
+    framed = jnp.pad(hidden_all, ((2, 0), (1, 1), (1, right_pad), (0, 0)))
 
     cot_frames = both_frames[..., channels:]
     cot_all = lax.all_to_all(cot_frames, "height", split_axis=3, concat_axis=1, tiled=True)

time: 188 us -> 134 us (0.71)
  local copies, waits for them, and re-layouts: 66.7 us -> 19.6 us
  waiting for transfers between devices: 38.5 us -> 34.6 us
    dynamic_update_slice x7 -> x0, local copies, waits for them, and re-layouts: 42.9 us -> none  [place_frames(): lax.dynamic_update_slice(framed, piece, (2 + position + offset, 1, 1, 0))]
    ppermute x3, waiting for transfers between devices: 15.6 us -> 9.91 us  [gather_frames(): falling = lax.ppermute(falling, 'tm', down)]
    concatenate x4 -> x1, other arithmetic: 4 us -> 0.19 us  [in_order(): jnp.concatenate([groups[step][:size] for step in reversed(range(1, count)...]
    broadcast_in_dim x1 -> x0, local copies, waits for them, and re-layouts: 3.69 us -> none  [place_frames(): jnp.zeros((frame_total + 2, row_total + 2, padded_cols, channels), groups...]
    conv_general_dilated x1, matrix products: 7.23 us -> 3.85 us  [forward_conv(): lax.conv_general_dilated(window[None], cube, (1, 1, 1), 'VALID', dimensio...]
    dot_general x3, matrix products: 5.5 us -> 7.55 us  [block_weight_grad(): lax.dot_general(shifted, slab, (((0, 1, 2), (0, 1, 2)), ((), ())), prefer...]
    unnamed x53 -> x49, local copies, waits for them, and re-layouts: 2.99 us -> 4.47 us
  transfers between devices with their start and end apart: 17 -> 17, of which waited for: 7 -> 6; matrix products, arithmetic and copies ran while one was open for 21% -> 28% of each run, Pallas kernels for 0% -> 0%
where the time goes in v12:
time: 134 us; the launch traced here: 132 us
  waiting for transfers between devices  34.6 us (26%)
  starting transfers between devices  31 us (23%)
  other arithmetic  27.3 us (20%)
  local copies, waits for them, and re-layouts  19.6 us (15%)
  matrix products  18.5 us (14%)
  between operations  1.36 us (1%)
    ppermute x3, waiting for transfers between devices, gather_frames(): rising = lax.ppermute(rising, 'tm', up)  18.7 us
    ppermute x3, starting transfers between devices, gather_frames(): rising = lax.ppermute(rising, 'tm', up)  12.3 us
    ppermute x3, waiting for transfers between devices, gather_frames(): falling = lax.ppermute(falling, 'tm', down)  9.91 us
    dot_general x3, matrix products, block_weight_grad(): lax.dot_general(shifted, slab, (((0, 1, 2), (0, 1, 2)), ((), ())), prefer...  7.55 us
    conv_general_dilated x1, matrix products, backward_conv(): lax.conv_general_dilated(window[None], jnp.flip(cube, (0, 1, 2)), (1, 1,...  7.08 us
    select_n x8, other arithmetic, gather_rows(): jnp.where(first, jnp.concatenate([ours, theirs], axis=1), jnp.concatenate...  6.7 us
    concatenate x4, other arithmetic, gather_rows(): stacked = jnp.concatenate(mine, axis=1)  6.35 us
    all_to_all x1, waiting for transfers between devices, local(): lax.all_to_all(cot_frames, 'height', split_axis=3, concat_axis=1, tiled=T...  5.81 us
  transfers between devices with their start and end apart: 17, of which 6 were waited for; matrix products, arithmetic and copies ran while one was open for 28% of the time, Pallas kernels for 0%

profile of v12, /device:TPU:0, one launch (start us, length us, event | category | flops | bytes accessed | tf_op | source)
XLA Modules:
  0.0 132.4 jit_solution(3190837944987266904)
XLA Ops:
  0.6 1.1 fusion.75
  1.7 1.2 multiply_convert_fusion
  3.0 3.0 %collective-permute-start.12 = (bf16[1,2,160,384]{3,2,1,0:T(8,128)(2,1)S(1)}, bf16[1,2,160,384]{3,2,1,0:T(8,128)(2,1)S(1)}, u32[]{:S(2)}, u32[]{:S(2)}) collective-permute-start(bf16[1,2,160,384]{3,2,1,0:T(8,128)(2,1)S(1)} %multiply_convert_fusion), channel_id=1, source_target_pairs={{0,2},{1,3},{2,0},{3,1},{4,6},{5,7},{6,4},{7,5},{8,10},{9,11},{10,... | collective-permute-start | bytes 737288 | tf_op jit(solution)/shard_map/ppermute | solution.py:123
  6.0 1.0 pad_maximum_fusion.19
  6.9 3.5 %collective-permute-start = (bf16[1,2,160,768]{3,2,1,0:T(8,128)(2,1)S(1)}, bf16[1,2,160,768]{3,2,1,0:T(8,128)(2,1)S(1)}, u32[]{:S(2)}, u32[]{:S(2)}) collective-permute-start(bf16[1,2,160,768]{3,2,1,0:T(8,128)(2,1)S(1)} %pad_maximum_fusion.19), channel_id=1, source_target_pairs={{0,4},{4,8},{8,12},{1,5},{5,9},{9,13},{2,6},{6,10},{10,14},{3,7},{... | collective-permute-start | bytes 1474568 | tf_op jit(solution)/shard_map/ppermute | solution.py:159
  10.5 1.3 collective-permute-start.3
  11.9 0.8 pad_maximum_fusion.14
  12.8 7.9 %collective-permute-done = bf16[1,2,160,768]{3,2,1,0:T(8,128)(2,1)S(1)} collective-permute-done((bf16[1,2,160,768]{3,2,1,0:T(8,128)(2,1)S(1)}, bf16[1,2,160,768]{3,2,1,0:T(8,128)(2,1)S(1)}, u32[]{:S(2)}, u32[]{:S(2)}) %collective-permute-start) | collective-permute-done | bytes 491552 | tf_op jit(solution)/shard_map/ppermute | solution.py:159
  20.6 4.4 %collective-permute-start.1 = (bf16[1,2,160,768]{3,2,1,0:T(8,128)(2,1)S(1)}, bf16[1,2,160,768]{3,2,1,0:T(8,128)(2,1)S(1)}, u32[]{:S(2)}, u32[]{:S(2)}) collective-permute-start(bf16[1,2,160,768]{3,2,1,0:T(8,128)(2,1)S(1)} %collective-permute-done), channel_id=1, source_target_pairs={{0,4},{4,8},{8,12},{1,5},{5,9},{9,13},{2,6},{6,10},{10,14},{3,7},{... | collective-permute-start | bytes 1474568 | tf_op jit(solution)/shard_map/ppermute | solution.py:159
  25.1 0.6 collective-permute-start.10
  25.7 1.3 collective-permute-start.4
  27.2 7.1 %collective-permute-done.1 = bf16[1,2,160,768]{3,2,1,0:T(8,128)(2,1)S(1)} collective-permute-done((bf16[1,2,160,768]{3,2,1,0:T(8,128)(2,1)S(1)}, bf16[1,2,160,768]{3,2,1,0:T(8,128)(2,1)S(1)}, u32[]{:S(2)}, u32[]{:S(2)}) %collective-permute-start.1) | collective-permute-done | bytes 491552 | tf_op jit(solution)/shard_map/ppermute | solution.py:159
  34.3 4.4 %collective-permute-start.2 = (bf16[1,2,160,768]{3,2,1,0:T(8,128)(2,1)S(1)}, bf16[1,2,160,768]{3,2,1,0:T(8,128)(2,1)S(1)}, u32[]{:S(2)}, u32[]{:S(2)}) collective-permute-start(bf16[1,2,160,768]{3,2,1,0:T(8,128)(2,1)S(1)} %collective-permute-done.1), channel_id=1, source_target_pairs={{0,4},{4,8},{8,12},{1,5},{5,9},{9,13},{2,6},{6,10},{10,14},{3,7},{... | collective-permute-start | bytes 1474568 | tf_op jit(solution)/shard_map/ppermute | solution.py:159
  38.8 1.4 %fusion.79 = (bf16[1,4,160,384]{3,2,1,0:T(8,128)(2,1)}, bf16[1,4,160,384]{3,2,1,0:T(8,128)(2,1)}) fusion(s32[]{:T(128)S(6)} %select_n.170, bf16[1,4,160,384]{3,2,1,0:T(8,128)(2,1)S(1)} %fusion.74, bf16[1,4,160,384]{3,2,1,0:T(8,128)(2,1)S(1)} %fusion.73, s32[]{:T(128)S(6)} %select_n.172), kind=kLoop, calls=%fused_computation.124 | loop fusion | flops 491520 | bytes 1966088 | tf_op jit(solution)/shard_map/concatenate | solution.py:142
  40.2 1.1 pad_maximum_fusion.8
  41.3 0.6 collective-permute-start.8
  41.9 1.3 collective-permute-start.5
  43.2 3.8 %collective-permute-done.2 = bf16[1,2,160,768]{3,2,1,0:T(8,128)(2,1)S(1)} collective-permute-done((bf16[1,2,160,768]{3,2,1,0:T(8,128)(2,1)S(1)}, bf16[1,2,160,768]{3,2,1,0:T(8,128)(2,1)S(1)}, u32[]{:S(2)}, u32[]{:S(2)}) %collective-permute-start.2) | collective-permute-done | bytes 491552 | tf_op jit(solution)/shard_map/ppermute | solution.py:159
  47.3 9.9 %collective-permute-done.5 = bf16[1,2,160,768]{3,2,1,0:T(8,128)(2,1)S(1)} collective-permute-done((bf16[1,2,160,768]{3,2,1,0:T(8,128)(2,1)S(1)}, bf16[1,2,160,768]{3,2,1,0:T(8,128)(2,1)S(1)}, u32[]{:S(2)}, u32[]{:S(2)}) %collective-permute-start.5) | collective-permute-done | bytes 491552 | tf_op jit(solution)/shard_map/ppermute | solution.py:160
  57.2 0.8 copy-done.10
  58.1 3.1 %copy.33 = bf16[4,2,160,384]{2,1,0,3:T(2,128)(2,1)} copy(bf16[4,2,160,384]{3,2,1,0:T(8,128)(2,1)S(1)} %constant_dynamic-slice_fusion) | data formatting | bytes 1966080 | tf_op jit(solution)/shard_map/slice | solution.py:205
  61.2 1.0 pad_dynamic-slice_fusion.17
  62.2 1.3 collective-permute-start.15
  63.5 3.8 %collective-permute-start.14 = (bf16[3,1,160,384]{3,2,1,0:T(8,128)(2,1)}, bf16[3,1,160,384]{3,2,1,0:T(8,128)(2,1)}, u32[]{:S(2)}, u32[]{:S(2)}) collective-permute-start(bf16[3,1,160,384]{3,2,1,0:T(8,128)(2,1)} %get-tuple-element.12), channel_id=1, source_target_pairs={{0,1},{1,2},{2,3},{4,5},{5,6},{6,7},{8,9},{9,10},{10,11},{12,13},{... | collective-permute-start | bytes 1105928 | tf_op jit(solution)/shard_map/ppermute | solution.py:23
  67.3 0.8 pad_maximum_fusion.18
  68.1 1.5 %collective-permute-start.6 = (bf16[2,2,160,384]{3,2,1,0:T(8,128)(2,1)}, bf16[2,2,160,384]{3,2,1,0:T(8,128)(2,1)}, u32[]{:S(2)}, u32[]{:S(2)}) collective-permute-start(bf16[2,2,160,384]{3,2,1,0:T(8,128)(2,1)} %pad_maximum_fusion.18), channel_id=1, source_target_pairs={{0,2},{1,3},{2,0},{3,1},{4,6},{5,7},{6,4},{7,5},{8,10},{9,11},{10,... | collective-permute-start | bytes 1474568 | tf_op jit(solution)/shard_map/ppermute | solution.py:123
  69.6 2.1 %pad_maximum_fusion.5 = bf16[2,4,160,384]{3,2,1,0:T(8,128)(2,1)} fusion(bf16[2,2,160,384]{3,2,1,0:T(8,128)(2,1)} %collective-permute-done.8, bf16[2,2,160,384]{3,2,1,0:T(8,128)(2,1)S(1)} %pad_maximum_fusion.17), kind=kLoop, calls=%fused_computation.73 | loop fusion | flops 491520 | bytes 1966080 | tf_op jit(solution)/shard_map/concatenate | solution.py:128
  71.7 3.6 %all-to-all-start = ((bf16[4,2,160,384]{2,1,0,3:T(2,128)(2,1)}), bf16[4,2,160,384]{2,1,0,3:T(2,128)(2,1)S(1)}, u32[]{:S(2)}, u32[]{:S(2)}) async-start(bf16[4,2,160,384]{2,1,0,3:T(2,128)(2,1)} %copy.33), calls=%async_computation | async-start | bytes 3145728 | tf_op jit(solution)/shard_map/all_to_all | solution.py:206
  75.5 1.6 %fusion.30 = bf16[3,4,1,162,384]{4,3,1,0,2:T(8,128)(2,1)S(1)} fusion(bf16[3,1,160,384]{3,2,1,0:T(8,128)(2,1)} %collective-permute-done.15, bf16[3,2,160,384]{3,2,1,0:T(8,128)(2,1)S(1)} %pad_dynamic-slice_fusion.18, bf16[3,1,160,384]{3,2,1,0:T(8,128)(2,1)} %collective-permute-done.14), kind=kLoop, calls=%fused_computation.54 | loop fusion | flops 9704448 | bytes 2967552 | tf_op jit(solution)/shard_map/broadcast_in_dim | solution.py:58
  77.0 0.6 copy.49
  77.6 0.6 pad.32.clone
  78.2 0.2 copy.30
  78.5 7.1 %fusion.41 = f32[1,2,8,21,384]{4,2,3,1,0:T(8,128)S(1)} fusion(bf16[3,3,3,384,384]{4,3,2,1,0:T(8,128)(2,1)} %bitcast.105, bf16[3,4,1,7,2,384]{5,3,4,1,0,2:T(8,128)(2,1)S(1)} %slice.108, bf16[3,4,1,8,21,384]{5,3,4,1,0,2:T(8,128)(2,1)S(1)} %copy.30, pred[8,21]{0,1:T(8,128)(4,1)S(1)} %copy-done.18), kind=kOutput, calls=%fused_computation.67 | convolution fusion | flops 2680657920 | bytes 10156200 | tf_op jit(solution)/shard_map/conv_general_dilated | solution.py:57
  85.6 0.3 copy.31
  86.1 0.4 multiply_reduce_fusion
  86.5 2.3 %pad_maximum_fusion.2 = bf16[2,4,160,384]{3,2,1,0:T(8,128)(2,1)} fusion(bf16[2,2,160,384]{3,2,1,0:T(8,128)(2,1)} %collective-permute-done.6, bf16[2,2,160,384]{3,2,1,0:T(8,128)(2,1)} %pad_maximum_fusion.18), kind=kLoop, calls=%fused_computation.70 | loop fusion | flops 491520 | bytes 1966080 | tf_op jit(solution)/shard_map/concatenate | solution.py:128
  88.8 0.5 collective-permute-start.7
  89.3 1.3 fusion.95
  90.6 1.1 fusion.50
  91.7 1.1 fusion.51
  92.8 5.8 %all-to-all-done = bf16[4,2,160,384]{2,1,0,3:T(2,128)(2,1)S(1)} async-done(((bf16[4,2,160,384]{2,1,0,3:T(2,128)(2,1)}), bf16[4,2,160,384]{2,1,0,3:T(2,128)(2,1)S(1)}, u32[]{:S(2)}, u32[]{:S(2)}) %all-to-all-start) | async-done | bytes 983072 | tf_op jit(solution)/shard_map/all_to_all | solution.py:206
  98.7 2.1 %copy.34 = bf16[4,2,160,4,96]{4,2,1,3,0:T(8,128)(2,1)S(1)} copy(bf16[4,2,160,4,96]{2,1,0,4,3:T(2,128)(2,1)S(1)} %bitcast.96) | data formatting | bytes 1966080 | tf_op jit(solution)/shard_map/all_to_all | solution.py:206
  100.8 0.9 pad_bitcast_fusion.2
  101.8 1.4 %fusion.96 = (bf16[2,2,160,384]{3,2,1,0:T(8,128)(2,1)S(1)}, bf16[2,2,160,384]{3,2,1,0:T(8,128)(2,1)S(1)}) fusion(bf16[2,4,160,384]{3,2,1,0:T(8,128)(2,1)} %collective-permute-done.9), kind=kLoop, calls=%fused_computation.162 | loop fusion | bytes 1966080 | tf_op jit(solution)/shard_map/slice | solution.py:134
  103.4 1.4 %fusion.53 = bf16[2,4,160,384]{3,2,1,0:T(8,128)(2,1)S(1)} fusion(bf16[2,2,160,384]{3,2,1,0:T(8,128)(2,1)} %collective-permute-done.8, bf16[2,2,160,384]{3,2,1,0:T(8,128)(2,1)S(1)} %get-tuple-element.19, pred[]{:T(512)S(6)} %eq.22), kind=kLoop, calls=%fused_computation.88 | loop fusion | flops 1474560 | bytes 1966081 | tf_op jit(solution)/shard_map/jit(_where)/select_n | solution.py:136
  104.8 1.7 %fusion.62 = (bf16[2,4,160,384]{3,2,1,0:T(8,128)(2,1)S(1)}, bf16[2,4,160,384]{3,2,1,0:T(8,128)(2,1)S(1)}, bf16[2,4,160,384]{3,2,1,0:T(8,128)(2,1)S(1)}, bf16[2,4,160,384]{3,2,1,0:T(8,128)(2,1)S(1)}) fusion(s32[]{:T(128)S(6)} %select_n.172, bf16[2,4,160,384]{3,2,1,0:T(8,128)(2,1)S(1)} %copy-done.5, bf16[2,4,160,384]{3,2,1,0:T(8,128)(2,1)S(1)} %copy-done.4, ...), kind=kLoop, calls=%fused_computation.97 | loop fusion | flops 1966080 | bytes 7864328 | tf_op jit(solution)/shard_map/concatenate | solution.py:142
  106.5 1.3 fusion.97
  107.8 1.4 %fusion.54 = bf16[2,4,160,384]{3,2,1,0:T(8,128)(2,1)S(1)} fusion(bf16[2,2,160,384]{3,2,1,0:T(8,128)(2,1)} %pad_maximum_fusion.18, bf16[2,2,160,384]{3,2,1,0:T(8,128)(2,1)S(1)} %get-tuple-element.20, pred[]{:T(512)S(6)} %eq.22), kind=kLoop, calls=%fused_computation.89 | loop fusion | flops 1474560 | bytes 1966081 | tf_op jit(solution)/shard_map/jit(_where)/select_n | solution.py:136
  109.1 1.4 %fusion.55 = bf16[2,4,160,384]{3,2,1,0:T(8,128)(2,1)S(1)} fusion(bf16[2,2,160,384]{3,2,1,0:T(8,128)(2,1)} %collective-permute-done.6, bf16[2,2,160,384]{3,2,1,0:T(8,128)(2,1)S(1)} %get-tuple-element.21, pred[]{:T(512)S(6)} %eq.22), kind=kLoop, calls=%fused_computation.90 | loop fusion | flops 1474560 | bytes 1966081 | tf_op jit(solution)/shard_map/jit(_where)/select_n | solution.py:136
  110.5 0.8 fusion.66
  111.8 0.6 copy-done.12
  113.4 0.4 constant_dynamic-slice_fusion.1
  113.8 0.5 fusion.28
  114.3 0.6 copy.48
  114.9 0.6 pad.30.clone
  115.8 0.2 slice-done
  116.0 1.3 slice-done.1
  117.3 3.9 %fusion.44 = f32[1,2,8,21,384]{4,2,3,1,0:T(8,128)S(1)} fusion(bf16[3,3,3,384,384]{4,3,2,1,0:T(8,128)(2,1)S(1)} %bitcast.108, bf16[3,4,1,7,2,384]{5,3,4,1,0,2:T(8,128)(2,1)S(1)} %slice.106, bf16[3,4,1,8,21,384]{5,3,4,1,0,2:T(8,128)(2,1)S(1)} %copy.25, pred[8,21]{0,1:T(8,128)(4,1)S(1)} %copy-done.18), kind=kOutput, calls=%fused_computation.68 | convolution fusion | flops 2680657920 | bytes 10156200 | tf_op jit(solution)/shard_map/conv_general_dilated | solution.py:44
  121.2 0.5 copy.26
  121.8 2.5 %fusion.38 = f32[3,12,8,384]{3,2,1,0:T(8,128)S(1)} fusion(s32[]{:T(128)S(6)} %select_n.185, s32[]{:T(128)S(6)} %select_n.187, bf16[4,8,160,384]{3,2,1,0:T(8,128)(2,1)S(1)} %constant_dynamic-slice_fusion.1, bf16[4,8,168,1,96]{4,2,1,3,0:T(8,128)(2,1)S(1)} %get-tuple-element.10, bf16[4,8,168,1,96]{4,2,1,3,0:T(8,128)(2,1)S(1)} %get-tuple-element.11, ...), kind=kOutput, calls=%fused_computation.66 | convolution fusion | flops 1192181760 | bytes 7471112 | tf_op jit(solution)/shard_map/dot_general | solution.py:106
  124.4 2.5 %fusion.35 = f32[3,12,8,384]{3,2,1,0:T(8,128)S(1)} fusion(s32[]{:T(128)S(6)} %select_n.189, s32[]{:T(128)S(6)} %select_n.191, bf16[4,8,160,384]{3,2,1,0:T(8,128)(2,1)S(1)} %constant_dynamic-slice_fusion.1, bf16[4,8,168,1,96]{4,2,1,3,0:T(8,128)(2,1)S(1)} %get-tuple-element.10, bf16[4,8,168,1,96]{4,2,1,3,0:T(8,128)(2,1)S(1)} %get-tuple-element.11, ...), kind=kOutput, calls=%fused_computation.65 | convolution fusion | flops 1192181760 | bytes 7471112 | tf_op jit(solution)/shard_map/dot_general | solution.py:106
  127.0 2.5 %fusion.32 = f32[3,12,8,384]{3,2,1,0:T(8,128)S(1)} fusion(s32[]{:T(128)S(6)} %select_n.193, s32[]{:T(128)S(6)} %select_n.195, bf16[4,8,160,384]{3,2,1,0:T(8,128)(2,1)S(1)} %constant_dynamic-slice_fusion.1, bf16[4,8,168,1,96]{4,2,1,3,0:T(8,128)(2,1)S(1)} %get-tuple-element.10, bf16[4,8,168,1,96]{4,2,1,3,0:T(8,128)(2,1)S(1)} %get-tuple-element.11, ...), kind=kOutput, calls=%fused_computation.64 | convolution fusion | flops 1192181760 | bytes 7471112 | tf_op jit(solution)/shard_map/dot_general | solution.py:106
  129.5 1.2 add_convert_fusion
  130.7 1.6 %fusion.49 = f32[2592,96]{0,1:T(8,128)} fusion(s32[]{:T(128)S(6)} %select_n.196, f32[1152,96]{0,1:T(8,128)S(1)} %bitcast.102, f32[1152,96]{0,1:T(8,128)S(1)} %bitcast.103, f32[1152,96]{0,1:T(8,128)S(1)} %bitcast.104), kind=kLoop, calls=%fused_computation.84 | loop fusion | flops 746496 | bytes 2322436 | tf_op jit(solution)/shard_map/mul | solution.py:218
  (86 shorter events, 3.4 us)
Async XLA Ops:
  3.0 9.0 %collective-permute-start.12 = (bf16[1,2,160,384]{3,2,1,0:T(8,128)(2,1)S(1)}, bf16[1,2,160,384]{3,2,1,0:T(8,128)(2,1)S(1)}, u32[]{:S(2)}, u32[]{:S(2)}) collective-permute-start(bf16[1,2,160,384]{3,2,1,0:T(8,128)(2,1)S(1)} %multiply_convert_fusion), channel_id=1, source_target_pairs={{0,2},{1,3},{2,0},{3,1},{4,6},{5,7},{6,4},{7,5},{8,10},{9,11},{10,... | collective-permute-start | bytes 737288 | tf_op jit(solution)/shard_map/ppermute | solution.py:123
  6.9 13.7 %collective-permute-start = (bf16[1,2,160,768]{3,2,1,0:T(8,128)(2,1)S(1)}, bf16[1,2,160,768]{3,2,1,0:T(8,128)(2,1)S(1)}, u32[]{:S(2)}, u32[]{:S(2)}) collective-permute-start(bf16[1,2,160,768]{3,2,1,0:T(8,128)(2,1)S(1)} %pad_maximum_fusion.19), channel_id=1, source_target_pairs={{0,4},{4,8},{8,12},{1,5},{5,9},{9,13},{2,6},{6,10},{10,14},{3,7},{... | collective-permute-start | bytes 1474568 | tf_op jit(solution)/shard_map/ppermute | solution.py:159
  10.5 14.6 %collective-permute-start.3 = (bf16[1,2,160,768]{3,2,1,0:T(8,128)(2,1)S(1)}, bf16[1,2,160,768]{3,2,1,0:T(8,128)(2,1)S(1)}, u32[]{:S(2)}, u32[]{:S(2)}) collective-permute-start(bf16[1,2,160,768]{3,2,1,0:T(8,128)(2,1)S(1)} %pad_maximum_fusion.19), channel_id=1, source_target_pairs={{4,0},{8,4},{12,8},{5,1},{9,5},{13,9},{6,2},{10,6},{14,10},{7,3},{... | collective-permute-start | bytes 1474568 | tf_op jit(solution)/shard_map/ppermute | solution.py:160
  12.8 14.2 %collective-permute-start.13 = (bf16[1,4,160,384]{3,2,1,0:T(8,128)(2,1)}, bf16[1,4,160,384]{3,2,1,0:T(8,128)(2,1)S(1)}, u32[]{:S(2)}, u32[]{:S(2)}) collective-permute-start(bf16[1,4,160,384]{3,2,1,0:T(8,128)(2,1)} %pad_maximum_fusion.14), channel_id=1, source_target_pairs={{0,1},{1,0},{2,3},{3,2},{4,5},{5,4},{6,7},{7,6},{8,9},{9,8},{10,11... | collective-permute-start | bytes 1474568 | tf_op jit(solution)/shard_map/ppermute | solution.py:129
  20.6 13.7 %collective-permute-start.1 = (bf16[1,2,160,768]{3,2,1,0:T(8,128)(2,1)S(1)}, bf16[1,2,160,768]{3,2,1,0:T(8,128)(2,1)S(1)}, u32[]{:S(2)}, u32[]{:S(2)}) collective-permute-start(bf16[1,2,160,768]{3,2,1,0:T(8,128)(2,1)S(1)} %collective-permute-done), channel_id=1, source_target_pairs={{0,4},{4,8},{8,12},{1,5},{5,9},{9,13},{2,6},{6,10},{10,14},{3,7},{... | collective-permute-start | bytes 1474568 | tf_op jit(solution)/shard_map/ppermute | solution.py:159
  25.1 15.1 %collective-permute-start.10 = (bf16[2,2,160,384]{3,2,1,0:T(8,128)(2,1)S(1)}, bf16[2,2,160,384]{3,2,1,0:T(8,128)(2,1)S(1)}, u32[]{:S(2)}, u32[]{:S(2)}) collective-permute-start(bf16[2,2,160,384]{3,2,1,0:T(8,128)(2,1)S(1)} %pad_maximum_fusion.16), channel_id=1, source_target_pairs={{0,2},{1,3},{2,0},{3,1},{4,6},{5,7},{6,4},{7,5},{8,10},{9,11},{10,... | collective-permute-start | bytes 1474568 | tf_op jit(solution)/shard_map/ppermute | solution.py:123
  25.7 15.6 %collective-permute-start.4 = (bf16[1,2,160,768]{3,2,1,0:T(8,128)(2,1)S(1)}, bf16[1,2,160,768]{3,2,1,0:T(8,128)(2,1)S(1)}, u32[]{:S(2)}, u32[]{:S(2)}) collective-permute-start(bf16[1,2,160,768]{3,2,1,0:T(8,128)(2,1)S(1)} %collective-permute-done.3), channel_id=1, source_target_pairs={{4,0},{8,4},{12,8},{5,1},{9,5},{13,9},{6,2},{10,6},{14,10},{7,3},{... | collective-permute-start | bytes 1474568 | tf_op jit(solution)/shard_map/ppermute | solution.py:160
  34.3 12.7 %collective-permute-start.2 = (bf16[1,2,160,768]{3,2,1,0:T(8,128)(2,1)S(1)}, bf16[1,2,160,768]{3,2,1,0:T(8,128)(2,1)S(1)}, u32[]{:S(2)}, u32[]{:S(2)}) collective-permute-start(bf16[1,2,160,768]{3,2,1,0:T(8,128)(2,1)S(1)} %collective-permute-done.1), channel_id=1, source_target_pairs={{0,4},{4,8},{8,12},{1,5},{5,9},{9,13},{2,6},{6,10},{10,14},{3,7},{... | collective-permute-start | bytes 1474568 | tf_op jit(solution)/shard_map/ppermute | solution.py:159
  40.2 7.0 %copy-start.7 = (bf16[1,2,160,384]{3,2,1,0:T(8,128)(2,1)S(1)}, bf16[1,2,160,384]{3,2,1,0:T(8,128)(2,1)}, u32[]{:S(2)}) copy-start(bf16[1,2,160,384]{3,2,1,0:T(8,128)(2,1)} %param.9) | copy-start | bytes 737284
  40.2 6.9 %copy-start.14 = (bf16[2,2,160,384]{3,2,1,0:T(8,128)(2,1)}, bf16[2,2,160,384]{3,2,1,0:T(8,128)(2,1)S(1)}, u32[]{:S(2)}) copy-start(bf16[2,2,160,384]{3,2,1,0:T(8,128)(2,1)S(1)} %collective-permute-done.10) | copy-start | bytes 1474564
  41.3 48.0 %collective-permute-start.11 = (bf16[2,4,160,384]{3,2,1,0:T(8,128)(2,1)}, bf16[2,4,160,384]{3,2,1,0:T(8,128)(2,1)}, u32[]{:S(2)}, u32[]{:S(2)}) collective-permute-start(bf16[2,4,160,384]{3,2,1,0:T(8,128)(2,1)} %pad_maximum_fusion.8), channel_id=1, source_target_pairs={{0,1},{1,0},{2,3},{3,2},{4,5},{5,4},{6,7},{7,6},{8,9},{9,8},{10,11... | collective-permute-start | bytes 2949128 | tf_op jit(solution)/shard_map/ppermute | solution.py:129
  41.3 28.2 %copy-start.2 = (bf16[2,2,160,384]{3,2,1,0:T(8,128)(2,1)}, bf16[2,2,160,384]{3,2,1,0:T(8,128)(2,1)S(1)}, u32[]{:S(2)}) copy-start(bf16[2,2,160,384]{3,2,1,0:T(8,128)(2,1)S(1)} %pad_maximum_fusion.17) | copy-start | bytes 1474564
  41.3 28.2 %collective-permute-start.8 = (bf16[2,2,160,384]{3,2,1,0:T(8,128)(2,1)S(1)}, bf16[2,2,160,384]{3,2,1,0:T(8,128)(2,1)}, u32[]{:S(2)}, u32[]{:S(2)}) collective-permute-start(bf16[2,2,160,384]{3,2,1,0:T(8,128)(2,1)S(1)} %pad_maximum_fusion.17), channel_id=1, source_target_pairs={{0,2},{1,3},{2,0},{3,1},{4,6},{5,7},{6,4},{7,5},{8,10},{9,11},{10,... | collective-permute-start | bytes 1474568 | tf_op jit(solution)/shard_map/ppermute | solution.py:123
  41.9 15.2 %collective-permute-start.5 = (bf16[1,2,160,768]{3,2,1,0:T(8,128)(2,1)S(1)}, bf16[1,2,160,768]{3,2,1,0:T(8,128)(2,1)S(1)}, u32[]{:S(2)}, u32[]{:S(2)}) collective-permute-start(bf16[1,2,160,768]{3,2,1,0:T(8,128)(2,1)S(1)} %collective-permute-done.4), channel_id=1, source_target_pairs={{4,0},{8,4},{12,8},{5,1},{9,5},{13,9},{6,2},{10,6},{14,10},{7,3},{... | collective-permute-start | bytes 1474568 | tf_op jit(solution)/shard_map/ppermute | solution.py:160
  47.0 10.2 %copy-start.8 = (bf16[1,2,160,768]{3,2,1,0:T(8,128)(2,1)}, bf16[1,2,160,768]{3,2,1,0:T(8,128)(2,1)S(1)}, u32[]{:S(2)}) copy-start(bf16[1,2,160,768]{3,2,1,0:T(8,128)(2,1)S(1)} %collective-permute-done.2) | copy-start | bytes 1474564
  57.2 0.8 copy-start.10
  58.0 9.3 %copy-start.9 = (bf16[1,2,160,768]{3,2,1,0:T(8,128)(2,1)S(1)}, bf16[1,2,160,768]{3,2,1,0:T(8,128)(2,1)}, u32[]{:S(2)}) copy-start(bf16[1,2,160,768]{3,2,1,0:T(8,128)(2,1)} %copy-done.8) | copy-start | bytes 1474564
  58.0 9.3 %copy-start.11 = (bf16[1,2,160,768]{3,2,1,0:T(8,128)(2,1)S(1)}, bf16[1,2,160,768]{3,2,1,0:T(8,128)(2,1)}, u32[]{:S(2)}) copy-start(bf16[1,2,160,768]{3,2,1,0:T(8,128)(2,1)} %copy-done.10) | copy-start | bytes 1474564
  62.2 13.3 %collective-permute-start.15 = (bf16[3,1,160,384]{3,2,1,0:T(8,128)(2,1)}, bf16[3,1,160,384]{3,2,1,0:T(8,128)(2,1)}, u32[]{:S(2)}, u32[]{:S(2)}) collective-permute-start(bf16[3,1,160,384]{3,2,1,0:T(8,128)(2,1)} %get-tuple-element.13), channel_id=1, source_target_pairs={{1,0},{2,1},{3,2},{5,4},{6,5},{7,6},{9,8},{10,9},{11,10},{13,12},{... | collective-permute-start | bytes 1105928 | tf_op jit(solution)/shard_map/ppermute | solution.py:25
  63.5 12.0 %collective-permute-start.14 = (bf16[3,1,160,384]{3,2,1,0:T(8,128)(2,1)}, bf16[3,1,160,384]{3,2,1,0:T(8,128)(2,1)}, u32[]{:S(2)}, u32[]{:S(2)}) collective-permute-start(bf16[3,1,160,384]{3,2,1,0:T(8,128)(2,1)} %get-tuple-element.12), channel_id=1, source_target_pairs={{0,1},{1,2},{2,3},{4,5},{5,6},{6,7},{8,9},{9,10},{10,11},{12,13},{... | collective-permute-start | bytes 1105928 | tf_op jit(solution)/shard_map/ppermute | solution.py:23
  68.1 18.4 %collective-permute-start.6 = (bf16[2,2,160,384]{3,2,1,0:T(8,128)(2,1)}, bf16[2,2,160,384]{3,2,1,0:T(8,128)(2,1)}, u32[]{:S(2)}, u32[]{:S(2)}) collective-permute-start(bf16[2,2,160,384]{3,2,1,0:T(8,128)(2,1)} %pad_maximum_fusion.18), channel_id=1, source_target_pairs={{0,2},{1,3},{2,0},{3,1},{4,6},{5,7},{6,4},{7,5},{8,10},{9,11},{10,... | collective-permute-start | bytes 1474568 | tf_op jit(solution)/shard_map/ppermute | solution.py:123
  71.7 30.0 %collective-permute-start.9 = (bf16[2,4,160,384]{3,2,1,0:T(8,128)(2,1)}, bf16[2,4,160,384]{3,2,1,0:T(8,128)(2,1)}, u32[]{:S(2)}, u32[]{:S(2)}) collective-permute-start(bf16[2,4,160,384]{3,2,1,0:T(8,128)(2,1)} %pad_maximum_fusion.5), channel_id=1, source_target_pairs={{0,1},{1,0},{2,3},{3,2},{4,5},{5,4},{6,7},{7,6},{8,9},{9,8},{10,11... | collective-permute-start | bytes 2949128 | tf_op jit(solution)/shard_map/ppermute | solution.py:129
  71.7 26.9 %all-to-all-start = ((bf16[4,2,160,384]{2,1,0,3:T(2,128)(2,1)}), bf16[4,2,160,384]{2,1,0,3:T(2,128)(2,1)S(1)}, u32[]{:S(2)}, u32[]{:S(2)}) async-start(bf16[4,2,160,384]{2,1,0,3:T(2,128)(2,1)} %copy.33), calls=%async_computation | async-start | bytes 3145728 | tf_op jit(solution)/shard_map/all_to_all | solution.py:206
  77.6 0.9 copy-start.18
  78.5 7.6 %copy-start.6 = (bf16[1,2,160,384]{3,2,1,0:T(8,128)(2,1)S(1)}, bf16[1,2,160,384]{3,2,1,0:T(8,128)(2,1)}, u32[]{:S(2)}) copy-start(bf16[1,2,160,384]{3,2,1,0:T(8,128)(2,1)} %param.5) | copy-start | bytes 737284
  78.5 7.6 %copy-start.16 = (f32[384]{0:T(512)S(1)}, f32[384]{0:T(512)}, u32[]{:S(2)}) copy-start(f32[384]{0:T(512)} %param.6) | copy-start | bytes 4612
  86.1 5.7 %copy-start = (f32[1,2,1,160,384]{4,1,3,2,0:T(2,128)}, f32[1,2,1,160,384]{4,1,3,2,0:T(2,128)S(1)}, u32[]{:S(2)}) copy-start(f32[1,2,1,160,384]{4,1,3,2,0:T(2,128)S(1)} %slice.109) | copy-start | bytes 1474564
  86.5 5.2 %copy-start.15 = (bf16[2,2,160,384]{3,2,1,0:T(8,128)(2,1)S(1)}, bf16[2,2,160,384]{3,2,1,0:T(8,128)(2,1)}, u32[]{:S(2)}) copy-start(bf16[2,2,160,384]{3,2,1,0:T(8,128)(2,1)} %copy-done.14) | copy-start | bytes 1474564
  88.8 17.7 %collective-permute-start.7 = (bf16[2,4,160,384]{3,2,1,0:T(8,128)(2,1)}, bf16[2,4,160,384]{3,2,1,0:T(8,128)(2,1)}, u32[]{:S(2)}, u32[]{:S(2)}) collective-permute-start(bf16[2,4,160,384]{3,2,1,0:T(8,128)(2,1)} %pad_maximum_fusion.2), channel_id=1, source_target_pairs={{0,1},{1,0},{2,3},{3,2},{4,5},{5,4},{6,7},{7,6},{8,9},{9,8},{10,11... | collective-permute-start | bytes 2949128 | tf_op jit(solution)/shard_map/ppermute | solution.py:129
  100.8 2.4 %copy-start.3 = (bf16[2,2,160,384]{3,2,1,0:T(8,128)(2,1)S(1)}, bf16[2,2,160,384]{3,2,1,0:T(8,128)(2,1)}, u32[]{:S(2)}) copy-start(bf16[2,2,160,384]{3,2,1,0:T(8,128)(2,1)} %copy-done.2) | copy-start | bytes 1474564
  101.7 3.0 %copy-start.4 = (bf16[2,4,160,384]{3,2,1,0:T(8,128)(2,1)S(1)}, bf16[2,4,160,384]{3,2,1,0:T(8,128)(2,1)}, u32[]{:S(2)}) copy-start(bf16[2,4,160,384]{3,2,1,0:T(8,128)(2,1)} %fusion.50) | copy-start | bytes 2949124
  101.8 3.0 %copy-start.5 = (bf16[2,4,160,384]{3,2,1,0:T(8,128)(2,1)S(1)}, bf16[2,4,160,384]{3,2,1,0:T(8,128)(2,1)}, u32[]{:S(2)}) copy-start(bf16[2,4,160,384]{3,2,1,0:T(8,128)(2,1)} %fusion.51) | copy-start | bytes 2949124
  111.4 1.0 copy-start.12
  111.4 1.2 copy-start.13
  113.8 2.2 %slice-start = ((s8[7962624]{0:T(1024)(128)(4,1)}), s8[4194304]{0:T(1024)(128)(4,1)S(1)}, s32[]{:S(2)}) async-start(s8[7962624]{0:T(1024)(128)(4,1)} %bitcast.106), calls=%async_computation.1 | async-start | bytes 8388608
  114.3 3.0 %slice-start.1 = ((s8[7962624]{0:T(1024)(128)(4,1)}), s8[3768320]{0:T(1024)(128)(4,1)S(1)}, s32[]{:S(2)}) async-start(s8[7962624]{0:T(1024)(128)(4,1)} %bitcast.106), calls=%async_computation.2 | async-start | bytes 7536640
  127.0 2.6 %copy-start.1 = (f32[1,2,1,160,384]{4,1,3,2,0:T(2,128)S(1)}, f32[1,2,1,160,384]{4,1,3,2,0:T(2,128)}, u32[]{:S(2)}) copy-start(f32[1,2,1,160,384]{4,1,3,2,0:T(2,128)} %copy-done) | copy-start | bytes 1474564
  127.0 2.6 %copy-start.17 = (f32[384]{0:T(512)S(1)}, f32[384]{0:T(512)}, u32[]{:S(2)}) copy-start(f32[384]{0:T(512)} %param.7) | copy-start | bytes 4612

commit v13 on v9

--- a/solution.py
+++ b/solution.py
@@ -127,26 +127,13 @@
     ]
     stacked = jnp.concatenate(mine, axis=1)
     twins = lax.ppermute(stacked, "height", sibling)
-    block = 2 * row_count
-    relative = []
-    for step in reversed(range(chips)):
-        ours = stacked[:, step * row_count : (step + 1) * row_count]
-        theirs = twins[:, step * row_count : (step + 1) * row_count]
-        relative.append(
-            jnp.where(
-                first,
-                jnp.concatenate([ours, theirs], axis=1),
-                jnp.concatenate([theirs, ours], axis=1),
-            )
-        )
-    relative = jnp.concatenate(relative, axis=1)
-    return jnp.concatenate(
-        [
-            lax.dynamic_slice_in_dim(relative, ((place - chip - 1) % chips) * block, block, 1)
-            for place in range(chips)
-        ],
-        axis=1,
-    )
+    source = jnp.concatenate([stacked, twins], axis=1)
+    blocks = []
+    for place in range(height_count):
+        other = (place % 2 != core).astype(jnp.int32)
+        index = other * chips + (chip - place // 2) % chips
+        blocks.append(lax.dynamic_slice_in_dim(source, index * row_count, row_count, 1))
+    return jnp.concatenate(blocks, axis=1)
 
 
 def gather_frames(block):

time: 126 us -> 129 us (1.024)
  other arithmetic: 20.7 us -> 24.1 us
    concatenate x2, other arithmetic: 7.47 us -> 13.1 us  [the longest x1 11.1 us: gather_rows(): return jnp.concatenate(blocks, axis=1)]
    select_n x2 -> x0, other arithmetic: 2.19 us -> none  [gather_rows(): jnp.where(first, jnp.concatenate([ours, theirs], axis=1), jnp.concatenate...]
    slice x1 -> x0, local copies, waits for them, and re-layouts: 1.7 us -> none  [gather_rows(): theirs = twins[:, step * row_count:(step + 1) * row_count]]
  transfers between devices with their start and end apart: 11 -> 11, of which waited for: 6 -> 6; matrix products, arithmetic and copies ran while one was open for 18% -> 17% of each run, Pallas kernels for 0% -> 0%
where the time goes in v13:
time: 129 us; the launch traced here: 128 us
  waiting for transfers between devices  44.3 us (34%)
  starting transfers between devices  28 us (22%)
  other arithmetic  24.1 us (19%)
  local copies, waits for them, and re-layouts  17.4 us (13%)
  matrix products  13.1 us (10%)
    ppermute x3, waiting for transfers between devices, gather_frames(): rising = lax.ppermute(rising, 'tm', up)  24.7 us
    ppermute x3, starting transfers between devices, gather_frames(): rising = lax.ppermute(rising, 'tm', up)  13.8 us
    concatenate x1, other arithmetic, gather_rows(): return jnp.concatenate(blocks, axis=1)  11.1 us
    ppermute x1, waiting for transfers between devices, gather_rows(): lax.ppermute(own, 'height', [(i, (i + 2 * step) % height_count) for i in...  9.44 us
    all_to_all x1, waiting for transfers between devices, local(): lax.all_to_all(cot_frames, 'height', split_axis=3, concat_axis=1, tiled=T...  6.25 us
    dot_general x3, matrix products, block_weight_grad(): lax.dot_general(shifted, slab, (((0, 1, 2), (0, 1, 2)), ((), ())), prefer...  5.49 us
    ppermute x3, waiting for transfers between devices, gather_frames(): falling = lax.ppermute(falling, 'tm', down)  3.9 us
    ppermute x3, starting transfers between devices, gather_frames(): falling = lax.ppermute(falling, 'tm', down)  3.88 us
  transfers between devices with their start and end apart: 11, of which 6 were waited for; matrix products, arithmetic and copies ran while one was open for 17% of the time, Pallas kernels for 0%

profile of v13, /device:TPU:0, one launch (start us, length us, event | category | flops | bytes accessed | tf_op | source)
XLA Modules:
  0.0 128.1 jit_solution(10669173704709041825)
XLA Ops:
  0.6 0.0 copy-start.4
  0.6 1.1 fusion.70
  1.8 1.2 multiply_convert_fusion
  3.0 1.0 pad_maximum_fusion.3
  4.0 5.0 %collective-permute-start = (bf16[1,2,160,768]{3,2,1,0:T(8,128)(2,1)S(1)}, bf16[1,2,160,768]{3,2,1,0:T(8,128)(2,1)S(1)}, u32[]{:S(2)}, u32[]{:S(2)}) collective-permute-start(bf16[1,2,160,768]{3,2,1,0:T(8,128)(2,1)S(1)} %pad_maximum_fusion.3), channel_id=1, source_target_pairs={{0,4},{4,8},{8,12},{1,5},{5,9},{9,13},{2,6},{6,10},{10,14},{3,7},{... | collective-permute-start | bytes 1474568 | tf_op jit(solution)/shard_map/ppermute | solution.py:147
  9.0 1.3 %collective-permute-start.3 = (bf16[1,2,160,768]{3,2,1,0:T(8,128)(2,1)S(1)}, bf16[1,2,160,768]{3,2,1,0:T(8,128)(2,1)S(1)}, u32[]{:S(2)}, u32[]{:S(2)}) collective-permute-start(bf16[1,2,160,768]{3,2,1,0:T(8,128)(2,1)S(1)} %pad_maximum_fusion.3), channel_id=1, source_target_pairs={{4,0},{8,4},{12,8},{5,1},{9,5},{13,9},{6,2},{10,6},{14,10},{7,3},{... | collective-permute-start | bytes 1474568 | tf_op jit(solution)/shard_map/ppermute | solution.py:148
  10.3 9.1 %collective-permute-done = bf16[1,2,160,768]{3,2,1,0:T(8,128)(2,1)S(1)} collective-permute-done((bf16[1,2,160,768]{3,2,1,0:T(8,128)(2,1)S(1)}, bf16[1,2,160,768]{3,2,1,0:T(8,128)(2,1)S(1)}, u32[]{:S(2)}, u32[]{:S(2)}) %collective-permute-start) | collective-permute-done | bytes 491552 | tf_op jit(solution)/shard_map/ppermute | solution.py:147
  19.4 4.4 %collective-permute-start.1 = (bf16[1,2,160,768]{3,2,1,0:T(8,128)(2,1)S(1)}, bf16[1,2,160,768]{3,2,1,0:T(8,128)(2,1)S(1)}, u32[]{:S(2)}, u32[]{:S(2)}) collective-permute-start(bf16[1,2,160,768]{3,2,1,0:T(8,128)(2,1)S(1)} %collective-permute-done), channel_id=1, source_target_pairs={{0,4},{4,8},{8,12},{1,5},{5,9},{9,13},{2,6},{6,10},{10,14},{3,7},{... | collective-permute-start | bytes 1474568 | tf_op jit(solution)/shard_map/ppermute | solution.py:147
  23.8 1.3 %collective-permute-start.4 = (bf16[1,2,160,768]{3,2,1,0:T(8,128)(2,1)S(1)}, bf16[1,2,160,768]{3,2,1,0:T(8,128)(2,1)S(1)}, u32[]{:S(2)}, u32[]{:S(2)}) collective-permute-start(bf16[1,2,160,768]{3,2,1,0:T(8,128)(2,1)S(1)} %collective-permute-done.3), channel_id=1, source_target_pairs={{4,0},{8,4},{12,8},{5,1},{9,5},{13,9},{6,2},{10,6},{14,10},{7,3},{... | collective-permute-start | bytes 1474568 | tf_op jit(solution)/shard_map/ppermute | solution.py:148
  25.1 8.2 %collective-permute-done.1 = bf16[1,2,160,768]{3,2,1,0:T(8,128)(2,1)S(1)} collective-permute-done((bf16[1,2,160,768]{3,2,1,0:T(8,128)(2,1)S(1)}, bf16[1,2,160,768]{3,2,1,0:T(8,128)(2,1)S(1)}, u32[]{:S(2)}, u32[]{:S(2)}) %collective-permute-start.1) | collective-permute-done | bytes 491552 | tf_op jit(solution)/shard_map/ppermute | solution.py:147
  33.4 4.4 %collective-permute-start.2 = (bf16[1,2,160,768]{3,2,1,0:T(8,128)(2,1)S(1)}, bf16[1,2,160,768]{3,2,1,0:T(8,128)(2,1)S(1)}, u32[]{:S(2)}, u32[]{:S(2)}) collective-permute-start(bf16[1,2,160,768]{3,2,1,0:T(8,128)(2,1)S(1)} %collective-permute-done.1), channel_id=1, source_target_pairs={{0,4},{4,8},{8,12},{1,5},{5,9},{9,13},{2,6},{6,10},{10,14},{3,7},{... | collective-permute-start | bytes 1474568 | tf_op jit(solution)/shard_map/ppermute | solution.py:147
  37.8 1.3 %collective-permute-start.5 = (bf16[1,2,160,768]{3,2,1,0:T(8,128)(2,1)S(1)}, bf16[1,2,160,768]{3,2,1,0:T(8,128)(2,1)S(1)}, u32[]{:S(2)}, u32[]{:S(2)}) collective-permute-start(bf16[1,2,160,768]{3,2,1,0:T(8,128)(2,1)S(1)} %collective-permute-done.4), channel_id=1, source_target_pairs={{4,0},{8,4},{12,8},{5,1},{9,5},{13,9},{6,2},{10,6},{14,10},{7,3},{... | collective-permute-start | bytes 1474568 | tf_op jit(solution)/shard_map/ppermute | solution.py:148
  39.1 7.3 %collective-permute-done.2 = bf16[1,2,160,768]{3,2,1,0:T(8,128)(2,1)S(1)} collective-permute-done((bf16[1,2,160,768]{3,2,1,0:T(8,128)(2,1)S(1)}, bf16[1,2,160,768]{3,2,1,0:T(8,128)(2,1)S(1)}, u32[]{:S(2)}, u32[]{:S(2)}) %collective-permute-start.2) | collective-permute-done | bytes 491552 | tf_op jit(solution)/shard_map/ppermute | solution.py:147
  46.7 3.9 %collective-permute-done.5 = bf16[1,2,160,768]{3,2,1,0:T(8,128)(2,1)S(1)} collective-permute-done((bf16[1,2,160,768]{3,2,1,0:T(8,128)(2,1)S(1)}, bf16[1,2,160,768]{3,2,1,0:T(8,128)(2,1)S(1)}, u32[]{:S(2)}, u32[]{:S(2)}) %collective-permute-start.5) | collective-permute-done | bytes 491552 | tf_op jit(solution)/shard_map/ppermute | solution.py:148
  50.6 0.3 constant_dynamic-slice_fusion.5
  50.9 1.6 %collective-permute-start.6 = (bf16[4,2,160,384]{3,2,1,0:T(8,128)(2,1)S(1)}, bf16[4,2,160,384]{3,2,1,0:T(8,128)(2,1)}, u32[]{:S(2)}, u32[]{:S(2)}) collective-permute-start(bf16[4,2,160,384]{3,2,1,0:T(8,128)(2,1)S(1)} %get-tuple-element.8), channel_id=1, source_target_pairs={{0,2},{1,3},{2,0},{3,1},{4,6},{5,7},{6,4},{7,5},{8,10},{9,11},{10,... | collective-permute-start | bytes 2949128 | tf_op jit(solution)/shard_map/ppermute | solution.py:123
  52.4 1.0 pad_dynamic-slice_fusion.1
  53.4 1.3 collective-permute-start.9
  54.7 3.8 %collective-permute-start.8 = (bf16[3,1,160,384]{3,2,1,0:T(8,128)(2,1)}, bf16[3,1,160,384]{3,2,1,0:T(8,128)(2,1)}, u32[]{:S(2)}, u32[]{:S(2)}) collective-permute-start(bf16[3,1,160,384]{3,2,1,0:T(8,128)(2,1)} %get-tuple-element.12), channel_id=1, source_target_pairs={{0,1},{1,2},{2,3},{4,5},{5,6},{6,7},{8,9},{9,10},{10,11},{12,13},{... | collective-permute-start | bytes 1105928 | tf_op jit(solution)/shard_map/ppermute | solution.py:23
  58.5 3.0 %copy.33 = bf16[4,2,160,384]{2,1,0,3:T(2,128)(2,1)} copy(bf16[4,2,160,384]{3,2,1,0:T(8,128)(2,1)S(1)} %get-tuple-element.7) | data formatting | bytes 1966080 | tf_op jit(solution)/shard_map/slice | solution.py:178
  61.5 3.7 %all-to-all-start = ((bf16[4,2,160,384]{2,1,0,3:T(2,128)(2,1)}), bf16[4,2,160,384]{2,1,0,3:T(2,128)(2,1)S(1)}, u32[]{:S(2)}, u32[]{:S(2)}) async-start(bf16[4,2,160,384]{2,1,0,3:T(2,128)(2,1)} %copy.33), calls=%async_computation | async-start | bytes 3145728 | tf_op jit(solution)/shard_map/all_to_all | solution.py:179
  65.2 9.4 %collective-permute-done.6 = bf16[4,2,160,384]{3,2,1,0:T(8,128)(2,1)} collective-permute-done((bf16[4,2,160,384]{3,2,1,0:T(8,128)(2,1)S(1)}, bf16[4,2,160,384]{3,2,1,0:T(8,128)(2,1)}, u32[]{:S(2)}, u32[]{:S(2)}) %collective-permute-start.6) | collective-permute-done | bytes 983072 | tf_op jit(solution)/shard_map/ppermute | solution.py:123
  74.7 2.8 %pad_maximum_fusion.2 = bf16[4,4,160,384]{3,2,1,0:T(8,128)(2,1)} fusion(bf16[4,2,160,384]{3,2,1,0:T(8,128)(2,1)} %collective-permute-done.6, bf16[4,2,160,384]{3,2,1,0:T(8,128)(2,1)S(1)} %get-tuple-element.8), kind=kLoop, calls=%fused_computation.42 | loop fusion | flops 983040 | bytes 3932160 | tf_op jit(solution)/shard_map/concatenate | solution.py:128
  77.5 0.0 collective-permute-start.7
  77.5 0.1 pad_dynamic-slice_fusion.2
  77.7 0.0 collective-permute-done.9
  77.7 1.6 %fusion.48 = bf16[3,4,1,162,384]{4,3,1,0,2:T(8,128)(2,1)S(1)} fusion(bf16[3,1,160,384]{3,2,1,0:T(8,128)(2,1)} %collective-permute-done.9, bf16[3,2,160,384]{3,2,1,0:T(8,128)(2,1)S(1)} %pad_dynamic-slice_fusion.2, bf16[3,1,160,384]{3,2,1,0:T(8,128)(2,1)} %collective-permute-done.8), kind=kLoop, calls=%fused_computation.60 | loop fusion | flops 9704448 | bytes 2967552 | tf_op jit(solution)/shard_map/broadcast_in_dim | solution.py:58
  79.2 0.0 slice-start.1
  79.2 0.6 copy.49
  79.8 0.0 copy-start.8
  79.8 0.6 pad.32.clone
  80.4 0.2 copy.30
  80.7 0.6 slice-done.1
  81.3 3.8 %fusion.59 = f32[1,2,8,21,384]{4,2,3,1,0:T(8,128)S(1)} fusion(bf16[3,3,3,384,384]{4,3,2,1,0:T(8,128)(2,1)S(1)} %bitcast.107, bf16[3,4,1,7,2,384]{5,3,4,1,0,2:T(8,128)(2,1)S(1)} %slice.30, bf16[3,4,1,8,21,384]{5,3,4,1,0,2:T(8,128)(2,1)S(1)} %copy.30, pred[8,21]{0,1:T(8,128)(4,1)S(1)} %copy-done.8), kind=kOutput, calls=%fused_computation.74 | convolution fusion | flops 2680657920 | bytes 10156200 | tf_op jit(solution)/shard_map/conv_general_dilated | solution.py:57
  85.1 0.3 copy.31
  85.4 0.2 slice.31
  85.6 0.0 copy-start
  85.6 0.4 multiply_reduce_fusion
  86.0 6.3 %all-to-all-done = bf16[4,2,160,384]{2,1,0,3:T(2,128)(2,1)S(1)} async-done(((bf16[4,2,160,384]{2,1,0,3:T(2,128)(2,1)}), bf16[4,2,160,384]{2,1,0,3:T(2,128)(2,1)S(1)}, u32[]{:S(2)}, u32[]{:S(2)}) %all-to-all-start) | async-done | bytes 983072 | tf_op jit(solution)/shard_map/all_to_all | solution.py:179
  92.2 3.8 %copy.34 = bf16[4,2,160,4,96]{4,2,1,3,0:T(8,128)(2,1)} copy(bf16[4,2,160,4,96]{2,1,0,4,3:T(2,128)(2,1)S(1)} %bitcast.96) | data formatting | bytes 1966080 | tf_op jit(solution)/shard_map/all_to_all | solution.py:179
  96.0 3.5 %pad_bitcast_fusion.2 = (bf16[4,8,168,1,96]{4,2,1,3,0:T(8,128)(2,1)S(1)}, bf16[4,8,168,1,96]{4,2,1,3,0:T(8,128)(2,1)S(1)}, bf16[4,8,168,1,96]{4,2,1,3,0:T(8,128)(2,1)S(1)}) fusion(bf16[4,8,160,96]{3,2,1,0:T(8,128)(2,1)} %bitcast.99), kind=kLoop, calls=%fused_computation.67 | loop fusion | bytes 4079616 | tf_op jit(solution)/shard_map/stack | solution.py:83
  99.6 0.0 collective-permute-done.7
  99.6 2.0 %pad_maximum_fusion.1 = bf16[4,8,160,384]{3,2,1,0:T(8,128)(2,1)S(1)} fusion(bf16[4,4,160,384]{3,2,1,0:T(8,128)(2,1)} %collective-permute-done.7, bf16[4,2,160,384]{3,2,1,0:T(8,128)(2,1)} %collective-permute-done.6, bf16[4,2,160,384]{3,2,1,0:T(8,128)(2,1)S(1)} %get-tuple-element.8), kind=kLoop, calls=%fused_computation.34 | loop fusion | flops 3932160 | bytes 7864320 | tf_op jit(solution)/shard_map/concatenate | solution.py:130
  101.7 0.5 constant_dynamic-slice_fusion.4
  102.1 0.0 slice-start.2
  102.1 11.1 %fusion.12 = bf16[6,10,168,384]{3,2,1,0:T(8,128)(2,1)S(1)} fusion(bf16[4,2,160,384]{3,2,1,0:T(8,128)(2,1)S(1)} %get-tuple-element.4, bf16[4,2,160,384]{3,2,1,0:T(8,128)(2,1)S(1)} %get-tuple-element.5, bf16[4,2,160,384]{3,2,1,0:T(8,128)(2,1)S(1)} %get-tuple-element.6, bf16[4,2,160,384]{3,2,1,0:T(8,128)(2,1)S(1)} %get-tuple-element.3), kind=kLoop, calls=%fused_computation.17 | loop fusion | flops 112250880 | bytes 11673600 | tf_op jit(solution)/shard_map/concatenate | solution.py:136
  113.2 0.0 slice-start.3
  113.2 0.2 dynamic-slice_bitcast_fusion
  113.4 0.6 copy.48
  114.0 0.6 pad.30.clone
  114.6 0.2 copy.25
  114.8 0.4 slice-done.3
  115.3 3.8 %fusion.62 = f32[1,2,8,21,384]{4,2,3,1,0:T(8,128)S(1)} fusion(bf16[3,3,3,384,384]{4,3,2,1,0:T(8,128)(2,1)S(1)} %bitcast.110, bf16[3,4,1,7,2,384]{5,3,4,1,0,2:T(8,128)(2,1)S(1)} %slice.28, bf16[3,4,1,8,21,384]{5,3,4,1,0,2:T(8,128)(2,1)S(1)} %copy.25, pred[8,21]{0,1:T(8,128)(4,1)S(1)} %copy-done.8), kind=kOutput, calls=%fused_computation.75 | convolution fusion | flops 2680657920 | bytes 10156200 | tf_op jit(solution)/shard_map/conv_general_dilated | solution.py:44
  119.1 0.3 copy.26
  119.4 0.2 slice.29
  119.6 1.8 %fusion.50 = f32[3,12,8,384]{3,2,1,0:T(8,128)S(1)} fusion(bf16[6,10,168,384]{3,2,1,0:T(8,128)(2,1)S(1)} %fusion.12, s32[]{:T(128)S(6)} %select_n.103, s32[]{:T(128)S(6)} %select_n.105, bf16[4,8,168,1,96]{4,2,1,3,0:T(8,128)(2,1)S(1)} %get-tuple-element.10, bf16[4,8,168,1,96]{4,2,1,3,0:T(8,128)(2,1)S(1)} %get-tuple-element.11, ...), kind=kOutput, calls=%fused_computation.71 | convolution fusion | flops 1192181760 | bytes 8699912 | tf_op jit(solution)/shard_map/dot_general | solution.py:106
  121.5 1.8 %fusion.53 = f32[3,12,8,384]{3,2,1,0:T(8,128)S(1)} fusion(bf16[6,10,168,384]{3,2,1,0:T(8,128)(2,1)S(1)} %fusion.12, s32[]{:T(128)S(6)} %select_n.107, s32[]{:T(128)S(6)} %select_n.109, bf16[4,8,168,1,96]{4,2,1,3,0:T(8,128)(2,1)S(1)} %get-tuple-element.10, bf16[4,8,168,1,96]{4,2,1,3,0:T(8,128)(2,1)S(1)} %get-tuple-element.11, ...), kind=kOutput, calls=%fused_computation.72 | convolution fusion | flops 1192181760 | bytes 8699912 | tf_op jit(solution)/shard_map/dot_general | solution.py:106
  123.3 0.0 copy-start.1
  123.3 0.0 copy-start.3
  123.4 0.0 copy-start.5
  123.4 0.0 copy-start.7
  123.4 1.8 %fusion.56 = f32[3,12,8,384]{3,2,1,0:T(8,128)S(1)} fusion(bf16[6,10,168,384]{3,2,1,0:T(8,128)(2,1)S(1)} %fusion.12, s32[]{:T(128)S(6)} %select_n.111, s32[]{:T(128)S(6)} %select_n.113, bf16[4,8,168,1,96]{4,2,1,3,0:T(8,128)(2,1)S(1)} %get-tuple-element.10, bf16[4,8,168,1,96]{4,2,1,3,0:T(8,128)(2,1)S(1)} %get-tuple-element.11, ...), kind=kOutput, calls=%fused_computation.73 | convolution fusion | flops 1192181760 | bytes 8699912 | tf_op jit(solution)/shard_map/dot_general | solution.py:106
  125.3 1.2 add_convert_fusion
  126.5 1.6 %fusion.67 = f32[2592,96]{0,1:T(8,128)} fusion(s32[]{:T(128)S(6)} %select_n.114, f32[1152,96]{0,1:T(8,128)S(1)} %bitcast.102, f32[1152,96]{0,1:T(8,128)S(1)} %bitcast.103, f32[1152,96]{0,1:T(8,128)S(1)} %bitcast.104), kind=kLoop, calls=%fused_computation.78 | loop fusion | flops 746496 | bytes 2322436 | tf_op jit(solution)/shard_map/mul | solution.py:191
  (33 shorter events, 0.5 us)
Async XLA Ops:
  0.6 45.9 %copy-start.4 = (bf16[1,2,160,384]{3,2,1,0:T(8,128)(2,1)S(1)}, bf16[1,2,160,384]{3,2,1,0:T(8,128)(2,1)}, u32[]{:S(2)}) copy-start(bf16[1,2,160,384]{3,2,1,0:T(8,128)(2,1)} %param.9) | copy-start | bytes 737284
  4.0 15.4 %collective-permute-start = (bf16[1,2,160,768]{3,2,1,0:T(8,128)(2,1)S(1)}, bf16[1,2,160,768]{3,2,1,0:T(8,128)(2,1)S(1)}, u32[]{:S(2)}, u32[]{:S(2)}) collective-permute-start(bf16[1,2,160,768]{3,2,1,0:T(8,128)(2,1)S(1)} %pad_maximum_fusion.3), channel_id=1, source_target_pairs={{0,4},{4,8},{8,12},{1,5},{5,9},{9,13},{2,6},{6,10},{10,14},{3,7},{... | collective-permute-start | bytes 1474568 | tf_op jit(solution)/shard_map/ppermute | solution.py:147
  9.0 14.8 %collective-permute-start.3 = (bf16[1,2,160,768]{3,2,1,0:T(8,128)(2,1)S(1)}, bf16[1,2,160,768]{3,2,1,0:T(8,128)(2,1)S(1)}, u32[]{:S(2)}, u32[]{:S(2)}) collective-permute-start(bf16[1,2,160,768]{3,2,1,0:T(8,128)(2,1)S(1)} %pad_maximum_fusion.3), channel_id=1, source_target_pairs={{4,0},{8,4},{12,8},{5,1},{9,5},{13,9},{6,2},{10,6},{14,10},{7,3},{... | collective-permute-start | bytes 1474568 | tf_op jit(solution)/shard_map/ppermute | solution.py:148
  19.4 14.0 %collective-permute-start.1 = (bf16[1,2,160,768]{3,2,1,0:T(8,128)(2,1)S(1)}, bf16[1,2,160,768]{3,2,1,0:T(8,128)(2,1)S(1)}, u32[]{:S(2)}, u32[]{:S(2)}) collective-permute-start(bf16[1,2,160,768]{3,2,1,0:T(8,128)(2,1)S(1)} %collective-permute-done), channel_id=1, source_target_pairs={{0,4},{4,8},{8,12},{1,5},{5,9},{9,13},{2,6},{6,10},{10,14},{3,7},{... | collective-permute-start | bytes 1474568 | tf_op jit(solution)/shard_map/ppermute | solution.py:147
  23.8 14.0 %collective-permute-start.4 = (bf16[1,2,160,768]{3,2,1,0:T(8,128)(2,1)S(1)}, bf16[1,2,160,768]{3,2,1,0:T(8,128)(2,1)S(1)}, u32[]{:S(2)}, u32[]{:S(2)}) collective-permute-start(bf16[1,2,160,768]{3,2,1,0:T(8,128)(2,1)S(1)} %collective-permute-done.3), channel_id=1, source_target_pairs={{4,0},{8,4},{12,8},{5,1},{9,5},{13,9},{6,2},{10,6},{14,10},{7,3},{... | collective-permute-start | bytes 1474568 | tf_op jit(solution)/shard_map/ppermute | solution.py:148
  33.4 13.1 %collective-permute-start.2 = (bf16[1,2,160,768]{3,2,1,0:T(8,128)(2,1)S(1)}, bf16[1,2,160,768]{3,2,1,0:T(8,128)(2,1)S(1)}, u32[]{:S(2)}, u32[]{:S(2)}) collective-permute-start(bf16[1,2,160,768]{3,2,1,0:T(8,128)(2,1)S(1)} %collective-permute-done.1), channel_id=1, source_target_pairs={{0,4},{4,8},{8,12},{1,5},{5,9},{9,13},{2,6},{6,10},{10,14},{3,7},{... | collective-permute-start | bytes 1474568 | tf_op jit(solution)/shard_map/ppermute | solution.py:147
  37.8 12.8 %collective-permute-start.5 = (bf16[1,2,160,768]{3,2,1,0:T(8,128)(2,1)S(1)}, bf16[1,2,160,768]{3,2,1,0:T(8,128)(2,1)S(1)}, u32[]{:S(2)}, u32[]{:S(2)}) collective-permute-start(bf16[1,2,160,768]{3,2,1,0:T(8,128)(2,1)S(1)} %collective-permute-done.4), channel_id=1, source_target_pairs={{4,0},{8,4},{12,8},{5,1},{9,5},{13,9},{6,2},{10,6},{14,10},{7,3},{... | collective-permute-start | bytes 1474568 | tf_op jit(solution)/shard_map/ppermute | solution.py:148
  50.9 23.8 %collective-permute-start.6 = (bf16[4,2,160,384]{3,2,1,0:T(8,128)(2,1)S(1)}, bf16[4,2,160,384]{3,2,1,0:T(8,128)(2,1)}, u32[]{:S(2)}, u32[]{:S(2)}) collective-permute-start(bf16[4,2,160,384]{3,2,1,0:T(8,128)(2,1)S(1)} %get-tuple-element.8), channel_id=1, source_target_pairs={{0,2},{1,3},{2,0},{3,1},{4,6},{5,7},{6,4},{7,5},{8,10},{9,11},{10,... | collective-permute-start | bytes 2949128 | tf_op jit(solution)/shard_map/ppermute | solution.py:123
  53.4 24.2 %collective-permute-start.9 = (bf16[3,1,160,384]{3,2,1,0:T(8,128)(2,1)}, bf16[3,1,160,384]{3,2,1,0:T(8,128)(2,1)}, u32[]{:S(2)}, u32[]{:S(2)}) collective-permute-start(bf16[3,1,160,384]{3,2,1,0:T(8,128)(2,1)} %get-tuple-element.13), channel_id=1, source_target_pairs={{1,0},{2,1},{3,2},{5,4},{6,5},{7,6},{9,8},{10,9},{11,10},{13,12},{... | collective-permute-start | bytes 1105928 | tf_op jit(solution)/shard_map/ppermute | solution.py:25
  54.7 23.0 %collective-permute-start.8 = (bf16[3,1,160,384]{3,2,1,0:T(8,128)(2,1)}, bf16[3,1,160,384]{3,2,1,0:T(8,128)(2,1)}, u32[]{:S(2)}, u32[]{:S(2)}) collective-permute-start(bf16[3,1,160,384]{3,2,1,0:T(8,128)(2,1)} %get-tuple-element.12), channel_id=1, source_target_pairs={{0,1},{1,2},{2,3},{4,5},{5,6},{6,7},{8,9},{9,10},{10,11},{12,13},{... | collective-permute-start | bytes 1105928 | tf_op jit(solution)/shard_map/ppermute | solution.py:23
  61.5 30.8 %all-to-all-start = ((bf16[4,2,160,384]{2,1,0,3:T(2,128)(2,1)}), bf16[4,2,160,384]{2,1,0,3:T(2,128)(2,1)S(1)}, u32[]{:S(2)}, u32[]{:S(2)}) async-start(bf16[4,2,160,384]{2,1,0,3:T(2,128)(2,1)} %copy.33), calls=%async_computation | async-start | bytes 3145728 | tf_op jit(solution)/shard_map/all_to_all | solution.py:179
  74.7 6.0 %slice-start = ((s8[7962624]{0:T(1024)(128)(4,1)}), s8[4194304]{0:T(1024)(128)(4,1)S(1)}, s32[]{:S(2)}) async-start(s8[7962624]{0:T(1024)(128)(4,1)} %bitcast.105), calls=%async_computation.1 | async-start | bytes 8388608
  77.5 22.1 %collective-permute-start.7 = (bf16[4,4,160,384]{3,2,1,0:T(8,128)(2,1)}, bf16[4,4,160,384]{3,2,1,0:T(8,128)(2,1)}, u32[]{:S(2)}, u32[]{:S(2)}) collective-permute-start(bf16[4,4,160,384]{3,2,1,0:T(8,128)(2,1)} %pad_maximum_fusion.2), channel_id=1, source_target_pairs={{0,1},{1,0},{2,3},{3,2},{4,5},{5,4},{6,7},{7,6},{8,9},{9,8},{10,11... | collective-permute-start | bytes 5898248 | tf_op jit(solution)/shard_map/ppermute | solution.py:129
  79.2 2.1 %slice-start.1 = ((s8[7962624]{0:T(1024)(128)(4,1)}), s8[3768320]{0:T(1024)(128)(4,1)S(1)}, s32[]{:S(2)}) async-start(s8[7962624]{0:T(1024)(128)(4,1)} %bitcast.105), calls=%async_computation.2 | async-start | bytes 7536640
  79.8 1.5 %copy-start.8 = (pred[8,21]{0,1:T(8,128)(4,1)S(1)}, pred[8,21]{0,1:T(8,128)(4,1)}, u32[]{:S(2)}) copy-start(pred[8,21]{0,1:T(8,128)(4,1)} %constant.125) | copy-start | bytes 508
  81.3 4.2 %copy-start.2 = (bf16[1,2,160,384]{3,2,1,0:T(8,128)(2,1)S(1)}, bf16[1,2,160,384]{3,2,1,0:T(8,128)(2,1)}, u32[]{:S(2)}) copy-start(bf16[1,2,160,384]{3,2,1,0:T(8,128)(2,1)} %param.5) | copy-start | bytes 737284
  81.3 4.2 %copy-start.6 = (f32[384]{0:T(512)S(1)}, f32[384]{0:T(512)}, u32[]{:S(2)}) copy-start(f32[384]{0:T(512)} %param.6) | copy-start | bytes 4612
  85.6 14.0 %copy-start = (f32[1,2,1,160,384]{4,1,3,2,0:T(2,128)}, f32[1,2,1,160,384]{4,1,3,2,0:T(2,128)S(1)}, u32[]{:S(2)}) copy-start(f32[1,2,1,160,384]{4,1,3,2,0:T(2,128)S(1)} %slice.31) | copy-start | bytes 1474564
  102.1 12.7 %slice-start.2 = ((s8[7962624]{0:T(1024)(128)(4,1)}), s8[4194304]{0:T(1024)(128)(4,1)S(1)}, s32[]{:S(2)}) async-start(s8[7962624]{0:T(1024)(128)(4,1)} %bitcast.108), calls=%async_computation.3 | async-start | bytes 8388608
  113.2 2.1 %slice-start.3 = ((s8[7962624]{0:T(1024)(128)(4,1)}), s8[3768320]{0:T(1024)(128)(4,1)S(1)}, s32[]{:S(2)}) async-start(s8[7962624]{0:T(1024)(128)(4,1)} %bitcast.108), calls=%async_computation.4 | async-start | bytes 7536640
  123.3 1.9 %copy-start.1 = (f32[1,2,1,160,384]{4,1,3,2,0:T(2,128)S(1)}, f32[1,2,1,160,384]{4,1,3,2,0:T(2,128)}, u32[]{:S(2)}) copy-start(f32[1,2,1,160,384]{4,1,3,2,0:T(2,128)} %copy-done) | copy-start | bytes 1474564
  123.3 1.9 %copy-start.3 = (bf16[1,2,160,384]{3,2,1,0:T(8,128)(2,1)S(1)}, bf16[1,2,160,384]{3,2,1,0:T(8,128)(2,1)}, u32[]{:S(2)}) copy-start(bf16[1,2,160,384]{3,2,1,0:T(8,128)(2,1)} %param.5) | copy-start | bytes 737284
  123.4 1.9 %copy-start.5 = (bf16[1,2,160,384]{3,2,1,0:T(8,128)(2,1)S(1)}, bf16[1,2,160,384]{3,2,1,0:T(8,128)(2,1)}, u32[]{:S(2)}) copy-start(bf16[1,2,160,384]{3,2,1,0:T(8,128)(2,1)} %param.9) | copy-start | bytes 737284
  123.4 1.9 %copy-start.7 = (f32[384]{0:T(512)S(1)}, f32[384]{0:T(512)}, u32[]{:S(2)}) copy-start(f32[384]{0:T(512)} %param.7) | copy-start | bytes 4612

commit v14 on v9

--- a/solution.py
+++ b/solution.py
@@ -74,21 +74,13 @@
     return most
 
 
-def block_weight_grad(framed, cot_all, frame_index, share_rows, channels):
+def block_weight_grad(hidden_all, cot_all, frame_index, share_rows, channels):
     frame_total, row_total, col_total, slots = cot_all.shape
-    padded_cols = framed.shape[2]
     pair_rows = 3 * channels
     tap_rows = 27 * channels
-    flat_count = frame_total * row_total * padded_cols
+    edged = jnp.pad(cot_all, ((0, 2), (1, 1), (1, 1), (0, 0)))
     shifted = jnp.stack(
-        [
-            jnp.pad(
-                cot_all,
-                ((0, 0), (0, 0), (col_tap, padded_cols - col_total - col_tap), (0, 0)),
-            )
-            for col_tap in range(3)
-        ],
-        axis=3,
+        [edged[:, :, 2 - col_tap : 2 - col_tap + col_total] for col_tap in range(3)], axis=3
     )
     first_row = frame_index * share_rows
     first_pair = first_row // pair_rows
@@ -98,13 +90,14 @@
         pair = jnp.minimum(first_pair + step, 8)
         depth_tap = pair // 3
         row_tap = pair % 3
-        slab = lax.dynamic_slice(
-            framed,
-            (depth_tap, row_tap, 0, 0),
-            (frame_total, row_total, padded_cols, channels),
+        window = lax.dynamic_slice(
+            shifted,
+            (2 - depth_tap, 2 - row_tap, 0, 0, 0),
+            (frame_total, row_total, col_total, 3, slots),
         )
         product = lax.dot_general(
-            shifted, slab, (((0, 1, 2), (0, 1, 2)), ((), ())), preferred_element_type=jnp.float32
+            window, hidden_all, (((0, 1, 2), (0, 1, 2)), ((), ())),
+            preferred_element_type=jnp.float32,
         )
         pieces.append(product.transpose(0, 2, 1).reshape(pair_rows, slots))
     stacked = jnp.concatenate(pieces, axis=0)
@@ -186,22 +179,23 @@
 
     both_frames = gather_frames(jnp.concatenate([hidden, cotangent], axis=-1))
     hidden_all = gather_rows(both_frames[..., :channels], height_count)
-    framed = jnp.pad(hidden_all, ((2, 0), (1, 1), (1, right_pad), (0, 0)))
 
     cot_frames = both_frames[..., channels:]
     cot_all = lax.all_to_all(cot_frames, "height", split_axis=3, concat_axis=1, tiled=True)
 
     window = lax.dynamic_slice(
-        framed,
+        jnp.pad(hidden_all, ((2, 0), (1, 1), (1, 1), (0, 0))),
         (frame_index * frame_count, row_index * row_count, 0, 0),
-        (frame_count + 2, row_count + 2, padded_cols, channels),
+        (frame_count + 2, row_count + 2, col_count + 2, channels),
     )
     conv_out = forward_conv(window, weight_cube, row_count, col_count).reshape(
         frame_count, row_count, col_count, channels
     )
     output = (latent_wide + conv_out + bias).astype(jnp.bfloat16)
 
-    weight_grad = block_weight_grad(framed, cot_all, frame_index, share_rows, channels) * inverse_root
+    weight_grad = (
+        block_weight_grad(hidden_all, cot_all, frame_index, share_rows, channels) * inverse_root
+    )
 
     cot_future = lax.dynamic_slice_in_dim(
         jnp.pad(cot_frames, ((0, 2), (0, 0), (0, 0), (0, 0))), frame_index * frame_count, 3, 0

time: 126 us -> 125 us (level)
  starting transfers between devices: 28 us -> 38.9 us
  waiting for transfers between devices: 44.2 us -> 34.8 us
  other arithmetic: 20.7 us -> 17.3 us
    ppermute x1, starting transfers between devices: 0.01 us -> 11.1 us  [gather_rows(): twins = lax.ppermute(stacked, 'height', sibling)]
    all_to_all x1, waiting for transfers between devices: 6.27 us -> 0.01 us  [local(): lax.all_to_all(cot_frames, 'height', split_axis=3, concat_axis=1, tiled=T...]
    concatenate x1, other arithmetic: 5.84 us -> 0.44 us  [gather_rows(): jnp.concatenate([lax.dynamic_slice_in_dim(relative, (place - chip - 1) %...]
    ppermute x1, waiting for transfers between devices: 9.36 us -> 6.21 us  [gather_rows(): lax.ppermute(own, 'height', [(i, (i + 2 * step) % height_count) for i in...]
    another operation x0 -> x1, other arithmetic: none -> 2.03 us  [block_weight_grad(): jnp.stack([edged[:, :, 2 - col_tap:2 - col_tap + col_total] for col_tap i...]
  transfers between devices with their start and end apart: 11 -> 11, of which waited for: 6 -> 5; matrix products, arithmetic and copies ran while one was open for 18% -> 19% of each run, Pallas kernels for 0% -> 0%
where the time goes in v14:
time: 125 us
  starting transfers between devices  38.9 us (31%)
  waiting for transfers between devices  34.8 us (28%)
  local copies, waits for them, and re-layouts  19.4 us (16%)
  other arithmetic  17.3 us (14%)
  matrix products  13 us (10%)
    ppermute x3, waiting for transfers between devices, gather_frames(): rising = lax.ppermute(rising, 'tm', up)  24.7 us
    ppermute x3, starting transfers between devices, gather_frames(): rising = lax.ppermute(rising, 'tm', up)  13.8 us
    ppermute x1, starting transfers between devices, gather_rows(): twins = lax.ppermute(stacked, 'height', sibling)  11.1 us
    ppermute x1, waiting for transfers between devices, gather_rows(): lax.ppermute(own, 'height', [(i, (i + 2 * step) % height_count) for i in...  6.21 us
    dot_general x3, matrix products, block_weight_grad(): lax.dot_general(window, hidden_all, (((0, 1, 2), (0, 1, 2)), ((), ())), p...  5.42 us
    ppermute x3, waiting for transfers between devices, gather_frames(): falling = lax.ppermute(falling, 'tm', down)  3.9 us
    ppermute x3, starting transfers between devices, gather_frames(): falling = lax.ppermute(falling, 'tm', down)  3.88 us
    conv_general_dilated x1, matrix products, forward_conv(): lax.conv_general_dilated(window[None], cube, (1, 1, 1), 'VALID', dimensio...  3.8 us
  transfers between devices with their start and end apart: 11, of which 5 were waited for; matrix products, arithmetic and copies ran while one was open for 19% of the time, Pallas kernels for 0%

profile of v14, /device:TPU:0, one launch (start us, length us, event | category | flops | bytes accessed | tf_op | source)
XLA Modules:
  0.0 124.7 jit_solution(12269572498874293535)
XLA Ops:
  0.6 1.1 fusion.65
  1.8 1.2 multiply_convert_fusion
  3.0 1.0 pad_maximum_fusion.5
  4.0 5.0 %collective-permute-start = (bf16[1,2,160,768]{3,2,1,0:T(8,128)(2,1)S(1)}, bf16[1,2,160,768]{3,2,1,0:T(8,128)(2,1)S(1)}, u32[]{:S(2)}, u32[]{:S(2)}) collective-permute-start(bf16[1,2,160,768]{3,2,1,0:T(8,128)(2,1)S(1)} %pad_maximum_fusion.5), channel_id=1, source_target_pairs={{0,4},{4,8},{8,12},{1,5},{5,9},{9,13},{2,6},{6,10},{10,14},{3,7},{... | collective-permute-start | bytes 1474568 | tf_op jit(solution)/shard_map/ppermute | solution.py:153
  9.0 1.3 %collective-permute-start.3 = (bf16[1,2,160,768]{3,2,1,0:T(8,128)(2,1)S(1)}, bf16[1,2,160,768]{3,2,1,0:T(8,128)(2,1)S(1)}, u32[]{:S(2)}, u32[]{:S(2)}) collective-permute-start(bf16[1,2,160,768]{3,2,1,0:T(8,128)(2,1)S(1)} %pad_maximum_fusion.5), channel_id=1, source_target_pairs={{4,0},{8,4},{12,8},{5,1},{9,5},{13,9},{6,2},{10,6},{14,10},{7,3},{... | collective-permute-start | bytes 1474568 | tf_op jit(solution)/shard_map/ppermute | solution.py:154
  10.3 9.1 %collective-permute-done = bf16[1,2,160,768]{3,2,1,0:T(8,128)(2,1)S(1)} collective-permute-done((bf16[1,2,160,768]{3,2,1,0:T(8,128)(2,1)S(1)}, bf16[1,2,160,768]{3,2,1,0:T(8,128)(2,1)S(1)}, u32[]{:S(2)}, u32[]{:S(2)}) %collective-permute-start) | collective-permute-done | bytes 491552 | tf_op jit(solution)/shard_map/ppermute | solution.py:153
  19.4 4.4 %collective-permute-start.1 = (bf16[1,2,160,768]{3,2,1,0:T(8,128)(2,1)S(1)}, bf16[1,2,160,768]{3,2,1,0:T(8,128)(2,1)S(1)}, u32[]{:S(2)}, u32[]{:S(2)}) collective-permute-start(bf16[1,2,160,768]{3,2,1,0:T(8,128)(2,1)S(1)} %collective-permute-done), channel_id=1, source_target_pairs={{0,4},{4,8},{8,12},{1,5},{5,9},{9,13},{2,6},{6,10},{10,14},{3,7},{... | collective-permute-start | bytes 1474568 | tf_op jit(solution)/shard_map/ppermute | solution.py:153
  23.8 1.3 %collective-permute-start.4 = (bf16[1,2,160,768]{3,2,1,0:T(8,128)(2,1)S(1)}, bf16[1,2,160,768]{3,2,1,0:T(8,128)(2,1)S(1)}, u32[]{:S(2)}, u32[]{:S(2)}) collective-permute-start(bf16[1,2,160,768]{3,2,1,0:T(8,128)(2,1)S(1)} %collective-permute-done.3), channel_id=1, source_target_pairs={{4,0},{8,4},{12,8},{5,1},{9,5},{13,9},{6,2},{10,6},{14,10},{7,3},{... | collective-permute-start | bytes 1474568 | tf_op jit(solution)/shard_map/ppermute | solution.py:154
  25.1 8.2 %collective-permute-done.1 = bf16[1,2,160,768]{3,2,1,0:T(8,128)(2,1)S(1)} collective-permute-done((bf16[1,2,160,768]{3,2,1,0:T(8,128)(2,1)S(1)}, bf16[1,2,160,768]{3,2,1,0:T(8,128)(2,1)S(1)}, u32[]{:S(2)}, u32[]{:S(2)}) %collective-permute-start.1) | collective-permute-done | bytes 491552 | tf_op jit(solution)/shard_map/ppermute | solution.py:153
  33.4 4.4 %collective-permute-start.2 = (bf16[1,2,160,768]{3,2,1,0:T(8,128)(2,1)S(1)}, bf16[1,2,160,768]{3,2,1,0:T(8,128)(2,1)S(1)}, u32[]{:S(2)}, u32[]{:S(2)}) collective-permute-start(bf16[1,2,160,768]{3,2,1,0:T(8,128)(2,1)S(1)} %collective-permute-done.1), channel_id=1, source_target_pairs={{0,4},{4,8},{8,12},{1,5},{5,9},{9,13},{2,6},{6,10},{10,14},{3,7},{... | collective-permute-start | bytes 1474568 | tf_op jit(solution)/shard_map/ppermute | solution.py:153
  37.8 1.3 %collective-permute-start.5 = (bf16[1,2,160,768]{3,2,1,0:T(8,128)(2,1)S(1)}, bf16[1,2,160,768]{3,2,1,0:T(8,128)(2,1)S(1)}, u32[]{:S(2)}, u32[]{:S(2)}) collective-permute-start(bf16[1,2,160,768]{3,2,1,0:T(8,128)(2,1)S(1)} %collective-permute-done.4), channel_id=1, source_target_pairs={{4,0},{8,4},{12,8},{5,1},{9,5},{13,9},{6,2},{10,6},{14,10},{7,3},{... | collective-permute-start | bytes 1474568 | tf_op jit(solution)/shard_map/ppermute | solution.py:154
  39.1 7.3 %collective-permute-done.2 = bf16[1,2,160,768]{3,2,1,0:T(8,128)(2,1)S(1)} collective-permute-done((bf16[1,2,160,768]{3,2,1,0:T(8,128)(2,1)S(1)}, bf16[1,2,160,768]{3,2,1,0:T(8,128)(2,1)S(1)}, u32[]{:S(2)}, u32[]{:S(2)}) %collective-permute-start.2) | collective-permute-done | bytes 491552 | tf_op jit(solution)/shard_map/ppermute | solution.py:153
  46.7 3.9 %collective-permute-done.5 = bf16[1,2,160,768]{3,2,1,0:T(8,128)(2,1)S(1)} collective-permute-done((bf16[1,2,160,768]{3,2,1,0:T(8,128)(2,1)S(1)}, bf16[1,2,160,768]{3,2,1,0:T(8,128)(2,1)S(1)}, u32[]{:S(2)}, u32[]{:S(2)}) %collective-permute-start.5) | collective-permute-done | bytes 491552 | tf_op jit(solution)/shard_map/ppermute | solution.py:154
  50.6 0.3 constant_dynamic-slice_fusion.1
  50.9 1.6 %collective-permute-start.6 = (bf16[4,2,160,384]{3,2,1,0:T(8,128)(2,1)S(1)}, bf16[4,2,160,384]{3,2,1,0:T(8,128)(2,1)}, u32[]{:S(2)}, u32[]{:S(2)}) collective-permute-start(bf16[4,2,160,384]{3,2,1,0:T(8,128)(2,1)S(1)} %get-tuple-element.6), channel_id=1, source_target_pairs={{0,2},{1,3},{2,0},{3,1},{4,6},{5,7},{6,4},{7,5},{8,10},{9,11},{10,... | collective-permute-start | bytes 2949128 | tf_op jit(solution)/shard_map/ppermute | solution.py:116
  52.4 1.0 pad_dynamic-slice_fusion.6
  53.4 1.3 %collective-permute-start.9 = (bf16[3,1,160,384]{3,2,1,0:T(8,128)(2,1)}, bf16[3,1,160,384]{3,2,1,0:T(8,128)(2,1)}, u32[]{:S(2)}, u32[]{:S(2)}) collective-permute-start(bf16[3,1,160,384]{3,2,1,0:T(8,128)(2,1)} %get-tuple-element.13), channel_id=1, source_target_pairs={{1,0},{2,1},{3,2},{5,4},{6,5},{7,6},{9,8},{10,9},{11,10},{13,12},{... | collective-permute-start | bytes 1105928 | tf_op jit(solution)/shard_map/ppermute | solution.py:25
  54.7 3.8 %collective-permute-start.8 = (bf16[3,1,160,384]{3,2,1,0:T(8,128)(2,1)}, bf16[3,1,160,384]{3,2,1,0:T(8,128)(2,1)}, u32[]{:S(2)}, u32[]{:S(2)}) collective-permute-start(bf16[3,1,160,384]{3,2,1,0:T(8,128)(2,1)} %get-tuple-element.12), channel_id=1, source_target_pairs={{0,1},{1,2},{2,3},{4,5},{5,6},{6,7},{8,9},{9,10},{10,11},{12,13},{... | collective-permute-start | bytes 1105928 | tf_op jit(solution)/shard_map/ppermute | solution.py:23
  58.5 3.0 %copy.48 = bf16[4,2,160,384]{2,1,0,3:T(2,128)(2,1)} copy(bf16[4,2,160,384]{3,2,1,0:T(8,128)(2,1)S(1)} %get-tuple-element.5) | data formatting | bytes 1966080 | tf_op jit(solution)/shard_map/slice | solution.py:183
  61.5 3.6 %all-to-all-start = ((bf16[4,2,160,384]{2,1,0,3:T(2,128)(2,1)}), bf16[4,2,160,384]{2,1,0,3:T(2,128)(2,1)S(1)}, u32[]{:S(2)}, u32[]{:S(2)}) async-start(bf16[4,2,160,384]{2,1,0,3:T(2,128)(2,1)} %copy.48), calls=%async_computation | async-start | bytes 3145728 | tf_op jit(solution)/shard_map/all_to_all | solution.py:184
  65.1 0.1 pad_dynamic-slice_fusion.7
  65.3 0.0 slice-start
  65.3 1.7 %fusion.37 = bf16[3,4,1,162,384]{4,3,1,0,2:T(8,128)(2,1)S(1)} fusion(bf16[3,1,160,384]{3,2,1,0:T(8,128)(2,1)} %collective-permute-done.9, bf16[3,2,160,384]{3,2,1,0:T(8,128)(2,1)S(1)} %pad_dynamic-slice_fusion.7, bf16[3,1,160,384]{3,2,1,0:T(8,128)(2,1)} %collective-permute-done.8), kind=kLoop, calls=%fused_computation.54 | loop fusion | flops 9704448 | bytes 2967552 | tf_op jit(solution)/shard_map/broadcast_in_dim | solution.py:58
  67.0 0.6 copy.62
  67.6 0.0 slice-start.1
  67.6 0.6 pad.22.clone
  68.2 0.2 copy.45
  68.4 0.0 copy-start.8
  68.4 6.2 %collective-permute-done.6 = bf16[4,2,160,384]{3,2,1,0:T(8,128)(2,1)} collective-permute-done((bf16[4,2,160,384]{3,2,1,0:T(8,128)(2,1)S(1)}, bf16[4,2,160,384]{3,2,1,0:T(8,128)(2,1)}, u32[]{:S(2)}, u32[]{:S(2)}) %collective-permute-start.6) | collective-permute-done | bytes 983072 | tf_op jit(solution)/shard_map/ppermute | solution.py:116
  74.6 2.7 %pad_maximum_fusion.3 = bf16[4,4,160,384]{3,2,1,0:T(8,128)(2,1)} fusion(bf16[4,2,160,384]{3,2,1,0:T(8,128)(2,1)} %collective-permute-done.6, bf16[4,2,160,384]{3,2,1,0:T(8,128)(2,1)S(1)} %get-tuple-element.6), kind=kLoop, calls=%fused_computation.30 | loop fusion | flops 983040 | bytes 3932160 | tf_op jit(solution)/shard_map/concatenate | solution.py:121
  77.4 11.1 %collective-permute-start.7 = (bf16[4,4,160,384]{3,2,1,0:T(8,128)(2,1)}, bf16[4,4,160,384]{3,2,1,0:T(8,128)(2,1)}, u32[]{:S(2)}, u32[]{:S(2)}) collective-permute-start(bf16[4,4,160,384]{3,2,1,0:T(8,128)(2,1)} %pad_maximum_fusion.3), channel_id=1, source_target_pairs={{0,1},{1,0},{2,3},{3,2},{4,5},{5,4},{6,7},{7,6},{8,9},{9,8},{10,11... | collective-permute-start | bytes 5898248 | tf_op jit(solution)/shard_map/ppermute | solution.py:122
  88.5 0.0 copy-start.2
  88.5 0.0 copy-start.6
  88.5 3.8 %fusion.54 = f32[1,2,8,21,384]{4,2,3,1,0:T(8,128)S(1)} fusion(bf16[3,3,3,384,384]{4,3,2,1,0:T(8,128)(2,1)S(1)} %bitcast.101, bf16[3,4,1,7,2,384]{5,3,4,1,0,2:T(8,128)(2,1)S(1)} %slice.48, bf16[3,4,1,8,21,384]{5,3,4,1,0,2:T(8,128)(2,1)S(1)} %copy.45, pred[8,21]{0,1:T(8,128)(4,1)S(1)} %copy-done.8), kind=kOutput, calls=%fused_computation.64 | convolution fusion | flops 2680657920 | bytes 10156200 | tf_op jit(solution)/shard_map/conv_general_dilated | solution.py:57
  92.3 0.3 copy.46
  92.5 0.2 slice.49
  92.8 0.4 multiply_reduce_fusion
  93.2 3.8 %copy.49 = bf16[4,2,160,4,96]{4,2,1,3,0:T(8,128)(2,1)} copy(bf16[4,2,160,4,96]{2,1,0,4,3:T(2,128)(2,1)S(1)} %bitcast.90) | data formatting | bytes 1966080 | tf_op jit(solution)/shard_map/all_to_all | solution.py:184
  96.9 3.5 %fusion.14 = (bf16[6,10,160,1,96]{4,2,1,3,0:T(8,128)(2,1)S(1)}, bf16[6,10,160,1,96]{4,2,1,3,0:T(8,128)(2,1)S(1)}, bf16[6,10,160,1,96]{4,2,1,3,0:T(8,128)(2,1)S(1)}) fusion(bf16[4,8,160,96]{3,2,1,0:T(8,128)(2,1)} %bitcast.93), kind=kLoop, calls=%fused_computation.26 | loop fusion | bytes 6512640 | tf_op jit(solution)/shard_map/stack | solution.py:82
  100.4 2.0 %pad_maximum_fusion = bf16[6,10,160,3,96]{4,2,1,3,0:T(8,128)(2,1)S(1)} fusion(bf16[6,10,160,1,96]{4,2,1,3,0:T(8,128)(2,1)S(1)} %get-tuple-element.11, bf16[6,10,160,1,96]{4,2,1,3,0:T(8,128)(2,1)S(1)} %get-tuple-element.10, bf16[6,10,160,1,96]{4,2,1,3,0:T(8,128)(2,1)S(1)} %get-tuple-element.9), kind=kLoop, calls=%fused_computation.1 | loop fusion | flops 5529600 | bytes 11059200 | tf_op jit(solution)/shard_map/stack | solution.py:82
  102.5 1.7 %fusion.80 = (bf16[4,2,160,384]{3,2,1,0:T(8,128)(2,1)S(1)}, bf16[4,2,160,384]{3,2,1,0:T(8,128)(2,1)S(1)}) fusion(bf16[4,4,160,384]{3,2,1,0:T(8,128)(2,1)} %collective-permute-done.7), kind=kLoop, calls=%fused_computation.107 | loop fusion | bytes 3932160 | tf_op jit(solution)/shard_map/slice | solution.py:127
  104.2 0.3 fusion.17
  104.5 1.8 %fusion.18 = bf16[4,4,160,384]{3,2,1,0:T(8,128)(2,1)S(1)} fusion(bf16[4,2,160,384]{3,2,1,0:T(8,128)(2,1)} %collective-permute-done.6, bf16[4,2,160,384]{3,2,1,0:T(8,128)(2,1)S(1)} %get-tuple-element.8, pred[]{:T(512)S(6)} %eq.10), kind=kLoop, calls=%fused_computation.33 | loop fusion | flops 2949120 | bytes 3932161 | tf_op jit(solution)/shard_map/jit(_where)/select_n | solution.py:129
  106.4 1.6 %fusion.20 = (bf16[4,4,160,384]{3,2,1,0:T(8,128)(2,1)S(1)}, bf16[4,4,160,384]{3,2,1,0:T(8,128)(2,1)S(1)}) fusion(s32[]{:T(128)S(6)} %select_n.99, bf16[4,4,160,384]{3,2,1,0:T(8,128)(2,1)S(1)} %fusion.18, bf16[4,4,160,384]{3,2,1,0:T(8,128)(2,1)S(1)} %fusion.17, s32[]{:T(128)S(6)} %select_n.101), kind=kLoop, calls=%fused_computation.35 | loop fusion | flops 1966080 | bytes 7864328 | tf_op jit(solution)/shard_map/concatenate | solution.py:135
  108.0 0.4 pad_maximum_fusion.1
  108.5 0.0 slice-start.2
  108.5 0.5 fusion.35
  109.0 0.0 slice-start.3
  109.0 0.6 copy.61
  109.6 0.6 pad.20.clone
  110.1 0.2 copy.40
  110.4 0.2 slice-done.2
  110.6 1.3 %slice-done.3 = s8[3768320]{0:T(1024)(128)(4,1)S(1)} async-done(((s8[7962624]{0:T(1024)(128)(4,1)}), s8[3768320]{0:T(1024)(128)(4,1)S(1)}, s32[]{:S(2)}) %slice-start.3) | async-done | bytes 3768344
  111.9 3.8 %fusion.57 = f32[1,2,8,21,384]{4,2,3,1,0:T(8,128)S(1)} fusion(bf16[3,3,3,384,384]{4,3,2,1,0:T(8,128)(2,1)S(1)} %bitcast.104, bf16[3,4,1,7,2,384]{5,3,4,1,0,2:T(8,128)(2,1)S(1)} %slice.46, bf16[3,4,1,8,21,384]{5,3,4,1,0,2:T(8,128)(2,1)S(1)} %copy.40, pred[8,21]{0,1:T(8,128)(4,1)S(1)} %copy-done.8), kind=kOutput, calls=%fused_computation.65 | convolution fusion | flops 2680657920 | bytes 10156200 | tf_op jit(solution)/shard_map/conv_general_dilated | solution.py:44
  115.7 0.3 copy.41
  116.0 0.2 slice.47
  116.2 1.7 %fusion.39 = f32[3,12,8,384]{3,2,1,0:T(8,128)S(1)} fusion(bf16[6,10,160,3,96]{4,2,1,3,0:T(8,128)(2,1)S(1)} %pad_maximum_fusion, s32[]{:T(128)S(6)} %select_n.106, s32[]{:T(128)S(6)} %select_n.108, bf16[4,4,160,384]{3,2,1,0:T(8,128)(2,1)S(1)} %get-tuple-element.4, bf16[4,4,160,384]{3,2,1,0:T(8,128)(2,1)S(1)} %get-tuple-element.3), kind=kOutput, calls=%fused_computation.61 | convolution fusion | flops 1134428160 | bytes 8306696 | tf_op jit(solution)/shard_map/dot_general | solution.py:98
  118.0 1.7 %fusion.44 = f32[3,12,8,384]{3,2,1,0:T(8,128)S(1)} fusion(bf16[6,10,160,3,96]{4,2,1,3,0:T(8,128)(2,1)S(1)} %pad_maximum_fusion, s32[]{:T(128)S(6)} %select_n.110, s32[]{:T(128)S(6)} %select_n.112, bf16[4,4,160,384]{3,2,1,0:T(8,128)(2,1)S(1)} %get-tuple-element.4, bf16[4,4,160,384]{3,2,1,0:T(8,128)(2,1)S(1)} %get-tuple-element.3), kind=kOutput, calls=%fused_computation.62 | convolution fusion | flops 1134428160 | bytes 8306696 | tf_op jit(solution)/shard_map/dot_general | solution.py:98
  119.8 0.0 copy-start.1
  119.8 0.0 copy-start.3
  119.8 0.0 copy-start.7
  119.8 2.0 %fusion.49 = f32[3,12,8,384]{3,2,1,0:T(8,128)S(1)} fusion(bf16[6,10,160,3,96]{4,2,1,3,0:T(8,128)(2,1)S(1)} %pad_maximum_fusion, s32[]{:T(128)S(6)} %select_n.114, s32[]{:T(128)S(6)} %select_n.116, bf16[4,4,160,384]{3,2,1,0:T(8,128)(2,1)S(1)} %get-tuple-element.4, bf16[4,4,160,384]{3,2,1,0:T(8,128)(2,1)S(1)} %get-tuple-element.3), kind=kOutput, calls=%fused_computation.63 | convolution fusion | flops 1134428160 | bytes 8306696 | tf_op jit(solution)/shard_map/dot_general | solution.py:98
  121.8 1.2 add_convert_fusion
  123.0 1.6 %fusion.62 = f32[2592,96]{0,1:T(8,128)} fusion(s32[]{:T(128)S(6)} %select_n.117, f32[1152,96]{0,1:T(8,128)S(1)} %bitcast.96, f32[1152,96]{0,1:T(8,128)S(1)} %bitcast.97, f32[1152,96]{0,1:T(8,128)S(1)} %bitcast.98), kind=kLoop, calls=%fused_computation.68 | loop fusion | flops 746496 | bytes 2322436 | tf_op jit(solution)/shard_map/mul | solution.py:197
  (36 shorter events, 0.5 us)
Async XLA Ops:
  0.6 45.9 %copy-start.4 = (bf16[1,2,160,384]{3,2,1,0:T(8,128)(2,1)S(1)}, bf16[1,2,160,384]{3,2,1,0:T(8,128)(2,1)}, u32[]{:S(2)}) copy-start(bf16[1,2,160,384]{3,2,1,0:T(8,128)(2,1)} %param.9) | copy-start | bytes 737284
  4.0 15.4 %collective-permute-start = (bf16[1,2,160,768]{3,2,1,0:T(8,128)(2,1)S(1)}, bf16[1,2,160,768]{3,2,1,0:T(8,128)(2,1)S(1)}, u32[]{:S(2)}, u32[]{:S(2)}) collective-permute-start(bf16[1,2,160,768]{3,2,1,0:T(8,128)(2,1)S(1)} %pad_maximum_fusion.5), channel_id=1, source_target_pairs={{0,4},{4,8},{8,12},{1,5},{5,9},{9,13},{2,6},{6,10},{10,14},{3,7},{... | collective-permute-start | bytes 1474568 | tf_op jit(solution)/shard_map/ppermute | solution.py:153
  9.0 14.8 %collective-permute-start.3 = (bf16[1,2,160,768]{3,2,1,0:T(8,128)(2,1)S(1)}, bf16[1,2,160,768]{3,2,1,0:T(8,128)(2,1)S(1)}, u32[]{:S(2)}, u32[]{:S(2)}) collective-permute-start(bf16[1,2,160,768]{3,2,1,0:T(8,128)(2,1)S(1)} %pad_maximum_fusion.5), channel_id=1, source_target_pairs={{4,0},{8,4},{12,8},{5,1},{9,5},{13,9},{6,2},{10,6},{14,10},{7,3},{... | collective-permute-start | bytes 1474568 | tf_op jit(solution)/shard_map/ppermute | solution.py:154
  19.4 14.0 %collective-permute-start.1 = (bf16[1,2,160,768]{3,2,1,0:T(8,128)(2,1)S(1)}, bf16[1,2,160,768]{3,2,1,0:T(8,128)(2,1)S(1)}, u32[]{:S(2)}, u32[]{:S(2)}) collective-permute-start(bf16[1,2,160,768]{3,2,1,0:T(8,128)(2,1)S(1)} %collective-permute-done), channel_id=1, source_target_pairs={{0,4},{4,8},{8,12},{1,5},{5,9},{9,13},{2,6},{6,10},{10,14},{3,7},{... | collective-permute-start | bytes 1474568 | tf_op jit(solution)/shard_map/ppermute | solution.py:153
  23.8 14.0 %collective-permute-start.4 = (bf16[1,2,160,768]{3,2,1,0:T(8,128)(2,1)S(1)}, bf16[1,2,160,768]{3,2,1,0:T(8,128)(2,1)S(1)}, u32[]{:S(2)}, u32[]{:S(2)}) collective-permute-start(bf16[1,2,160,768]{3,2,1,0:T(8,128)(2,1)S(1)} %collective-permute-done.3), channel_id=1, source_target_pairs={{4,0},{8,4},{12,8},{5,1},{9,5},{13,9},{6,2},{10,6},{14,10},{7,3},{... | collective-permute-start | bytes 1474568 | tf_op jit(solution)/shard_map/ppermute | solution.py:154
  33.4 13.1 %collective-permute-start.2 = (bf16[1,2,160,768]{3,2,1,0:T(8,128)(2,1)S(1)}, bf16[1,2,160,768]{3,2,1,0:T(8,128)(2,1)S(1)}, u32[]{:S(2)}, u32[]{:S(2)}) collective-permute-start(bf16[1,2,160,768]{3,2,1,0:T(8,128)(2,1)S(1)} %collective-permute-done.1), channel_id=1, source_target_pairs={{0,4},{4,8},{8,12},{1,5},{5,9},{9,13},{2,6},{6,10},{10,14},{3,7},{... | collective-permute-start | bytes 1474568 | tf_op jit(solution)/shard_map/ppermute | solution.py:153
  37.8 12.8 %collective-permute-start.5 = (bf16[1,2,160,768]{3,2,1,0:T(8,128)(2,1)S(1)}, bf16[1,2,160,768]{3,2,1,0:T(8,128)(2,1)S(1)}, u32[]{:S(2)}, u32[]{:S(2)}) collective-permute-start(bf16[1,2,160,768]{3,2,1,0:T(8,128)(2,1)S(1)} %collective-permute-done.4), channel_id=1, source_target_pairs={{4,0},{8,4},{12,8},{5,1},{9,5},{13,9},{6,2},{10,6},{14,10},{7,3},{... | collective-permute-start | bytes 1474568 | tf_op jit(solution)/shard_map/ppermute | solution.py:154
  50.9 23.8 %collective-permute-start.6 = (bf16[4,2,160,384]{3,2,1,0:T(8,128)(2,1)S(1)}, bf16[4,2,160,384]{3,2,1,0:T(8,128)(2,1)}, u32[]{:S(2)}, u32[]{:S(2)}) collective-permute-start(bf16[4,2,160,384]{3,2,1,0:T(8,128)(2,1)S(1)} %get-tuple-element.6), channel_id=1, source_target_pairs={{0,2},{1,3},{2,0},{3,1},{4,6},{5,7},{6,4},{7,5},{8,10},{9,11},{10,... | collective-permute-start | bytes 2949128 | tf_op jit(solution)/shard_map/ppermute | solution.py:116
  53.4 11.8 %collective-permute-start.9 = (bf16[3,1,160,384]{3,2,1,0:T(8,128)(2,1)}, bf16[3,1,160,384]{3,2,1,0:T(8,128)(2,1)}, u32[]{:S(2)}, u32[]{:S(2)}) collective-permute-start(bf16[3,1,160,384]{3,2,1,0:T(8,128)(2,1)} %get-tuple-element.13), channel_id=1, source_target_pairs={{1,0},{2,1},{3,2},{5,4},{6,5},{7,6},{9,8},{10,9},{11,10},{13,12},{... | collective-permute-start | bytes 1105928 | tf_op jit(solution)/shard_map/ppermute | solution.py:25
  54.7 10.6 %collective-permute-start.8 = (bf16[3,1,160,384]{3,2,1,0:T(8,128)(2,1)}, bf16[3,1,160,384]{3,2,1,0:T(8,128)(2,1)}, u32[]{:S(2)}, u32[]{:S(2)}) collective-permute-start(bf16[3,1,160,384]{3,2,1,0:T(8,128)(2,1)} %get-tuple-element.12), channel_id=1, source_target_pairs={{0,1},{1,2},{2,3},{4,5},{5,6},{6,7},{8,9},{9,10},{10,11},{12,13},{... | collective-permute-start | bytes 1105928 | tf_op jit(solution)/shard_map/ppermute | solution.py:23
  61.5 31.6 %all-to-all-start = ((bf16[4,2,160,384]{2,1,0,3:T(2,128)(2,1)}), bf16[4,2,160,384]{2,1,0,3:T(2,128)(2,1)S(1)}, u32[]{:S(2)}, u32[]{:S(2)}) async-start(bf16[4,2,160,384]{2,1,0,3:T(2,128)(2,1)} %copy.48), calls=%async_computation | async-start | bytes 3145728 | tf_op jit(solution)/shard_map/all_to_all | solution.py:184
  65.3 23.2 %slice-start = ((s8[7962624]{0:T(1024)(128)(4,1)}), s8[4194304]{0:T(1024)(128)(4,1)S(1)}, s32[]{:S(2)}) async-start(s8[7962624]{0:T(1024)(128)(4,1)} %bitcast.99), calls=%async_computation.1 | async-start | bytes 8388608
  67.6 20.9 %slice-start.1 = ((s8[7962624]{0:T(1024)(128)(4,1)}), s8[3768320]{0:T(1024)(128)(4,1)S(1)}, s32[]{:S(2)}) async-start(s8[7962624]{0:T(1024)(128)(4,1)} %bitcast.99), calls=%async_computation.2 | async-start | bytes 7536640
  68.4 20.1 %copy-start.8 = (pred[8,21]{0,1:T(8,128)(4,1)S(1)}, pred[8,21]{0,1:T(8,128)(4,1)}, u32[]{:S(2)}) copy-start(pred[8,21]{0,1:T(8,128)(4,1)} %constant.126) | copy-start | bytes 508
  77.4 25.1 %collective-permute-start.7 = (bf16[4,4,160,384]{3,2,1,0:T(8,128)(2,1)}, bf16[4,4,160,384]{3,2,1,0:T(8,128)(2,1)}, u32[]{:S(2)}, u32[]{:S(2)}) collective-permute-start(bf16[4,4,160,384]{3,2,1,0:T(8,128)(2,1)} %pad_maximum_fusion.3), channel_id=1, source_target_pairs={{0,1},{1,0},{2,3},{3,2},{4,5},{5,4},{6,7},{7,6},{8,9},{9,8},{10,11... | collective-permute-start | bytes 5898248 | tf_op jit(solution)/shard_map/ppermute | solution.py:122
  88.5 4.3 %copy-start.2 = (bf16[1,2,160,384]{3,2,1,0:T(8,128)(2,1)S(1)}, bf16[1,2,160,384]{3,2,1,0:T(8,128)(2,1)}, u32[]{:S(2)}) copy-start(bf16[1,2,160,384]{3,2,1,0:T(8,128)(2,1)} %param.5) | copy-start | bytes 737284
  88.5 4.3 %copy-start.6 = (f32[384]{0:T(512)S(1)}, f32[384]{0:T(512)}, u32[]{:S(2)}) copy-start(f32[384]{0:T(512)} %param.6) | copy-start | bytes 4612
  92.7 7.7 %copy-start = (f32[1,2,1,160,384]{4,1,3,2,0:T(2,128)}, f32[1,2,1,160,384]{4,1,3,2,0:T(2,128)S(1)}, u32[]{:S(2)}) copy-start(f32[1,2,1,160,384]{4,1,3,2,0:T(2,128)S(1)} %slice.49) | copy-start | bytes 1474564
  108.5 2.2 %slice-start.2 = ((s8[7962624]{0:T(1024)(128)(4,1)}), s8[4194304]{0:T(1024)(128)(4,1)S(1)}, s32[]{:S(2)}) async-start(s8[7962624]{0:T(1024)(128)(4,1)} %bitcast.102), calls=%async_computation.3 | async-start | bytes 8388608
  109.0 3.0 %slice-start.3 = ((s8[7962624]{0:T(1024)(128)(4,1)}), s8[3768320]{0:T(1024)(128)(4,1)S(1)}, s32[]{:S(2)}) async-start(s8[7962624]{0:T(1024)(128)(4,1)} %bitcast.102), calls=%async_computation.4 | async-start | bytes 7536640
  119.8 2.0 %copy-start.1 = (f32[1,2,1,160,384]{4,1,3,2,0:T(2,128)S(1)}, f32[1,2,1,160,384]{4,1,3,2,0:T(2,128)}, u32[]{:S(2)}) copy-start(f32[1,2,1,160,384]{4,1,3,2,0:T(2,128)} %copy-done) | copy-start | bytes 1474564
  119.8 2.0 %copy-start.3 = (bf16[1,2,160,384]{3,2,1,0:T(8,128)(2,1)S(1)}, bf16[1,2,160,384]{3,2,1,0:T(8,128)(2,1)}, u32[]{:S(2)}) copy-start(bf16[1,2,160,384]{3,2,1,0:T(8,128)(2,1)} %param.5) | copy-start | bytes 737284
  119.8 2.0 %copy-start.5 = (bf16[1,2,160,384]{3,2,1,0:T(8,128)(2,1)S(1)}, bf16[1,2,160,384]{3,2,1,0:T(8,128)(2,1)}, u32[]{:S(2)}) copy-start(bf16[1,2,160,384]{3,2,1,0:T(8,128)(2,1)} %param.9) | copy-start | bytes 737284
  119.8 2.0 %copy-start.7 = (f32[384]{0:T(512)S(1)}, f32[384]{0:T(512)}, u32[]{:S(2)}) copy-start(f32[384]{0:T(512)} %param.7) | copy-start | bytes 4612

commit v15 on v14

--- a/solution.py
+++ b/solution.py
@@ -177,10 +177,9 @@
     inverse_root = 1.0 / math.sqrt(total_frames * total_rows * col_count)
     weight_cube = weight.reshape(3, 3, 3, channels, channels)
 
-    both_frames = gather_frames(jnp.concatenate([hidden, cotangent], axis=-1))
-    hidden_all = gather_rows(both_frames[..., :channels], height_count)
-
-    cot_frames = both_frames[..., channels:]
+    hidden_all = gather_rows(gather_frames(hidden), height_count)
+
+    cot_frames = gather_frames(cotangent)
     cot_all = lax.all_to_all(cot_frames, "height", split_axis=3, concat_axis=1, tiled=True)
 
     window = lax.dynamic_slice(

time: 125 us -> 159 us (1.27)
  waiting for transfers between devices: 34.8 us -> 64.1 us
  starting transfers between devices: 38.9 us -> 49.4 us
  other arithmetic: 17.3 us -> 10.9 us
    all_to_all x1, waiting for transfers between devices: 0.01 us -> 19.8 us  [local(): lax.all_to_all(cot_frames, 'height', split_axis=3, concat_axis=1, tiled=T...]
    ppermute x3 -> x6, starting transfers between devices: 13.8 us -> 25.9 us  [gather_frames(): rising = lax.ppermute(rising, 'tm', up)]
    ppermute x1, starting transfers between devices: 11.1 us -> 0.01 us  [gather_rows(): twins = lax.ppermute(stacked, 'height', sibling)]
    ppermute x1, waiting for transfers between devices: 6.21 us -> 16.5 us  [gather_rows(): lax.ppermute(own, 'height', [(i, (i + 2 * step) % height_count) for i in...]
    ppermute x1, starting transfers between devices: 1.56 us -> 9.67 us  [gather_rows(): lax.ppermute(own, 'height', [(i, (i + 2 * step) % height_count) for i in...]
    ppermute x3 -> x6, waiting for transfers between devices: 24.7 us -> 16.7 us  [gather_frames(): rising = lax.ppermute(rising, 'tm', up)]
    ppermute x3 -> x6, starting transfers between devices: 3.88 us -> 7.74 us  [gather_frames(): falling = lax.ppermute(falling, 'tm', down)]
    ppermute x1, waiting for transfers between devices: 0.01 us -> 3.65 us  [padded(): lax.ppermute(head, axis, [((i + 1) % count, i) for i in range(ends)])]
  transfers between devices with their start and end apart: 11 -> 17, of which waited for: 5 -> 11; matrix products, arithmetic and copies ran while one was open for 19% -> 8% of each run, Pallas kernels for 0% -> 0%
where the time goes in v15:
time: 159 us
  waiting for transfers between devices  64.1 us (40%)
  starting transfers between devices  49.4 us (31%)
  local copies, waits for them, and re-layouts  20 us (13%)
  matrix products  12.8 us (8%)
  other arithmetic  10.9 us (7%)
    ppermute x6, starting transfers between devices, gather_frames(): rising = lax.ppermute(rising, 'tm', up)  25.9 us
    all_to_all x1, waiting for transfers between devices, local(): lax.all_to_all(cot_frames, 'height', split_axis=3, concat_axis=1, tiled=T...  19.8 us
    ppermute x6, waiting for transfers between devices, gather_frames(): rising = lax.ppermute(rising, 'tm', up)  16.7 us
    ppermute x1, waiting for transfers between devices, gather_rows(): lax.ppermute(own, 'height', [(i, (i + 2 * step) % height_count) for i in...  16.5 us
    ppermute x1, starting transfers between devices, gather_rows(): lax.ppermute(own, 'height', [(i, (i + 2 * step) % height_count) for i in...  9.67 us
    ppermute x6, starting transfers between devices, gather_frames(): falling = lax.ppermute(falling, 'tm', down)  7.74 us
    ppermute x6, waiting for transfers between devices, gather_frames(): falling = lax.ppermute(falling, 'tm', down)  7.39 us
    unnamed x36, local copies, waits for them, and re-layouts  6.02 us
  transfers between devices with their start and end apart: 17, of which 11 were waited for; matrix products, arithmetic and copies ran while one was open for 8% of the time, Pallas kernels for 0%

profile of v15, /device:TPU:0, one launch (start us, length us, event | category | flops | bytes accessed | tf_op | source)
XLA Modules:
  0.0 158.7 jit_solution(13859714794268916510)
XLA Ops:
  0.6 4.9 %collective-permute-start.8 = (bf16[1,2,160,384]{3,2,1,0:T(8,128)(2,1)}, bf16[1,2,160,384]{3,2,1,0:T(8,128)(2,1)S(1)}, u32[]{:S(2)}, u32[]{:S(2)}) collective-permute-start(bf16[1,2,160,384]{3,2,1,0:T(8,128)(2,1)} %param.9), channel_id=1, source_target_pairs={{0,4},{4,8},{8,12},{1,5},{5,9},{9,13},{2,6},{6,10},{10,14},{3,7},{... | collective-permute-start | bytes 737288 | tf_op jit(solution)/shard_map/ppermute | solution.py:153
  5.6 1.3 collective-permute-start.11
  6.9 4.2 %collective-permute-done.8 = bf16[1,2,160,384]{3,2,1,0:T(8,128)(2,1)S(1)} collective-permute-done((bf16[1,2,160,384]{3,2,1,0:T(8,128)(2,1)}, bf16[1,2,160,384]{3,2,1,0:T(8,128)(2,1)S(1)}, u32[]{:S(2)}, u32[]{:S(2)}) %collective-permute-start.8) | collective-permute-done | bytes 245792 | tf_op jit(solution)/shard_map/ppermute | solution.py:153
  11.1 4.3 %collective-permute-start.9 = (bf16[1,2,160,384]{3,2,1,0:T(8,128)(2,1)S(1)}, bf16[1,2,160,384]{3,2,1,0:T(8,128)(2,1)S(1)}, u32[]{:S(2)}, u32[]{:S(2)}) collective-permute-start(bf16[1,2,160,384]{3,2,1,0:T(8,128)(2,1)S(1)} %collective-permute-done.8), channel_id=1, source_target_pairs={{0,4},{4,8},{8,12},{1,5},{5,9},{9,13},{2,6},{6,10},{10,14},{3,7},{... | collective-permute-start | bytes 737288 | tf_op jit(solution)/shard_map/ppermute | solution.py:153
  15.4 1.3 collective-permute-start.12
  16.7 3.0 %collective-permute-done.9 = bf16[1,2,160,384]{3,2,1,0:T(8,128)(2,1)S(1)} collective-permute-done((bf16[1,2,160,384]{3,2,1,0:T(8,128)(2,1)S(1)}, bf16[1,2,160,384]{3,2,1,0:T(8,128)(2,1)S(1)}, u32[]{:S(2)}, u32[]{:S(2)}) %collective-permute-start.9) | collective-permute-done | bytes 245792 | tf_op jit(solution)/shard_map/ppermute | solution.py:153
  19.7 4.4 %collective-permute-start.10 = (bf16[1,2,160,384]{3,2,1,0:T(8,128)(2,1)S(1)}, bf16[1,2,160,384]{3,2,1,0:T(8,128)(2,1)S(1)}, u32[]{:S(2)}, u32[]{:S(2)}) collective-permute-start(bf16[1,2,160,384]{3,2,1,0:T(8,128)(2,1)S(1)} %collective-permute-done.9), channel_id=1, source_target_pairs={{0,4},{4,8},{8,12},{1,5},{5,9},{9,13},{2,6},{6,10},{10,14},{3,7},{... | collective-permute-start | bytes 737288 | tf_op jit(solution)/shard_map/ppermute | solution.py:153
  24.1 1.3 collective-permute-start.13
  25.4 2.4 %collective-permute-done.10 = bf16[1,2,160,384]{3,2,1,0:T(8,128)(2,1)S(1)} collective-permute-done((bf16[1,2,160,384]{3,2,1,0:T(8,128)(2,1)S(1)}, bf16[1,2,160,384]{3,2,1,0:T(8,128)(2,1)S(1)}, u32[]{:S(2)}, u32[]{:S(2)}) %collective-permute-start.10) | collective-permute-done | bytes 245792 | tf_op jit(solution)/shard_map/ppermute | solution.py:153
  27.9 1.0 constant_dynamic-update-slice_fusion.10
  29.0 3.2 %collective-permute-done.13 = bf16[1,2,160,384]{3,2,1,0:T(8,128)(2,1)S(1)} collective-permute-done((bf16[1,2,160,384]{3,2,1,0:T(8,128)(2,1)S(1)}, bf16[1,2,160,384]{3,2,1,0:T(8,128)(2,1)S(1)}, u32[]{:S(2)}, u32[]{:S(2)}) %collective-permute-start.13) | collective-permute-done | bytes 245792 | tf_op jit(solution)/shard_map/ppermute | solution.py:154
  32.5 1.3 collective-permute-start.14
  33.8 1.3 collective-permute-start.15
  35.4 3.6 %collective-permute-done.15 = bf16[3,1,160,384]{3,2,1,0:T(8,128)(2,1)S(1)} collective-permute-done((bf16[3,1,160,384]{3,2,1,0:T(8,128)(2,1)S(1)}, bf16[3,1,160,384]{3,2,1,0:T(8,128)(2,1)S(1)}, u32[]{:S(2)}, u32[]{:S(2)}) %collective-permute-start.15) | collective-permute-done | bytes 368672 | tf_op jit(solution)/shard_map/ppermute | solution.py:25
  39.1 0.5 fusion.37
  39.6 0.6 copy.81
  40.2 0.6 pad.22.clone
  40.8 0.2 copy.64
  41.0 0.6 slice-done.1
  41.6 3.8 %fusion.54 = f32[1,2,8,21,384]{4,2,3,1,0:T(8,128)S(1)} fusion(bf16[3,3,3,384,384]{4,3,2,1,0:T(8,128)(2,1)S(1)} %bitcast.101, bf16[3,4,1,7,2,384]{5,3,4,1,0,2:T(8,128)(2,1)S(1)} %slice.40, bf16[3,4,1,8,21,384]{5,3,4,1,0,2:T(8,128)(2,1)S(1)} %copy.64, pred[8,21]{0,1:T(8,128)(4,1)S(1)} %copy-done.6), kind=kOutput, calls=%fused_computation.64 | convolution fusion | flops 2680657920 | bytes 10156200 | tf_op jit(solution)/shard_map/conv_general_dilated | solution.py:57
  45.4 0.3 copy.65
  45.7 0.2 slice.41
  45.9 0.2 copy-done.4
  46.1 0.4 multiply_reduce_fusion
  46.5 1.1 add_convert_fusion
  47.6 3.5 %collective-permute-start = (bf16[1,2,160,384]{3,2,1,0:T(8,128)(2,1)S(1)}, bf16[1,2,160,384]{3,2,1,0:T(8,128)(2,1)S(1)}, u32[]{:S(2)}, u32[]{:S(2)}) collective-permute-start(bf16[1,2,160,384]{3,2,1,0:T(8,128)(2,1)S(1)} %get-tuple-element.13), channel_id=1, source_target_pairs={{0,4},{4,8},{8,12},{1,5},{5,9},{9,13},{2,6},{6,10},{10,14},{3,7},{... | collective-permute-start | bytes 737288 | tf_op jit(solution)/shard_map/ppermute | solution.py:153
  51.1 1.3 collective-permute-start.3
  52.4 2.4 %collective-permute-done = bf16[1,2,160,384]{3,2,1,0:T(8,128)(2,1)S(1)} collective-permute-done((bf16[1,2,160,384]{3,2,1,0:T(8,128)(2,1)S(1)}, bf16[1,2,160,384]{3,2,1,0:T(8,128)(2,1)S(1)}, u32[]{:S(2)}, u32[]{:S(2)}) %collective-permute-start) | collective-permute-done | bytes 245792 | tf_op jit(solution)/shard_map/ppermute | solution.py:153
  54.8 4.4 %collective-permute-start.1 = (bf16[1,2,160,384]{3,2,1,0:T(8,128)(2,1)S(1)}, bf16[1,2,160,384]{3,2,1,0:T(8,128)(2,1)S(1)}, u32[]{:S(2)}, u32[]{:S(2)}) collective-permute-start(bf16[1,2,160,384]{3,2,1,0:T(8,128)(2,1)S(1)} %collective-permute-done), channel_id=1, source_target_pairs={{0,4},{4,8},{8,12},{1,5},{5,9},{9,13},{2,6},{6,10},{10,14},{3,7},{... | collective-permute-start | bytes 737288 | tf_op jit(solution)/shard_map/ppermute | solution.py:153
  59.2 1.3 collective-permute-start.4
  60.5 2.4 %collective-permute-done.1 = bf16[1,2,160,384]{3,2,1,0:T(8,128)(2,1)S(1)} collective-permute-done((bf16[1,2,160,384]{3,2,1,0:T(8,128)(2,1)S(1)}, bf16[1,2,160,384]{3,2,1,0:T(8,128)(2,1)S(1)}, u32[]{:S(2)}, u32[]{:S(2)}) %collective-permute-start.1) | collective-permute-done | bytes 245792 | tf_op jit(solution)/shard_map/ppermute | solution.py:153
  62.9 4.4 %collective-permute-start.2 = (bf16[1,2,160,384]{3,2,1,0:T(8,128)(2,1)S(1)}, bf16[1,2,160,384]{3,2,1,0:T(8,128)(2,1)S(1)}, u32[]{:S(2)}, u32[]{:S(2)}) collective-permute-start(bf16[1,2,160,384]{3,2,1,0:T(8,128)(2,1)S(1)} %collective-permute-done.1), channel_id=1, source_target_pairs={{0,4},{4,8},{8,12},{1,5},{5,9},{9,13},{2,6},{6,10},{10,14},{3,7},{... | collective-permute-start | bytes 737288 | tf_op jit(solution)/shard_map/ppermute | solution.py:153
  67.3 1.3 collective-permute-start.5
  68.6 2.4 %collective-permute-done.2 = bf16[1,2,160,384]{3,2,1,0:T(8,128)(2,1)S(1)} collective-permute-done((bf16[1,2,160,384]{3,2,1,0:T(8,128)(2,1)S(1)}, bf16[1,2,160,384]{3,2,1,0:T(8,128)(2,1)S(1)}, u32[]{:S(2)}, u32[]{:S(2)}) %collective-permute-start.2) | collective-permute-done | bytes 245792 | tf_op jit(solution)/shard_map/ppermute | solution.py:153
  71.2 4.1 %collective-permute-done.5 = bf16[1,2,160,384]{3,2,1,0:T(8,128)(2,1)S(1)} collective-permute-done((bf16[1,2,160,384]{3,2,1,0:T(8,128)(2,1)S(1)}, bf16[1,2,160,384]{3,2,1,0:T(8,128)(2,1)S(1)}, u32[]{:S(2)}, u32[]{:S(2)}) %collective-permute-start.5) | collective-permute-done | bytes 245792 | tf_op jit(solution)/shard_map/ppermute | solution.py:154
  75.5 9.7 %collective-permute-start.6 = (bf16[4,2,160,384]{3,2,1,0:T(8,128)(2,1)S(1)}, bf16[4,2,160,384]{3,2,1,0:T(8,128)(2,1)S(1)}, u32[]{:S(2)}, u32[]{:S(2)}) collective-permute-start(bf16[4,2,160,384]{3,2,1,0:T(8,128)(2,1)S(1)} %constant_dynamic-slice_fusion.1), channel_id=1, source_target_pairs={{0,2},{1,3},{2,0},{3,1},{4,6},{5,7},{6,4},{7,5},{8,10},{9,11},{10,... | collective-permute-start | bytes 2949128 | tf_op jit(solution)/shard_map/ppermute | solution.py:116
  85.2 16.5 %collective-permute-done.6 = bf16[4,2,160,384]{3,2,1,0:T(8,128)(2,1)S(1)} collective-permute-done((bf16[4,2,160,384]{3,2,1,0:T(8,128)(2,1)S(1)}, bf16[4,2,160,384]{3,2,1,0:T(8,128)(2,1)S(1)}, u32[]{:S(2)}, u32[]{:S(2)}) %collective-permute-start.6) | collective-permute-done | bytes 983072 | tf_op jit(solution)/shard_map/ppermute | solution.py:116
  101.7 1.6 %pad_maximum_fusion.3 = bf16[4,4,160,384]{3,2,1,0:T(8,128)(2,1)} fusion(bf16[4,2,160,384]{3,2,1,0:T(8,128)(2,1)S(1)} %collective-permute-done.6, bf16[4,2,160,384]{3,2,1,0:T(8,128)(2,1)S(1)} %constant_dynamic-slice_fusion.1), kind=kLoop, calls=%fused_computation.30 | loop fusion | flops 983040 | bytes 3932160 | tf_op jit(solution)/shard_map/concatenate | solution.py:121
  103.3 2.5 %copy.67 = bf16[4,2,160,384]{2,0,1,3:T(4,128)(2,1)} copy(bf16[4,2,160,384]{3,2,1,0:T(8,128)(2,1)S(1)} %constant_dynamic-slice_fusion) | data formatting | bytes 1966080 | tf_op jit(solution)/shard_map/dynamic_slice | solution.py:158
  105.9 3.6 %all-to-all-start = ((bf16[4,2,160,384]{2,0,1,3:T(4,128)(2,1)}), bf16[4,2,160,384]{2,0,1,3:T(4,128)(2,1)S(1)}, u32[]{:S(2)}, u32[]{:S(2)}) async-start(bf16[4,2,160,384]{2,0,1,3:T(4,128)(2,1)} %copy.67), calls=%async_computation | async-start | bytes 3145728 | tf_op jit(solution)/shard_map/all_to_all | solution.py:183
  109.7 19.8 %all-to-all-done = bf16[4,2,160,384]{2,0,1,3:T(4,128)(2,1)S(1)} async-done(((bf16[4,2,160,384]{2,0,1,3:T(4,128)(2,1)}), bf16[4,2,160,384]{2,0,1,3:T(4,128)(2,1)S(1)}, u32[]{:S(2)}, u32[]{:S(2)}) %all-to-all-start) | async-done | bytes 983072 | tf_op jit(solution)/shard_map/all_to_all | solution.py:183
  129.5 2.6 %copy.68 = bf16[4,2,160,4,96]{4,2,1,3,0:T(8,128)(2,1)} copy(bf16[4,2,160,4,96]{2,0,1,4,3:T(4,128)(2,1)S(1)} %bitcast.90) | data formatting | bytes 1966080 | tf_op jit(solution)/shard_map/all_to_all | solution.py:183
  132.1 3.5 %fusion.14 = (bf16[6,10,160,1,96]{4,2,1,3,0:T(8,128)(2,1)S(1)}, bf16[6,10,160,1,96]{4,2,1,3,0:T(8,128)(2,1)S(1)}, bf16[6,10,160,1,96]{4,2,1,3,0:T(8,128)(2,1)S(1)}) fusion(bf16[4,8,160,96]{3,2,1,0:T(8,128)(2,1)} %bitcast.93), kind=kLoop, calls=%fused_computation.26 | loop fusion | bytes 6512640 | tf_op jit(solution)/shard_map/stack | solution.py:82
  135.6 2.0 %pad_maximum_fusion = bf16[6,10,160,3,96]{4,2,1,3,0:T(8,128)(2,1)S(1)} fusion(bf16[6,10,160,1,96]{4,2,1,3,0:T(8,128)(2,1)S(1)} %get-tuple-element.9, bf16[6,10,160,1,96]{4,2,1,3,0:T(8,128)(2,1)S(1)} %get-tuple-element.8, bf16[6,10,160,1,96]{4,2,1,3,0:T(8,128)(2,1)S(1)} %get-tuple-element.7), kind=kLoop, calls=%fused_computation.1 | loop fusion | flops 5529600 | bytes 11059200 | tf_op jit(solution)/shard_map/stack | solution.py:82
  137.6 1.7 %fusion.80 = (bf16[4,2,160,384]{3,2,1,0:T(8,128)(2,1)S(1)}, bf16[4,2,160,384]{3,2,1,0:T(8,128)(2,1)S(1)}) fusion(bf16[4,4,160,384]{3,2,1,0:T(8,128)(2,1)} %collective-permute-done.7), kind=kLoop, calls=%fused_computation.113 | loop fusion | bytes 3932160 | tf_op jit(solution)/shard_map/slice | solution.py:127
  139.3 0.3 fusion.17
  139.7 0.8 copy-done.2
  140.5 0.3 fusion.18
  140.9 1.6 %fusion.20 = (bf16[4,4,160,384]{3,2,1,0:T(8,128)(2,1)S(1)}, bf16[4,4,160,384]{3,2,1,0:T(8,128)(2,1)S(1)}) fusion(s32[]{:T(128)S(6)} %select_n.100, bf16[4,4,160,384]{3,2,1,0:T(8,128)(2,1)S(1)} %fusion.18, bf16[4,4,160,384]{3,2,1,0:T(8,128)(2,1)S(1)} %fusion.17, s32[]{:T(128)S(6)} %select_n.102), kind=kLoop, calls=%fused_computation.35 | loop fusion | flops 1966080 | bytes 7864328 | tf_op jit(solution)/shard_map/concatenate | solution.py:135
  142.5 0.4 pad_maximum_fusion.1
  142.9 1.7 %fusion.49 = f32[3,12,8,384]{3,2,1,0:T(8,128)S(1)} fusion(bf16[6,10,160,3,96]{4,2,1,3,0:T(8,128)(2,1)S(1)} %pad_maximum_fusion, s32[]{:T(128)S(6)} %select_n.115, s32[]{:T(128)S(6)} %select_n.117, bf16[4,4,160,384]{3,2,1,0:T(8,128)(2,1)S(1)} %get-tuple-element.4, bf16[4,4,160,384]{3,2,1,0:T(8,128)(2,1)S(1)} %get-tuple-element.3), kind=kOutput, calls=%fused_computation.63 | convolution fusion | flops 1134428160 | bytes 8306696 | tf_op jit(solution)/shard_map/dot_general | solution.py:98
  144.7 1.7 %fusion.44 = f32[3,12,8,384]{3,2,1,0:T(8,128)S(1)} fusion(bf16[6,10,160,3,96]{4,2,1,3,0:T(8,128)(2,1)S(1)} %pad_maximum_fusion, s32[]{:T(128)S(6)} %select_n.111, s32[]{:T(128)S(6)} %select_n.113, bf16[4,4,160,384]{3,2,1,0:T(8,128)(2,1)S(1)} %get-tuple-element.4, bf16[4,4,160,384]{3,2,1,0:T(8,128)(2,1)S(1)} %get-tuple-element.3), kind=kOutput, calls=%fused_computation.62 | convolution fusion | flops 1134428160 | bytes 8306696 | tf_op jit(solution)/shard_map/dot_general | solution.py:98
  146.5 1.7 %fusion.39 = f32[3,12,8,384]{3,2,1,0:T(8,128)S(1)} fusion(bf16[6,10,160,3,96]{4,2,1,3,0:T(8,128)(2,1)S(1)} %pad_maximum_fusion, s32[]{:T(128)S(6)} %select_n.107, s32[]{:T(128)S(6)} %select_n.109, bf16[4,4,160,384]{3,2,1,0:T(8,128)(2,1)S(1)} %get-tuple-element.4, bf16[4,4,160,384]{3,2,1,0:T(8,128)(2,1)S(1)} %get-tuple-element.3), kind=kOutput, calls=%fused_computation.61 | convolution fusion | flops 1134428160 | bytes 8306696 | tf_op jit(solution)/shard_map/dot_general | solution.py:98
  148.3 0.5 fusion.35
  148.8 0.6 copy.80
  149.4 0.6 pad.20.clone
  150.0 0.2 copy.59
  150.2 0.2 slice-done.2
  150.5 1.3 slice-done.3
  151.7 3.8 %fusion.57 = f32[1,2,8,21,384]{4,2,3,1,0:T(8,128)S(1)} fusion(bf16[3,3,3,384,384]{4,3,2,1,0:T(8,128)(2,1)S(1)} %bitcast.104, bf16[3,4,1,7,2,384]{5,3,4,1,0,2:T(8,128)(2,1)S(1)} %slice.38, bf16[3,4,1,8,21,384]{5,3,4,1,0,2:T(8,128)(2,1)S(1)} %copy.59, pred[8,21]{0,1:T(8,128)(4,1)S(1)} %copy-done.6), kind=kOutput, calls=%fused_computation.65 | convolution fusion | flops 2680657920 | bytes 10156200 | tf_op jit(solution)/shard_map/conv_general_dilated | solution.py:44
  155.6 0.3 copy.60
  156.1 0.2 copy-done.5
  156.3 0.8 fusion.67
  157.0 1.6 %fusion.62 = f32[2592,96]{0,1:T(8,128)} fusion(s32[]{:T(128)S(6)} %select_n.118, f32[1152,96]{0,1:T(8,128)S(1)} %bitcast.98, f32[1152,96]{0,1:T(8,128)S(1)} %bitcast.97, f32[1152,96]{0,1:T(8,128)S(1)} %bitcast.96), kind=kLoop, calls=%fused_computation.68 | loop fusion | flops 746496 | bytes 2322436 | tf_op jit(solution)/shard_map/mul | solution.py:196
  (51 shorter events, 1.6 us)
Async XLA Ops:
  0.6 10.4 %collective-permute-start.8 = (bf16[1,2,160,384]{3,2,1,0:T(8,128)(2,1)}, bf16[1,2,160,384]{3,2,1,0:T(8,128)(2,1)S(1)}, u32[]{:S(2)}, u32[]{:S(2)}) collective-permute-start(bf16[1,2,160,384]{3,2,1,0:T(8,128)(2,1)} %param.9), channel_id=1, source_target_pairs={{0,4},{4,8},{8,12},{1,5},{5,9},{9,13},{2,6},{6,10},{10,14},{3,7},{... | collective-permute-start | bytes 737288 | tf_op jit(solution)/shard_map/ppermute | solution.py:153
  5.6 9.8 %collective-permute-start.11 = (bf16[1,2,160,384]{3,2,1,0:T(8,128)(2,1)}, bf16[1,2,160,384]{3,2,1,0:T(8,128)(2,1)S(1)}, u32[]{:S(2)}, u32[]{:S(2)}) collective-permute-start(bf16[1,2,160,384]{3,2,1,0:T(8,128)(2,1)} %param.9), channel_id=1, source_target_pairs={{4,0},{8,4},{12,8},{5,1},{9,5},{13,9},{6,2},{10,6},{14,10},{7,3},{... | collective-permute-start | bytes 737288 | tf_op jit(solution)/shard_map/ppermute | solution.py:154
  11.1 8.6 %collective-permute-start.9 = (bf16[1,2,160,384]{3,2,1,0:T(8,128)(2,1)S(1)}, bf16[1,2,160,384]{3,2,1,0:T(8,128)(2,1)S(1)}, u32[]{:S(2)}, u32[]{:S(2)}) collective-permute-start(bf16[1,2,160,384]{3,2,1,0:T(8,128)(2,1)S(1)} %collective-permute-done.8), channel_id=1, source_target_pairs={{0,4},{4,8},{8,12},{1,5},{5,9},{9,13},{2,6},{6,10},{10,14},{3,7},{... | collective-permute-start | bytes 737288 | tf_op jit(solution)/shard_map/ppermute | solution.py:153
  15.4 8.7 %collective-permute-start.12 = (bf16[1,2,160,384]{3,2,1,0:T(8,128)(2,1)S(1)}, bf16[1,2,160,384]{3,2,1,0:T(8,128)(2,1)S(1)}, u32[]{:S(2)}, u32[]{:S(2)}) collective-permute-start(bf16[1,2,160,384]{3,2,1,0:T(8,128)(2,1)S(1)} %collective-permute-done.11), channel_id=1, source_target_pairs={{4,0},{8,4},{12,8},{5,1},{9,5},{13,9},{6,2},{10,6},{14,10},{7,3},{... | collective-permute-start | bytes 737288 | tf_op jit(solution)/shard_map/ppermute | solution.py:154
  19.7 8.1 %collective-permute-start.10 = (bf16[1,2,160,384]{3,2,1,0:T(8,128)(2,1)S(1)}, bf16[1,2,160,384]{3,2,1,0:T(8,128)(2,1)S(1)}, u32[]{:S(2)}, u32[]{:S(2)}) collective-permute-start(bf16[1,2,160,384]{3,2,1,0:T(8,128)(2,1)S(1)} %collective-permute-done.9), channel_id=1, source_target_pairs={{0,4},{4,8},{8,12},{1,5},{5,9},{9,13},{2,6},{6,10},{10,14},{3,7},{... | collective-permute-start | bytes 737288 | tf_op jit(solution)/shard_map/ppermute | solution.py:153
  24.1 8.1 %collective-permute-start.13 = (bf16[1,2,160,384]{3,2,1,0:T(8,128)(2,1)S(1)}, bf16[1,2,160,384]{3,2,1,0:T(8,128)(2,1)S(1)}, u32[]{:S(2)}, u32[]{:S(2)}) collective-permute-start(bf16[1,2,160,384]{3,2,1,0:T(8,128)(2,1)S(1)} %collective-permute-done.12), channel_id=1, source_target_pairs={{4,0},{8,4},{12,8},{5,1},{9,5},{13,9},{6,2},{10,6},{14,10},{7,3},{... | collective-permute-start | bytes 737288 | tf_op jit(solution)/shard_map/ppermute | solution.py:154
  32.2 2.9 %copy-start = (bf16[1,2,160,384]{3,2,1,0:T(8,128)(2,1)S(1)}, bf16[1,2,160,384]{3,2,1,0:T(8,128)(2,1)}, u32[]{:S(2)}) copy-start(bf16[1,2,160,384]{3,2,1,0:T(8,128)(2,1)} %param.5) | copy-start | bytes 737284
  32.5 2.9 %collective-permute-start.14 = (bf16[3,1,160,384]{3,2,1,0:T(8,128)(2,1)S(1)}, bf16[3,1,160,384]{3,2,1,0:T(8,128)(2,1)S(1)}, u32[]{:S(2)}, u32[]{:S(2)}) collective-permute-start(bf16[3,1,160,384]{3,2,1,0:T(8,128)(2,1)S(1)} %get-tuple-element.10), channel_id=1, source_target_pairs={{0,1},{1,2},{2,3},{4,5},{5,6},{6,7},{8,9},{9,10},{10,11},{12,13},{... | collective-permute-start | bytes 1105928 | tf_op jit(solution)/shard_map/ppermute | solution.py:23
  33.8 5.3 %collective-permute-start.15 = (bf16[3,1,160,384]{3,2,1,0:T(8,128)(2,1)S(1)}, bf16[3,1,160,384]{3,2,1,0:T(8,128)(2,1)S(1)}, u32[]{:S(2)}, u32[]{:S(2)}) collective-permute-start(bf16[3,1,160,384]{3,2,1,0:T(8,128)(2,1)S(1)} %get-tuple-element.11), channel_id=1, source_target_pairs={{1,0},{2,1},{3,2},{5,4},{6,5},{7,6},{9,8},{10,9},{11,10},{13,12},{... | collective-permute-start | bytes 1105928 | tf_op jit(solution)/shard_map/ppermute | solution.py:25
  35.1 5.9 %slice-start = ((s8[7962624]{0:T(1024)(128)(4,1)}), s8[4194304]{0:T(1024)(128)(4,1)S(1)}, s32[]{:S(2)}) async-start(s8[7962624]{0:T(1024)(128)(4,1)} %bitcast.99), calls=%async_computation.1 | async-start | bytes 8388608
  39.6 2.1 %slice-start.1 = ((s8[7962624]{0:T(1024)(128)(4,1)}), s8[3768320]{0:T(1024)(128)(4,1)S(1)}, s32[]{:S(2)}) async-start(s8[7962624]{0:T(1024)(128)(4,1)} %bitcast.99), calls=%async_computation.2 | async-start | bytes 7536640
  40.7 0.9 copy-start.6
  45.4 0.7 copy-start.4
  45.4 1.1 copy-start.3
  47.6 7.2 %collective-permute-start = (bf16[1,2,160,384]{3,2,1,0:T(8,128)(2,1)S(1)}, bf16[1,2,160,384]{3,2,1,0:T(8,128)(2,1)S(1)}, u32[]{:S(2)}, u32[]{:S(2)}) collective-permute-start(bf16[1,2,160,384]{3,2,1,0:T(8,128)(2,1)S(1)} %get-tuple-element.13), channel_id=1, source_target_pairs={{0,4},{4,8},{8,12},{1,5},{5,9},{9,13},{2,6},{6,10},{10,14},{3,7},{... | collective-permute-start | bytes 737288 | tf_op jit(solution)/shard_map/ppermute | solution.py:153
  51.1 8.1 %collective-permute-start.3 = (bf16[1,2,160,384]{3,2,1,0:T(8,128)(2,1)S(1)}, bf16[1,2,160,384]{3,2,1,0:T(8,128)(2,1)S(1)}, u32[]{:S(2)}, u32[]{:S(2)}) collective-permute-start(bf16[1,2,160,384]{3,2,1,0:T(8,128)(2,1)S(1)} %get-tuple-element.13), channel_id=1, source_target_pairs={{4,0},{8,4},{12,8},{5,1},{9,5},{13,9},{6,2},{10,6},{14,10},{7,3},{... | collective-permute-start | bytes 737288 | tf_op jit(solution)/shard_map/ppermute | solution.py:154
  54.8 8.1 %collective-permute-start.1 = (bf16[1,2,160,384]{3,2,1,0:T(8,128)(2,1)S(1)}, bf16[1,2,160,384]{3,2,1,0:T(8,128)(2,1)S(1)}, u32[]{:S(2)}, u32[]{:S(2)}) collective-permute-start(bf16[1,2,160,384]{3,2,1,0:T(8,128)(2,1)S(1)} %collective-permute-done), channel_id=1, source_target_pairs={{0,4},{4,8},{8,12},{1,5},{5,9},{9,13},{2,6},{6,10},{10,14},{3,7},{... | collective-permute-start | bytes 737288 | tf_op jit(solution)/shard_map/ppermute | solution.py:153
  59.2 8.1 %collective-permute-start.4 = (bf16[1,2,160,384]{3,2,1,0:T(8,128)(2,1)S(1)}, bf16[1,2,160,384]{3,2,1,0:T(8,128)(2,1)S(1)}, u32[]{:S(2)}, u32[]{:S(2)}) collective-permute-start(bf16[1,2,160,384]{3,2,1,0:T(8,128)(2,1)S(1)} %collective-permute-done.3), channel_id=1, source_target_pairs={{4,0},{8,4},{12,8},{5,1},{9,5},{13,9},{6,2},{10,6},{14,10},{7,3},{... | collective-permute-start | bytes 737288 | tf_op jit(solution)/shard_map/ppermute | solution.py:154
  62.9 8.1 %collective-permute-start.2 = (bf16[1,2,160,384]{3,2,1,0:T(8,128)(2,1)S(1)}, bf16[1,2,160,384]{3,2,1,0:T(8,128)(2,1)S(1)}, u32[]{:S(2)}, u32[]{:S(2)}) collective-permute-start(bf16[1,2,160,384]{3,2,1,0:T(8,128)(2,1)S(1)} %collective-permute-done.1), channel_id=1, source_target_pairs={{0,4},{4,8},{8,12},{1,5},{5,9},{9,13},{2,6},{6,10},{10,14},{3,7},{... | collective-permute-start | bytes 737288 | tf_op jit(solution)/shard_map/ppermute | solution.py:153
  67.3 8.1 %collective-permute-start.5 = (bf16[1,2,160,384]{3,2,1,0:T(8,128)(2,1)S(1)}, bf16[1,2,160,384]{3,2,1,0:T(8,128)(2,1)S(1)}, u32[]{:S(2)}, u32[]{:S(2)}) collective-permute-start(bf16[1,2,160,384]{3,2,1,0:T(8,128)(2,1)S(1)} %collective-permute-done.4), channel_id=1, source_target_pairs={{4,0},{8,4},{12,8},{5,1},{9,5},{13,9},{6,2},{10,6},{14,10},{7,3},{... | collective-permute-start | bytes 737288 | tf_op jit(solution)/shard_map/ppermute | solution.py:154
  75.5 26.2 %collective-permute-start.6 = (bf16[4,2,160,384]{3,2,1,0:T(8,128)(2,1)S(1)}, bf16[4,2,160,384]{3,2,1,0:T(8,128)(2,1)S(1)}, u32[]{:S(2)}, u32[]{:S(2)}) collective-permute-start(bf16[4,2,160,384]{3,2,1,0:T(8,128)(2,1)S(1)} %constant_dynamic-slice_fusion.1), channel_id=1, source_target_pairs={{0,2},{1,3},{2,0},{3,1},{4,6},{5,7},{6,4},{7,5},{8,10},{9,11},{10,... | collective-permute-start | bytes 2949128 | tf_op jit(solution)/shard_map/ppermute | solution.py:116
  101.7 1.6 %copy-start.1 = (bf16[4,2,160,384]{3,2,1,0:T(8,128)(2,1)}, bf16[4,2,160,384]{3,2,1,0:T(8,128)(2,1)S(1)}, u32[]{:S(2)}) copy-start(bf16[4,2,160,384]{3,2,1,0:T(8,128)(2,1)S(1)} %collective-permute-done.6) | copy-start | bytes 2949124
  103.3 34.3 %collective-permute-start.7 = (bf16[4,4,160,384]{3,2,1,0:T(8,128)(2,1)}, bf16[4,4,160,384]{3,2,1,0:T(8,128)(2,1)}, u32[]{:S(2)}, u32[]{:S(2)}) collective-permute-start(bf16[4,4,160,384]{3,2,1,0:T(8,128)(2,1)} %pad_maximum_fusion.3), channel_id=1, source_target_pairs={{0,1},{1,0},{2,3},{3,2},{4,5},{5,4},{6,7},{7,6},{8,9},{9,8},{10,11... | collective-permute-start | bytes 5898248 | tf_op jit(solution)/shard_map/ppermute | solution.py:122
  105.9 23.6 %all-to-all-start = ((bf16[4,2,160,384]{2,0,1,3:T(4,128)(2,1)}), bf16[4,2,160,384]{2,0,1,3:T(4,128)(2,1)S(1)}, u32[]{:S(2)}, u32[]{:S(2)}) async-start(bf16[4,2,160,384]{2,0,1,3:T(4,128)(2,1)} %copy.67), calls=%async_computation | async-start | bytes 3145728 | tf_op jit(solution)/shard_map/all_to_all | solution.py:183
  139.3 1.2 copy-start.2
  148.3 2.2 %slice-start.2 = ((s8[7962624]{0:T(1024)(128)(4,1)}), s8[4194304]{0:T(1024)(128)(4,1)S(1)}, s32[]{:S(2)}) async-start(s8[7962624]{0:T(1024)(128)(4,1)} %bitcast.102), calls=%async_computation.3 | async-start | bytes 8388608
  148.8 3.0 %slice-start.3 = ((s8[7962624]{0:T(1024)(128)(4,1)}), s8[3768320]{0:T(1024)(128)(4,1)S(1)}, s32[]{:S(2)}) async-start(s8[7962624]{0:T(1024)(128)(4,1)} %bitcast.102), calls=%async_computation.4 | async-start | bytes 7536640
  155.6 0.7 copy-start.5

commit v16 on v14

--- a/solution.py
+++ b/solution.py
@@ -144,18 +144,9 @@
 
 def gather_frames(block):
     count = lax.axis_size("tm")
-    position = lax.axis_index("tm")
-    up = [(i, i + 1) for i in range(count - 1)]
-    down = [(i + 1, i) for i in range(count - 1)]
-    earlier, later = [], []
-    rising, falling = block, block
-    for step in range(1, count):
-        rising = lax.ppermute(rising, "tm", up)
-        falling = lax.ppermute(falling, "tm", down)
-        earlier.append(rising)
-        later.append(falling)
-    relative = jnp.concatenate(earlier[::-1] + [block] + later, axis=0)
-    return lax.dynamic_slice_in_dim(relative, count - 1 - position, count * block.shape[0], 0)
+    copies = jnp.broadcast_to(block[None], (count,) + block.shape)
+    frames = lax.all_to_all(copies, "tm", split_axis=0, concat_axis=0, tiled=True)
+    return frames.reshape((count * block.shape[0],) + block.shape[1:])
 
 
 def local(latents, gain, bias, weight, cotangent):

time: 125 us -> 132 us (1.056)
  blocking collectives: 0 us -> 51.5 us
  waiting for transfers between devices: 34.8 us -> 7.33 us
  starting transfers between devices: 38.9 us -> 21.3 us
    all_to_all x0 -> x1, blocking collectives: none -> 51.5 us  [gather_frames(): lax.all_to_all(copies, 'tm', split_axis=0, concat_axis=0, tiled=True)]
    ppermute x6 -> x0, waiting for transfers between devices: 28.6 us -> none  [the longest x3 24.7 us: gather_frames(): rising = lax.ppermute(rising, 'tm', up)]
    ppermute x6 -> x0, starting transfers between devices: 17.6 us -> none  [the longest x3 13.8 us: gather_frames(): rising = lax.ppermute(rising, 'tm', up)]
    unnamed x33 -> x26, local copies, waits for them, and re-layouts: 2.93 us -> 3.22 us
  transfers between devices with their start and end apart: 11 -> 5, of which waited for: 5 -> 1; matrix products, arithmetic and copies ran while one was open for 19% -> 18% of each run, Pallas kernels for 0% -> 0%
where the time goes in v16:
time: 132 us; the launch traced here: 131 us
  blocking collectives  51.5 us (39%)
  starting transfers between devices  21.3 us (16%)
  local copies, waits for them, and re-layouts  19.9 us (15%)
  other arithmetic  17.3 us (13%)
  matrix products  13 us (10%)
  waiting for transfers between devices  7.33 us (6%)
    all_to_all x1, blocking collectives, gather_frames(): lax.all_to_all(copies, 'tm', split_axis=0, concat_axis=0, tiled=True)  51.5 us
    ppermute x1, starting transfers between devices, gather_rows(): twins = lax.ppermute(stacked, 'height', sibling)  11.1 us
    ppermute x1, waiting for transfers between devices, gather_rows(): lax.ppermute(own, 'height', [(i, (i + 2 * step) % height_count) for i in...  7.32 us
    dot_general x3, matrix products, block_weight_grad(): lax.dot_general(window, hidden_all, (((0, 1, 2), (0, 1, 2)), ((), ())), p...  5.43 us
    all_to_all x1, local copies, waits for them, and re-layouts, local(): lax.all_to_all(cot_frames, 'height', split_axis=3, concat_axis=1, tiled=T...  3.8 us
    conv_general_dilated x1, matrix products, forward_conv(): lax.conv_general_dilated(window[None], cube, (1, 1, 1), 'VALID', dimensio...  3.8 us
    ppermute x1, starting transfers between devices, padded(): lax.ppermute(tail, axis, [(i, (i + 1) % count) for i in range(ends)])  3.79 us
    conv_general_dilated x1, matrix products, backward_conv(): lax.conv_general_dilated(window[None], jnp.flip(cube, (0, 1, 2)), (1, 1,...  3.78 us
  transfers between devices with their start and end apart: 5, of which 1 were waited for; matrix products, arithmetic and copies ran while one was open for 18% of the time, Pallas kernels for 0%

profile of v16, /device:TPU:0, one launch (start us, length us, event | category | flops | bytes accessed | tf_op | source)
XLA Modules:
  0.0 131.4 jit_solution(3812170826956981981)
XLA Ops:
  0.6 1.1 fusion.65
  1.7 1.2 multiply_convert_fusion
  3.0 1.0 maximum_bitcast_fusion
  3.9 0.1 broadcast_in_dim.9
  4.1 51.5 %all_to_all.23 = bf16[4,1,2,160,768]{4,3,2,1,0:T(8,128)(2,1)S(1)} all-to-all(bf16[4,1,2,160,768]{4,3,2,1,0:T(8,128)(2,1)S(1)} %broadcast_in_dim.9), channel_id=1, replica_groups=mesh['grp'=2,'tm'=4,'height'=4] {'tm'}, dimensions={0} | all-to-all | bytes 3932160 | tf_op jit(solution)/shard_map/all_to_all | solution.py:148
  55.6 0.3 fusion.80
  55.9 1.6 %collective-permute-start = (bf16[4,2,160,384]{3,2,1,0:T(8,128)(2,1)S(1)}, bf16[4,2,160,384]{3,2,1,0:T(8,128)(2,1)}, u32[]{:S(2)}, u32[]{:S(2)}) collective-permute-start(bf16[4,2,160,384]{3,2,1,0:T(8,128)(2,1)S(1)} %get-tuple-element.15), channel_id=1, source_target_pairs={{0,2},{1,3},{2,0},{3,1},{4,6},{5,7},{6,4},{7,5},{8,10},{9,11},{10,... | collective-permute-start | bytes 2949128 | tf_op jit(solution)/shard_map/ppermute | solution.py:116
  57.4 1.0 pad_dynamic-slice_fusion.6
  58.4 1.3 collective-permute-start.3
  59.7 3.8 %collective-permute-start.2 = (bf16[3,1,160,384]{3,2,1,0:T(8,128)(2,1)}, bf16[3,1,160,384]{3,2,1,0:T(8,128)(2,1)}, u32[]{:S(2)}, u32[]{:S(2)}) collective-permute-start(bf16[3,1,160,384]{3,2,1,0:T(8,128)(2,1)} %get-tuple-element.21), channel_id=1, source_target_pairs={{0,1},{1,2},{2,3},{4,5},{5,6},{6,7},{8,9},{9,10},{10,11},{12,13},{... | collective-permute-start | bytes 1105928 | tf_op jit(solution)/shard_map/ppermute | solution.py:23
  63.5 3.0 %copy.77 = bf16[4,2,160,384]{2,1,0,3:T(2,128)(2,1)} copy(bf16[4,2,160,384]{3,2,1,0:T(8,128)(2,1)S(1)} %get-tuple-element.14) | data formatting | bytes 1966080 | tf_op jit(solution)/shard_map/slice | solution.py:174
  66.5 3.6 %all-to-all-start.1 = ((bf16[4,2,160,384]{2,1,0,3:T(2,128)(2,1)}), bf16[4,2,160,384]{2,1,0,3:T(2,128)(2,1)S(1)}, u32[]{:S(2)}, u32[]{:S(2)}) async-start(bf16[4,2,160,384]{2,1,0,3:T(2,128)(2,1)} %copy.77), calls=%async_computation.1 | async-start | bytes 3145728 | tf_op jit(solution)/shard_map/all_to_all | solution.py:175
  70.1 0.1 pad_dynamic-slice_fusion.7
  70.2 0.0 collective-permute-done.3
  70.2 0.0 collective-permute-done.2
  70.2 0.0 slice-start
  70.2 1.7 %fusion.37 = bf16[3,4,1,162,384]{4,3,1,0,2:T(8,128)(2,1)S(1)} fusion(bf16[3,1,160,384]{3,2,1,0:T(8,128)(2,1)} %collective-permute-done.3, bf16[3,2,160,384]{3,2,1,0:T(8,128)(2,1)S(1)} %pad_dynamic-slice_fusion.7, bf16[3,1,160,384]{3,2,1,0:T(8,128)(2,1)} %collective-permute-done.2), kind=kLoop, calls=%fused_computation.54 | loop fusion | flops 9704448 | bytes 2967552 | tf_op jit(solution)/shard_map/broadcast_in_dim | solution.py:58
  71.9 0.6 copy.91
  72.5 0.0 slice-start.1
  72.5 0.6 pad.22.clone
  73.1 0.2 copy.74
  73.4 0.0 copy-start.7
  73.4 7.3 %collective-permute-done = bf16[4,2,160,384]{3,2,1,0:T(8,128)(2,1)} collective-permute-done((bf16[4,2,160,384]{3,2,1,0:T(8,128)(2,1)S(1)}, bf16[4,2,160,384]{3,2,1,0:T(8,128)(2,1)}, u32[]{:S(2)}, u32[]{:S(2)}) %collective-permute-start) | collective-permute-done | bytes 983072 | tf_op jit(solution)/shard_map/ppermute | solution.py:116
  80.7 2.7 %pad_maximum_fusion.3 = bf16[4,4,160,384]{3,2,1,0:T(8,128)(2,1)} fusion(bf16[4,2,160,384]{3,2,1,0:T(8,128)(2,1)} %collective-permute-done, bf16[4,2,160,384]{3,2,1,0:T(8,128)(2,1)S(1)} %get-tuple-element.15), kind=kLoop, calls=%fused_computation.30 | loop fusion | flops 983040 | bytes 3932160 | tf_op jit(solution)/shard_map/concatenate | solution.py:121
  83.4 11.1 %collective-permute-start.1 = (bf16[4,4,160,384]{3,2,1,0:T(8,128)(2,1)}, bf16[4,4,160,384]{3,2,1,0:T(8,128)(2,1)}, u32[]{:S(2)}, u32[]{:S(2)}) collective-permute-start(bf16[4,4,160,384]{3,2,1,0:T(8,128)(2,1)} %pad_maximum_fusion.3), channel_id=1, source_target_pairs={{0,1},{1,0},{2,3},{3,2},{4,5},{5,4},{6,7},{7,6},{8,9},{9,8},{10,11... | collective-permute-start | bytes 5898248 | tf_op jit(solution)/shard_map/ppermute | solution.py:122
  94.5 0.0 slice-done
  94.5 0.0 copy-done.7
  94.6 3.8 %fusion.54 = f32[1,2,8,21,384]{4,2,3,1,0:T(8,128)S(1)} fusion(bf16[3,3,3,384,384]{4,3,2,1,0:T(8,128)(2,1)S(1)} %bitcast.105, bf16[3,4,1,7,2,384]{5,3,4,1,0,2:T(8,128)(2,1)S(1)} %slice.50, bf16[3,4,1,8,21,384]{5,3,4,1,0,2:T(8,128)(2,1)S(1)} %copy.74, pred[8,21]{0,1:T(8,128)(4,1)S(1)} %copy-done.7), kind=kOutput, calls=%fused_computation.64 | convolution fusion | flops 2680657920 | bytes 10156200 | tf_op jit(solution)/shard_map/conv_general_dilated | solution.py:57
  98.3 0.0 copy-start.2
  98.4 0.0 copy-start.5
  98.4 0.3 copy.75
  98.6 0.2 slice.51
  98.8 0.5 copy-done.2
  99.3 0.4 multiply_reduce_fusion
  99.7 0.0 all-to-all-done.1
  99.7 3.8 %copy.78 = bf16[4,2,160,4,96]{4,2,1,3,0:T(8,128)(2,1)} copy(bf16[4,2,160,4,96]{2,1,0,4,3:T(2,128)(2,1)S(1)} %bitcast.94) | data formatting | bytes 1966080 | tf_op jit(solution)/shard_map/all_to_all | solution.py:175
  103.5 3.6 %fusion.14 = (bf16[6,10,160,1,96]{4,2,1,3,0:T(8,128)(2,1)S(1)}, bf16[6,10,160,1,96]{4,2,1,3,0:T(8,128)(2,1)S(1)}, bf16[6,10,160,1,96]{4,2,1,3,0:T(8,128)(2,1)S(1)}) fusion(bf16[4,8,160,96]{3,2,1,0:T(8,128)(2,1)} %bitcast.97), kind=kLoop, calls=%fused_computation.26 | loop fusion | bytes 6512640 | tf_op jit(solution)/shard_map/stack | solution.py:82
  107.1 2.0 %pad_maximum_fusion = bf16[6,10,160,3,96]{4,2,1,3,0:T(8,128)(2,1)S(1)} fusion(bf16[6,10,160,1,96]{4,2,1,3,0:T(8,128)(2,1)S(1)} %get-tuple-element.20, bf16[6,10,160,1,96]{4,2,1,3,0:T(8,128)(2,1)S(1)} %get-tuple-element.19, bf16[6,10,160,1,96]{4,2,1,3,0:T(8,128)(2,1)S(1)} %get-tuple-element.18), kind=kLoop, calls=%fused_computation.1 | loop fusion | flops 5529600 | bytes 11059200 | tf_op jit(solution)/shard_map/stack | solution.py:82
  109.1 0.0 collective-permute-done.1
  109.2 1.7 %fusion.81 = (bf16[4,2,160,384]{3,2,1,0:T(8,128)(2,1)S(1)}, bf16[4,2,160,384]{3,2,1,0:T(8,128)(2,1)S(1)}) fusion(bf16[4,4,160,384]{3,2,1,0:T(8,128)(2,1)} %collective-permute-done.1), kind=kLoop, calls=%fused_computation.99 | loop fusion | bytes 3932160 | tf_op jit(solution)/shard_map/slice | solution.py:127
  110.9 0.3 fusion.17
  111.2 1.9 %fusion.18 = bf16[4,4,160,384]{3,2,1,0:T(8,128)(2,1)S(1)} fusion(bf16[4,2,160,384]{3,2,1,0:T(8,128)(2,1)} %collective-permute-done, bf16[4,2,160,384]{3,2,1,0:T(8,128)(2,1)S(1)} %get-tuple-element.17, pred[]{:T(512)S(6)} %eq.10), kind=kLoop, calls=%fused_computation.33 | loop fusion | flops 2949120 | bytes 3932161 | tf_op jit(solution)/shard_map/jit(_where)/select_n | solution.py:129
  113.1 1.6 %fusion.20 = (bf16[4,4,160,384]{3,2,1,0:T(8,128)(2,1)S(1)}, bf16[4,4,160,384]{3,2,1,0:T(8,128)(2,1)S(1)}) fusion(s32[]{:T(128)S(6)} %select_n.95, bf16[4,4,160,384]{3,2,1,0:T(8,128)(2,1)S(1)} %fusion.18, bf16[4,4,160,384]{3,2,1,0:T(8,128)(2,1)S(1)} %fusion.17, s32[]{:T(128)S(6)} %select_n.97), kind=kLoop, calls=%fused_computation.35 | loop fusion | flops 1966080 | bytes 7864328 | tf_op jit(solution)/shard_map/concatenate | solution.py:135
  114.7 0.4 pad_maximum_fusion.1
  115.2 0.0 slice-start.2
  115.2 0.5 fusion.35
  115.7 0.0 slice-start.3
  115.7 0.6 copy.90
  116.3 0.6 pad.20.clone
  116.8 0.2 copy.69
  117.1 0.2 slice-done.2
  117.3 1.3 slice-done.3
  118.6 3.8 %fusion.57 = f32[1,2,8,21,384]{4,2,3,1,0:T(8,128)S(1)} fusion(bf16[3,3,3,384,384]{4,3,2,1,0:T(8,128)(2,1)S(1)} %bitcast.108, bf16[3,4,1,7,2,384]{5,3,4,1,0,2:T(8,128)(2,1)S(1)} %slice.47, bf16[3,4,1,8,21,384]{5,3,4,1,0,2:T(8,128)(2,1)S(1)} %copy.69, pred[8,21]{0,1:T(8,128)(4,1)S(1)} %copy-done.7), kind=kOutput, calls=%fused_computation.65 | convolution fusion | flops 2680657920 | bytes 10156200 | tf_op jit(solution)/shard_map/conv_general_dilated | solution.py:44
  122.4 0.3 copy.70
  122.7 0.2 slice.48
  122.9 1.7 %fusion.39 = f32[3,12,8,384]{3,2,1,0:T(8,128)S(1)} fusion(bf16[6,10,160,3,96]{4,2,1,3,0:T(8,128)(2,1)S(1)} %pad_maximum_fusion, s32[]{:T(128)S(6)} %select_n.102, s32[]{:T(128)S(6)} %select_n.104, bf16[4,4,160,384]{3,2,1,0:T(8,128)(2,1)S(1)} %get-tuple-element.13, bf16[4,4,160,384]{3,2,1,0:T(8,128)(2,1)S(1)} %get-tuple-element.12), kind=kOutput, calls=%fused_computation.61 | convolution fusion | flops 1134428160 | bytes 8306696 | tf_op jit(solution)/shard_map/dot_general | solution.py:98
  124.7 1.7 %fusion.44 = f32[3,12,8,384]{3,2,1,0:T(8,128)S(1)} fusion(bf16[6,10,160,3,96]{4,2,1,3,0:T(8,128)(2,1)S(1)} %pad_maximum_fusion, s32[]{:T(128)S(6)} %select_n.106, s32[]{:T(128)S(6)} %select_n.108, bf16[4,4,160,384]{3,2,1,0:T(8,128)(2,1)S(1)} %get-tuple-element.13, bf16[4,4,160,384]{3,2,1,0:T(8,128)(2,1)S(1)} %get-tuple-element.12), kind=kOutput, calls=%fused_computation.62 | convolution fusion | flops 1134428160 | bytes 8306696 | tf_op jit(solution)/shard_map/dot_general | solution.py:98
  126.5 0.0 copy-start.1
  126.5 0.0 copy-start.3
  126.5 0.0 copy-start.4
  126.5 0.0 copy-start.6
  126.5 2.0 %fusion.49 = f32[3,12,8,384]{3,2,1,0:T(8,128)S(1)} fusion(bf16[6,10,160,3,96]{4,2,1,3,0:T(8,128)(2,1)S(1)} %pad_maximum_fusion, s32[]{:T(128)S(6)} %select_n.110, s32[]{:T(128)S(6)} %select_n.112, bf16[4,4,160,384]{3,2,1,0:T(8,128)(2,1)S(1)} %get-tuple-element.13, bf16[4,4,160,384]{3,2,1,0:T(8,128)(2,1)S(1)} %get-tuple-element.12), kind=kOutput, calls=%fused_computation.63 | convolution fusion | flops 1134428160 | bytes 8306696 | tf_op jit(solution)/shard_map/dot_general | solution.py:98
  128.5 1.2 add_convert_fusion
  129.7 1.6 %fusion.62 = f32[2592,96]{0,1:T(8,128)} fusion(s32[]{:T(128)S(6)} %select_n.113, f32[1152,96]{0,1:T(8,128)S(1)} %bitcast.100, f32[1152,96]{0,1:T(8,128)S(1)} %bitcast.101, f32[1152,96]{0,1:T(8,128)S(1)} %bitcast.102), kind=kLoop, calls=%fused_computation.68 | loop fusion | flops 746496 | bytes 2322436 | tf_op jit(solution)/shard_map/mul | solution.py:188
  (17 shorter events, 0.2 us)
Async XLA Ops:
  55.9 24.9 %collective-permute-start = (bf16[4,2,160,384]{3,2,1,0:T(8,128)(2,1)S(1)}, bf16[4,2,160,384]{3,2,1,0:T(8,128)(2,1)}, u32[]{:S(2)}, u32[]{:S(2)}) collective-permute-start(bf16[4,2,160,384]{3,2,1,0:T(8,128)(2,1)S(1)} %get-tuple-element.15), channel_id=1, source_target_pairs={{0,2},{1,3},{2,0},{3,1},{4,6},{5,7},{6,4},{7,5},{8,10},{9,11},{10,... | collective-permute-start | bytes 2949128 | tf_op jit(solution)/shard_map/ppermute | solution.py:116
  58.4 11.8 %collective-permute-start.3 = (bf16[3,1,160,384]{3,2,1,0:T(8,128)(2,1)}, bf16[3,1,160,384]{3,2,1,0:T(8,128)(2,1)}, u32[]{:S(2)}, u32[]{:S(2)}) collective-permute-start(bf16[3,1,160,384]{3,2,1,0:T(8,128)(2,1)} %get-tuple-element.22), channel_id=1, source_target_pairs={{1,0},{2,1},{3,2},{5,4},{6,5},{7,6},{9,8},{10,9},{11,10},{13,12},{... | collective-permute-start | bytes 1105928 | tf_op jit(solution)/shard_map/ppermute | solution.py:25
  59.7 10.5 %collective-permute-start.2 = (bf16[3,1,160,384]{3,2,1,0:T(8,128)(2,1)}, bf16[3,1,160,384]{3,2,1,0:T(8,128)(2,1)}, u32[]{:S(2)}, u32[]{:S(2)}) collective-permute-start(bf16[3,1,160,384]{3,2,1,0:T(8,128)(2,1)} %get-tuple-element.21), channel_id=1, source_target_pairs={{0,1},{1,2},{2,3},{4,5},{5,6},{6,7},{8,9},{9,10},{10,11},{12,13},{... | collective-permute-start | bytes 1105928 | tf_op jit(solution)/shard_map/ppermute | solution.py:23
  66.5 33.2 %all-to-all-start.1 = ((bf16[4,2,160,384]{2,1,0,3:T(2,128)(2,1)}), bf16[4,2,160,384]{2,1,0,3:T(2,128)(2,1)S(1)}, u32[]{:S(2)}, u32[]{:S(2)}) async-start(bf16[4,2,160,384]{2,1,0,3:T(2,128)(2,1)} %copy.77), calls=%async_computation.1 | async-start | bytes 3145728 | tf_op jit(solution)/shard_map/all_to_all | solution.py:175
  70.2 24.3 %slice-start = ((s8[7962624]{0:T(1024)(128)(4,1)}), s8[4194304]{0:T(1024)(128)(4,1)S(1)}, s32[]{:S(2)}) async-start(s8[7962624]{0:T(1024)(128)(4,1)} %bitcast.103), calls=%async_computation.2 | async-start | bytes 8388608
  72.5 22.0 %slice-start.1 = ((s8[7962624]{0:T(1024)(128)(4,1)}), s8[3768320]{0:T(1024)(128)(4,1)S(1)}, s32[]{:S(2)}) async-start(s8[7962624]{0:T(1024)(128)(4,1)} %bitcast.103), calls=%async_computation.3 | async-start | bytes 7536640
  73.4 21.2 %copy-start.7 = (pred[8,21]{0,1:T(8,128)(4,1)S(1)}, pred[8,21]{0,1:T(8,128)(4,1)}, u32[]{:S(2)}) copy-start(pred[8,21]{0,1:T(8,128)(4,1)} %constant.124) | copy-start | bytes 508
  83.4 25.7 %collective-permute-start.1 = (bf16[4,4,160,384]{3,2,1,0:T(8,128)(2,1)}, bf16[4,4,160,384]{3,2,1,0:T(8,128)(2,1)}, u32[]{:S(2)}, u32[]{:S(2)}) collective-permute-start(bf16[4,4,160,384]{3,2,1,0:T(8,128)(2,1)} %pad_maximum_fusion.3), channel_id=1, source_target_pairs={{0,1},{1,0},{2,3},{3,2},{4,5},{5,4},{6,7},{7,6},{8,9},{9,8},{10,11... | collective-permute-start | bytes 5898248 | tf_op jit(solution)/shard_map/ppermute | solution.py:122
  98.3 0.9 copy-start.2
  98.4 0.9 copy-start.5
  99.3 7.8 %copy-start = (f32[1,2,1,160,384]{4,1,3,2,0:T(2,128)}, f32[1,2,1,160,384]{4,1,3,2,0:T(2,128)S(1)}, u32[]{:S(2)}) copy-start(f32[1,2,1,160,384]{4,1,3,2,0:T(2,128)S(1)} %slice.51) | copy-start | bytes 1474564
  115.2 2.2 %slice-start.2 = ((s8[7962624]{0:T(1024)(128)(4,1)}), s8[4194304]{0:T(1024)(128)(4,1)S(1)}, s32[]{:S(2)}) async-start(s8[7962624]{0:T(1024)(128)(4,1)} %bitcast.106), calls=%async_computation.4 | async-start | bytes 8388608
  115.7 3.0 %slice-start.3 = ((s8[7962624]{0:T(1024)(128)(4,1)}), s8[3768320]{0:T(1024)(128)(4,1)S(1)}, s32[]{:S(2)}) async-start(s8[7962624]{0:T(1024)(128)(4,1)} %bitcast.106), calls=%async_computation.5 | async-start | bytes 7536640
  126.5 2.1 %copy-start.1 = (f32[1,2,1,160,384]{4,1,3,2,0:T(2,128)S(1)}, f32[1,2,1,160,384]{4,1,3,2,0:T(2,128)}, u32[]{:S(2)}) copy-start(f32[1,2,1,160,384]{4,1,3,2,0:T(2,128)} %copy-done) | copy-start | bytes 1474564
  126.5 2.0 %copy-start.3 = (bf16[1,2,160,384]{3,2,1,0:T(8,128)(2,1)S(1)}, bf16[1,2,160,384]{3,2,1,0:T(8,128)(2,1)}, u32[]{:S(2)}) copy-start(bf16[1,2,160,384]{3,2,1,0:T(8,128)(2,1)} %param.5) | copy-start | bytes 737284
  126.5 2.0 %copy-start.4 = (bf16[1,2,160,384]{3,2,1,0:T(8,128)(2,1)S(1)}, bf16[1,2,160,384]{3,2,1,0:T(8,128)(2,1)}, u32[]{:S(2)}) copy-start(bf16[1,2,160,384]{3,2,1,0:T(8,128)(2,1)} %param.9) | copy-start | bytes 737284
  126.5 2.0 %copy-start.6 = (f32[384]{0:T(512)S(1)}, f32[384]{0:T(512)}, u32[]{:S(2)}) copy-start(f32[384]{0:T(512)} %param.7) | copy-start | bytes 4612

commit v17 on v14

--- a/solution.py
+++ b/solution.py
@@ -119,7 +119,11 @@
         for step in range(1, chips)
     ]
     stacked = jnp.concatenate(mine, axis=1)
-    twins = lax.ppermute(stacked, "height", sibling)
+    twins = jnp.concatenate(
+        [lax.ppermute(own, "height", sibling)]
+        + ([lax.ppermute(stacked[:, row_count:], "height", sibling)] if chips > 1 else []),
+        axis=1,
+    )
     block = 2 * row_count
     relative = []
     for step in reversed(range(chips)):

time: 125 us -> 132 us (1.056)
  waiting for transfers between devices: 34.8 us -> 51 us
  starting transfers between devices: 38.9 us -> 29.2 us
  matrix products: 13 us -> 16.1 us
  local copies, waits for them, and re-layouts: 19.4 us -> 17.6 us
    all_to_all x1, waiting for transfers between devices: 0.01 us -> 22.4 us  [local(): lax.all_to_all(cot_frames, 'height', split_axis=3, concat_axis=1, tiled=T...]
    ppermute x1 -> x2, starting transfers between devices: 11.1 us -> 1.18 us  [the longest x1 1.17 us: gather_rows(): lax.ppermute(stacked[:, row_count:], 'height', sibling)]
    ppermute x1, waiting for transfers between devices: 6.21 us -> 0.01 us  [gather_rows(): lax.ppermute(own, 'height', [(i, (i + 2 * step) % height_count) for i in...]
    conv_general_dilated x1, matrix products: 3.78 us -> 7.09 us  [backward_conv(): lax.conv_general_dilated(window[None], jnp.flip(cube, (0, 1, 2)), (1, 1,...]
    concatenate x1 -> x0, other arithmetic: 2.71 us -> none  [gather_rows(): stacked = jnp.concatenate(mine, axis=1)]
    slice x1 -> x0, local copies, waits for them, and re-layouts: 1.7 us -> none  [gather_rows(): theirs = twins[:, step * row_count:(step + 1) * row_count]]
    select_n x2, other arithmetic: 2.19 us -> 3.71 us  [gather_rows(): jnp.where(first, jnp.concatenate([ours, theirs], axis=1), jnp.concatenate...]
    unnamed x33 -> x23, local copies, waits for them, and re-layouts: 2.93 us -> 2.9 us
  transfers between devices with their start and end apart: 11 -> 12, of which waited for: 5 -> 5; matrix products, arithmetic and copies ran while one was open for 19% -> 19% of each run, Pallas kernels for 0% -> 0%
where the time goes in v17:
time: 132 us; the launch traced here: 131 us
  waiting for transfers between devices  51 us (39%)
  starting transfers between devices  29.2 us (22%)
  local copies, waits for them, and re-layouts  17.6 us (13%)
  matrix products  16.1 us (12%)
  other arithmetic  16 us (12%)
    ppermute x3, waiting for transfers between devices, gather_frames(): rising = lax.ppermute(rising, 'tm', up)  24.7 us
    all_to_all x1, waiting for transfers between devices, local(): lax.all_to_all(cot_frames, 'height', split_axis=3, concat_axis=1, tiled=T...  22.4 us
    ppermute x3, starting transfers between devices, gather_frames(): rising = lax.ppermute(rising, 'tm', up)  13.8 us
    conv_general_dilated x1, matrix products, backward_conv(): lax.conv_general_dilated(window[None], jnp.flip(cube, (0, 1, 2)), (1, 1,...  7.09 us
    dot_general x3, matrix products, block_weight_grad(): lax.dot_general(window, hidden_all, (((0, 1, 2), (0, 1, 2)), ((), ())), p...  5.18 us
    ppermute x3, waiting for transfers between devices, gather_frames(): falling = lax.ppermute(falling, 'tm', down)  3.9 us
    ppermute x3, starting transfers between devices, gather_frames(): falling = lax.ppermute(falling, 'tm', down)  3.88 us
    conv_general_dilated x1, matrix products, forward_conv(): lax.conv_general_dilated(window[None], cube, (1, 1, 1), 'VALID', dimensio...  3.84 us
  transfers between devices with their start and end apart: 12, of which 5 were waited for; matrix products, arithmetic and copies ran while one was open for 19% of the time, Pallas kernels for 0%

profile of v17, /device:TPU:0, one launch (start us, length us, event | category | flops | bytes accessed | tf_op | source)
XLA Modules:
  0.0 131.1 jit_solution(6912619841861076649)
XLA Ops:
  0.6 0.0 copy-start.1
  0.6 1.1 fusion.63
  1.8 1.2 multiply_convert_fusion
  3.0 1.0 pad_maximum_fusion.2
  4.0 5.0 %collective-permute-start = (bf16[1,2,160,768]{3,2,1,0:T(8,128)(2,1)S(1)}, bf16[1,2,160,768]{3,2,1,0:T(8,128)(2,1)S(1)}, u32[]{:S(2)}, u32[]{:S(2)}) collective-permute-start(bf16[1,2,160,768]{3,2,1,0:T(8,128)(2,1)S(1)} %pad_maximum_fusion.2), channel_id=1, source_target_pairs={{0,4},{4,8},{8,12},{1,5},{5,9},{9,13},{2,6},{6,10},{10,14},{3,7},{... | collective-permute-start | bytes 1474568 | tf_op jit(solution)/shard_map/ppermute | solution.py:157
  9.0 1.3 collective-permute-start.3
  10.3 9.1 %collective-permute-done = bf16[1,2,160,768]{3,2,1,0:T(8,128)(2,1)S(1)} collective-permute-done((bf16[1,2,160,768]{3,2,1,0:T(8,128)(2,1)S(1)}, bf16[1,2,160,768]{3,2,1,0:T(8,128)(2,1)S(1)}, u32[]{:S(2)}, u32[]{:S(2)}) %collective-permute-start) | collective-permute-done | bytes 491552 | tf_op jit(solution)/shard_map/ppermute | solution.py:157
  19.4 4.4 %collective-permute-start.1 = (bf16[1,2,160,768]{3,2,1,0:T(8,128)(2,1)S(1)}, bf16[1,2,160,768]{3,2,1,0:T(8,128)(2,1)S(1)}, u32[]{:S(2)}, u32[]{:S(2)}) collective-permute-start(bf16[1,2,160,768]{3,2,1,0:T(8,128)(2,1)S(1)} %collective-permute-done), channel_id=1, source_target_pairs={{0,4},{4,8},{8,12},{1,5},{5,9},{9,13},{2,6},{6,10},{10,14},{3,7},{... | collective-permute-start | bytes 1474568 | tf_op jit(solution)/shard_map/ppermute | solution.py:157
  23.8 1.3 collective-permute-start.4
  25.1 8.2 %collective-permute-done.1 = bf16[1,2,160,768]{3,2,1,0:T(8,128)(2,1)S(1)} collective-permute-done((bf16[1,2,160,768]{3,2,1,0:T(8,128)(2,1)S(1)}, bf16[1,2,160,768]{3,2,1,0:T(8,128)(2,1)S(1)}, u32[]{:S(2)}, u32[]{:S(2)}) %collective-permute-start.1) | collective-permute-done | bytes 491552 | tf_op jit(solution)/shard_map/ppermute | solution.py:157
  33.4 4.4 %collective-permute-start.2 = (bf16[1,2,160,768]{3,2,1,0:T(8,128)(2,1)S(1)}, bf16[1,2,160,768]{3,2,1,0:T(8,128)(2,1)S(1)}, u32[]{:S(2)}, u32[]{:S(2)}) collective-permute-start(bf16[1,2,160,768]{3,2,1,0:T(8,128)(2,1)S(1)} %collective-permute-done.1), channel_id=1, source_target_pairs={{0,4},{4,8},{8,12},{1,5},{5,9},{9,13},{2,6},{6,10},{10,14},{3,7},{... | collective-permute-start | bytes 1474568 | tf_op jit(solution)/shard_map/ppermute | solution.py:157
  37.8 1.3 collective-permute-start.5
  39.1 7.3 %collective-permute-done.2 = bf16[1,2,160,768]{3,2,1,0:T(8,128)(2,1)S(1)} collective-permute-done((bf16[1,2,160,768]{3,2,1,0:T(8,128)(2,1)S(1)}, bf16[1,2,160,768]{3,2,1,0:T(8,128)(2,1)S(1)}, u32[]{:S(2)}, u32[]{:S(2)}) %collective-permute-start.2) | collective-permute-done | bytes 491552 | tf_op jit(solution)/shard_map/ppermute | solution.py:157
  46.7 3.9 %collective-permute-done.5 = bf16[1,2,160,768]{3,2,1,0:T(8,128)(2,1)S(1)} collective-permute-done((bf16[1,2,160,768]{3,2,1,0:T(8,128)(2,1)S(1)}, bf16[1,2,160,768]{3,2,1,0:T(8,128)(2,1)S(1)}, u32[]{:S(2)}, u32[]{:S(2)}) %collective-permute-start.5) | collective-permute-done | bytes 491552 | tf_op jit(solution)/shard_map/ppermute | solution.py:158
  50.6 0.3 constant_dynamic-slice_fusion.1
  50.9 1.0 pad_dynamic-slice_fusion.6
  51.9 1.3 collective-permute-start.10
  53.2 3.8 %collective-permute-start.9 = (bf16[3,1,160,384]{3,2,1,0:T(8,128)(2,1)}, bf16[3,1,160,384]{3,2,1,0:T(8,128)(2,1)}, u32[]{:S(2)}, u32[]{:S(2)}) collective-permute-start(bf16[3,1,160,384]{3,2,1,0:T(8,128)(2,1)} %get-tuple-element.10), channel_id=1, source_target_pairs={{0,1},{1,2},{2,3},{4,5},{5,6},{6,7},{8,9},{9,10},{10,11},{12,13},{... | collective-permute-start | bytes 1105928 | tf_op jit(solution)/shard_map/ppermute | solution.py:23
  57.0 1.7 %collective-permute-start.6 = (bf16[4,2,160,384]{3,2,1,0:T(8,128)(2,1)S(1)}, bf16[4,2,160,384]{3,2,1,0:T(8,128)(2,1)}, u32[]{:S(2)}, u32[]{:S(2)}) collective-permute-start(bf16[4,2,160,384]{3,2,1,0:T(8,128)(2,1)S(1)} %get-tuple-element.6), channel_id=1, source_target_pairs={{0,2},{1,3},{2,0},{3,1},{4,6},{5,7},{6,4},{7,5},{8,10},{9,11},{10,... | collective-permute-start | bytes 2949128 | tf_op jit(solution)/shard_map/ppermute | solution.py:116
  58.7 0.0 collective-permute-start.8
  58.7 3.0 %copy.48 = bf16[4,2,160,384]{2,1,0,3:T(2,128)(2,1)} copy(bf16[4,2,160,384]{3,2,1,0:T(8,128)(2,1)S(1)} %get-tuple-element.5) | data formatting | bytes 1966080 | tf_op jit(solution)/shard_map/slice | solution.py:187
  61.7 3.6 %all-to-all-start = ((bf16[4,2,160,384]{2,1,0,3:T(2,128)(2,1)}), bf16[4,2,160,384]{2,1,0,3:T(2,128)(2,1)S(1)}, u32[]{:S(2)}, u32[]{:S(2)}) async-start(bf16[4,2,160,384]{2,1,0,3:T(2,128)(2,1)} %copy.48), calls=%async_computation | async-start | bytes 3145728 | tf_op jit(solution)/shard_map/all_to_all | solution.py:188
  65.3 0.1 pad_dynamic-slice_fusion.7
  65.4 0.0 collective-permute-done.10
  65.4 0.0 collective-permute-done.9
  65.4 1.6 %fusion.35 = bf16[3,4,1,162,384]{4,3,1,0,2:T(8,128)(2,1)S(1)} fusion(bf16[3,1,160,384]{3,2,1,0:T(8,128)(2,1)} %collective-permute-done.10, bf16[3,2,160,384]{3,2,1,0:T(8,128)(2,1)S(1)} %pad_dynamic-slice_fusion.7, bf16[3,1,160,384]{3,2,1,0:T(8,128)(2,1)} %collective-permute-done.9), kind=kLoop, calls=%fused_computation.51 | loop fusion | flops 9704448 | bytes 2967552 | tf_op jit(solution)/shard_map/broadcast_in_dim | solution.py:58
  67.0 0.6 copy.62
  67.6 0.0 copy-start.5
  67.6 0.6 pad.22.clone
  68.2 0.2 copy.45
  68.4 0.0 copy-start
  68.5 0.0 copy-start.3
  68.5 7.1 %fusion.52 = f32[1,2,8,21,384]{4,2,3,1,0:T(8,128)S(1)} fusion(bf16[3,3,3,384,384]{4,3,2,1,0:T(8,128)(2,1)} %bitcast.99, bf16[3,4,1,7,2,384]{5,3,4,1,0,2:T(8,128)(2,1)S(1)} %slice.38, bf16[3,4,1,8,21,384]{5,3,4,1,0,2:T(8,128)(2,1)S(1)} %copy.45, pred[8,21]{0,1:T(8,128)(4,1)S(1)} %copy-done.5), kind=kOutput, calls=%fused_computation.61 | convolution fusion | flops 2680657920 | bytes 10156200 | tf_op jit(solution)/shard_map/conv_general_dilated | solution.py:57
  75.6 0.3 copy.46
  75.8 0.2 slice.39
  76.0 0.4 multiply_reduce_fusion
  76.5 22.4 %all-to-all-done = bf16[4,2,160,384]{2,1,0,3:T(2,128)(2,1)S(1)} async-done(((bf16[4,2,160,384]{2,1,0,3:T(2,128)(2,1)}), bf16[4,2,160,384]{2,1,0,3:T(2,128)(2,1)S(1)}, u32[]{:S(2)}, u32[]{:S(2)}) %all-to-all-start) | async-done | bytes 983072 | tf_op jit(solution)/shard_map/all_to_all | solution.py:188
  98.9 3.7 %copy.49 = bf16[4,2,160,4,96]{4,2,1,3,0:T(8,128)(2,1)} copy(bf16[4,2,160,4,96]{2,1,0,4,3:T(2,128)(2,1)S(1)} %bitcast.90) | data formatting | bytes 1966080 | tf_op jit(solution)/shard_map/all_to_all | solution.py:188
  102.6 3.4 %fusion.14 = (bf16[6,10,160,1,96]{4,2,1,3,0:T(8,128)(2,1)S(1)}, bf16[6,10,160,1,96]{4,2,1,3,0:T(8,128)(2,1)S(1)}, bf16[6,10,160,1,96]{4,2,1,3,0:T(8,128)(2,1)S(1)}) fusion(bf16[4,8,160,96]{3,2,1,0:T(8,128)(2,1)} %bitcast.93), kind=kLoop, calls=%fused_computation.26 | loop fusion | bytes 6512640 | tf_op jit(solution)/shard_map/stack | solution.py:82
  106.1 0.0 collective-permute-done.6
  106.1 1.2 collective-permute-start.7
  107.3 2.1 %pad_maximum_fusion = bf16[6,10,160,3,96]{4,2,1,3,0:T(8,128)(2,1)S(1)} fusion(bf16[6,10,160,1,96]{4,2,1,3,0:T(8,128)(2,1)S(1)} %get-tuple-element.9, bf16[6,10,160,1,96]{4,2,1,3,0:T(8,128)(2,1)S(1)} %get-tuple-element.8, bf16[6,10,160,1,96]{4,2,1,3,0:T(8,128)(2,1)S(1)} %get-tuple-element.7), kind=kLoop, calls=%fused_computation.1 | loop fusion | flops 5529600 | bytes 11059200 | tf_op jit(solution)/shard_map/stack | solution.py:82
  109.3 1.9 %maximum_select_fusion.1 = bf16[4,4,160,384]{3,2,1,0:T(8,128)(2,1)S(1)} fusion(bf16[4,2,160,384]{3,2,1,0:T(8,128)(2,1)} %collective-permute-done.8, bf16[4,2,160,384]{3,2,1,0:T(8,128)(2,1)S(1)} %get-tuple-element.6, pred[]{:T(512)S(6)} %eq.10), kind=kLoop, calls=%fused_computation.32 | loop fusion | flops 2949120 | bytes 3932161 | tf_op jit(solution)/shard_map/jit(_where)/select_n | solution.py:133
  111.2 1.8 %maximum_select_fusion = bf16[4,4,160,384]{3,2,1,0:T(8,128)(2,1)S(1)} fusion(bf16[4,2,160,384]{3,2,1,0:T(8,128)(2,1)S(1)} %collective-permute-done.7, bf16[4,2,160,384]{3,2,1,0:T(8,128)(2,1)} %collective-permute-done.6, pred[]{:T(512)S(6)} %eq.10), kind=kLoop, calls=%fused_computation.31 | loop fusion | flops 2949120 | bytes 3932161 | tf_op jit(solution)/shard_map/jit(_where)/select_n | solution.py:133
  113.1 1.6 %fusion.18 = (bf16[4,4,160,384]{3,2,1,0:T(8,128)(2,1)S(1)}, bf16[4,4,160,384]{3,2,1,0:T(8,128)(2,1)S(1)}) fusion(s32[]{:T(128)S(6)} %select_n.99, bf16[4,4,160,384]{3,2,1,0:T(8,128)(2,1)S(1)} %maximum_select_fusion, bf16[4,4,160,384]{3,2,1,0:T(8,128)(2,1)S(1)} %maximum_select_fusion.1, s32[]{:T(128)S(6)} %select_n.101), kind=kLoop, calls=%fused_computation.30 | loop fusion | flops 1966080 | bytes 7864328 | tf_op jit(solution)/shard_map/concatenate | solution.py:139
  114.7 0.4 pad_maximum_fusion.1
  115.1 0.0 slice-start
  115.2 0.5 fusion.33
  115.6 0.0 slice-start.1
  115.7 0.6 copy.61
  116.2 0.6 pad.20.clone
  116.8 0.2 copy.40
  117.1 0.2 slice-done
  117.3 1.3 slice-done.1
  118.6 3.8 %fusion.55 = f32[1,2,8,21,384]{4,2,3,1,0:T(8,128)S(1)} fusion(bf16[3,3,3,384,384]{4,3,2,1,0:T(8,128)(2,1)S(1)} %bitcast.102, bf16[3,4,1,7,2,384]{5,3,4,1,0,2:T(8,128)(2,1)S(1)} %slice.36, bf16[3,4,1,8,21,384]{5,3,4,1,0,2:T(8,128)(2,1)S(1)} %copy.40, pred[8,21]{0,1:T(8,128)(4,1)S(1)} %copy-done.5), kind=kOutput, calls=%fused_computation.62 | convolution fusion | flops 2680657920 | bytes 10156200 | tf_op jit(solution)/shard_map/conv_general_dilated | solution.py:44
  122.5 0.3 copy.41
  122.7 0.2 slice.37
  122.9 1.7 %fusion.37 = f32[3,12,8,384]{3,2,1,0:T(8,128)S(1)} fusion(bf16[6,10,160,3,96]{4,2,1,3,0:T(8,128)(2,1)S(1)} %pad_maximum_fusion, s32[]{:T(128)S(6)} %select_n.106, s32[]{:T(128)S(6)} %select_n.108, bf16[4,4,160,384]{3,2,1,0:T(8,128)(2,1)S(1)} %get-tuple-element.4, bf16[4,4,160,384]{3,2,1,0:T(8,128)(2,1)S(1)} %get-tuple-element.3), kind=kOutput, calls=%fused_computation.58 | convolution fusion | flops 1134428160 | bytes 8306696 | tf_op jit(solution)/shard_map/dot_general | solution.py:98
  124.7 1.7 %fusion.42 = f32[3,12,8,384]{3,2,1,0:T(8,128)S(1)} fusion(bf16[6,10,160,3,96]{4,2,1,3,0:T(8,128)(2,1)S(1)} %pad_maximum_fusion, s32[]{:T(128)S(6)} %select_n.110, s32[]{:T(128)S(6)} %select_n.112, bf16[4,4,160,384]{3,2,1,0:T(8,128)(2,1)S(1)} %get-tuple-element.4, bf16[4,4,160,384]{3,2,1,0:T(8,128)(2,1)S(1)} %get-tuple-element.3), kind=kOutput, calls=%fused_computation.59 | convolution fusion | flops 1134428160 | bytes 8306696 | tf_op jit(solution)/shard_map/dot_general | solution.py:98
  126.5 0.0 copy-start.2
  126.5 0.0 copy-start.4
  126.5 1.7 %fusion.47 = f32[3,12,8,384]{3,2,1,0:T(8,128)S(1)} fusion(bf16[6,10,160,3,96]{4,2,1,3,0:T(8,128)(2,1)S(1)} %pad_maximum_fusion, s32[]{:T(128)S(6)} %select_n.114, s32[]{:T(128)S(6)} %select_n.116, bf16[4,4,160,384]{3,2,1,0:T(8,128)(2,1)S(1)} %get-tuple-element.4, bf16[4,4,160,384]{3,2,1,0:T(8,128)(2,1)S(1)} %get-tuple-element.3), kind=kOutput, calls=%fused_computation.60 | convolution fusion | flops 1134428160 | bytes 8306696 | tf_op jit(solution)/shard_map/dot_general | solution.py:98
  128.3 1.2 add_convert_fusion
  129.5 1.6 %fusion.60 = f32[2592,96]{0,1:T(8,128)} fusion(s32[]{:T(128)S(6)} %select_n.117, f32[1152,96]{0,1:T(8,128)S(1)} %bitcast.96, f32[1152,96]{0,1:T(8,128)S(1)} %bitcast.97, f32[1152,96]{0,1:T(8,128)S(1)} %bitcast.98), kind=kLoop, calls=%fused_computation.65 | loop fusion | flops 746496 | bytes 2322436 | tf_op jit(solution)/shard_map/mul | solution.py:201
  (25 shorter events, 0.5 us)
Async XLA Ops:
  0.6 45.9 %copy-start.1 = (bf16[1,2,160,384]{3,2,1,0:T(8,128)(2,1)S(1)}, bf16[1,2,160,384]{3,2,1,0:T(8,128)(2,1)}, u32[]{:S(2)}) copy-start(bf16[1,2,160,384]{3,2,1,0:T(8,128)(2,1)} %param.9) | copy-start | bytes 737284
  4.0 15.4 %collective-permute-start = (bf16[1,2,160,768]{3,2,1,0:T(8,128)(2,1)S(1)}, bf16[1,2,160,768]{3,2,1,0:T(8,128)(2,1)S(1)}, u32[]{:S(2)}, u32[]{:S(2)}) collective-permute-start(bf16[1,2,160,768]{3,2,1,0:T(8,128)(2,1)S(1)} %pad_maximum_fusion.2), channel_id=1, source_target_pairs={{0,4},{4,8},{8,12},{1,5},{5,9},{9,13},{2,6},{6,10},{10,14},{3,7},{... | collective-permute-start | bytes 1474568 | tf_op jit(solution)/shard_map/ppermute | solution.py:157
  9.0 14.8 %collective-permute-start.3 = (bf16[1,2,160,768]{3,2,1,0:T(8,128)(2,1)S(1)}, bf16[1,2,160,768]{3,2,1,0:T(8,128)(2,1)S(1)}, u32[]{:S(2)}, u32[]{:S(2)}) collective-permute-start(bf16[1,2,160,768]{3,2,1,0:T(8,128)(2,1)S(1)} %pad_maximum_fusion.2), channel_id=1, source_target_pairs={{4,0},{8,4},{12,8},{5,1},{9,5},{13,9},{6,2},{10,6},{14,10},{7,3},{... | collective-permute-start | bytes 1474568 | tf_op jit(solution)/shard_map/ppermute | solution.py:158
  19.4 14.0 %collective-permute-start.1 = (bf16[1,2,160,768]{3,2,1,0:T(8,128)(2,1)S(1)}, bf16[1,2,160,768]{3,2,1,0:T(8,128)(2,1)S(1)}, u32[]{:S(2)}, u32[]{:S(2)}) collective-permute-start(bf16[1,2,160,768]{3,2,1,0:T(8,128)(2,1)S(1)} %collective-permute-done), channel_id=1, source_target_pairs={{0,4},{4,8},{8,12},{1,5},{5,9},{9,13},{2,6},{6,10},{10,14},{3,7},{... | collective-permute-start | bytes 1474568 | tf_op jit(solution)/shard_map/ppermute | solution.py:157
  23.8 14.0 %collective-permute-start.4 = (bf16[1,2,160,768]{3,2,1,0:T(8,128)(2,1)S(1)}, bf16[1,2,160,768]{3,2,1,0:T(8,128)(2,1)S(1)}, u32[]{:S(2)}, u32[]{:S(2)}) collective-permute-start(bf16[1,2,160,768]{3,2,1,0:T(8,128)(2,1)S(1)} %collective-permute-done.3), channel_id=1, source_target_pairs={{4,0},{8,4},{12,8},{5,1},{9,5},{13,9},{6,2},{10,6},{14,10},{7,3},{... | collective-permute-start | bytes 1474568 | tf_op jit(solution)/shard_map/ppermute | solution.py:158
  33.4 13.1 %collective-permute-start.2 = (bf16[1,2,160,768]{3,2,1,0:T(8,128)(2,1)S(1)}, bf16[1,2,160,768]{3,2,1,0:T(8,128)(2,1)S(1)}, u32[]{:S(2)}, u32[]{:S(2)}) collective-permute-start(bf16[1,2,160,768]{3,2,1,0:T(8,128)(2,1)S(1)} %collective-permute-done.1), channel_id=1, source_target_pairs={{0,4},{4,8},{8,12},{1,5},{5,9},{9,13},{2,6},{6,10},{10,14},{3,7},{... | collective-permute-start | bytes 1474568 | tf_op jit(solution)/shard_map/ppermute | solution.py:157
  37.8 12.8 %collective-permute-start.5 = (bf16[1,2,160,768]{3,2,1,0:T(8,128)(2,1)S(1)}, bf16[1,2,160,768]{3,2,1,0:T(8,128)(2,1)S(1)}, u32[]{:S(2)}, u32[]{:S(2)}) collective-permute-start(bf16[1,2,160,768]{3,2,1,0:T(8,128)(2,1)S(1)} %collective-permute-done.4), channel_id=1, source_target_pairs={{4,0},{8,4},{12,8},{5,1},{9,5},{13,9},{6,2},{10,6},{14,10},{7,3},{... | collective-permute-start | bytes 1474568 | tf_op jit(solution)/shard_map/ppermute | solution.py:158
  51.9 13.5 %collective-permute-start.10 = (bf16[3,1,160,384]{3,2,1,0:T(8,128)(2,1)}, bf16[3,1,160,384]{3,2,1,0:T(8,128)(2,1)}, u32[]{:S(2)}, u32[]{:S(2)}) collective-permute-start(bf16[3,1,160,384]{3,2,1,0:T(8,128)(2,1)} %get-tuple-element.11), channel_id=1, source_target_pairs={{1,0},{2,1},{3,2},{5,4},{6,5},{7,6},{9,8},{10,9},{11,10},{13,12},{... | collective-permute-start | bytes 1105928 | tf_op jit(solution)/shard_map/ppermute | solution.py:25
  53.2 12.2 %collective-permute-start.9 = (bf16[3,1,160,384]{3,2,1,0:T(8,128)(2,1)}, bf16[3,1,160,384]{3,2,1,0:T(8,128)(2,1)}, u32[]{:S(2)}, u32[]{:S(2)}) collective-permute-start(bf16[3,1,160,384]{3,2,1,0:T(8,128)(2,1)} %get-tuple-element.10), channel_id=1, source_target_pairs={{0,1},{1,2},{2,3},{4,5},{5,6},{6,7},{8,9},{9,10},{10,11},{12,13},{... | collective-permute-start | bytes 1105928 | tf_op jit(solution)/shard_map/ppermute | solution.py:23
  57.0 49.1 %collective-permute-start.6 = (bf16[4,2,160,384]{3,2,1,0:T(8,128)(2,1)S(1)}, bf16[4,2,160,384]{3,2,1,0:T(8,128)(2,1)}, u32[]{:S(2)}, u32[]{:S(2)}) collective-permute-start(bf16[4,2,160,384]{3,2,1,0:T(8,128)(2,1)S(1)} %get-tuple-element.6), channel_id=1, source_target_pairs={{0,2},{1,3},{2,0},{3,1},{4,6},{5,7},{6,4},{7,5},{8,10},{9,11},{10,... | collective-permute-start | bytes 2949128 | tf_op jit(solution)/shard_map/ppermute | solution.py:116
  58.7 50.6 %collective-permute-start.8 = (bf16[4,2,160,384]{3,2,1,0:T(8,128)(2,1)S(1)}, bf16[4,2,160,384]{3,2,1,0:T(8,128)(2,1)}, u32[]{:S(2)}, u32[]{:S(2)}) collective-permute-start(bf16[4,2,160,384]{3,2,1,0:T(8,128)(2,1)S(1)} %get-tuple-element.6), channel_id=1, source_target_pairs={{0,1},{1,0},{2,3},{3,2},{4,5},{5,4},{6,7},{7,6},{8,9},{9,8},{10,11... | collective-permute-start | bytes 2949128 | tf_op jit(solution)/shard_map/ppermute | solution.py:123
  61.7 37.2 %all-to-all-start = ((bf16[4,2,160,384]{2,1,0,3:T(2,128)(2,1)}), bf16[4,2,160,384]{2,1,0,3:T(2,128)(2,1)S(1)}, u32[]{:S(2)}, u32[]{:S(2)}) async-start(bf16[4,2,160,384]{2,1,0,3:T(2,128)(2,1)} %copy.48), calls=%async_computation | async-start | bytes 3145728 | tf_op jit(solution)/shard_map/all_to_all | solution.py:188
  67.6 0.9 copy-start.5
  68.4 7.6 %copy-start = (bf16[1,2,160,384]{3,2,1,0:T(8,128)(2,1)S(1)}, bf16[1,2,160,384]{3,2,1,0:T(8,128)(2,1)}, u32[]{:S(2)}) copy-start(bf16[1,2,160,384]{3,2,1,0:T(8,128)(2,1)} %param.5) | copy-start | bytes 737284
  68.5 7.6 %copy-start.3 = (f32[384]{0:T(512)S(1)}, f32[384]{0:T(512)}, u32[]{:S(2)}) copy-start(f32[384]{0:T(512)} %param.6) | copy-start | bytes 4612
  106.1 5.1 %collective-permute-start.7 = (bf16[4,2,160,384]{3,2,1,0:T(8,128)(2,1)}, bf16[4,2,160,384]{3,2,1,0:T(8,128)(2,1)S(1)}, u32[]{:S(2)}, u32[]{:S(2)}) collective-permute-start(bf16[4,2,160,384]{3,2,1,0:T(8,128)(2,1)} %collective-permute-done.6), channel_id=1, source_target_pairs={{0,1},{1,0},{2,3},{3,2},{4,5},{5,4},{6,7},{7,6},{8,9},{9,8},{10,11... | collective-permute-start | bytes 2949128 | tf_op jit(solution)/shard_map/ppermute | solution.py:124
  115.1 2.2 %slice-start = ((s8[7962624]{0:T(1024)(128)(4,1)}), s8[4194304]{0:T(1024)(128)(4,1)S(1)}, s32[]{:S(2)}) async-start(s8[7962624]{0:T(1024)(128)(4,1)} %bitcast.100), calls=%async_computation.1 | async-start | bytes 8388608
  115.6 3.0 %slice-start.1 = ((s8[7962624]{0:T(1024)(128)(4,1)}), s8[3768320]{0:T(1024)(128)(4,1)S(1)}, s32[]{:S(2)}) async-start(s8[7962624]{0:T(1024)(128)(4,1)} %bitcast.100), calls=%async_computation.2 | async-start | bytes 7536640
  126.5 1.8 %copy-start.2 = (bf16[1,2,160,384]{3,2,1,0:T(8,128)(2,1)S(1)}, bf16[1,2,160,384]{3,2,1,0:T(8,128)(2,1)}, u32[]{:S(2)}) copy-start(bf16[1,2,160,384]{3,2,1,0:T(8,128)(2,1)} %param.9) | copy-start | bytes 737284
  126.5 1.8 %copy-start.4 = (f32[384]{0:T(512)S(1)}, f32[384]{0:T(512)}, u32[]{:S(2)}) copy-start(f32[384]{0:T(512)} %param.7) | copy-start | bytes 4612

commit v18 on v14

--- a/solution.py
+++ b/solution.py
@@ -142,7 +142,7 @@
     )
 
 
-def gather_frames(block):
+def gather_frames(block, lead, carried):
     count = lax.axis_size("tm")
     position = lax.axis_index("tm")
     up = [(i, i + 1) for i in range(count - 1)]
@@ -151,11 +151,35 @@
     rising, falling = block, block
     for step in range(1, count):
         rising = lax.ppermute(rising, "tm", up)
+        if not carried(step) and falling.shape[-1] == block.shape[-1]:
+            falling = falling[..., lead:]
         falling = lax.ppermute(falling, "tm", down)
         earlier.append(rising)
-        later.append(falling)
+        if falling.shape[-1] == block.shape[-1]:
+            later.append(falling)
+        else:
+            later.append(
+                jnp.concatenate(
+                    [jnp.zeros(falling.shape[:-1] + (lead,), falling.dtype), falling], axis=-1
+                )
+            )
     relative = jnp.concatenate(earlier[::-1] + [block] + later, axis=0)
     return lax.dynamic_slice_in_dim(relative, count - 1 - position, count * block.shape[0], 0)
+
+
+def falling_hidden(total_frames, frame_devices, share_rows, channels):
+    plane_rows = 9 * channels
+
+    def deepest(device):
+        return ((device + 1) * share_rows - 1) // plane_rows
+
+    def carried(step):
+        return any(
+            frame <= total_frames - 3 + deepest(frame - step)
+            for frame in range(step, frame_devices)
+        )
+
+    return carried
 
 
 def local(latents, gain, bias, weight, cotangent):
@@ -177,7 +201,11 @@
     inverse_root = 1.0 / math.sqrt(total_frames * total_rows * col_count)
     weight_cube = weight.reshape(3, 3, 3, channels, channels)
 
-    both_frames = gather_frames(jnp.concatenate([hidden, cotangent], axis=-1))
+    both_frames = gather_frames(
+        jnp.concatenate([hidden, cotangent], axis=-1),
+        channels,
+        falling_hidden(total_frames, frame_devices, share_rows, channels),
+    )
     hidden_all = gather_rows(both_frames[..., :channels], height_count)
 
     cot_frames = both_frames[..., channels:]

time: 125 us -> 126 us (level)
  waiting for transfers between devices: 34.8 us -> 38.6 us
  starting transfers between devices: 38.9 us -> 36.4 us
    ppermute x3, waiting for transfers between devices: 3.9 us -> 13.3 us  [gather_frames(): falling = lax.ppermute(falling, 'tm', down)]
    ppermute x3, waiting for transfers between devices: 24.7 us -> 18.7 us  [gather_frames(): rising = lax.ppermute(rising, 'tm', up)]
    ppermute x1, starting transfers between devices: 11.1 us -> 8.55 us  [gather_rows(): twins = lax.ppermute(stacked, 'height', sibling)]
  transfers between devices with their start and end apart: 11 -> 11, of which waited for: 5 -> 6; matrix products, arithmetic and copies ran while one was open for 19% -> 19% of each run, Pallas kernels for 0% -> 0%
where the time goes in v18:
time: 126 us
  waiting for transfers between devices  38.6 us (31%)
  starting transfers between devices  36.4 us (29%)
  local copies, waits for them, and re-layouts  19.4 us (15%)
  other arithmetic  17.3 us (14%)
  matrix products  13 us (10%)
    ppermute x3, waiting for transfers between devices, gather_frames(): rising = lax.ppermute(rising, 'tm', up)  18.7 us
    ppermute x3, starting transfers between devices, gather_frames(): rising = lax.ppermute(rising, 'tm', up)  13.8 us
    ppermute x3, waiting for transfers between devices, gather_frames(): falling = lax.ppermute(falling, 'tm', down)  13.3 us
    ppermute x1, starting transfers between devices, gather_rows(): twins = lax.ppermute(stacked, 'height', sibling)  8.55 us
    ppermute x1, waiting for transfers between devices, gather_rows(): lax.ppermute(own, 'height', [(i, (i + 2 * step) % height_count) for i in...  6.21 us
    dot_general x3, matrix products, block_weight_grad(): lax.dot_general(window, hidden_all, (((0, 1, 2), (0, 1, 2)), ((), ())), p...  5.42 us
    ppermute x3, starting transfers between devices, gather_frames(): falling = lax.ppermute(falling, 'tm', down)  3.86 us
    ppermute x1, starting transfers between devices, padded(): lax.ppermute(tail, axis, [(i, (i + 1) % count) for i in range(ends)])  3.79 us
  transfers between devices with their start and end apart: 11, of which 6 were waited for; matrix products, arithmetic and copies ran while one was open for 19% of the time, Pallas kernels for 0%

profile of v18, /device:TPU:0, one launch (start us, length us, event | category | flops | bytes accessed | tf_op | source)
XLA Modules:
  0.0 125.9 jit_solution(3492924445862594195)
XLA Ops:
  0.6 1.1 fusion.65
  1.7 0.0 copy-start.4
  1.8 1.2 multiply_convert_fusion
  3.0 1.0 pad_maximum_fusion.5
  4.0 5.0 %collective-permute-start = (bf16[1,2,160,768]{3,2,1,0:T(8,128)(2,1)S(1)}, bf16[1,2,160,768]{3,2,1,0:T(8,128)(2,1)S(1)}, u32[]{:S(2)}, u32[]{:S(2)}) collective-permute-start(bf16[1,2,160,768]{3,2,1,0:T(8,128)(2,1)S(1)} %pad_maximum_fusion.5), channel_id=1, source_target_pairs={{0,4},{4,8},{8,12},{1,5},{5,9},{9,13},{2,6},{6,10},{10,14},{3,7},{... | collective-permute-start | bytes 1474568 | tf_op jit(solution)/shard_map/ppermute | solution.py:153
  9.0 10.4 %collective-permute-done = bf16[1,2,160,768]{3,2,1,0:T(8,128)(2,1)S(1)} collective-permute-done((bf16[1,2,160,768]{3,2,1,0:T(8,128)(2,1)S(1)}, bf16[1,2,160,768]{3,2,1,0:T(8,128)(2,1)S(1)}, u32[]{:S(2)}, u32[]{:S(2)}) %collective-permute-start) | collective-permute-done | bytes 491552 | tf_op jit(solution)/shard_map/ppermute | solution.py:153
  19.4 4.4 %collective-permute-start.1 = (bf16[1,2,160,768]{3,2,1,0:T(8,128)(2,1)S(1)}, bf16[1,2,160,768]{3,2,1,0:T(8,128)(2,1)S(1)}, u32[]{:S(2)}, u32[]{:S(2)}) collective-permute-start(bf16[1,2,160,768]{3,2,1,0:T(8,128)(2,1)S(1)} %collective-permute-done), channel_id=1, source_target_pairs={{0,4},{4,8},{8,12},{1,5},{5,9},{9,13},{2,6},{6,10},{10,14},{3,7},{... | collective-permute-start | bytes 1474568 | tf_op jit(solution)/shard_map/ppermute | solution.py:153
  23.8 1.3 %collective-permute-start.3 = (bf16[1,2,160,768]{3,2,1,0:T(8,128)(2,1)S(1)}, bf16[1,2,160,768]{3,2,1,0:T(8,128)(2,1)S(1)}, u32[]{:S(2)}, u32[]{:S(2)}) collective-permute-start(bf16[1,2,160,768]{3,2,1,0:T(8,128)(2,1)S(1)} %pad_maximum_fusion.5), channel_id=1, source_target_pairs={{4,0},{8,4},{12,8},{5,1},{9,5},{13,9},{6,2},{10,6},{14,10},{7,3},{... | collective-permute-start | bytes 1474568 | tf_op jit(solution)/shard_map/ppermute | solution.py:156
  25.1 8.3 %collective-permute-done.1 = bf16[1,2,160,768]{3,2,1,0:T(8,128)(2,1)S(1)} collective-permute-done((bf16[1,2,160,768]{3,2,1,0:T(8,128)(2,1)S(1)}, bf16[1,2,160,768]{3,2,1,0:T(8,128)(2,1)S(1)}, u32[]{:S(2)}, u32[]{:S(2)}) %collective-permute-start.1) | collective-permute-done | bytes 491552 | tf_op jit(solution)/shard_map/ppermute | solution.py:153
  33.4 4.4 %collective-permute-start.2 = (bf16[1,2,160,768]{3,2,1,0:T(8,128)(2,1)S(1)}, bf16[1,2,160,768]{3,2,1,0:T(8,128)(2,1)S(1)}, u32[]{:S(2)}, u32[]{:S(2)}) collective-permute-start(bf16[1,2,160,768]{3,2,1,0:T(8,128)(2,1)S(1)} %collective-permute-done.1), channel_id=1, source_target_pairs={{0,4},{4,8},{8,12},{1,5},{5,9},{9,13},{2,6},{6,10},{10,14},{3,7},{... | collective-permute-start | bytes 1474568 | tf_op jit(solution)/shard_map/ppermute | solution.py:153
  37.8 1.3 %collective-permute-start.4 = (bf16[1,2,160,384]{3,2,1,0:T(8,128)(2,1)S(1)}, bf16[1,2,160,384]{3,2,1,0:T(8,128)(2,1)S(1)}, u32[]{:S(2)}, u32[]{:S(2)}) collective-permute-start(bf16[1,2,160,384]{3,2,1,0:T(8,128)(2,1)S(1)} %slice.48), channel_id=1, source_target_pairs={{4,0},{8,4},{12,8},{5,1},{9,5},{13,9},{6,2},{10,6},{14,10},{7,3},{... | collective-permute-start | bytes 737288 | tf_op jit(solution)/shard_map/ppermute | solution.py:156
  39.1 6.8 %collective-permute-done.4 = bf16[1,2,160,384]{3,2,1,0:T(8,128)(2,1)S(1)} collective-permute-done((bf16[1,2,160,384]{3,2,1,0:T(8,128)(2,1)S(1)}, bf16[1,2,160,384]{3,2,1,0:T(8,128)(2,1)S(1)}, u32[]{:S(2)}, u32[]{:S(2)}) %collective-permute-start.4) | collective-permute-done | bytes 245792 | tf_op jit(solution)/shard_map/ppermute | solution.py:156
  45.9 1.3 %collective-permute-start.5 = (bf16[1,2,160,384]{3,2,1,0:T(8,128)(2,1)S(1)}, bf16[1,2,160,384]{3,2,1,0:T(8,128)(2,1)S(1)}, u32[]{:S(2)}, u32[]{:S(2)}) collective-permute-start(bf16[1,2,160,384]{3,2,1,0:T(8,128)(2,1)S(1)} %collective-permute-done.4), channel_id=1, source_target_pairs={{4,0},{8,4},{12,8},{5,1},{9,5},{13,9},{6,2},{10,6},{14,10},{7,3},{... | collective-permute-start | bytes 737288 | tf_op jit(solution)/shard_map/ppermute | solution.py:156
  47.5 6.5 %collective-permute-done.5 = bf16[1,2,160,384]{3,2,1,0:T(8,128)(2,1)S(1)} collective-permute-done((bf16[1,2,160,384]{3,2,1,0:T(8,128)(2,1)S(1)}, bf16[1,2,160,384]{3,2,1,0:T(8,128)(2,1)S(1)}, u32[]{:S(2)}, u32[]{:S(2)}) %collective-permute-start.5) | collective-permute-done | bytes 245792 | tf_op jit(solution)/shard_map/ppermute | solution.py:156
  54.0 0.3 constant_dynamic-slice_fusion.1
  54.3 1.6 %collective-permute-start.6 = (bf16[4,2,160,384]{3,2,1,0:T(8,128)(2,1)S(1)}, bf16[4,2,160,384]{3,2,1,0:T(8,128)(2,1)}, u32[]{:S(2)}, u32[]{:S(2)}) collective-permute-start(bf16[4,2,160,384]{3,2,1,0:T(8,128)(2,1)S(1)} %get-tuple-element.6), channel_id=1, source_target_pairs={{0,2},{1,3},{2,0},{3,1},{4,6},{5,7},{6,4},{7,5},{8,10},{9,11},{10,... | collective-permute-start | bytes 2949128 | tf_op jit(solution)/shard_map/ppermute | solution.py:116
  55.9 1.0 pad_dynamic-slice_fusion.6
  56.8 1.3 %collective-permute-start.9 = (bf16[3,1,160,384]{3,2,1,0:T(8,128)(2,1)}, bf16[3,1,160,384]{3,2,1,0:T(8,128)(2,1)}, u32[]{:S(2)}, u32[]{:S(2)}) collective-permute-start(bf16[3,1,160,384]{3,2,1,0:T(8,128)(2,1)} %get-tuple-element.13), channel_id=1, source_target_pairs={{1,0},{2,1},{3,2},{5,4},{6,5},{7,6},{9,8},{10,9},{11,10},{13,12},{... | collective-permute-start | bytes 1105928 | tf_op jit(solution)/shard_map/ppermute | solution.py:25
  58.1 3.8 %collective-permute-start.8 = (bf16[3,1,160,384]{3,2,1,0:T(8,128)(2,1)}, bf16[3,1,160,384]{3,2,1,0:T(8,128)(2,1)}, u32[]{:S(2)}, u32[]{:S(2)}) collective-permute-start(bf16[3,1,160,384]{3,2,1,0:T(8,128)(2,1)} %get-tuple-element.12), channel_id=1, source_target_pairs={{0,1},{1,2},{2,3},{4,5},{5,6},{6,7},{8,9},{9,10},{10,11},{12,13},{... | collective-permute-start | bytes 1105928 | tf_op jit(solution)/shard_map/ppermute | solution.py:23
  61.9 3.0 %copy.48 = bf16[4,2,160,384]{2,1,0,3:T(2,128)(2,1)} copy(bf16[4,2,160,384]{3,2,1,0:T(8,128)(2,1)S(1)} %get-tuple-element.5) | data formatting | bytes 1966080 | tf_op jit(solution)/shard_map/slice | solution.py:211
  65.0 3.6 %all-to-all-start = ((bf16[4,2,160,384]{2,1,0,3:T(2,128)(2,1)}), bf16[4,2,160,384]{2,1,0,3:T(2,128)(2,1)S(1)}, u32[]{:S(2)}, u32[]{:S(2)}) async-start(bf16[4,2,160,384]{2,1,0,3:T(2,128)(2,1)} %copy.48), calls=%async_computation | async-start | bytes 3145728 | tf_op jit(solution)/shard_map/all_to_all | solution.py:212
  68.5 0.1 pad_dynamic-slice_fusion.7
  68.7 0.0 slice-start
  68.7 1.7 %fusion.37 = bf16[3,4,1,162,384]{4,3,1,0,2:T(8,128)(2,1)S(1)} fusion(bf16[3,1,160,384]{3,2,1,0:T(8,128)(2,1)} %collective-permute-done.9, bf16[3,2,160,384]{3,2,1,0:T(8,128)(2,1)S(1)} %pad_dynamic-slice_fusion.7, bf16[3,1,160,384]{3,2,1,0:T(8,128)(2,1)} %collective-permute-done.8), kind=kLoop, calls=%fused_computation.54 | loop fusion | flops 9704448 | bytes 2967552 | tf_op jit(solution)/shard_map/broadcast_in_dim | solution.py:58
  70.4 0.6 copy.62
  71.0 0.0 slice-start.1
  71.0 0.6 pad.24.clone
  71.6 0.2 copy.45
  71.8 0.0 copy-start.8
  71.9 6.2 %collective-permute-done.6 = bf16[4,2,160,384]{3,2,1,0:T(8,128)(2,1)} collective-permute-done((bf16[4,2,160,384]{3,2,1,0:T(8,128)(2,1)S(1)}, bf16[4,2,160,384]{3,2,1,0:T(8,128)(2,1)}, u32[]{:S(2)}, u32[]{:S(2)}) %collective-permute-start.6) | collective-permute-done | bytes 983072 | tf_op jit(solution)/shard_map/ppermute | solution.py:116
  78.1 2.7 %pad_maximum_fusion.3 = bf16[4,4,160,384]{3,2,1,0:T(8,128)(2,1)} fusion(bf16[4,2,160,384]{3,2,1,0:T(8,128)(2,1)} %collective-permute-done.6, bf16[4,2,160,384]{3,2,1,0:T(8,128)(2,1)S(1)} %get-tuple-element.6), kind=kLoop, calls=%fused_computation.30 | loop fusion | flops 983040 | bytes 3932160 | tf_op jit(solution)/shard_map/concatenate | solution.py:121
  80.8 8.6 %collective-permute-start.7 = (bf16[4,4,160,384]{3,2,1,0:T(8,128)(2,1)}, bf16[4,4,160,384]{3,2,1,0:T(8,128)(2,1)}, u32[]{:S(2)}, u32[]{:S(2)}) collective-permute-start(bf16[4,4,160,384]{3,2,1,0:T(8,128)(2,1)} %pad_maximum_fusion.3), channel_id=1, source_target_pairs={{0,1},{1,0},{2,3},{3,2},{4,5},{5,4},{6,7},{7,6},{8,9},{9,8},{10,11... | collective-permute-start | bytes 5898248 | tf_op jit(solution)/shard_map/ppermute | solution.py:122
  89.3 0.0 copy-start.2
  89.4 3.8 %fusion.54 = f32[1,2,8,21,384]{4,2,3,1,0:T(8,128)S(1)} fusion(bf16[3,3,3,384,384]{4,3,2,1,0:T(8,128)(2,1)S(1)} %bitcast.101, bf16[3,4,1,7,2,384]{5,3,4,1,0,2:T(8,128)(2,1)S(1)} %slice.53, bf16[3,4,1,8,21,384]{5,3,4,1,0,2:T(8,128)(2,1)S(1)} %copy.45, pred[8,21]{0,1:T(8,128)(4,1)S(1)} %copy-done.8), kind=kOutput, calls=%fused_computation.64 | convolution fusion | flops 2680657920 | bytes 10156200 | tf_op jit(solution)/shard_map/conv_general_dilated | solution.py:57
  93.1 0.3 copy.46
  93.4 0.2 slice.54
  93.6 0.0 copy-start
  93.6 0.4 multiply_reduce_fusion
  94.0 0.4 all-to-all-done
  94.4 3.8 %copy.49 = bf16[4,2,160,4,96]{4,2,1,3,0:T(8,128)(2,1)} copy(bf16[4,2,160,4,96]{2,1,0,4,3:T(2,128)(2,1)S(1)} %bitcast.90) | data formatting | bytes 1966080 | tf_op jit(solution)/shard_map/all_to_all | solution.py:212
  98.2 3.5 %fusion.14 = (bf16[6,10,160,1,96]{4,2,1,3,0:T(8,128)(2,1)S(1)}, bf16[6,10,160,1,96]{4,2,1,3,0:T(8,128)(2,1)S(1)}, bf16[6,10,160,1,96]{4,2,1,3,0:T(8,128)(2,1)S(1)}) fusion(bf16[4,8,160,96]{3,2,1,0:T(8,128)(2,1)} %bitcast.93), kind=kLoop, calls=%fused_computation.26 | loop fusion | bytes 6512640 | tf_op jit(solution)/shard_map/stack | solution.py:82
  101.6 2.0 %pad_maximum_fusion = bf16[6,10,160,3,96]{4,2,1,3,0:T(8,128)(2,1)S(1)} fusion(bf16[6,10,160,1,96]{4,2,1,3,0:T(8,128)(2,1)S(1)} %get-tuple-element.11, bf16[6,10,160,1,96]{4,2,1,3,0:T(8,128)(2,1)S(1)} %get-tuple-element.10, bf16[6,10,160,1,96]{4,2,1,3,0:T(8,128)(2,1)S(1)} %get-tuple-element.9), kind=kLoop, calls=%fused_computation.1 | loop fusion | flops 5529600 | bytes 11059200 | tf_op jit(solution)/shard_map/stack | solution.py:82
  103.7 1.7 %fusion.80 = (bf16[4,2,160,384]{3,2,1,0:T(8,128)(2,1)S(1)}, bf16[4,2,160,384]{3,2,1,0:T(8,128)(2,1)S(1)}) fusion(bf16[4,4,160,384]{3,2,1,0:T(8,128)(2,1)} %collective-permute-done.7), kind=kLoop, calls=%fused_computation.107 | loop fusion | bytes 3932160 | tf_op jit(solution)/shard_map/slice | solution.py:127
  105.4 0.3 fusion.17
  105.7 1.8 %fusion.18 = bf16[4,4,160,384]{3,2,1,0:T(8,128)(2,1)S(1)} fusion(bf16[4,2,160,384]{3,2,1,0:T(8,128)(2,1)} %collective-permute-done.6, bf16[4,2,160,384]{3,2,1,0:T(8,128)(2,1)S(1)} %get-tuple-element.8, pred[]{:T(512)S(6)} %eq.10), kind=kLoop, calls=%fused_computation.33 | loop fusion | flops 2949120 | bytes 3932161 | tf_op jit(solution)/shard_map/jit(_where)/select_n | solution.py:129
  107.6 1.6 %fusion.20 = (bf16[4,4,160,384]{3,2,1,0:T(8,128)(2,1)S(1)}, bf16[4,4,160,384]{3,2,1,0:T(8,128)(2,1)S(1)}) fusion(s32[]{:T(128)S(6)} %select_n.99, bf16[4,4,160,384]{3,2,1,0:T(8,128)(2,1)S(1)} %fusion.18, bf16[4,4,160,384]{3,2,1,0:T(8,128)(2,1)S(1)} %fusion.17, s32[]{:T(128)S(6)} %select_n.101), kind=kLoop, calls=%fused_computation.35 | loop fusion | flops 1966080 | bytes 7864328 | tf_op jit(solution)/shard_map/concatenate | solution.py:135
  109.2 0.4 pad_maximum_fusion.1
  109.7 0.0 slice-start.2
  109.7 0.5 fusion.35
  110.2 0.0 slice-start.3
  110.2 0.6 copy.61
  110.8 0.6 pad.22.clone
  111.4 0.2 copy.40
  111.6 0.2 slice-done.2
  111.9 1.3 %slice-done.3 = s8[3768320]{0:T(1024)(128)(4,1)S(1)} async-done(((s8[7962624]{0:T(1024)(128)(4,1)}), s8[3768320]{0:T(1024)(128)(4,1)S(1)}, s32[]{:S(2)}) %slice-start.3) | async-done | bytes 3768344
  113.1 3.8 %fusion.57 = f32[1,2,8,21,384]{4,2,3,1,0:T(8,128)S(1)} fusion(bf16[3,3,3,384,384]{4,3,2,1,0:T(8,128)(2,1)S(1)} %bitcast.104, bf16[3,4,1,7,2,384]{5,3,4,1,0,2:T(8,128)(2,1)S(1)} %slice.51, bf16[3,4,1,8,21,384]{5,3,4,1,0,2:T(8,128)(2,1)S(1)} %copy.40, pred[8,21]{0,1:T(8,128)(4,1)S(1)} %copy-done.8), kind=kOutput, calls=%fused_computation.65 | convolution fusion | flops 2680657920 | bytes 10156200 | tf_op jit(solution)/shard_map/conv_general_dilated | solution.py:44
  116.9 0.3 copy.41
  117.2 0.2 slice.52
  117.4 1.7 %fusion.39 = f32[3,12,8,384]{3,2,1,0:T(8,128)S(1)} fusion(bf16[6,10,160,3,96]{4,2,1,3,0:T(8,128)(2,1)S(1)} %pad_maximum_fusion, s32[]{:T(128)S(6)} %select_n.106, s32[]{:T(128)S(6)} %select_n.108, bf16[4,4,160,384]{3,2,1,0:T(8,128)(2,1)S(1)} %get-tuple-element.4, bf16[4,4,160,384]{3,2,1,0:T(8,128)(2,1)S(1)} %get-tuple-element.3), kind=kOutput, calls=%fused_computation.61 | convolution fusion | flops 1134428160 | bytes 8306696 | tf_op jit(solution)/shard_map/dot_general | solution.py:98
  119.2 1.8 %fusion.44 = f32[3,12,8,384]{3,2,1,0:T(8,128)S(1)} fusion(bf16[6,10,160,3,96]{4,2,1,3,0:T(8,128)(2,1)S(1)} %pad_maximum_fusion, s32[]{:T(128)S(6)} %select_n.110, s32[]{:T(128)S(6)} %select_n.112, bf16[4,4,160,384]{3,2,1,0:T(8,128)(2,1)S(1)} %get-tuple-element.4, bf16[4,4,160,384]{3,2,1,0:T(8,128)(2,1)S(1)} %get-tuple-element.3), kind=kOutput, calls=%fused_computation.62 | convolution fusion | flops 1134428160 | bytes 8306696 | tf_op jit(solution)/shard_map/dot_general | solution.py:98
  121.0 0.0 copy-start.1
  121.0 2.0 %fusion.49 = f32[3,12,8,384]{3,2,1,0:T(8,128)S(1)} fusion(bf16[6,10,160,3,96]{4,2,1,3,0:T(8,128)(2,1)S(1)} %pad_maximum_fusion, s32[]{:T(128)S(6)} %select_n.114, s32[]{:T(128)S(6)} %select_n.116, bf16[4,4,160,384]{3,2,1,0:T(8,128)(2,1)S(1)} %get-tuple-element.4, bf16[4,4,160,384]{3,2,1,0:T(8,128)(2,1)S(1)} %get-tuple-element.3), kind=kOutput, calls=%fused_computation.63 | convolution fusion | flops 1134428160 | bytes 8306696 | tf_op jit(solution)/shard_map/dot_general | solution.py:98
  123.0 1.2 add_convert_fusion
  124.2 1.6 %fusion.62 = f32[2592,96]{0,1:T(8,128)} fusion(s32[]{:T(128)S(6)} %select_n.117, f32[1152,96]{0,1:T(8,128)S(1)} %bitcast.96, f32[1152,96]{0,1:T(8,128)S(1)} %bitcast.97, f32[1152,96]{0,1:T(8,128)S(1)} %bitcast.98), kind=kLoop, calls=%fused_computation.68 | loop fusion | flops 746496 | bytes 2322436 | tf_op jit(solution)/shard_map/mul | solution.py:225
  (37 shorter events, 0.5 us)
Async XLA Ops:
  1.7 45.6 %copy-start.4 = (bf16[1,2,160,384]{3,2,1,0:T(8,128)(2,1)S(1)}, bf16[1,2,160,384]{3,2,1,0:T(8,128)(2,1)}, u32[]{:S(2)}) copy-start(bf16[1,2,160,384]{3,2,1,0:T(8,128)(2,1)} %param.9) | copy-start | bytes 737284
  4.0 15.4 %collective-permute-start = (bf16[1,2,160,768]{3,2,1,0:T(8,128)(2,1)S(1)}, bf16[1,2,160,768]{3,2,1,0:T(8,128)(2,1)S(1)}, u32[]{:S(2)}, u32[]{:S(2)}) collective-permute-start(bf16[1,2,160,768]{3,2,1,0:T(8,128)(2,1)S(1)} %pad_maximum_fusion.5), channel_id=1, source_target_pairs={{0,4},{4,8},{8,12},{1,5},{5,9},{9,13},{2,6},{6,10},{10,14},{3,7},{... | collective-permute-start | bytes 1474568 | tf_op jit(solution)/shard_map/ppermute | solution.py:153
  19.4 14.0 %collective-permute-start.1 = (bf16[1,2,160,768]{3,2,1,0:T(8,128)(2,1)S(1)}, bf16[1,2,160,768]{3,2,1,0:T(8,128)(2,1)S(1)}, u32[]{:S(2)}, u32[]{:S(2)}) collective-permute-start(bf16[1,2,160,768]{3,2,1,0:T(8,128)(2,1)S(1)} %collective-permute-done), channel_id=1, source_target_pairs={{0,4},{4,8},{8,12},{1,5},{5,9},{9,13},{2,6},{6,10},{10,14},{3,7},{... | collective-permute-start | bytes 1474568 | tf_op jit(solution)/shard_map/ppermute | solution.py:153
  23.8 14.0 %collective-permute-start.3 = (bf16[1,2,160,768]{3,2,1,0:T(8,128)(2,1)S(1)}, bf16[1,2,160,768]{3,2,1,0:T(8,128)(2,1)S(1)}, u32[]{:S(2)}, u32[]{:S(2)}) collective-permute-start(bf16[1,2,160,768]{3,2,1,0:T(8,128)(2,1)S(1)} %pad_maximum_fusion.5), channel_id=1, source_target_pairs={{4,0},{8,4},{12,8},{5,1},{9,5},{13,9},{6,2},{10,6},{14,10},{7,3},{... | collective-permute-start | bytes 1474568 | tf_op jit(solution)/shard_map/ppermute | solution.py:156
  33.4 13.8 %collective-permute-start.2 = (bf16[1,2,160,768]{3,2,1,0:T(8,128)(2,1)S(1)}, bf16[1,2,160,768]{3,2,1,0:T(8,128)(2,1)S(1)}, u32[]{:S(2)}, u32[]{:S(2)}) collective-permute-start(bf16[1,2,160,768]{3,2,1,0:T(8,128)(2,1)S(1)} %collective-permute-done.1), channel_id=1, source_target_pairs={{0,4},{4,8},{8,12},{1,5},{5,9},{9,13},{2,6},{6,10},{10,14},{3,7},{... | collective-permute-start | bytes 1474568 | tf_op jit(solution)/shard_map/ppermute | solution.py:153
  37.8 8.1 %collective-permute-start.4 = (bf16[1,2,160,384]{3,2,1,0:T(8,128)(2,1)S(1)}, bf16[1,2,160,384]{3,2,1,0:T(8,128)(2,1)S(1)}, u32[]{:S(2)}, u32[]{:S(2)}) collective-permute-start(bf16[1,2,160,384]{3,2,1,0:T(8,128)(2,1)S(1)} %slice.48), channel_id=1, source_target_pairs={{4,0},{8,4},{12,8},{5,1},{9,5},{13,9},{6,2},{10,6},{14,10},{7,3},{... | collective-permute-start | bytes 737288 | tf_op jit(solution)/shard_map/ppermute | solution.py:156
  45.9 8.1 %collective-permute-start.5 = (bf16[1,2,160,384]{3,2,1,0:T(8,128)(2,1)S(1)}, bf16[1,2,160,384]{3,2,1,0:T(8,128)(2,1)S(1)}, u32[]{:S(2)}, u32[]{:S(2)}) collective-permute-start(bf16[1,2,160,384]{3,2,1,0:T(8,128)(2,1)S(1)} %collective-permute-done.4), channel_id=1, source_target_pairs={{4,0},{8,4},{12,8},{5,1},{9,5},{13,9},{6,2},{10,6},{14,10},{7,3},{... | collective-permute-start | bytes 737288 | tf_op jit(solution)/shard_map/ppermute | solution.py:156
  54.3 23.8 %collective-permute-start.6 = (bf16[4,2,160,384]{3,2,1,0:T(8,128)(2,1)S(1)}, bf16[4,2,160,384]{3,2,1,0:T(8,128)(2,1)}, u32[]{:S(2)}, u32[]{:S(2)}) collective-permute-start(bf16[4,2,160,384]{3,2,1,0:T(8,128)(2,1)S(1)} %get-tuple-element.6), channel_id=1, source_target_pairs={{0,2},{1,3},{2,0},{3,1},{4,6},{5,7},{6,4},{7,5},{8,10},{9,11},{10,... | collective-permute-start | bytes 2949128 | tf_op jit(solution)/shard_map/ppermute | solution.py:116
  56.8 11.8 %collective-permute-start.9 = (bf16[3,1,160,384]{3,2,1,0:T(8,128)(2,1)}, bf16[3,1,160,384]{3,2,1,0:T(8,128)(2,1)}, u32[]{:S(2)}, u32[]{:S(2)}) collective-permute-start(bf16[3,1,160,384]{3,2,1,0:T(8,128)(2,1)} %get-tuple-element.13), channel_id=1, source_target_pairs={{1,0},{2,1},{3,2},{5,4},{6,5},{7,6},{9,8},{10,9},{11,10},{13,12},{... | collective-permute-start | bytes 1105928 | tf_op jit(solution)/shard_map/ppermute | solution.py:25
  58.1 10.6 %collective-permute-start.8 = (bf16[3,1,160,384]{3,2,1,0:T(8,128)(2,1)}, bf16[3,1,160,384]{3,2,1,0:T(8,128)(2,1)}, u32[]{:S(2)}, u32[]{:S(2)}) collective-permute-start(bf16[3,1,160,384]{3,2,1,0:T(8,128)(2,1)} %get-tuple-element.12), channel_id=1, source_target_pairs={{0,1},{1,2},{2,3},{4,5},{5,6},{6,7},{8,9},{9,10},{10,11},{12,13},{... | collective-permute-start | bytes 1105928 | tf_op jit(solution)/shard_map/ppermute | solution.py:23
  65.0 29.4 %all-to-all-start = ((bf16[4,2,160,384]{2,1,0,3:T(2,128)(2,1)}), bf16[4,2,160,384]{2,1,0,3:T(2,128)(2,1)S(1)}, u32[]{:S(2)}, u32[]{:S(2)}) async-start(bf16[4,2,160,384]{2,1,0,3:T(2,128)(2,1)} %copy.48), calls=%async_computation | async-start | bytes 3145728 | tf_op jit(solution)/shard_map/all_to_all | solution.py:212
  68.7 20.6 %slice-start = ((s8[7962624]{0:T(1024)(128)(4,1)}), s8[4194304]{0:T(1024)(128)(4,1)S(1)}, s32[]{:S(2)}) async-start(s8[7962624]{0:T(1024)(128)(4,1)} %bitcast.99), calls=%async_computation.1 | async-start | bytes 8388608
  71.0 18.3 %slice-start.1 = ((s8[7962624]{0:T(1024)(128)(4,1)}), s8[3768320]{0:T(1024)(128)(4,1)S(1)}, s32[]{:S(2)}) async-start(s8[7962624]{0:T(1024)(128)(4,1)} %bitcast.99), calls=%async_computation.2 | async-start | bytes 7536640
  71.8 17.5 %copy-start.8 = (pred[8,21]{0,1:T(8,128)(4,1)S(1)}, pred[8,21]{0,1:T(8,128)(4,1)}, u32[]{:S(2)}) copy-start(pred[8,21]{0,1:T(8,128)(4,1)} %constant.131) | copy-start | bytes 508
  80.8 22.9 %collective-permute-start.7 = (bf16[4,4,160,384]{3,2,1,0:T(8,128)(2,1)}, bf16[4,4,160,384]{3,2,1,0:T(8,128)(2,1)}, u32[]{:S(2)}, u32[]{:S(2)}) collective-permute-start(bf16[4,4,160,384]{3,2,1,0:T(8,128)(2,1)} %pad_maximum_fusion.3), channel_id=1, source_target_pairs={{0,1},{1,0},{2,3},{3,2},{4,5},{5,4},{6,7},{7,6},{8,9},{9,8},{10,11... | collective-permute-start | bytes 5898248 | tf_op jit(solution)/shard_map/ppermute | solution.py:122
  89.3 4.3 %copy-start.2 = (bf16[1,2,160,384]{3,2,1,0:T(8,128)(2,1)S(1)}, bf16[1,2,160,384]{3,2,1,0:T(8,128)(2,1)}, u32[]{:S(2)}) copy-start(bf16[1,2,160,384]{3,2,1,0:T(8,128)(2,1)} %param.5) | copy-start | bytes 737284
  89.4 4.3 %copy-start.6 = (f32[384]{0:T(512)S(1)}, f32[384]{0:T(512)}, u32[]{:S(2)}) copy-start(f32[384]{0:T(512)} %param.6) | copy-start | bytes 4612
  93.6 8.0 %copy-start = (f32[1,2,1,160,384]{4,1,3,2,0:T(2,128)}, f32[1,2,1,160,384]{4,1,3,2,0:T(2,128)S(1)}, u32[]{:S(2)}) copy-start(f32[1,2,1,160,384]{4,1,3,2,0:T(2,128)S(1)} %slice.54) | copy-start | bytes 1474564
  109.7 2.2 %slice-start.2 = ((s8[7962624]{0:T(1024)(128)(4,1)}), s8[4194304]{0:T(1024)(128)(4,1)S(1)}, s32[]{:S(2)}) async-start(s8[7962624]{0:T(1024)(128)(4,1)} %bitcast.102), calls=%async_computation.3 | async-start | bytes 8388608
  110.2 3.0 %slice-start.3 = ((s8[7962624]{0:T(1024)(128)(4,1)}), s8[3768320]{0:T(1024)(128)(4,1)S(1)}, s32[]{:S(2)}) async-start(s8[7962624]{0:T(1024)(128)(4,1)} %bitcast.102), calls=%async_computation.4 | async-start | bytes 7536640
  121.0 2.1 %copy-start.1 = (f32[1,2,1,160,384]{4,1,3,2,0:T(2,128)S(1)}, f32[1,2,1,160,384]{4,1,3,2,0:T(2,128)}, u32[]{:S(2)}) copy-start(f32[1,2,1,160,384]{4,1,3,2,0:T(2,128)} %copy-done) | copy-start | bytes 1474564
  121.0 2.0 %copy-start.3 = (bf16[1,2,160,384]{3,2,1,0:T(8,128)(2,1)S(1)}, bf16[1,2,160,384]{3,2,1,0:T(8,128)(2,1)}, u32[]{:S(2)}) copy-start(bf16[1,2,160,384]{3,2,1,0:T(8,128)(2,1)} %param.5) | copy-start | bytes 737284
  121.0 2.0 %copy-start.5 = (bf16[1,2,160,384]{3,2,1,0:T(8,128)(2,1)S(1)}, bf16[1,2,160,384]{3,2,1,0:T(8,128)(2,1)}, u32[]{:S(2)}) copy-start(bf16[1,2,160,384]{3,2,1,0:T(8,128)(2,1)} %param.9) | copy-start | bytes 737284
  121.0 2.0 %copy-start.7 = (f32[384]{0:T(512)S(1)}, f32[384]{0:T(512)}, u32[]{:S(2)}) copy-start(f32[384]{0:T(512)} %param.7) | copy-start | bytes 4612

commit v19 on v14

--- a/solution.py
+++ b/solution.py
@@ -181,7 +181,15 @@
     hidden_all = gather_rows(both_frames[..., :channels], height_count)
 
     cot_frames = both_frames[..., channels:]
-    cot_all = lax.all_to_all(cot_frames, "height", split_axis=3, concat_axis=1, tiled=True)
+    share_width = channels // height_count
+    by_share = cot_frames.reshape(
+        total_frames, row_count, col_count, height_count, share_width
+    ).transpose(3, 0, 1, 2, 4)
+    cot_all = (
+        lax.all_to_all(by_share, "height", split_axis=0, concat_axis=0, tiled=True)
+        .transpose(1, 0, 2, 3, 4)
+        .reshape(total_frames, total_rows, col_count, share_width)
+    )
 
     window = lax.dynamic_slice(
         jnp.pad(hidden_all, ((2, 0), (1, 1), (1, 1), (0, 0))),

time: 125 us -> 120 us (0.960)
  local copies, waits for them, and re-layouts: 19.4 us -> 13.2 us
  waiting for transfers between devices: 34.8 us -> 36.2 us
    all_to_all x1 -> x0, local copies, waits for them, and re-layouts: 3.76 us -> none  [local(): lax.all_to_all(cot_frames, 'height', split_axis=3, concat_axis=1, tiled=T...]
    slice x2 -> x1, local copies, waits for them, and re-layouts: 3.3 us -> 0.25 us  [local(): cot_frames = both_frames[..., channels:]]
    reshape x0 -> x2, local copies, waits for them, and re-layouts: none -> 2.35 us  [local(): cot_frames.reshape(total_frames, row_count, col_count, height_count, shar...]
    another operation x1, local copies, waits for them, and re-layouts: 3.47 us -> 1.67 us  [block_weight_grad(): jnp.stack([edged[:, :, 2 - col_tap:2 - col_tap + col_total] for col_tap i...]
    ppermute x1, waiting for transfers between devices: 6.21 us -> 7.57 us  [gather_rows(): lax.ppermute(own, 'height', [(i, (i + 2 * step) % height_count) for i in...]
    unnamed x33 -> x31, local copies, waits for them, and re-layouts: 2.93 us -> 2.93 us
  transfers between devices with their start and end apart: 11 -> 11, of which waited for: 5 -> 5; matrix products, arithmetic and copies ran while one was open for 19% -> 15% of each run, Pallas kernels for 0% -> 0%
where the time goes in v19:
time: 120 us; the launch traced here: 119 us
  starting transfers between devices  38.2 us (32%)
  waiting for transfers between devices  36.2 us (30%)
  other arithmetic  17.3 us (14%)
  local copies, waits for them, and re-layouts  13.2 us (11%)
  matrix products  13.1 us (11%)
  between operations  1.21 us (1%)
    ppermute x3, waiting for transfers between devices, gather_frames(): rising = lax.ppermute(rising, 'tm', up)  24.7 us
    ppermute x3, starting transfers between devices, gather_frames(): rising = lax.ppermute(rising, 'tm', up)  13.8 us
    ppermute x1, starting transfers between devices, gather_rows(): twins = lax.ppermute(stacked, 'height', sibling)  10.4 us
    ppermute x1, waiting for transfers between devices, gather_rows(): lax.ppermute(own, 'height', [(i, (i + 2 * step) % height_count) for i in...  7.57 us
    dot_general x3, matrix products, block_weight_grad(): lax.dot_general(window, hidden_all, (((0, 1, 2), (0, 1, 2)), ((), ())), p...  5.43 us
    ppermute x3, waiting for transfers between devices, gather_frames(): falling = lax.ppermute(falling, 'tm', down)  3.9 us
    ppermute x3, starting transfers between devices, gather_frames(): falling = lax.ppermute(falling, 'tm', down)  3.88 us
    conv_general_dilated x1, matrix products, backward_conv(): lax.conv_general_dilated(window[None], jnp.flip(cube, (0, 1, 2)), (1, 1,...  3.82 us
  transfers between devices with their start and end apart: 11, of which 5 were waited for; matrix products, arithmetic and copies ran while one was open for 15% of the time, Pallas kernels for 0%

profile of v19, /device:TPU:0, one launch (start us, length us, event | category | flops | bytes accessed | tf_op | source)
XLA Modules:
  0.0 119.3 jit_solution(16198858220047459615)
XLA Ops:
  0.6 0.0 copy-start.3
  0.6 1.1 fusion.65
  1.8 1.2 %multiply_convert_fusion = bf16[1,2,160,384]{3,2,1,0:T(8,128)(2,1)S(1)} fusion(f32[384]{0:T(512)} %param.6, f32[2,160]{1,0:T(2,128)S(1)} %add_sqrt_fusion, bf16[1,2,160,384]{3,2,1,0:T(8,128)(2,1)} %param.5), kind=kLoop, calls=%fused_computation.86 | loop fusion | flops 983040 | bytes 494336 | tf_op jit(solution)/shard_map/convert_element_type | solution.py:166
  3.0 1.0 pad_maximum_fusion.5
  4.0 5.0 %collective-permute-start = (bf16[1,2,160,768]{3,2,1,0:T(8,128)(2,1)S(1)}, bf16[1,2,160,768]{3,2,1,0:T(8,128)(2,1)S(1)}, u32[]{:S(2)}, u32[]{:S(2)}) collective-permute-start(bf16[1,2,160,768]{3,2,1,0:T(8,128)(2,1)S(1)} %pad_maximum_fusion.5), channel_id=1, source_target_pairs={{0,4},{4,8},{8,12},{1,5},{5,9},{9,13},{2,6},{6,10},{10,14},{3,7},{... | collective-permute-start | bytes 1474568 | tf_op jit(solution)/shard_map/ppermute | solution.py:153
  9.0 1.3 %collective-permute-start.3 = (bf16[1,2,160,768]{3,2,1,0:T(8,128)(2,1)S(1)}, bf16[1,2,160,768]{3,2,1,0:T(8,128)(2,1)S(1)}, u32[]{:S(2)}, u32[]{:S(2)}) collective-permute-start(bf16[1,2,160,768]{3,2,1,0:T(8,128)(2,1)S(1)} %pad_maximum_fusion.5), channel_id=1, source_target_pairs={{4,0},{8,4},{12,8},{5,1},{9,5},{13,9},{6,2},{10,6},{14,10},{7,3},{... | collective-permute-start | bytes 1474568 | tf_op jit(solution)/shard_map/ppermute | solution.py:154
  10.3 9.1 %collective-permute-done = bf16[1,2,160,768]{3,2,1,0:T(8,128)(2,1)S(1)} collective-permute-done((bf16[1,2,160,768]{3,2,1,0:T(8,128)(2,1)S(1)}, bf16[1,2,160,768]{3,2,1,0:T(8,128)(2,1)S(1)}, u32[]{:S(2)}, u32[]{:S(2)}) %collective-permute-start) | collective-permute-done | bytes 491552 | tf_op jit(solution)/shard_map/ppermute | solution.py:153
  19.4 4.4 %collective-permute-start.1 = (bf16[1,2,160,768]{3,2,1,0:T(8,128)(2,1)S(1)}, bf16[1,2,160,768]{3,2,1,0:T(8,128)(2,1)S(1)}, u32[]{:S(2)}, u32[]{:S(2)}) collective-permute-start(bf16[1,2,160,768]{3,2,1,0:T(8,128)(2,1)S(1)} %collective-permute-done), channel_id=1, source_target_pairs={{0,4},{4,8},{8,12},{1,5},{5,9},{9,13},{2,6},{6,10},{10,14},{3,7},{... | collective-permute-start | bytes 1474568 | tf_op jit(solution)/shard_map/ppermute | solution.py:153
  23.8 1.3 %collective-permute-start.4 = (bf16[1,2,160,768]{3,2,1,0:T(8,128)(2,1)S(1)}, bf16[1,2,160,768]{3,2,1,0:T(8,128)(2,1)S(1)}, u32[]{:S(2)}, u32[]{:S(2)}) collective-permute-start(bf16[1,2,160,768]{3,2,1,0:T(8,128)(2,1)S(1)} %collective-permute-done.3), channel_id=1, source_target_pairs={{4,0},{8,4},{12,8},{5,1},{9,5},{13,9},{6,2},{10,6},{14,10},{7,3},{... | collective-permute-start | bytes 1474568 | tf_op jit(solution)/shard_map/ppermute | solution.py:154
  25.1 8.2 %collective-permute-done.1 = bf16[1,2,160,768]{3,2,1,0:T(8,128)(2,1)S(1)} collective-permute-done((bf16[1,2,160,768]{3,2,1,0:T(8,128)(2,1)S(1)}, bf16[1,2,160,768]{3,2,1,0:T(8,128)(2,1)S(1)}, u32[]{:S(2)}, u32[]{:S(2)}) %collective-permute-start.1) | collective-permute-done | bytes 491552 | tf_op jit(solution)/shard_map/ppermute | solution.py:153
  33.4 4.4 %collective-permute-start.2 = (bf16[1,2,160,768]{3,2,1,0:T(8,128)(2,1)S(1)}, bf16[1,2,160,768]{3,2,1,0:T(8,128)(2,1)S(1)}, u32[]{:S(2)}, u32[]{:S(2)}) collective-permute-start(bf16[1,2,160,768]{3,2,1,0:T(8,128)(2,1)S(1)} %collective-permute-done.1), channel_id=1, source_target_pairs={{0,4},{4,8},{8,12},{1,5},{5,9},{9,13},{2,6},{6,10},{10,14},{3,7},{... | collective-permute-start | bytes 1474568 | tf_op jit(solution)/shard_map/ppermute | solution.py:153
  37.8 1.3 %collective-permute-start.5 = (bf16[1,2,160,768]{3,2,1,0:T(8,128)(2,1)S(1)}, bf16[1,2,160,768]{3,2,1,0:T(8,128)(2,1)S(1)}, u32[]{:S(2)}, u32[]{:S(2)}) collective-permute-start(bf16[1,2,160,768]{3,2,1,0:T(8,128)(2,1)S(1)} %collective-permute-done.4), channel_id=1, source_target_pairs={{4,0},{8,4},{12,8},{5,1},{9,5},{13,9},{6,2},{10,6},{14,10},{7,3},{... | collective-permute-start | bytes 1474568 | tf_op jit(solution)/shard_map/ppermute | solution.py:154
  39.1 7.3 %collective-permute-done.2 = bf16[1,2,160,768]{3,2,1,0:T(8,128)(2,1)S(1)} collective-permute-done((bf16[1,2,160,768]{3,2,1,0:T(8,128)(2,1)S(1)}, bf16[1,2,160,768]{3,2,1,0:T(8,128)(2,1)S(1)}, u32[]{:S(2)}, u32[]{:S(2)}) %collective-permute-start.2) | collective-permute-done | bytes 491552 | tf_op jit(solution)/shard_map/ppermute | solution.py:153
  46.7 3.9 %collective-permute-done.5 = bf16[1,2,160,768]{3,2,1,0:T(8,128)(2,1)S(1)} collective-permute-done((bf16[1,2,160,768]{3,2,1,0:T(8,128)(2,1)S(1)}, bf16[1,2,160,768]{3,2,1,0:T(8,128)(2,1)S(1)}, u32[]{:S(2)}, u32[]{:S(2)}) %collective-permute-start.5) | collective-permute-done | bytes 491552 | tf_op jit(solution)/shard_map/ppermute | solution.py:154
  50.6 0.3 constant_dynamic-slice_fusion.1
  50.9 1.6 %collective-permute-start.6 = (bf16[4,2,160,384]{3,2,1,0:T(8,128)(2,1)S(1)}, bf16[4,2,160,384]{3,2,1,0:T(8,128)(2,1)}, u32[]{:S(2)}, u32[]{:S(2)}) collective-permute-start(bf16[4,2,160,384]{3,2,1,0:T(8,128)(2,1)S(1)} %get-tuple-element.6), channel_id=1, source_target_pairs={{0,2},{1,3},{2,0},{3,1},{4,6},{5,7},{6,4},{7,5},{8,10},{9,11},{10,... | collective-permute-start | bytes 2949128 | tf_op jit(solution)/shard_map/ppermute | solution.py:116
  52.4 1.0 pad_dynamic-slice_fusion.6
  53.4 1.3 %collective-permute-start.9 = (bf16[3,1,160,384]{3,2,1,0:T(8,128)(2,1)}, bf16[3,1,160,384]{3,2,1,0:T(8,128)(2,1)}, u32[]{:S(2)}, u32[]{:S(2)}) collective-permute-start(bf16[3,1,160,384]{3,2,1,0:T(8,128)(2,1)} %get-tuple-element.13), channel_id=1, source_target_pairs={{1,0},{2,1},{3,2},{5,4},{6,5},{7,6},{9,8},{10,9},{11,10},{13,12},{... | collective-permute-start | bytes 1105928 | tf_op jit(solution)/shard_map/ppermute | solution.py:25
  54.7 3.8 %collective-permute-start.8 = (bf16[3,1,160,384]{3,2,1,0:T(8,128)(2,1)}, bf16[3,1,160,384]{3,2,1,0:T(8,128)(2,1)}, u32[]{:S(2)}, u32[]{:S(2)}) collective-permute-start(bf16[3,1,160,384]{3,2,1,0:T(8,128)(2,1)} %get-tuple-element.12), channel_id=1, source_target_pairs={{0,1},{1,2},{2,3},{4,5},{5,6},{6,7},{8,9},{9,10},{10,11},{12,13},{... | collective-permute-start | bytes 1105928 | tf_op jit(solution)/shard_map/ppermute | solution.py:23
  58.5 1.0 reshape.53
  59.5 1.3 %copy.81 = bf16[4,2,160,4,96]{4,2,1,0,3:T(8,128)(2,1)} copy(bf16[4,2,160,4,96]{4,3,2,1,0:T(4,128)(2,1)S(1)} %reshape.53) | data formatting | bytes 1966080 | tf_op jit(solution)/shard_map/reshape | solution.py:185
  60.9 3.5 %all-to-all-start = ((bf16[4,4,2,160,96]{4,3,2,1,0:T(8,128)(2,1)}), bf16[4,4,2,160,96]{4,3,2,1,0:T(8,128)(2,1)S(1)}, u32[]{:S(2)}, u32[]{:S(2)}) async-start(bf16[4,4,2,160,96]{4,3,2,1,0:T(8,128)(2,1)} %bitcast.96), calls=%async_computation | async-start | bytes 2621440 | tf_op jit(solution)/shard_map/all_to_all | solution.py:189
  64.4 0.1 pad_dynamic-slice_fusion.7
  64.6 0.0 slice-start
  64.6 1.7 %fusion.37 = bf16[3,4,1,162,384]{4,3,1,0,2:T(8,128)(2,1)S(1)} fusion(bf16[3,1,160,384]{3,2,1,0:T(8,128)(2,1)} %collective-permute-done.9, bf16[3,2,160,384]{3,2,1,0:T(8,128)(2,1)S(1)} %pad_dynamic-slice_fusion.7, bf16[3,1,160,384]{3,2,1,0:T(8,128)(2,1)} %collective-permute-done.8), kind=kLoop, calls=%fused_computation.54 | loop fusion | flops 9704448 | bytes 2967552 | tf_op jit(solution)/shard_map/broadcast_in_dim | solution.py:58
  66.3 0.6 copy.62
  66.9 0.0 slice-start.1
  66.9 0.6 pad.22.clone
  67.5 0.2 copy.45
  67.7 0.0 copy-start.7
  67.7 7.6 %collective-permute-done.6 = bf16[4,2,160,384]{3,2,1,0:T(8,128)(2,1)} collective-permute-done((bf16[4,2,160,384]{3,2,1,0:T(8,128)(2,1)S(1)}, bf16[4,2,160,384]{3,2,1,0:T(8,128)(2,1)}, u32[]{:S(2)}, u32[]{:S(2)}) %collective-permute-start.6) | collective-permute-done | bytes 983072 | tf_op jit(solution)/shard_map/ppermute | solution.py:116
  75.3 2.7 %pad_maximum_fusion.3 = bf16[4,4,160,384]{3,2,1,0:T(8,128)(2,1)} fusion(bf16[4,2,160,384]{3,2,1,0:T(8,128)(2,1)} %collective-permute-done.6, bf16[4,2,160,384]{3,2,1,0:T(8,128)(2,1)S(1)} %get-tuple-element.6), kind=kLoop, calls=%fused_computation.30 | loop fusion | flops 983040 | bytes 3932160 | tf_op jit(solution)/shard_map/concatenate | solution.py:121
  78.0 10.4 %collective-permute-start.7 = (bf16[4,4,160,384]{3,2,1,0:T(8,128)(2,1)}, bf16[4,4,160,384]{3,2,1,0:T(8,128)(2,1)}, u32[]{:S(2)}, u32[]{:S(2)}) collective-permute-start(bf16[4,4,160,384]{3,2,1,0:T(8,128)(2,1)} %pad_maximum_fusion.3), channel_id=1, source_target_pairs={{0,1},{1,0},{2,3},{3,2},{4,5},{5,4},{6,7},{7,6},{8,9},{9,8},{10,11... | collective-permute-start | bytes 5898248 | tf_op jit(solution)/shard_map/ppermute | solution.py:122
  88.5 0.0 copy-start.2
  88.5 0.0 copy-start.5
  88.5 3.8 %fusion.54 = f32[1,2,8,21,384]{4,2,3,1,0:T(8,128)S(1)} fusion(bf16[3,3,3,384,384]{4,3,2,1,0:T(8,128)(2,1)S(1)} %bitcast.105, bf16[3,4,1,7,2,384]{5,3,4,1,0,2:T(8,128)(2,1)S(1)} %slice.48, bf16[3,4,1,8,21,384]{5,3,4,1,0,2:T(8,128)(2,1)S(1)} %copy.45, pred[8,21]{0,1:T(8,128)(4,1)S(1)} %copy-done.7), kind=kOutput, calls=%fused_computation.65 | convolution fusion | flops 2680657920 | bytes 10156200 | tf_op jit(solution)/shard_map/conv_general_dilated | solution.py:57
  92.3 0.3 copy.46
  92.6 0.2 slice.49
  92.8 0.4 multiply_reduce_fusion
  93.2 0.1 copy.49
  93.3 1.7 %fusion.14 = (bf16[6,10,160,1,96]{4,2,1,3,0:T(8,128)(2,1)S(1)}, bf16[6,10,160,1,96]{4,2,1,3,0:T(8,128)(2,1)S(1)}, bf16[6,10,160,1,96]{4,2,1,3,0:T(8,128)(2,1)S(1)}) fusion(bf16[4,8,160,96]{3,2,1,0:T(8,128)(2,1)S(1)} %bitcast.97), kind=kLoop, calls=%fused_computation.26 | loop fusion | bytes 6512640 | tf_op jit(solution)/shard_map/stack | solution.py:82
  95.0 2.0 %pad_maximum_fusion = bf16[6,10,160,3,96]{4,2,1,3,0:T(8,128)(2,1)S(1)} fusion(bf16[6,10,160,1,96]{4,2,1,3,0:T(8,128)(2,1)S(1)} %get-tuple-element.11, bf16[6,10,160,1,96]{4,2,1,3,0:T(8,128)(2,1)S(1)} %get-tuple-element.10, bf16[6,10,160,1,96]{4,2,1,3,0:T(8,128)(2,1)S(1)} %get-tuple-element.9), kind=kLoop, calls=%fused_computation.1 | loop fusion | flops 5529600 | bytes 11059200 | tf_op jit(solution)/shard_map/stack | solution.py:82
  97.1 1.7 %fusion.80 = (bf16[4,2,160,384]{3,2,1,0:T(8,128)(2,1)S(1)}, bf16[4,2,160,384]{3,2,1,0:T(8,128)(2,1)S(1)}) fusion(bf16[4,4,160,384]{3,2,1,0:T(8,128)(2,1)} %collective-permute-done.7), kind=kLoop, calls=%fused_computation.108 | loop fusion | bytes 3932160 | tf_op jit(solution)/shard_map/slice | solution.py:127
  98.8 0.3 fusion.17
  99.1 1.8 %fusion.18 = bf16[4,4,160,384]{3,2,1,0:T(8,128)(2,1)S(1)} fusion(bf16[4,2,160,384]{3,2,1,0:T(8,128)(2,1)} %collective-permute-done.6, bf16[4,2,160,384]{3,2,1,0:T(8,128)(2,1)S(1)} %get-tuple-element.8, pred[]{:T(512)S(6)} %eq.10), kind=kLoop, calls=%fused_computation.33 | loop fusion | flops 2949120 | bytes 3932161 | tf_op jit(solution)/shard_map/jit(_where)/select_n | solution.py:129
  101.0 1.6 %fusion.20 = (bf16[4,4,160,384]{3,2,1,0:T(8,128)(2,1)S(1)}, bf16[4,4,160,384]{3,2,1,0:T(8,128)(2,1)S(1)}) fusion(s32[]{:T(128)S(6)} %select_n.99, bf16[4,4,160,384]{3,2,1,0:T(8,128)(2,1)S(1)} %fusion.18, bf16[4,4,160,384]{3,2,1,0:T(8,128)(2,1)S(1)} %fusion.17, s32[]{:T(128)S(6)} %select_n.101), kind=kLoop, calls=%fused_computation.35 | loop fusion | flops 1966080 | bytes 7864328 | tf_op jit(solution)/shard_map/concatenate | solution.py:135
  102.6 0.4 pad_maximum_fusion.1
  103.0 0.0 slice-start.2
  103.1 0.5 fusion.35
  103.6 0.0 slice-start.3
  103.6 0.6 copy.61
  104.2 0.6 pad.20.clone
  104.7 0.2 copy.40
  105.0 0.2 slice-done.2
  105.2 1.3 %slice-done.3 = s8[3768320]{0:T(1024)(128)(4,1)S(1)} async-done(((s8[7962624]{0:T(1024)(128)(4,1)}), s8[3768320]{0:T(1024)(128)(4,1)S(1)}, s32[]{:S(2)}) %slice-start.3) | async-done | bytes 3768344
  106.5 3.8 %fusion.57 = f32[1,2,8,21,384]{4,2,3,1,0:T(8,128)S(1)} fusion(bf16[3,3,3,384,384]{4,3,2,1,0:T(8,128)(2,1)S(1)} %bitcast.108, bf16[3,4,1,7,2,384]{5,3,4,1,0,2:T(8,128)(2,1)S(1)} %slice.46, bf16[3,4,1,8,21,384]{5,3,4,1,0,2:T(8,128)(2,1)S(1)} %copy.40, pred[8,21]{0,1:T(8,128)(4,1)S(1)} %copy-done.7), kind=kOutput, calls=%fused_computation.66 | convolution fusion | flops 2680657920 | bytes 10156200 | tf_op jit(solution)/shard_map/conv_general_dilated | solution.py:44
  110.3 0.3 copy.41
  110.6 0.2 slice.47
  110.8 1.7 %fusion.39 = f32[3,12,8,384]{3,2,1,0:T(8,128)S(1)} fusion(bf16[6,10,160,3,96]{4,2,1,3,0:T(8,128)(2,1)S(1)} %pad_maximum_fusion, s32[]{:T(128)S(6)} %select_n.106, s32[]{:T(128)S(6)} %select_n.108, bf16[4,4,160,384]{3,2,1,0:T(8,128)(2,1)S(1)} %get-tuple-element.4, bf16[4,4,160,384]{3,2,1,0:T(8,128)(2,1)S(1)} %get-tuple-element.3), kind=kOutput, calls=%fused_computation.62 | convolution fusion | flops 1134428160 | bytes 8306696 | tf_op jit(solution)/shard_map/dot_general | solution.py:98
  112.6 1.8 %fusion.44 = f32[3,12,8,384]{3,2,1,0:T(8,128)S(1)} fusion(bf16[6,10,160,3,96]{4,2,1,3,0:T(8,128)(2,1)S(1)} %pad_maximum_fusion, s32[]{:T(128)S(6)} %select_n.110, s32[]{:T(128)S(6)} %select_n.112, bf16[4,4,160,384]{3,2,1,0:T(8,128)(2,1)S(1)} %get-tuple-element.4, bf16[4,4,160,384]{3,2,1,0:T(8,128)(2,1)S(1)} %get-tuple-element.3), kind=kOutput, calls=%fused_computation.63 | convolution fusion | flops 1134428160 | bytes 8306696 | tf_op jit(solution)/shard_map/dot_general | solution.py:98
  114.4 0.0 copy-start.4
  114.4 2.0 %fusion.49 = f32[3,12,8,384]{3,2,1,0:T(8,128)S(1)} fusion(bf16[6,10,160,3,96]{4,2,1,3,0:T(8,128)(2,1)S(1)} %pad_maximum_fusion, s32[]{:T(128)S(6)} %select_n.114, s32[]{:T(128)S(6)} %select_n.116, bf16[4,4,160,384]{3,2,1,0:T(8,128)(2,1)S(1)} %get-tuple-element.4, bf16[4,4,160,384]{3,2,1,0:T(8,128)(2,1)S(1)} %get-tuple-element.3), kind=kOutput, calls=%fused_computation.64 | convolution fusion | flops 1134428160 | bytes 8306696 | tf_op jit(solution)/shard_map/dot_general | solution.py:98
  116.4 1.2 add_convert_fusion
  117.6 1.6 %fusion.62 = f32[2592,96]{0,1:T(8,128)} fusion(s32[]{:T(128)S(6)} %select_n.117, f32[1152,96]{0,1:T(8,128)S(1)} %bitcast.100, f32[1152,96]{0,1:T(8,128)S(1)} %bitcast.101, f32[1152,96]{0,1:T(8,128)S(1)} %bitcast.102), kind=kLoop, calls=%fused_computation.69 | loop fusion | flops 746496 | bytes 2322436 | tf_op jit(solution)/shard_map/mul | solution.py:205
  (35 shorter events, 0.5 us)
Async XLA Ops:
  0.6 45.9 %copy-start.3 = (bf16[1,2,160,384]{3,2,1,0:T(8,128)(2,1)S(1)}, bf16[1,2,160,384]{3,2,1,0:T(8,128)(2,1)}, u32[]{:S(2)}) copy-start(bf16[1,2,160,384]{3,2,1,0:T(8,128)(2,1)} %param.9) | copy-start | bytes 737284
  4.0 15.4 %collective-permute-start = (bf16[1,2,160,768]{3,2,1,0:T(8,128)(2,1)S(1)}, bf16[1,2,160,768]{3,2,1,0:T(8,128)(2,1)S(1)}, u32[]{:S(2)}, u32[]{:S(2)}) collective-permute-start(bf16[1,2,160,768]{3,2,1,0:T(8,128)(2,1)S(1)} %pad_maximum_fusion.5), channel_id=1, source_target_pairs={{0,4},{4,8},{8,12},{1,5},{5,9},{9,13},{2,6},{6,10},{10,14},{3,7},{... | collective-permute-start | bytes 1474568 | tf_op jit(solution)/shard_map/ppermute | solution.py:153
  9.0 14.8 %collective-permute-start.3 = (bf16[1,2,160,768]{3,2,1,0:T(8,128)(2,1)S(1)}, bf16[1,2,160,768]{3,2,1,0:T(8,128)(2,1)S(1)}, u32[]{:S(2)}, u32[]{:S(2)}) collective-permute-start(bf16[1,2,160,768]{3,2,1,0:T(8,128)(2,1)S(1)} %pad_maximum_fusion.5), channel_id=1, source_target_pairs={{4,0},{8,4},{12,8},{5,1},{9,5},{13,9},{6,2},{10,6},{14,10},{7,3},{... | collective-permute-start | bytes 1474568 | tf_op jit(solution)/shard_map/ppermute | solution.py:154
  19.4 14.0 %collective-permute-start.1 = (bf16[1,2,160,768]{3,2,1,0:T(8,128)(2,1)S(1)}, bf16[1,2,160,768]{3,2,1,0:T(8,128)(2,1)S(1)}, u32[]{:S(2)}, u32[]{:S(2)}) collective-permute-start(bf16[1,2,160,768]{3,2,1,0:T(8,128)(2,1)S(1)} %collective-permute-done), channel_id=1, source_target_pairs={{0,4},{4,8},{8,12},{1,5},{5,9},{9,13},{2,6},{6,10},{10,14},{3,7},{... | collective-permute-start | bytes 1474568 | tf_op jit(solution)/shard_map/ppermute | solution.py:153
  23.8 14.0 %collective-permute-start.4 = (bf16[1,2,160,768]{3,2,1,0:T(8,128)(2,1)S(1)}, bf16[1,2,160,768]{3,2,1,0:T(8,128)(2,1)S(1)}, u32[]{:S(2)}, u32[]{:S(2)}) collective-permute-start(bf16[1,2,160,768]{3,2,1,0:T(8,128)(2,1)S(1)} %collective-permute-done.3), channel_id=1, source_target_pairs={{4,0},{8,4},{12,8},{5,1},{9,5},{13,9},{6,2},{10,6},{14,10},{7,3},{... | collective-permute-start | bytes 1474568 | tf_op jit(solution)/shard_map/ppermute | solution.py:154
  33.4 13.1 %collective-permute-start.2 = (bf16[1,2,160,768]{3,2,1,0:T(8,128)(2,1)S(1)}, bf16[1,2,160,768]{3,2,1,0:T(8,128)(2,1)S(1)}, u32[]{:S(2)}, u32[]{:S(2)}) collective-permute-start(bf16[1,2,160,768]{3,2,1,0:T(8,128)(2,1)S(1)} %collective-permute-done.1), channel_id=1, source_target_pairs={{0,4},{4,8},{8,12},{1,5},{5,9},{9,13},{2,6},{6,10},{10,14},{3,7},{... | collective-permute-start | bytes 1474568 | tf_op jit(solution)/shard_map/ppermute | solution.py:153
  37.8 12.8 %collective-permute-start.5 = (bf16[1,2,160,768]{3,2,1,0:T(8,128)(2,1)S(1)}, bf16[1,2,160,768]{3,2,1,0:T(8,128)(2,1)S(1)}, u32[]{:S(2)}, u32[]{:S(2)}) collective-permute-start(bf16[1,2,160,768]{3,2,1,0:T(8,128)(2,1)S(1)} %collective-permute-done.4), channel_id=1, source_target_pairs={{4,0},{8,4},{12,8},{5,1},{9,5},{13,9},{6,2},{10,6},{14,10},{7,3},{... | collective-permute-start | bytes 1474568 | tf_op jit(solution)/shard_map/ppermute | solution.py:154
  50.9 24.4 %collective-permute-start.6 = (bf16[4,2,160,384]{3,2,1,0:T(8,128)(2,1)S(1)}, bf16[4,2,160,384]{3,2,1,0:T(8,128)(2,1)}, u32[]{:S(2)}, u32[]{:S(2)}) collective-permute-start(bf16[4,2,160,384]{3,2,1,0:T(8,128)(2,1)S(1)} %get-tuple-element.6), channel_id=1, source_target_pairs={{0,2},{1,3},{2,0},{3,1},{4,6},{5,7},{6,4},{7,5},{8,10},{9,11},{10,... | collective-permute-start | bytes 2949128 | tf_op jit(solution)/shard_map/ppermute | solution.py:116
  53.4 11.1 %collective-permute-start.9 = (bf16[3,1,160,384]{3,2,1,0:T(8,128)(2,1)}, bf16[3,1,160,384]{3,2,1,0:T(8,128)(2,1)}, u32[]{:S(2)}, u32[]{:S(2)}) collective-permute-start(bf16[3,1,160,384]{3,2,1,0:T(8,128)(2,1)} %get-tuple-element.13), channel_id=1, source_target_pairs={{1,0},{2,1},{3,2},{5,4},{6,5},{7,6},{9,8},{10,9},{11,10},{13,12},{... | collective-permute-start | bytes 1105928 | tf_op jit(solution)/shard_map/ppermute | solution.py:25
  54.7 9.9 %collective-permute-start.8 = (bf16[3,1,160,384]{3,2,1,0:T(8,128)(2,1)}, bf16[3,1,160,384]{3,2,1,0:T(8,128)(2,1)}, u32[]{:S(2)}, u32[]{:S(2)}) collective-permute-start(bf16[3,1,160,384]{3,2,1,0:T(8,128)(2,1)} %get-tuple-element.12), channel_id=1, source_target_pairs={{0,1},{1,2},{2,3},{4,5},{5,6},{6,7},{8,9},{9,10},{10,11},{12,13},{... | collective-permute-start | bytes 1105928 | tf_op jit(solution)/shard_map/ppermute | solution.py:23
  60.9 32.4 %all-to-all-start = ((bf16[4,4,2,160,96]{4,3,2,1,0:T(8,128)(2,1)}), bf16[4,4,2,160,96]{4,3,2,1,0:T(8,128)(2,1)S(1)}, u32[]{:S(2)}, u32[]{:S(2)}) async-start(bf16[4,4,2,160,96]{4,3,2,1,0:T(8,128)(2,1)} %bitcast.96), calls=%async_computation | async-start | bytes 2621440 | tf_op jit(solution)/shard_map/all_to_all | solution.py:189
  64.6 23.9 %slice-start = ((s8[7962624]{0:T(1024)(128)(4,1)}), s8[4194304]{0:T(1024)(128)(4,1)S(1)}, s32[]{:S(2)}) async-start(s8[7962624]{0:T(1024)(128)(4,1)} %bitcast.103), calls=%async_computation.1 | async-start | bytes 8388608
  66.9 21.6 %slice-start.1 = ((s8[7962624]{0:T(1024)(128)(4,1)}), s8[3768320]{0:T(1024)(128)(4,1)S(1)}, s32[]{:S(2)}) async-start(s8[7962624]{0:T(1024)(128)(4,1)} %bitcast.103), calls=%async_computation.2 | async-start | bytes 7536640
  67.7 20.8 %copy-start.7 = (pred[8,21]{0,1:T(8,128)(4,1)S(1)}, pred[8,21]{0,1:T(8,128)(4,1)}, u32[]{:S(2)}) copy-start(pred[8,21]{0,1:T(8,128)(4,1)} %constant.126) | copy-start | bytes 508
  78.0 19.0 %collective-permute-start.7 = (bf16[4,4,160,384]{3,2,1,0:T(8,128)(2,1)}, bf16[4,4,160,384]{3,2,1,0:T(8,128)(2,1)}, u32[]{:S(2)}, u32[]{:S(2)}) collective-permute-start(bf16[4,4,160,384]{3,2,1,0:T(8,128)(2,1)} %pad_maximum_fusion.3), channel_id=1, source_target_pairs={{0,1},{1,0},{2,3},{3,2},{4,5},{5,4},{6,7},{7,6},{8,9},{9,8},{10,11... | collective-permute-start | bytes 5898248 | tf_op jit(solution)/shard_map/ppermute | solution.py:122
  88.5 4.3 %copy-start.2 = (bf16[1,2,160,384]{3,2,1,0:T(8,128)(2,1)S(1)}, bf16[1,2,160,384]{3,2,1,0:T(8,128)(2,1)}, u32[]{:S(2)}) copy-start(bf16[1,2,160,384]{3,2,1,0:T(8,128)(2,1)} %param.5) | copy-start | bytes 737284
  88.5 4.3 %copy-start.5 = (f32[384]{0:T(512)S(1)}, f32[384]{0:T(512)}, u32[]{:S(2)}) copy-start(f32[384]{0:T(512)} %param.6) | copy-start | bytes 4612
  92.8 2.2 %copy-start = (f32[1,2,1,160,384]{4,1,3,2,0:T(2,128)}, f32[1,2,1,160,384]{4,1,3,2,0:T(2,128)S(1)}, u32[]{:S(2)}) copy-start(f32[1,2,1,160,384]{4,1,3,2,0:T(2,128)S(1)} %slice.49) | copy-start | bytes 1474564
  103.0 2.2 %slice-start.2 = ((s8[7962624]{0:T(1024)(128)(4,1)}), s8[4194304]{0:T(1024)(128)(4,1)S(1)}, s32[]{:S(2)}) async-start(s8[7962624]{0:T(1024)(128)(4,1)} %bitcast.106), calls=%async_computation.3 | async-start | bytes 8388608
  103.6 3.0 %slice-start.3 = ((s8[7962624]{0:T(1024)(128)(4,1)}), s8[3768320]{0:T(1024)(128)(4,1)S(1)}, s32[]{:S(2)}) async-start(s8[7962624]{0:T(1024)(128)(4,1)} %bitcast.106), calls=%async_computation.4 | async-start | bytes 7536640
  114.4 2.0 %copy-start.1 = (f32[1,2,1,160,384]{4,1,3,2,0:T(2,128)S(1)}, f32[1,2,1,160,384]{4,1,3,2,0:T(2,128)}, u32[]{:S(2)}) copy-start(f32[1,2,1,160,384]{4,1,3,2,0:T(2,128)} %copy-done) | copy-start | bytes 1474564
  114.4 2.0 %copy-start.4 = (bf16[1,2,160,384]{3,2,1,0:T(8,128)(2,1)S(1)}, bf16[1,2,160,384]{3,2,1,0:T(8,128)(2,1)}, u32[]{:S(2)}) copy-start(bf16[1,2,160,384]{3,2,1,0:T(8,128)(2,1)} %param.9) | copy-start | bytes 737284
  114.4 2.0 %copy-start.6 = (f32[384]{0:T(512)S(1)}, f32[384]{0:T(512)}, u32[]{:S(2)}) copy-start(f32[384]{0:T(512)} %param.7) | copy-start | bytes 4612

commit v20 on v19

--- a/solution.py
+++ b/solution.py
@@ -120,26 +120,14 @@
     ]
     stacked = jnp.concatenate(mine, axis=1)
     twins = lax.ppermute(stacked, "height", sibling)
-    block = 2 * row_count
-    relative = []
-    for step in reversed(range(chips)):
-        ours = stacked[:, step * row_count : (step + 1) * row_count]
-        theirs = twins[:, step * row_count : (step + 1) * row_count]
-        relative.append(
-            jnp.where(
-                first,
-                jnp.concatenate([ours, theirs], axis=1),
-                jnp.concatenate([theirs, ours], axis=1),
-            )
-        )
-    relative = jnp.concatenate(relative, axis=1)
-    return jnp.concatenate(
-        [
-            lax.dynamic_slice_in_dim(relative, ((place - chip - 1) % chips) * block, block, 1)
-            for place in range(chips)
-        ],
-        axis=1,
-    )
+    lower = jnp.where(first, stacked, twins)
+    upper = jnp.where(first, twins, stacked)
+    blocks = []
+    for place in range(chips):
+        step = (chip - place) % chips
+        for half in (lower, upper):
+            blocks.append(lax.dynamic_slice_in_dim(half, step * row_count, row_count, 1))
+    return jnp.concatenate(blocks, axis=1)
 
 
 def gather_frames(block):

time: 120 us -> 117 us (0.975)
  local copies, waits for them, and re-layouts: 13.2 us -> 11.9 us
    slice x1 -> x0, local copies, waits for them, and re-layouts: 1.7 us -> none  [gather_rows(): theirs = twins[:, step * row_count:(step + 1) * row_count]]
    unnamed x31 -> x29, local copies, waits for them, and re-layouts: 2.93 us -> 2.92 us
where the time goes in v20:
time: 117 us
  starting transfers between devices  38.4 us (33%)
  waiting for transfers between devices  36 us (31%)
  other arithmetic  16.1 us (14%)
  matrix products  12.9 us (11%)
  local copies, waits for them, and re-layouts  11.9 us (10%)
  between operations  1.19 us (1%)
    ppermute x3, waiting for transfers between devices, gather_frames(): rising = lax.ppermute(rising, 'tm', up)  24.7 us
    ppermute x3, starting transfers between devices, gather_frames(): rising = lax.ppermute(rising, 'tm', up)  13.8 us
    ppermute x1, starting transfers between devices, gather_rows(): twins = lax.ppermute(stacked, 'height', sibling)  10.4 us
    ppermute x1, waiting for transfers between devices, gather_rows(): lax.ppermute(own, 'height', [(i, (i + 2 * step) % height_count) for i in...  7.42 us
    dot_general x3, matrix products, block_weight_grad(): lax.dot_general(window, hidden_all, (((0, 1, 2), (0, 1, 2)), ((), ())), p...  5.21 us
    ppermute x3, waiting for transfers between devices, gather_frames(): falling = lax.ppermute(falling, 'tm', down)  3.9 us
    ppermute x3, starting transfers between devices, gather_frames(): falling = lax.ppermute(falling, 'tm', down)  3.88 us
    conv_general_dilated x1, matrix products, forward_conv(): lax.conv_general_dilated(window[None], cube, (1, 1, 1), 'VALID', dimensio...  3.84 us
  transfers between devices with their start and end apart: 11, of which 5 were waited for; matrix products, arithmetic and copies ran while one was open for 15% of the time, Pallas kernels for 0%

profile of v20, /device:TPU:0, one launch (start us, length us, event | category | flops | bytes accessed | tf_op | source)
XLA Modules:
  0.0 116.6 jit_solution(14252145431993162671)
XLA Ops:
  0.6 0.0 copy-start.3
  0.6 1.1 fusion.61
  1.8 1.2 %multiply_convert_fusion = bf16[1,2,160,384]{3,2,1,0:T(8,128)(2,1)S(1)} fusion(f32[384]{0:T(512)} %param.6, f32[2,160]{1,0:T(2,128)S(1)} %add_sqrt_fusion, bf16[1,2,160,384]{3,2,1,0:T(8,128)(2,1)} %param.5), kind=kLoop, calls=%fused_computation.78 | loop fusion | flops 983040 | bytes 494336 | tf_op jit(solution)/shard_map/convert_element_type | solution.py:154
  3.0 1.0 pad_maximum_fusion.3
  4.0 5.0 %collective-permute-start = (bf16[1,2,160,768]{3,2,1,0:T(8,128)(2,1)S(1)}, bf16[1,2,160,768]{3,2,1,0:T(8,128)(2,1)S(1)}, u32[]{:S(2)}, u32[]{:S(2)}) collective-permute-start(bf16[1,2,160,768]{3,2,1,0:T(8,128)(2,1)S(1)} %pad_maximum_fusion.3), channel_id=1, source_target_pairs={{0,4},{4,8},{8,12},{1,5},{5,9},{9,13},{2,6},{6,10},{10,14},{3,7},{... | collective-permute-start | bytes 1474568 | tf_op jit(solution)/shard_map/ppermute | solution.py:141
  9.0 1.3 %collective-permute-start.3 = (bf16[1,2,160,768]{3,2,1,0:T(8,128)(2,1)S(1)}, bf16[1,2,160,768]{3,2,1,0:T(8,128)(2,1)S(1)}, u32[]{:S(2)}, u32[]{:S(2)}) collective-permute-start(bf16[1,2,160,768]{3,2,1,0:T(8,128)(2,1)S(1)} %pad_maximum_fusion.3), channel_id=1, source_target_pairs={{4,0},{8,4},{12,8},{5,1},{9,5},{13,9},{6,2},{10,6},{14,10},{7,3},{... | collective-permute-start | bytes 1474568 | tf_op jit(solution)/shard_map/ppermute | solution.py:142
  10.3 9.1 %collective-permute-done = bf16[1,2,160,768]{3,2,1,0:T(8,128)(2,1)S(1)} collective-permute-done((bf16[1,2,160,768]{3,2,1,0:T(8,128)(2,1)S(1)}, bf16[1,2,160,768]{3,2,1,0:T(8,128)(2,1)S(1)}, u32[]{:S(2)}, u32[]{:S(2)}) %collective-permute-start) | collective-permute-done | bytes 491552 | tf_op jit(solution)/shard_map/ppermute | solution.py:141
  19.4 4.4 %collective-permute-start.1 = (bf16[1,2,160,768]{3,2,1,0:T(8,128)(2,1)S(1)}, bf16[1,2,160,768]{3,2,1,0:T(8,128)(2,1)S(1)}, u32[]{:S(2)}, u32[]{:S(2)}) collective-permute-start(bf16[1,2,160,768]{3,2,1,0:T(8,128)(2,1)S(1)} %collective-permute-done), channel_id=1, source_target_pairs={{0,4},{4,8},{8,12},{1,5},{5,9},{9,13},{2,6},{6,10},{10,14},{3,7},{... | collective-permute-start | bytes 1474568 | tf_op jit(solution)/shard_map/ppermute | solution.py:141
  23.8 1.3 %collective-permute-start.4 = (bf16[1,2,160,768]{3,2,1,0:T(8,128)(2,1)S(1)}, bf16[1,2,160,768]{3,2,1,0:T(8,128)(2,1)S(1)}, u32[]{:S(2)}, u32[]{:S(2)}) collective-permute-start(bf16[1,2,160,768]{3,2,1,0:T(8,128)(2,1)S(1)} %collective-permute-done.3), channel_id=1, source_target_pairs={{4,0},{8,4},{12,8},{5,1},{9,5},{13,9},{6,2},{10,6},{14,10},{7,3},{... | collective-permute-start | bytes 1474568 | tf_op jit(solution)/shard_map/ppermute | solution.py:142
  25.1 8.2 %collective-permute-done.1 = bf16[1,2,160,768]{3,2,1,0:T(8,128)(2,1)S(1)} collective-permute-done((bf16[1,2,160,768]{3,2,1,0:T(8,128)(2,1)S(1)}, bf16[1,2,160,768]{3,2,1,0:T(8,128)(2,1)S(1)}, u32[]{:S(2)}, u32[]{:S(2)}) %collective-permute-start.1) | collective-permute-done | bytes 491552 | tf_op jit(solution)/shard_map/ppermute | solution.py:141
  33.4 4.4 %collective-permute-start.2 = (bf16[1,2,160,768]{3,2,1,0:T(8,128)(2,1)S(1)}, bf16[1,2,160,768]{3,2,1,0:T(8,128)(2,1)S(1)}, u32[]{:S(2)}, u32[]{:S(2)}) collective-permute-start(bf16[1,2,160,768]{3,2,1,0:T(8,128)(2,1)S(1)} %collective-permute-done.1), channel_id=1, source_target_pairs={{0,4},{4,8},{8,12},{1,5},{5,9},{9,13},{2,6},{6,10},{10,14},{3,7},{... | collective-permute-start | bytes 1474568 | tf_op jit(solution)/shard_map/ppermute | solution.py:141
  37.8 1.3 %collective-permute-start.5 = (bf16[1,2,160,768]{3,2,1,0:T(8,128)(2,1)S(1)}, bf16[1,2,160,768]{3,2,1,0:T(8,128)(2,1)S(1)}, u32[]{:S(2)}, u32[]{:S(2)}) collective-permute-start(bf16[1,2,160,768]{3,2,1,0:T(8,128)(2,1)S(1)} %collective-permute-done.4), channel_id=1, source_target_pairs={{4,0},{8,4},{12,8},{5,1},{9,5},{13,9},{6,2},{10,6},{14,10},{7,3},{... | collective-permute-start | bytes 1474568 | tf_op jit(solution)/shard_map/ppermute | solution.py:142
  39.1 7.3 %collective-permute-done.2 = bf16[1,2,160,768]{3,2,1,0:T(8,128)(2,1)S(1)} collective-permute-done((bf16[1,2,160,768]{3,2,1,0:T(8,128)(2,1)S(1)}, bf16[1,2,160,768]{3,2,1,0:T(8,128)(2,1)S(1)}, u32[]{:S(2)}, u32[]{:S(2)}) %collective-permute-start.2) | collective-permute-done | bytes 491552 | tf_op jit(solution)/shard_map/ppermute | solution.py:141
  46.7 3.9 %collective-permute-done.5 = bf16[1,2,160,768]{3,2,1,0:T(8,128)(2,1)S(1)} collective-permute-done((bf16[1,2,160,768]{3,2,1,0:T(8,128)(2,1)S(1)}, bf16[1,2,160,768]{3,2,1,0:T(8,128)(2,1)S(1)}, u32[]{:S(2)}, u32[]{:S(2)}) %collective-permute-start.5) | collective-permute-done | bytes 491552 | tf_op jit(solution)/shard_map/ppermute | solution.py:142
  50.6 0.3 constant_dynamic-slice_fusion.5
  50.9 1.6 %collective-permute-start.6 = (bf16[4,2,160,384]{3,2,1,0:T(8,128)(2,1)S(1)}, bf16[4,2,160,384]{3,2,1,0:T(8,128)(2,1)}, u32[]{:S(2)}, u32[]{:S(2)}) collective-permute-start(bf16[4,2,160,384]{3,2,1,0:T(8,128)(2,1)S(1)} %get-tuple-element.6), channel_id=1, source_target_pairs={{0,2},{1,3},{2,0},{3,1},{4,6},{5,7},{6,4},{7,5},{8,10},{9,11},{10,... | collective-permute-start | bytes 2949128 | tf_op jit(solution)/shard_map/ppermute | solution.py:116
  52.4 1.0 pad_dynamic-slice_fusion.2
  53.4 1.3 %collective-permute-start.9 = (bf16[3,1,160,384]{3,2,1,0:T(8,128)(2,1)}, bf16[3,1,160,384]{3,2,1,0:T(8,128)(2,1)}, u32[]{:S(2)}, u32[]{:S(2)}) collective-permute-start(bf16[3,1,160,384]{3,2,1,0:T(8,128)(2,1)} %get-tuple-element.15), channel_id=1, source_target_pairs={{1,0},{2,1},{3,2},{5,4},{6,5},{7,6},{9,8},{10,9},{11,10},{13,12},{... | collective-permute-start | bytes 1105928 | tf_op jit(solution)/shard_map/ppermute | solution.py:25
  54.7 3.8 %collective-permute-start.8 = (bf16[3,1,160,384]{3,2,1,0:T(8,128)(2,1)}, bf16[3,1,160,384]{3,2,1,0:T(8,128)(2,1)}, u32[]{:S(2)}, u32[]{:S(2)}) collective-permute-start(bf16[3,1,160,384]{3,2,1,0:T(8,128)(2,1)} %get-tuple-element.14), channel_id=1, source_target_pairs={{0,1},{1,2},{2,3},{4,5},{5,6},{6,7},{8,9},{9,10},{10,11},{12,13},{... | collective-permute-start | bytes 1105928 | tf_op jit(solution)/shard_map/ppermute | solution.py:23
  58.5 1.0 reshape.53
  59.5 1.3 %copy.81 = bf16[4,2,160,4,96]{4,2,1,0,3:T(8,128)(2,1)} copy(bf16[4,2,160,4,96]{4,3,2,1,0:T(4,128)(2,1)S(1)} %reshape.53) | data formatting | bytes 1966080 | tf_op jit(solution)/shard_map/reshape | solution.py:173
  60.9 3.7 %all-to-all-start = ((bf16[4,4,2,160,96]{4,3,2,1,0:T(8,128)(2,1)}), bf16[4,4,2,160,96]{4,3,2,1,0:T(8,128)(2,1)S(1)}, u32[]{:S(2)}, u32[]{:S(2)}) async-start(bf16[4,4,2,160,96]{4,3,2,1,0:T(8,128)(2,1)} %bitcast.96), calls=%async_computation | async-start | bytes 2621440 | tf_op jit(solution)/shard_map/all_to_all | solution.py:177
  64.6 0.1 pad_dynamic-slice_fusion.3
  64.7 0.0 slice-start
  64.7 1.7 %fusion.33 = bf16[3,4,1,162,384]{4,3,1,0,2:T(8,128)(2,1)S(1)} fusion(bf16[3,1,160,384]{3,2,1,0:T(8,128)(2,1)} %collective-permute-done.9, bf16[3,2,160,384]{3,2,1,0:T(8,128)(2,1)S(1)} %pad_dynamic-slice_fusion.3, bf16[3,1,160,384]{3,2,1,0:T(8,128)(2,1)} %collective-permute-done.8), kind=kLoop, calls=%fused_computation.46 | loop fusion | flops 9704448 | bytes 2967552 | tf_op jit(solution)/shard_map/broadcast_in_dim | solution.py:58
  66.5 0.6 copy.62
  67.0 0.0 slice-start.1
  67.1 0.6 pad.22.clone
  67.6 0.0 copy-start.6
  67.7 0.2 copy.45
  67.9 7.4 %collective-permute-done.6 = bf16[4,2,160,384]{3,2,1,0:T(8,128)(2,1)} collective-permute-done((bf16[4,2,160,384]{3,2,1,0:T(8,128)(2,1)S(1)}, bf16[4,2,160,384]{3,2,1,0:T(8,128)(2,1)}, u32[]{:S(2)}, u32[]{:S(2)}) %collective-permute-start.6) | collective-permute-done | bytes 983072 | tf_op jit(solution)/shard_map/ppermute | solution.py:116
  75.3 2.7 %pad_maximum_fusion.2 = bf16[4,4,160,384]{3,2,1,0:T(8,128)(2,1)} fusion(bf16[4,2,160,384]{3,2,1,0:T(8,128)(2,1)} %collective-permute-done.6, bf16[4,2,160,384]{3,2,1,0:T(8,128)(2,1)S(1)} %get-tuple-element.6), kind=kLoop, calls=%fused_computation.25 | loop fusion | flops 983040 | bytes 3932160 | tf_op jit(solution)/shard_map/concatenate | solution.py:121
  78.0 10.4 %collective-permute-start.7 = (bf16[4,4,160,384]{3,2,1,0:T(8,128)(2,1)}, bf16[4,4,160,384]{3,2,1,0:T(8,128)(2,1)}, u32[]{:S(2)}, u32[]{:S(2)}) collective-permute-start(bf16[4,4,160,384]{3,2,1,0:T(8,128)(2,1)} %pad_maximum_fusion.2), channel_id=1, source_target_pairs={{0,1},{1,0},{2,3},{3,2},{4,5},{5,4},{6,7},{7,6},{8,9},{9,8},{10,11... | collective-permute-start | bytes 5898248 | tf_op jit(solution)/shard_map/ppermute | solution.py:122
  88.4 0.0 copy-start.2
  88.5 0.0 copy-start.4
  88.5 3.8 %fusion.50 = f32[1,2,8,21,384]{4,2,3,1,0:T(8,128)S(1)} fusion(bf16[3,3,3,384,384]{4,3,2,1,0:T(8,128)(2,1)S(1)} %bitcast.105, bf16[3,4,1,7,2,384]{5,3,4,1,0,2:T(8,128)(2,1)S(1)} %slice.38, bf16[3,4,1,8,21,384]{5,3,4,1,0,2:T(8,128)(2,1)S(1)} %copy.45, pred[8,21]{0,1:T(8,128)(4,1)S(1)} %copy-done.6), kind=kOutput, calls=%fused_computation.57 | convolution fusion | flops 2680657920 | bytes 10156200 | tf_op jit(solution)/shard_map/conv_general_dilated | solution.py:57
  92.3 0.3 copy.46
  92.6 0.2 slice.39
  92.8 0.0 copy-start
  92.8 0.4 multiply_reduce_fusion
  93.2 0.1 copy.49
  93.3 1.6 %fusion.14 = (bf16[6,10,160,1,96]{4,2,1,3,0:T(8,128)(2,1)S(1)}, bf16[6,10,160,1,96]{4,2,1,3,0:T(8,128)(2,1)S(1)}, bf16[6,10,160,1,96]{4,2,1,3,0:T(8,128)(2,1)S(1)}) fusion(bf16[4,8,160,96]{3,2,1,0:T(8,128)(2,1)S(1)} %bitcast.97), kind=kLoop, calls=%fused_computation.22 | loop fusion | bytes 6512640 | tf_op jit(solution)/shard_map/stack | solution.py:82
  95.0 1.9 %pad_maximum_fusion = bf16[6,10,160,3,96]{4,2,1,3,0:T(8,128)(2,1)S(1)} fusion(bf16[6,10,160,1,96]{4,2,1,3,0:T(8,128)(2,1)S(1)} %get-tuple-element.13, bf16[6,10,160,1,96]{4,2,1,3,0:T(8,128)(2,1)S(1)} %get-tuple-element.12, bf16[6,10,160,1,96]{4,2,1,3,0:T(8,128)(2,1)S(1)} %get-tuple-element.11), kind=kLoop, calls=%fused_computation.1 | loop fusion | flops 5529600 | bytes 11059200 | tf_op jit(solution)/shard_map/stack | solution.py:82
  96.9 2.3 %broadcast_select_fusion.1 = (bf16[4,4,160,384]{3,2,1,0:T(8,128)(2,1)S(1)}, bf16[4,4,160,384]{3,2,1,0:T(8,128)(2,1)S(1)}) fusion(bf16[4,4,160,384]{3,2,1,0:T(8,128)(2,1)} %collective-permute-done.7, pred[]{:T(512)S(6)} %eq.10, bf16[4,2,160,384]{3,2,1,0:T(8,128)(2,1)} %collective-permute-done.6, bf16[4,2,160,384]{3,2,1,0:T(8,128)(2,1)S(1)} %get-tuple-element.6), kind=kLoop, calls=%fused_computation.27 | loop fusion | flops 2949120 | bytes 7864321 | tf_op jit(solution)/shard_map/jit(_where)/select_n | solution.py:123
  99.2 0.5 constant_dynamic-slice_fusion.3
  99.7 0.9 pad_maximum_fusion.1
  100.6 0.0 slice-start.2
  100.6 0.5 fusion.31
  101.1 0.0 slice-start.3
  101.1 0.6 copy.61
  101.7 0.6 pad.20.clone
  102.2 0.2 copy.40
  102.5 0.2 slice-done.2
  102.7 1.3 %slice-done.3 = s8[3768320]{0:T(1024)(128)(4,1)S(1)} async-done(((s8[7962624]{0:T(1024)(128)(4,1)}), s8[3768320]{0:T(1024)(128)(4,1)S(1)}, s32[]{:S(2)}) %slice-start.3) | async-done | bytes 3768344
  104.0 3.8 %fusion.53 = f32[1,2,8,21,384]{4,2,3,1,0:T(8,128)S(1)} fusion(bf16[3,3,3,384,384]{4,3,2,1,0:T(8,128)(2,1)S(1)} %bitcast.108, bf16[3,4,1,7,2,384]{5,3,4,1,0,2:T(8,128)(2,1)S(1)} %slice.36, bf16[3,4,1,8,21,384]{5,3,4,1,0,2:T(8,128)(2,1)S(1)} %copy.40, pred[8,21]{0,1:T(8,128)(4,1)S(1)} %copy-done.6), kind=kOutput, calls=%fused_computation.58 | convolution fusion | flops 2680657920 | bytes 10156200 | tf_op jit(solution)/shard_map/conv_general_dilated | solution.py:44
  107.9 0.3 copy.41
  108.1 0.2 slice.37
  108.3 1.7 %fusion.35 = f32[3,12,8,384]{3,2,1,0:T(8,128)S(1)} fusion(bf16[6,10,160,3,96]{4,2,1,3,0:T(8,128)(2,1)S(1)} %pad_maximum_fusion, s32[]{:T(128)S(6)} %select_n.108, s32[]{:T(128)S(6)} %select_n.110, bf16[4,2,160,384]{3,2,1,0:T(8,128)(2,1)S(1)} %get-tuple-element.10, bf16[4,2,160,384]{3,2,1,0:T(8,128)(2,1)S(1)} %get-tuple-element.18, ...), kind=kOutput, calls=%fused_computation.54 | convolution fusion | flops 1138360320 | bytes 8306696 | tf_op jit(solution)/shard_map/dot_general | solution.py:98
  110.1 1.8 %fusion.40 = f32[3,12,8,384]{3,2,1,0:T(8,128)S(1)} fusion(bf16[6,10,160,3,96]{4,2,1,3,0:T(8,128)(2,1)S(1)} %pad_maximum_fusion, s32[]{:T(128)S(6)} %select_n.112, s32[]{:T(128)S(6)} %select_n.114, bf16[4,2,160,384]{3,2,1,0:T(8,128)(2,1)S(1)} %get-tuple-element.10, bf16[4,2,160,384]{3,2,1,0:T(8,128)(2,1)S(1)} %get-tuple-element.18, ...), kind=kOutput, calls=%fused_computation.55 | convolution fusion | flops 1138360320 | bytes 8306696 | tf_op jit(solution)/shard_map/dot_general | solution.py:98
  111.9 0.0 copy-start.1
  111.9 0.0 copy-start.5
  111.9 1.7 %fusion.45 = f32[3,12,8,384]{3,2,1,0:T(8,128)S(1)} fusion(bf16[6,10,160,3,96]{4,2,1,3,0:T(8,128)(2,1)S(1)} %pad_maximum_fusion, s32[]{:T(128)S(6)} %select_n.116, s32[]{:T(128)S(6)} %select_n.118, bf16[4,2,160,384]{3,2,1,0:T(8,128)(2,1)S(1)} %get-tuple-element.10, bf16[4,2,160,384]{3,2,1,0:T(8,128)(2,1)S(1)} %get-tuple-element.18, ...), kind=kOutput, calls=%fused_computation.56 | convolution fusion | flops 1138360320 | bytes 8306696 | tf_op jit(solution)/shard_map/dot_general | solution.py:98
  113.7 1.2 %add_convert_fusion = (bf16[1,2,160,384]{3,2,1,0:T(8,128)(2,1)}, bf16[1,2,160,384]{3,2,1,0:T(8,128)(2,1)}) fusion(bf16[1,2,160,384]{3,2,1,0:T(8,128)(2,1)S(1)} %copy-done.3, f32[2,160]{1,0:T(2,128)S(1)} %broadcast_multiply_fusion, f32[2,160]{1,0:T(2,128)S(1)} %add_sqrt_fusion, f32[384]{0:T(512)S(1)} %copy-done.4, f32[1,2,1,160,384]{4,1,3,2,0:T(2,128)S(1)} %copy-done.1, ...), kind=kLoop, calls=%fused_computation.76 | loop fusion | flops 2580480 | bytes 1971712 | tf_op jit(solution)/shard_map/convert_element_type | solution.py:209
  114.9 1.6 %fusion.58 = f32[2592,96]{0,1:T(8,128)} fusion(s32[]{:T(128)S(6)} %select_n.119, f32[1152,96]{0,1:T(8,128)S(1)} %bitcast.100, f32[1152,96]{0,1:T(8,128)S(1)} %bitcast.101, f32[1152,96]{0,1:T(8,128)S(1)} %bitcast.102), kind=kLoop, calls=%fused_computation.61 | loop fusion | flops 746496 | bytes 2322436 | tf_op jit(solution)/shard_map/mul | solution.py:193
  (31 shorter events, 0.5 us)
Async XLA Ops:
  0.6 45.9 %copy-start.3 = (bf16[1,2,160,384]{3,2,1,0:T(8,128)(2,1)S(1)}, bf16[1,2,160,384]{3,2,1,0:T(8,128)(2,1)}, u32[]{:S(2)}) copy-start(bf16[1,2,160,384]{3,2,1,0:T(8,128)(2,1)} %param.9) | copy-start | bytes 737284
  4.0 15.4 %collective-permute-start = (bf16[1,2,160,768]{3,2,1,0:T(8,128)(2,1)S(1)}, bf16[1,2,160,768]{3,2,1,0:T(8,128)(2,1)S(1)}, u32[]{:S(2)}, u32[]{:S(2)}) collective-permute-start(bf16[1,2,160,768]{3,2,1,0:T(8,128)(2,1)S(1)} %pad_maximum_fusion.3), channel_id=1, source_target_pairs={{0,4},{4,8},{8,12},{1,5},{5,9},{9,13},{2,6},{6,10},{10,14},{3,7},{... | collective-permute-start | bytes 1474568 | tf_op jit(solution)/shard_map/ppermute | solution.py:141
  9.0 14.8 %collective-permute-start.3 = (bf16[1,2,160,768]{3,2,1,0:T(8,128)(2,1)S(1)}, bf16[1,2,160,768]{3,2,1,0:T(8,128)(2,1)S(1)}, u32[]{:S(2)}, u32[]{:S(2)}) collective-permute-start(bf16[1,2,160,768]{3,2,1,0:T(8,128)(2,1)S(1)} %pad_maximum_fusion.3), channel_id=1, source_target_pairs={{4,0},{8,4},{12,8},{5,1},{9,5},{13,9},{6,2},{10,6},{14,10},{7,3},{... | collective-permute-start | bytes 1474568 | tf_op jit(solution)/shard_map/ppermute | solution.py:142
  19.4 14.0 %collective-permute-start.1 = (bf16[1,2,160,768]{3,2,1,0:T(8,128)(2,1)S(1)}, bf16[1,2,160,768]{3,2,1,0:T(8,128)(2,1)S(1)}, u32[]{:S(2)}, u32[]{:S(2)}) collective-permute-start(bf16[1,2,160,768]{3,2,1,0:T(8,128)(2,1)S(1)} %collective-permute-done), channel_id=1, source_target_pairs={{0,4},{4,8},{8,12},{1,5},{5,9},{9,13},{2,6},{6,10},{10,14},{3,7},{... | collective-permute-start | bytes 1474568 | tf_op jit(solution)/shard_map/ppermute | solution.py:141
  23.8 14.0 %collective-permute-start.4 = (bf16[1,2,160,768]{3,2,1,0:T(8,128)(2,1)S(1)}, bf16[1,2,160,768]{3,2,1,0:T(8,128)(2,1)S(1)}, u32[]{:S(2)}, u32[]{:S(2)}) collective-permute-start(bf16[1,2,160,768]{3,2,1,0:T(8,128)(2,1)S(1)} %collective-permute-done.3), channel_id=1, source_target_pairs={{4,0},{8,4},{12,8},{5,1},{9,5},{13,9},{6,2},{10,6},{14,10},{7,3},{... | collective-permute-start | bytes 1474568 | tf_op jit(solution)/shard_map/ppermute | solution.py:142
  33.4 13.1 %collective-permute-start.2 = (bf16[1,2,160,768]{3,2,1,0:T(8,128)(2,1)S(1)}, bf16[1,2,160,768]{3,2,1,0:T(8,128)(2,1)S(1)}, u32[]{:S(2)}, u32[]{:S(2)}) collective-permute-start(bf16[1,2,160,768]{3,2,1,0:T(8,128)(2,1)S(1)} %collective-permute-done.1), channel_id=1, source_target_pairs={{0,4},{4,8},{8,12},{1,5},{5,9},{9,13},{2,6},{6,10},{10,14},{3,7},{... | collective-permute-start | bytes 1474568 | tf_op jit(solution)/shard_map/ppermute | solution.py:141
  37.8 12.8 %collective-permute-start.5 = (bf16[1,2,160,768]{3,2,1,0:T(8,128)(2,1)S(1)}, bf16[1,2,160,768]{3,2,1,0:T(8,128)(2,1)S(1)}, u32[]{:S(2)}, u32[]{:S(2)}) collective-permute-start(bf16[1,2,160,768]{3,2,1,0:T(8,128)(2,1)S(1)} %collective-permute-done.4), channel_id=1, source_target_pairs={{4,0},{8,4},{12,8},{5,1},{9,5},{13,9},{6,2},{10,6},{14,10},{7,3},{... | collective-permute-start | bytes 1474568 | tf_op jit(solution)/shard_map/ppermute | solution.py:142
  50.9 24.4 %collective-permute-start.6 = (bf16[4,2,160,384]{3,2,1,0:T(8,128)(2,1)S(1)}, bf16[4,2,160,384]{3,2,1,0:T(8,128)(2,1)}, u32[]{:S(2)}, u32[]{:S(2)}) collective-permute-start(bf16[4,2,160,384]{3,2,1,0:T(8,128)(2,1)S(1)} %get-tuple-element.6), channel_id=1, source_target_pairs={{0,2},{1,3},{2,0},{3,1},{4,6},{5,7},{6,4},{7,5},{8,10},{9,11},{10,... | collective-permute-start | bytes 2949128 | tf_op jit(solution)/shard_map/ppermute | solution.py:116
  53.4 11.3 %collective-permute-start.9 = (bf16[3,1,160,384]{3,2,1,0:T(8,128)(2,1)}, bf16[3,1,160,384]{3,2,1,0:T(8,128)(2,1)}, u32[]{:S(2)}, u32[]{:S(2)}) collective-permute-start(bf16[3,1,160,384]{3,2,1,0:T(8,128)(2,1)} %get-tuple-element.15), channel_id=1, source_target_pairs={{1,0},{2,1},{3,2},{5,4},{6,5},{7,6},{9,8},{10,9},{11,10},{13,12},{... | collective-permute-start | bytes 1105928 | tf_op jit(solution)/shard_map/ppermute | solution.py:25
  54.7 10.0 %collective-permute-start.8 = (bf16[3,1,160,384]{3,2,1,0:T(8,128)(2,1)}, bf16[3,1,160,384]{3,2,1,0:T(8,128)(2,1)}, u32[]{:S(2)}, u32[]{:S(2)}) collective-permute-start(bf16[3,1,160,384]{3,2,1,0:T(8,128)(2,1)} %get-tuple-element.14), channel_id=1, source_target_pairs={{0,1},{1,2},{2,3},{4,5},{5,6},{6,7},{8,9},{9,10},{10,11},{12,13},{... | collective-permute-start | bytes 1105928 | tf_op jit(solution)/shard_map/ppermute | solution.py:23
  60.9 32.4 %all-to-all-start = ((bf16[4,4,2,160,96]{4,3,2,1,0:T(8,128)(2,1)}), bf16[4,4,2,160,96]{4,3,2,1,0:T(8,128)(2,1)S(1)}, u32[]{:S(2)}, u32[]{:S(2)}) async-start(bf16[4,4,2,160,96]{4,3,2,1,0:T(8,128)(2,1)} %bitcast.96), calls=%async_computation | async-start | bytes 2621440 | tf_op jit(solution)/shard_map/all_to_all | solution.py:177
  64.7 23.7 %slice-start = ((s8[7962624]{0:T(1024)(128)(4,1)}), s8[4194304]{0:T(1024)(128)(4,1)S(1)}, s32[]{:S(2)}) async-start(s8[7962624]{0:T(1024)(128)(4,1)} %bitcast.103), calls=%async_computation.1 | async-start | bytes 8388608
  67.0 21.4 %slice-start.1 = ((s8[7962624]{0:T(1024)(128)(4,1)}), s8[3768320]{0:T(1024)(128)(4,1)S(1)}, s32[]{:S(2)}) async-start(s8[7962624]{0:T(1024)(128)(4,1)} %bitcast.103), calls=%async_computation.2 | async-start | bytes 7536640
  67.6 20.8 %copy-start.6 = (pred[8,21]{0,1:T(8,128)(4,1)S(1)}, pred[8,21]{0,1:T(8,128)(4,1)}, u32[]{:S(2)}) copy-start(pred[8,21]{0,1:T(8,128)(4,1)} %constant.124) | copy-start | bytes 508
  78.0 18.8 %collective-permute-start.7 = (bf16[4,4,160,384]{3,2,1,0:T(8,128)(2,1)}, bf16[4,4,160,384]{3,2,1,0:T(8,128)(2,1)}, u32[]{:S(2)}, u32[]{:S(2)}) collective-permute-start(bf16[4,4,160,384]{3,2,1,0:T(8,128)(2,1)} %pad_maximum_fusion.2), channel_id=1, source_target_pairs={{0,1},{1,0},{2,3},{3,2},{4,5},{5,4},{6,7},{7,6},{8,9},{9,8},{10,11... | collective-permute-start | bytes 5898248 | tf_op jit(solution)/shard_map/ppermute | solution.py:122
  88.4 4.3 %copy-start.2 = (bf16[1,2,160,384]{3,2,1,0:T(8,128)(2,1)S(1)}, bf16[1,2,160,384]{3,2,1,0:T(8,128)(2,1)}, u32[]{:S(2)}) copy-start(bf16[1,2,160,384]{3,2,1,0:T(8,128)(2,1)} %param.5) | copy-start | bytes 737284
  88.5 4.3 %copy-start.4 = (f32[384]{0:T(512)S(1)}, f32[384]{0:T(512)}, u32[]{:S(2)}) copy-start(f32[384]{0:T(512)} %param.6) | copy-start | bytes 4612
  92.8 2.2 %copy-start = (f32[1,2,1,160,384]{4,1,3,2,0:T(2,128)}, f32[1,2,1,160,384]{4,1,3,2,0:T(2,128)S(1)}, u32[]{:S(2)}) copy-start(f32[1,2,1,160,384]{4,1,3,2,0:T(2,128)S(1)} %slice.39) | copy-start | bytes 1474564
  100.6 2.2 %slice-start.2 = ((s8[7962624]{0:T(1024)(128)(4,1)}), s8[4194304]{0:T(1024)(128)(4,1)S(1)}, s32[]{:S(2)}) async-start(s8[7962624]{0:T(1024)(128)(4,1)} %bitcast.106), calls=%async_computation.3 | async-start | bytes 8388608
  101.1 3.0 %slice-start.3 = ((s8[7962624]{0:T(1024)(128)(4,1)}), s8[3768320]{0:T(1024)(128)(4,1)S(1)}, s32[]{:S(2)}) async-start(s8[7962624]{0:T(1024)(128)(4,1)} %bitcast.106), calls=%async_computation.4 | async-start | bytes 7536640
  111.9 1.8 %copy-start.1 = (f32[1,2,1,160,384]{4,1,3,2,0:T(2,128)S(1)}, f32[1,2,1,160,384]{4,1,3,2,0:T(2,128)}, u32[]{:S(2)}) copy-start(f32[1,2,1,160,384]{4,1,3,2,0:T(2,128)} %copy-done) | copy-start | bytes 1474564
  111.9 1.8 %copy-start.5 = (f32[384]{0:T(512)S(1)}, f32[384]{0:T(512)}, u32[]{:S(2)}) copy-start(f32[384]{0:T(512)} %param.7) | copy-start | bytes 4612

commit v21 on v20

--- a/solution.py
+++ b/solution.py
@@ -166,9 +166,16 @@
     weight_cube = weight.reshape(3, 3, 3, channels, channels)
 
     both_frames = gather_frames(jnp.concatenate([hidden, cotangent], axis=-1))
-    hidden_all = gather_rows(both_frames[..., :channels], height_count)
-
     cot_frames = both_frames[..., channels:]
+    cot_future = lax.dynamic_slice_in_dim(
+        jnp.pad(cot_frames, ((0, 2), (0, 0), (0, 0), (0, 0))), frame_index * frame_count, 3, 0
+    )
+    cotangent_edged = padded(cot_future, (("height", 1),), 1)
+    hidden_rows, cotangent_edged = lax.optimization_barrier(
+        (both_frames[..., :channels], cotangent_edged)
+    )
+    hidden_all = gather_rows(hidden_rows, height_count)
+
     share_width = channels // height_count
     by_share = cot_frames.reshape(
         total_frames, row_count, col_count, height_count, share_width
@@ -193,10 +200,6 @@
         block_weight_grad(hidden_all, cot_all, frame_index, share_rows, channels) * inverse_root
     )
 
-    cot_future = lax.dynamic_slice_in_dim(
-        jnp.pad(cot_frames, ((0, 2), (0, 0), (0, 0), (0, 0))), frame_index * frame_count, 3, 0
-    )
-    cotangent_edged = padded(cot_future, (("height", 1),), 1)
     future_block = jnp.pad(cotangent_edged, ((0, 0), (0, 0), (1, right_pad), (0, 0)))
     hidden_grad = backward_conv(future_block, weight_cube, row_count, col_count).reshape(frame_count, row_count, col_count, channels)
     sigmoid_pre = jax.nn.sigmoid(normed)

time: 117 us -> 124 us (1.060)
  waiting for transfers between devices: 36 us -> 46.3 us
  local copies, waits for them, and re-layouts: 11.9 us -> 18.2 us
  starting transfers between devices: 38.4 us -> 33.1 us
  other arithmetic: 16.1 us -> 12.1 us
    ppermute x1, starting transfers between devices: 10.4 us -> 0.01 us  [gather_rows(): twins = lax.ppermute(stacked, 'height', sibling)]
    all_to_all x1, waiting for transfers between devices: 0.01 us -> 5.64 us  [local(): lax.all_to_all(by_share, 'height', split_axis=0, concat_axis=0, tiled=True)]
    ppermute x1, starting transfers between devices: 1.56 us -> 6.68 us  [gather_rows(): lax.ppermute(own, 'height', [(i, (i + 2 * step) % height_count) for i in...]
    ppermute x1, waiting for transfers between devices: 7.42 us -> 10.9 us  [gather_rows(): lax.ppermute(own, 'height', [(i, (i + 2 * step) % height_count) for i in...]
    concatenate x1, other arithmetic: 2.7 us -> 0.2 us  [padded(): jnp.concatenate([lax.ppermute(tail, axis, [(i, (i + 1) % count) for i in...]
    concatenate x0 -> x1, local copies, waits for them, and re-layouts: none -> 2.27 us  [gather_rows(): stacked = jnp.concatenate(mine, axis=1)]
    reshape x2, local copies, waits for them, and re-layouts: 2.34 us -> 4.49 us  [local(): cot_frames.reshape(total_frames, row_count, col_count, height_count, shar...]
    broadcast_in_dim x1 -> x0, other arithmetic: 1.7 us -> none  [backward_conv(): window[None]]
  transfers between devices with their start and end apart: 11 -> 11, of which waited for: 5 -> 7; matrix products, arithmetic and copies ran while one was open for 15% -> 16% of each run, Pallas kernels for 0% -> 0%
where the time goes in v21:
time: 124 us
  waiting for transfers between devices  46.3 us (37%)
  starting transfers between devices  33.1 us (27%)
  local copies, waits for them, and re-layouts  18.2 us (15%)
  matrix products  12.9 us (10%)
  other arithmetic  12.1 us (10%)
    ppermute x3, waiting for transfers between devices, gather_frames(): rising = lax.ppermute(rising, 'tm', up)  24.7 us
    ppermute x3, starting transfers between devices, gather_frames(): rising = lax.ppermute(rising, 'tm', up)  13.8 us
    ppermute x1, waiting for transfers between devices, gather_rows(): lax.ppermute(own, 'height', [(i, (i + 2 * step) % height_count) for i in...  10.9 us
    ppermute x1, starting transfers between devices, gather_rows(): lax.ppermute(own, 'height', [(i, (i + 2 * step) % height_count) for i in...  6.68 us
    all_to_all x1, waiting for transfers between devices, local(): lax.all_to_all(by_share, 'height', split_axis=0, concat_axis=0, tiled=True)  5.64 us
    dot_general x3, matrix products, block_weight_grad(): lax.dot_general(window, hidden_all, (((0, 1, 2), (0, 1, 2)), ((), ())), p...  5.21 us
    reshape x2, local copies, waits for them, and re-layouts, local(): cot_frames.reshape(total_frames, row_count, col_count, height_count, shar...  4.49 us
    all_to_all x1, starting transfers between devices, local(): lax.all_to_all(by_share, 'height', split_axis=0, concat_axis=0, tiled=True)  4.47 us
  transfers between devices with their start and end apart: 11, of which 7 were waited for; matrix products, arithmetic and copies ran while one was open for 16% of the time, Pallas kernels for 0%

profile of v21, /device:TPU:0, one launch (start us, length us, event | category | flops | bytes accessed | tf_op | source)
XLA Modules:
  0.0 123.8 jit_solution(4630937619434017053)
XLA Ops:
  0.6 0.0 copy-start.1
  0.6 1.1 fusion.55
  1.8 1.2 multiply_convert_fusion
  3.0 1.0 pad_maximum_fusion.3
  4.0 5.0 %collective-permute-start = (bf16[1,2,160,768]{3,2,1,0:T(8,128)(2,1)S(1)}, bf16[1,2,160,768]{3,2,1,0:T(8,128)(2,1)S(1)}, u32[]{:S(2)}, u32[]{:S(2)}) collective-permute-start(bf16[1,2,160,768]{3,2,1,0:T(8,128)(2,1)S(1)} %pad_maximum_fusion.3), channel_id=1, source_target_pairs={{0,4},{4,8},{8,12},{1,5},{5,9},{9,13},{2,6},{6,10},{10,14},{3,7},{... | collective-permute-start | bytes 1474568 | tf_op jit(solution)/shard_map/ppermute | solution.py:141
  9.0 1.3 %collective-permute-start.3 = (bf16[1,2,160,768]{3,2,1,0:T(8,128)(2,1)S(1)}, bf16[1,2,160,768]{3,2,1,0:T(8,128)(2,1)S(1)}, u32[]{:S(2)}, u32[]{:S(2)}) collective-permute-start(bf16[1,2,160,768]{3,2,1,0:T(8,128)(2,1)S(1)} %pad_maximum_fusion.3), channel_id=1, source_target_pairs={{4,0},{8,4},{12,8},{5,1},{9,5},{13,9},{6,2},{10,6},{14,10},{7,3},{... | collective-permute-start | bytes 1474568 | tf_op jit(solution)/shard_map/ppermute | solution.py:142
  10.3 9.1 %collective-permute-done = bf16[1,2,160,768]{3,2,1,0:T(8,128)(2,1)S(1)} collective-permute-done((bf16[1,2,160,768]{3,2,1,0:T(8,128)(2,1)S(1)}, bf16[1,2,160,768]{3,2,1,0:T(8,128)(2,1)S(1)}, u32[]{:S(2)}, u32[]{:S(2)}) %collective-permute-start) | collective-permute-done | bytes 491552 | tf_op jit(solution)/shard_map/ppermute | solution.py:141
  19.4 4.4 %collective-permute-start.1 = (bf16[1,2,160,768]{3,2,1,0:T(8,128)(2,1)S(1)}, bf16[1,2,160,768]{3,2,1,0:T(8,128)(2,1)S(1)}, u32[]{:S(2)}, u32[]{:S(2)}) collective-permute-start(bf16[1,2,160,768]{3,2,1,0:T(8,128)(2,1)S(1)} %collective-permute-done), channel_id=1, source_target_pairs={{0,4},{4,8},{8,12},{1,5},{5,9},{9,13},{2,6},{6,10},{10,14},{3,7},{... | collective-permute-start | bytes 1474568 | tf_op jit(solution)/shard_map/ppermute | solution.py:141
  23.8 1.3 %collective-permute-start.4 = (bf16[1,2,160,768]{3,2,1,0:T(8,128)(2,1)S(1)}, bf16[1,2,160,768]{3,2,1,0:T(8,128)(2,1)S(1)}, u32[]{:S(2)}, u32[]{:S(2)}) collective-permute-start(bf16[1,2,160,768]{3,2,1,0:T(8,128)(2,1)S(1)} %collective-permute-done.3), channel_id=1, source_target_pairs={{4,0},{8,4},{12,8},{5,1},{9,5},{13,9},{6,2},{10,6},{14,10},{7,3},{... | collective-permute-start | bytes 1474568 | tf_op jit(solution)/shard_map/ppermute | solution.py:142
  25.1 8.2 %collective-permute-done.1 = bf16[1,2,160,768]{3,2,1,0:T(8,128)(2,1)S(1)} collective-permute-done((bf16[1,2,160,768]{3,2,1,0:T(8,128)(2,1)S(1)}, bf16[1,2,160,768]{3,2,1,0:T(8,128)(2,1)S(1)}, u32[]{:S(2)}, u32[]{:S(2)}) %collective-permute-start.1) | collective-permute-done | bytes 491552 | tf_op jit(solution)/shard_map/ppermute | solution.py:141
  33.4 4.4 %collective-permute-start.2 = (bf16[1,2,160,768]{3,2,1,0:T(8,128)(2,1)S(1)}, bf16[1,2,160,768]{3,2,1,0:T(8,128)(2,1)S(1)}, u32[]{:S(2)}, u32[]{:S(2)}) collective-permute-start(bf16[1,2,160,768]{3,2,1,0:T(8,128)(2,1)S(1)} %collective-permute-done.1), channel_id=1, source_target_pairs={{0,4},{4,8},{8,12},{1,5},{5,9},{9,13},{2,6},{6,10},{10,14},{3,7},{... | collective-permute-start | bytes 1474568 | tf_op jit(solution)/shard_map/ppermute | solution.py:141
  37.8 1.3 %collective-permute-start.5 = (bf16[1,2,160,768]{3,2,1,0:T(8,128)(2,1)S(1)}, bf16[1,2,160,768]{3,2,1,0:T(8,128)(2,1)S(1)}, u32[]{:S(2)}, u32[]{:S(2)}) collective-permute-start(bf16[1,2,160,768]{3,2,1,0:T(8,128)(2,1)S(1)} %collective-permute-done.4), channel_id=1, source_target_pairs={{4,0},{8,4},{12,8},{5,1},{9,5},{13,9},{6,2},{10,6},{14,10},{7,3},{... | collective-permute-start | bytes 1474568 | tf_op jit(solution)/shard_map/ppermute | solution.py:142
  39.1 7.3 %collective-permute-done.2 = bf16[1,2,160,768]{3,2,1,0:T(8,128)(2,1)S(1)} collective-permute-done((bf16[1,2,160,768]{3,2,1,0:T(8,128)(2,1)S(1)}, bf16[1,2,160,768]{3,2,1,0:T(8,128)(2,1)S(1)}, u32[]{:S(2)}, u32[]{:S(2)}) %collective-permute-start.2) | collective-permute-done | bytes 491552 | tf_op jit(solution)/shard_map/ppermute | solution.py:141
  46.7 3.9 %collective-permute-done.5 = bf16[1,2,160,768]{3,2,1,0:T(8,128)(2,1)S(1)} collective-permute-done((bf16[1,2,160,768]{3,2,1,0:T(8,128)(2,1)S(1)}, bf16[1,2,160,768]{3,2,1,0:T(8,128)(2,1)S(1)}, u32[]{:S(2)}, u32[]{:S(2)}) %collective-permute-start.5) | collective-permute-done | bytes 491552 | tf_op jit(solution)/shard_map/ppermute | solution.py:142
  50.6 0.3 constant_dynamic-slice_fusion.5
  50.9 0.1 pad_dynamic-slice_fusion.2
  51.0 1.3 %collective-permute-start.7 = (bf16[3,1,160,384]{3,2,1,0:T(8,128)(2,1)S(1)}, bf16[3,1,160,384]{3,2,1,0:T(8,128)(2,1)S(1)}, u32[]{:S(2)}, u32[]{:S(2)}) collective-permute-start(bf16[3,1,160,384]{3,2,1,0:T(8,128)(2,1)S(1)} %get-tuple-element.19), channel_id=1, source_target_pairs={{1,0},{2,1},{3,2},{5,4},{6,5},{7,6},{9,8},{10,9},{11,10},{13,12},{... | collective-permute-start | bytes 1105928 | tf_op jit(solution)/shard_map/ppermute | solution.py:25
  52.3 3.1 %collective-permute-start.6 = (bf16[3,1,160,384]{3,2,1,0:T(8,128)(2,1)S(1)}, bf16[3,1,160,384]{3,2,1,0:T(8,128)(2,1)S(1)}, u32[]{:S(2)}, u32[]{:S(2)}) collective-permute-start(bf16[3,1,160,384]{3,2,1,0:T(8,128)(2,1)S(1)} %get-tuple-element.18), channel_id=1, source_target_pairs={{0,1},{1,2},{2,3},{4,5},{5,6},{6,7},{8,9},{9,10},{10,11},{12,13},{... | collective-permute-start | bytes 1105928 | tf_op jit(solution)/shard_map/ppermute | solution.py:23
  55.4 0.1 pad_dynamic-slice_fusion.3
  55.5 1.1 collective-permute-done.6
  56.7 0.2 pad_maximum_fusion.2
  56.9 6.7 %collective-permute-start.8 = (bf16[4,2,160,384]{3,2,1,0:T(8,128)(2,1)S(1)}, bf16[4,2,160,384]{3,2,1,0:T(8,128)(2,1)}, u32[]{:S(2)}, u32[]{:S(2)}) collective-permute-start(bf16[4,2,160,384]{3,2,1,0:T(8,128)(2,1)S(1)} %get-tuple-element.5), channel_id=1, source_target_pairs={{0,2},{1,3},{2,0},{3,1},{4,6},{5,7},{6,4},{7,5},{8,10},{9,11},{10,... | collective-permute-start | bytes 2949128 | tf_op jit(solution)/shard_map/ppermute | solution.py:116
  63.5 1.8 %reshape.53 = bf16[4,2,160,4,96]{4,3,2,1,0:T(4,128)(2,1)} reshape(bf16[4,2,160,384]{3,2,1,0:T(8,128)(2,1)S(1)} %get-tuple-element.9) | data formatting | bytes 1966080 | tf_op jit(solution)/shard_map/reshape | solution.py:180
  65.4 2.6 %copy.81 = bf16[4,2,160,4,96]{4,2,1,0,3:T(8,128)(2,1)} copy(bf16[4,2,160,4,96]{4,3,2,1,0:T(4,128)(2,1)} %reshape.53) | data formatting | bytes 1966080 | tf_op jit(solution)/shard_map/reshape | solution.py:180
  68.0 4.5 %all-to-all-start = ((bf16[4,4,2,160,96]{4,3,2,1,0:T(8,128)(2,1)}), bf16[4,4,2,160,96]{4,3,2,1,0:T(8,128)(2,1)}, u32[]{:S(2)}, u32[]{:S(2)}) async-start(bf16[4,4,2,160,96]{4,3,2,1,0:T(8,128)(2,1)} %bitcast.95), calls=%async_computation | async-start | bytes 2621440 | tf_op jit(solution)/shard_map/all_to_all | solution.py:184
  72.5 0.0 slice-start
  72.5 0.4 slice_bitcast_fusion
  72.9 0.6 copy.62
  73.5 0.0 slice-start.1
  73.5 0.6 pad.22.clone
  74.1 0.0 copy-start.5
  74.1 0.2 copy.45
  74.4 1.0 constant_dynamic-update-slice_fusion.8
  75.4 10.9 %collective-permute-done.8 = bf16[4,2,160,384]{3,2,1,0:T(8,128)(2,1)} collective-permute-done((bf16[4,2,160,384]{3,2,1,0:T(8,128)(2,1)S(1)}, bf16[4,2,160,384]{3,2,1,0:T(8,128)(2,1)}, u32[]{:S(2)}, u32[]{:S(2)}) %collective-permute-start.8) | collective-permute-done | bytes 983072 | tf_op jit(solution)/shard_map/ppermute | solution.py:116
  86.3 2.3 %constant_dynamic-update-slice_fusion.7 = bf16[4,4,160,384]{3,2,1,0:T(8,128)(2,1)} fusion(bf16[4,4,160,384]{3,2,1,0:T(8,128)(2,1)} %constant_dynamic-update-slice_fusion.8, bf16[4,2,160,384]{3,2,1,0:T(8,128)(2,1)} %collective-permute-done.8), kind=kLoop, calls=%fused_computation.78 | loop fusion | bytes 1966080 | tf_op jit(solution)/shard_map/concatenate | solution.py:121
  88.6 0.0 copy-start
  88.6 3.8 %fusion.44 = f32[1,2,8,21,384]{4,2,3,1,0:T(8,128)S(1)} fusion(bf16[3,3,3,384,384]{4,3,2,1,0:T(8,128)(2,1)S(1)} %bitcast.104, bf16[3,4,1,7,2,384]{5,3,4,1,0,2:T(8,128)(2,1)S(1)} %slice.38, bf16[3,4,1,8,21,384]{5,3,4,1,0,2:T(8,128)(2,1)S(1)} %copy.45, pred[8,21]{0,1:T(8,128)(4,1)S(1)} %copy-done.5), kind=kOutput, calls=%fused_computation.48 | convolution fusion | flops 2680657920 | bytes 10156200 | tf_op jit(solution)/shard_map/conv_general_dilated | solution.py:57
  92.5 0.3 copy.46
  92.7 0.2 slice.39
  92.9 0.4 multiply_reduce_fusion
  93.3 5.6 %all-to-all-done = bf16[4,4,2,160,96]{4,3,2,1,0:T(8,128)(2,1)} async-done(((bf16[4,4,2,160,96]{4,3,2,1,0:T(8,128)(2,1)}), bf16[4,4,2,160,96]{4,3,2,1,0:T(8,128)(2,1)}, u32[]{:S(2)}, u32[]{:S(2)}) %all-to-all-start) | async-done | bytes 983072 | tf_op jit(solution)/shard_map/all_to_all | solution.py:184
  99.0 1.4 %copy.49 = bf16[4,4,2,160,96]{4,3,2,1,0:T(8,128)(2,1)S(1)} copy(bf16[4,4,2,160,96]{4,3,2,0,1:T(8,128)(2,1)} %bitcast.12) | data formatting | bytes 1966080 | tf_op jit(solution)/shard_map/transpose | solution.py:185
  100.4 1.6 %fusion.11 = (bf16[6,10,160,1,96]{4,2,1,3,0:T(8,128)(2,1)S(1)}, bf16[6,10,160,1,96]{4,2,1,3,0:T(8,128)(2,1)S(1)}, bf16[6,10,160,1,96]{4,2,1,3,0:T(8,128)(2,1)S(1)}) fusion(bf16[4,8,160,96]{3,2,1,0:T(8,128)(2,1)S(1)} %bitcast.96), kind=kLoop, calls=%fused_computation.18 | loop fusion | bytes 6512640 | tf_op jit(solution)/shard_map/stack | solution.py:82
  102.0 1.9 %pad_maximum_fusion = bf16[6,10,160,3,96]{4,2,1,3,0:T(8,128)(2,1)S(1)} fusion(bf16[6,10,160,1,96]{4,2,1,3,0:T(8,128)(2,1)S(1)} %get-tuple-element.17, bf16[6,10,160,1,96]{4,2,1,3,0:T(8,128)(2,1)S(1)} %get-tuple-element.16, bf16[6,10,160,1,96]{4,2,1,3,0:T(8,128)(2,1)S(1)} %get-tuple-element.15), kind=kLoop, calls=%fused_computation.1 | loop fusion | flops 5529600 | bytes 11059200 | tf_op jit(solution)/shard_map/stack | solution.py:82
  103.9 2.5 %broadcast_select_fusion.1 = (bf16[4,4,160,384]{3,2,1,0:T(8,128)(2,1)S(1)}, bf16[4,4,160,384]{3,2,1,0:T(8,128)(2,1)S(1)}) fusion(bf16[4,4,160,384]{3,2,1,0:T(8,128)(2,1)} %constant_dynamic-update-slice_fusion.7, bf16[4,4,160,384]{3,2,1,0:T(8,128)(2,1)} %collective-permute-done.9, pred[]{:T(512)S(6)} %eq.10), kind=kLoop, calls=%fused_computation.22 | loop fusion | flops 1966080 | bytes 7864321 | tf_op jit(solution)/shard_map/jit(_where)/select_n | solution.py:123
  106.4 0.4 constant_dynamic-slice_fusion.3
  106.9 0.9 pad_maximum_fusion.1
  107.8 0.0 slice-start.2
  107.8 0.5 fusion.28
  108.3 0.0 slice-start.3
  108.3 0.6 copy.61
  108.9 0.6 pad.20.clone
  109.5 0.2 copy.40
  109.7 0.2 slice-done.2
  110.0 1.3 %slice-done.3 = s8[3768320]{0:T(1024)(128)(4,1)S(1)} async-done(((s8[7962624]{0:T(1024)(128)(4,1)}), s8[3768320]{0:T(1024)(128)(4,1)S(1)}, s32[]{:S(2)}) %slice-start.3) | async-done | bytes 3768344
  111.2 3.8 %fusion.47 = f32[1,2,8,21,384]{4,2,3,1,0:T(8,128)S(1)} fusion(bf16[3,3,3,384,384]{4,3,2,1,0:T(8,128)(2,1)S(1)} %bitcast.107, bf16[3,4,1,7,2,384]{5,3,4,1,0,2:T(8,128)(2,1)S(1)} %slice.36, bf16[3,4,1,8,21,384]{5,3,4,1,0,2:T(8,128)(2,1)S(1)} %copy.40, pred[8,21]{0,1:T(8,128)(4,1)S(1)} %copy-done.5), kind=kOutput, calls=%fused_computation.49 | convolution fusion | flops 2680657920 | bytes 10156200 | tf_op jit(solution)/shard_map/conv_general_dilated | solution.py:44
  115.1 0.3 copy.41
  115.4 0.2 slice.37
  115.6 1.7 %fusion.29 = f32[3,12,8,384]{3,2,1,0:T(8,128)S(1)} fusion(bf16[6,10,160,3,96]{4,2,1,3,0:T(8,128)(2,1)S(1)} %pad_maximum_fusion, s32[]{:T(128)S(6)} %select_n.108, s32[]{:T(128)S(6)} %select_n.110, bf16[4,2,160,384]{3,2,1,0:T(8,128)(2,1)S(1)} %get-tuple-element.14, bf16[4,2,160,384]{3,2,1,0:T(8,128)(2,1)S(1)} %get-tuple-element.22, ...), kind=kOutput, calls=%fused_computation.45 | convolution fusion | flops 1138360320 | bytes 8306696 | tf_op jit(solution)/shard_map/dot_general | solution.py:98
  117.3 1.8 %fusion.34 = f32[3,12,8,384]{3,2,1,0:T(8,128)S(1)} fusion(bf16[6,10,160,3,96]{4,2,1,3,0:T(8,128)(2,1)S(1)} %pad_maximum_fusion, s32[]{:T(128)S(6)} %select_n.112, s32[]{:T(128)S(6)} %select_n.114, bf16[4,2,160,384]{3,2,1,0:T(8,128)(2,1)S(1)} %get-tuple-element.14, bf16[4,2,160,384]{3,2,1,0:T(8,128)(2,1)S(1)} %get-tuple-element.22, ...), kind=kOutput, calls=%fused_computation.46 | convolution fusion | flops 1138360320 | bytes 8306696 | tf_op jit(solution)/shard_map/dot_general | solution.py:98
  119.1 0.0 copy-start.2
  119.2 1.7 %fusion.39 = f32[3,12,8,384]{3,2,1,0:T(8,128)S(1)} fusion(bf16[6,10,160,3,96]{4,2,1,3,0:T(8,128)(2,1)S(1)} %pad_maximum_fusion, s32[]{:T(128)S(6)} %select_n.116, s32[]{:T(128)S(6)} %select_n.118, bf16[4,2,160,384]{3,2,1,0:T(8,128)(2,1)S(1)} %get-tuple-element.14, bf16[4,2,160,384]{3,2,1,0:T(8,128)(2,1)S(1)} %get-tuple-element.22, ...), kind=kOutput, calls=%fused_computation.47 | convolution fusion | flops 1138360320 | bytes 8306696 | tf_op jit(solution)/shard_map/dot_general | solution.py:98
  120.9 1.2 add_convert_fusion
  122.1 1.6 %fusion.52 = f32[2592,96]{0,1:T(8,128)} fusion(s32[]{:T(128)S(6)} %select_n.119, f32[1152,96]{0,1:T(8,128)S(1)} %bitcast.99, f32[1152,96]{0,1:T(8,128)S(1)} %bitcast.100, f32[1152,96]{0,1:T(8,128)S(1)} %bitcast.101), kind=kLoop, calls=%fused_computation.52 | loop fusion | flops 746496 | bytes 2322436 | tf_op jit(solution)/shard_map/mul | solution.py:200
  (31 shorter events, 0.5 us)
Async XLA Ops:
  0.6 45.9 %copy-start.1 = (bf16[1,2,160,384]{3,2,1,0:T(8,128)(2,1)S(1)}, bf16[1,2,160,384]{3,2,1,0:T(8,128)(2,1)}, u32[]{:S(2)}) copy-start(bf16[1,2,160,384]{3,2,1,0:T(8,128)(2,1)} %param.9) | copy-start | bytes 737284
  4.0 15.4 %collective-permute-start = (bf16[1,2,160,768]{3,2,1,0:T(8,128)(2,1)S(1)}, bf16[1,2,160,768]{3,2,1,0:T(8,128)(2,1)S(1)}, u32[]{:S(2)}, u32[]{:S(2)}) collective-permute-start(bf16[1,2,160,768]{3,2,1,0:T(8,128)(2,1)S(1)} %pad_maximum_fusion.3), channel_id=1, source_target_pairs={{0,4},{4,8},{8,12},{1,5},{5,9},{9,13},{2,6},{6,10},{10,14},{3,7},{... | collective-permute-start | bytes 1474568 | tf_op jit(solution)/shard_map/ppermute | solution.py:141
  9.0 14.8 %collective-permute-start.3 = (bf16[1,2,160,768]{3,2,1,0:T(8,128)(2,1)S(1)}, bf16[1,2,160,768]{3,2,1,0:T(8,128)(2,1)S(1)}, u32[]{:S(2)}, u32[]{:S(2)}) collective-permute-start(bf16[1,2,160,768]{3,2,1,0:T(8,128)(2,1)S(1)} %pad_maximum_fusion.3), channel_id=1, source_target_pairs={{4,0},{8,4},{12,8},{5,1},{9,5},{13,9},{6,2},{10,6},{14,10},{7,3},{... | collective-permute-start | bytes 1474568 | tf_op jit(solution)/shard_map/ppermute | solution.py:142
  19.4 14.0 %collective-permute-start.1 = (bf16[1,2,160,768]{3,2,1,0:T(8,128)(2,1)S(1)}, bf16[1,2,160,768]{3,2,1,0:T(8,128)(2,1)S(1)}, u32[]{:S(2)}, u32[]{:S(2)}) collective-permute-start(bf16[1,2,160,768]{3,2,1,0:T(8,128)(2,1)S(1)} %collective-permute-done), channel_id=1, source_target_pairs={{0,4},{4,8},{8,12},{1,5},{5,9},{9,13},{2,6},{6,10},{10,14},{3,7},{... | collective-permute-start | bytes 1474568 | tf_op jit(solution)/shard_map/ppermute | solution.py:141
  23.8 14.0 %collective-permute-start.4 = (bf16[1,2,160,768]{3,2,1,0:T(8,128)(2,1)S(1)}, bf16[1,2,160,768]{3,2,1,0:T(8,128)(2,1)S(1)}, u32[]{:S(2)}, u32[]{:S(2)}) collective-permute-start(bf16[1,2,160,768]{3,2,1,0:T(8,128)(2,1)S(1)} %collective-permute-done.3), channel_id=1, source_target_pairs={{4,0},{8,4},{12,8},{5,1},{9,5},{13,9},{6,2},{10,6},{14,10},{7,3},{... | collective-permute-start | bytes 1474568 | tf_op jit(solution)/shard_map/ppermute | solution.py:142
  33.4 13.1 %collective-permute-start.2 = (bf16[1,2,160,768]{3,2,1,0:T(8,128)(2,1)S(1)}, bf16[1,2,160,768]{3,2,1,0:T(8,128)(2,1)S(1)}, u32[]{:S(2)}, u32[]{:S(2)}) collective-permute-start(bf16[1,2,160,768]{3,2,1,0:T(8,128)(2,1)S(1)} %collective-permute-done.1), channel_id=1, source_target_pairs={{0,4},{4,8},{8,12},{1,5},{5,9},{9,13},{2,6},{6,10},{10,14},{3,7},{... | collective-permute-start | bytes 1474568 | tf_op jit(solution)/shard_map/ppermute | solution.py:141
  37.8 12.8 %collective-permute-start.5 = (bf16[1,2,160,768]{3,2,1,0:T(8,128)(2,1)S(1)}, bf16[1,2,160,768]{3,2,1,0:T(8,128)(2,1)S(1)}, u32[]{:S(2)}, u32[]{:S(2)}) collective-permute-start(bf16[1,2,160,768]{3,2,1,0:T(8,128)(2,1)S(1)} %collective-permute-done.4), channel_id=1, source_target_pairs={{4,0},{8,4},{12,8},{5,1},{9,5},{13,9},{6,2},{10,6},{14,10},{7,3},{... | collective-permute-start | bytes 1474568 | tf_op jit(solution)/shard_map/ppermute | solution.py:142
  51.0 4.5 %collective-permute-start.7 = (bf16[3,1,160,384]{3,2,1,0:T(8,128)(2,1)S(1)}, bf16[3,1,160,384]{3,2,1,0:T(8,128)(2,1)S(1)}, u32[]{:S(2)}, u32[]{:S(2)}) collective-permute-start(bf16[3,1,160,384]{3,2,1,0:T(8,128)(2,1)S(1)} %get-tuple-element.19), channel_id=1, source_target_pairs={{1,0},{2,1},{3,2},{5,4},{6,5},{7,6},{9,8},{10,9},{11,10},{13,12},{... | collective-permute-start | bytes 1105928 | tf_op jit(solution)/shard_map/ppermute | solution.py:25
  52.3 4.3 %collective-permute-start.6 = (bf16[3,1,160,384]{3,2,1,0:T(8,128)(2,1)S(1)}, bf16[3,1,160,384]{3,2,1,0:T(8,128)(2,1)S(1)}, u32[]{:S(2)}, u32[]{:S(2)}) collective-permute-start(bf16[3,1,160,384]{3,2,1,0:T(8,128)(2,1)S(1)} %get-tuple-element.18), channel_id=1, source_target_pairs={{0,1},{1,2},{2,3},{4,5},{5,6},{6,7},{8,9},{9,10},{10,11},{12,13},{... | collective-permute-start | bytes 1105928 | tf_op jit(solution)/shard_map/ppermute | solution.py:23
  56.9 29.4 %collective-permute-start.8 = (bf16[4,2,160,384]{3,2,1,0:T(8,128)(2,1)S(1)}, bf16[4,2,160,384]{3,2,1,0:T(8,128)(2,1)}, u32[]{:S(2)}, u32[]{:S(2)}) collective-permute-start(bf16[4,2,160,384]{3,2,1,0:T(8,128)(2,1)S(1)} %get-tuple-element.5), channel_id=1, source_target_pairs={{0,2},{1,3},{2,0},{3,1},{4,6},{5,7},{6,4},{7,5},{8,10},{9,11},{10,... | collective-permute-start | bytes 2949128 | tf_op jit(solution)/shard_map/ppermute | solution.py:116
  68.0 31.0 %all-to-all-start = ((bf16[4,4,2,160,96]{4,3,2,1,0:T(8,128)(2,1)}), bf16[4,4,2,160,96]{4,3,2,1,0:T(8,128)(2,1)}, u32[]{:S(2)}, u32[]{:S(2)}) async-start(bf16[4,4,2,160,96]{4,3,2,1,0:T(8,128)(2,1)} %bitcast.95), calls=%async_computation | async-start | bytes 2621440 | tf_op jit(solution)/shard_map/all_to_all | solution.py:184
  72.5 16.1 %slice-start = ((s8[7962624]{0:T(1024)(128)(4,1)}), s8[4194304]{0:T(1024)(128)(4,1)S(1)}, s32[]{:S(2)}) async-start(s8[7962624]{0:T(1024)(128)(4,1)} %bitcast.102), calls=%async_computation.1 | async-start | bytes 8388608
  73.5 15.1 %slice-start.1 = ((s8[7962624]{0:T(1024)(128)(4,1)}), s8[3768320]{0:T(1024)(128)(4,1)S(1)}, s32[]{:S(2)}) async-start(s8[7962624]{0:T(1024)(128)(4,1)} %bitcast.102), calls=%async_computation.2 | async-start | bytes 7536640
  74.1 14.5 %copy-start.5 = (pred[8,21]{0,1:T(8,128)(4,1)S(1)}, pred[8,21]{0,1:T(8,128)(4,1)}, u32[]{:S(2)}) copy-start(pred[8,21]{0,1:T(8,128)(4,1)} %constant.124) | copy-start | bytes 508
  88.6 15.4 %collective-permute-start.9 = (bf16[4,4,160,384]{3,2,1,0:T(8,128)(2,1)}, bf16[4,4,160,384]{3,2,1,0:T(8,128)(2,1)}, u32[]{:S(2)}, u32[]{:S(2)}) collective-permute-start(bf16[4,4,160,384]{3,2,1,0:T(8,128)(2,1)} %constant_dynamic-update-slice_fusion.7), channel_id=1, source_target_pairs={{0,1},{1,0},{2,3},{3,2},{4,5},{5,4},{6,7},{7,6},{8,9},{9,8},{10,11... | collective-permute-start | bytes 5898248 | tf_op jit(solution)/shard_map/ppermute | solution.py:122
  88.6 4.3 %copy-start = (bf16[1,2,160,384]{3,2,1,0:T(8,128)(2,1)S(1)}, bf16[1,2,160,384]{3,2,1,0:T(8,128)(2,1)}, u32[]{:S(2)}) copy-start(bf16[1,2,160,384]{3,2,1,0:T(8,128)(2,1)} %param.5) | copy-start | bytes 737284
  88.6 4.3 %copy-start.3 = (f32[384]{0:T(512)S(1)}, f32[384]{0:T(512)}, u32[]{:S(2)}) copy-start(f32[384]{0:T(512)} %param.6) | copy-start | bytes 4612
  107.8 2.2 %slice-start.2 = ((s8[7962624]{0:T(1024)(128)(4,1)}), s8[4194304]{0:T(1024)(128)(4,1)S(1)}, s32[]{:S(2)}) async-start(s8[7962624]{0:T(1024)(128)(4,1)} %bitcast.105), calls=%async_computation.3 | async-start | bytes 8388608
  108.3 3.0 %slice-start.3 = ((s8[7962624]{0:T(1024)(128)(4,1)}), s8[3768320]{0:T(1024)(128)(4,1)S(1)}, s32[]{:S(2)}) async-start(s8[7962624]{0:T(1024)(128)(4,1)} %bitcast.105), calls=%async_computation.4 | async-start | bytes 7536640
  119.1 1.8 %copy-start.2 = (bf16[1,2,160,384]{3,2,1,0:T(8,128)(2,1)S(1)}, bf16[1,2,160,384]{3,2,1,0:T(8,128)(2,1)}, u32[]{:S(2)}) copy-start(bf16[1,2,160,384]{3,2,1,0:T(8,128)(2,1)} %param.9) | copy-start | bytes 737284
  119.2 1.8 %copy-start.4 = (f32[384]{0:T(512)S(1)}, f32[384]{0:T(512)}, u32[]{:S(2)}) copy-start(f32[384]{0:T(512)} %param.7) | copy-start | bytes 4612
